TPU v7x, 512 devices: a whole 4x4x16 slice. The times are simulated.
512 devices in a mesh: band: 16 (over x, y), lon: 32 (over z, core).
Axes of the slice: x: 4, y: 4, z: 16, core: 2. Of those that a mesh axis runs over, the one named last changes fastest.
Arguments:
- sky_maps: float32 [16, 8192, 256], P(None, ('band', 'lon')), may hold values from -9 to 9
- noise_var: float32 [8192, 256], P(('band', 'lon')), may hold values from 1 to 4
- position: float32 [3, 8192, 256], P(None, ('band', 'lon')), may hold values from -1 to 1
- leaf_basis: float32 [8192, 256, 64], P(('band', 'lon')), may hold values from -1 to 1
- leaf_couple: float32 [8192, 4, 64, 64], P(('band', 'lon')), as said below
- transfer: float32 [8192, 64, 64], P(('band', 'lon')), may hold values from -2 to 2
- panel_couple: float32 [1024, 2, 64, 64], P(('band', 'lon')), as said below
- near_list: int32 [8192, 5], P(('band', 'lon')), may hold values from -1 to 8191, as said below
- far_list: int32 [8192, 4], P(('band', 'lon')), may hold values from 0 to 8191, as said below
- panel_list: int32 [1024, 2], P(('band', 'lon')), may hold values from 0 to 1023, as said below
- leaf_panel: int32 [8192], P(('band', 'lon')), may hold values from 0 to 1
Outputs:
- solution: float32 [16, 8192, 256], P(None, ('band', 'lon'))
- residual: float32 [16, 8192, 256], P(None, ('band', 'lon'))
Inputs may be any that keep to these rules, and one draw needn't show every extreme that they name: `near_list`: entry 0 of a row is the leaf itself; the entries after it that are not -1 come first and are distinct leaves of the same band at cycle distance 1 or 2, the cycle closing; leaf j stands in leaf i's row exactly when i stands in j's. `far_list`: distinct leaves of the same band at cycle distance 3 to 6, the cycle closing; leaf j stands in leaf i's row exactly when i stands in j's. If leaf j stands in slot s of far_list[i] and leaf i in slot t of far_list[j], then leaf_couple[j, t] is the transpose of leaf_couple[i, s]. `panel_list`: entries are panel s of sectors of other bands at the same longitude (sector ids differing by a nonzero multiple of the sectors of a band), s being the panel's own index in its sector; panel j stands in panel k's row as often as k stands in j's. If panel j stands in slot s of panel_list[k] and these slots pair up with the slots t of panel_list[j] that hold k, then panel_couple[j, t] is the transpose of panel_couple[k, s].
All inputs are finite; a program needn't handle non-finite values.
Results may differ from a plain program's by a relative error of at most 0.0003.
Values sent between devices are 32-bit elements; how exact they have to be, the bound alone decides.
No kernel may reach another device: no remote copies, remote signals or barrier semaphores. Data moves between devices by JAX's collectives and lax.ppermute only.
A program may use at most 128 MiB of HBM per device.

v0:
```python
import math

import jax
import jax.numpy as jnp
from jax import lax
from jax.sharding import PartitionSpec as P

REACH = 6
ITERS = 2


HIGHEST_PRECISION = lax.Precision.HIGHEST
ROOT_THREE = math.sqrt(3.0)
AMPLITUDE = 0.02


def extended(cells, sides, width):
    for axis, dim in sides:
        count = lax.axis_size(axis)
        head = lax.slice_in_dim(cells, 0, width, axis=dim)
        tail = lax.slice_in_dim(cells, cells.shape[dim] - width, cells.shape[dim], axis=dim)
        cells = jnp.concatenate(
            [
                lax.ppermute(tail, axis, [(i, (i + 1) % count) for i in range(count)]),
                cells,
                lax.ppermute(head, axis, [((i + 1) % count, i) for i in range(count)]),
            ],
            axis=dim,
        )
    return cells


def matern_block(rows_pos, cols_pos, length_scale):
    squared = jnp.zeros((cols_pos.shape[1], rows_pos.shape[1], cols_pos.shape[2]), jnp.float32)
    for component in range(3):
        offset = rows_pos[component][None, :, None] - cols_pos[component][:, None, :]
        squared = squared + offset * offset
    scaled = ROOT_THREE * jnp.sqrt(squared) / length_scale
    return AMPLITUDE * (1.0 + scaled) * jnp.exp(-scaled)


def on_device(
    sky_maps,
    noise_var,
    position,
    leaf_basis,
    leaf_couple,
    transfer,
    panel_couple,
    near_list,
    far_list,
    panel_list,
    leaf_panel,
):
    lon_index = lax.axis_index("lon")
    lon_count = lax.axis_size("lon")
    local_leaves = sky_maps.shape[1]
    pixel_count = sky_maps.shape[2]
    cycle_size = local_leaves * lon_count
    panel_count = panel_couple.shape[0]
    length_scale = 2.0 * math.pi / cycle_size
    first_leaf = lon_index * local_leaves
    near_depth = 2

    def rim_index(leaf_ids, depth):
        return (leaf_ids % cycle_size - first_leaf + depth) % cycle_size

    near_valid = near_list >= 0
    near_rows = rim_index(jnp.where(near_valid, near_list, near_list[:, :1]), near_depth)
    far_rows = rim_index(far_list, REACH)
    rim_pos = extended(position, (("lon", 1),), near_depth)

    def leaf_blocks(inputs):
        rows_pos, rows_index, slot_mask = inputs
        cols_pos = rim_pos[:, rows_index]
        return matern_block(rows_pos, cols_pos, length_scale) * slot_mask[:, None, None]

    near_blocks = lax.map(
        leaf_blocks, (jnp.transpose(position, (1, 0, 2)), near_rows, near_valid.astype(jnp.float32))
    )
    band_slot = panel_list // (lon_count * panel_count)
    gathered_rows = band_slot * panel_count + panel_list % panel_count
    membership = (leaf_panel[:, None] == jnp.arange(panel_count, dtype=jnp.int32)[None, :]).astype(
        jnp.float32
    )

    def square_total(vector):
        return lax.psum(jnp.sum(vector * vector, axis=(1, 2)), ("band", "lon"))

    solution = jnp.zeros_like(sky_maps)
    residual = sky_maps
    direction = sky_maps
    norm_now = square_total(residual)
    for iteration in range(ITERS):
        coeffs = jnp.einsum("lpr,mlp->mlr", leaf_basis, direction, precision=HIGHEST_PRECISION)
        joined = jnp.concatenate([direction, coeffs], axis=2)
        rim_joined = extended(joined, (("lon", 1),), REACH)
        rim_values = rim_joined[
            :, REACH - near_depth : REACH + local_leaves + near_depth, :pixel_count
        ]
        rim_coeffs = rim_joined[:, :, pixel_count:]
        near_part = jnp.einsum(
            "lspq,mlsq->mlp", near_blocks, rim_values[:, near_rows], precision=HIGHEST_PRECISION
        )
        leaf_far = jnp.einsum(
            "lsab,mlsb->mla", leaf_couple, rim_coeffs[:, far_rows], precision=HIGHEST_PRECISION
        )
        upward = jnp.einsum("lab,mla->mlb", transfer, coeffs, precision=HIGHEST_PRECISION)
        panel_coeffs = jnp.einsum("lk,mlb->mkb", membership, upward, precision=HIGHEST_PRECISION)
        band_coeffs = lax.all_gather(panel_coeffs, "band", axis=1, tiled=True)
        panel_far = jnp.einsum(
            "ksab,mksb->mka",
            panel_couple,
            band_coeffs[:, gathered_rows],
            precision=HIGHEST_PRECISION,
        )
        downward = jnp.einsum("lk,mkb->mlb", membership, panel_far, precision=HIGHEST_PRECISION)
        leaf_far = leaf_far + jnp.einsum(
            "lab,mlb->mla", transfer, downward, precision=HIGHEST_PRECISION
        )
        far_part = jnp.einsum("lpr,mlr->mlp", leaf_basis, leaf_far, precision=HIGHEST_PRECISION)
        applied = noise_var[None] * direction + near_part + far_part
        curvature_sum = lax.psum(jnp.sum(direction * applied, axis=(1, 2)), ("band", "lon"))
        step_size = norm_now / curvature_sum
        solution = solution + step_size[:, None, None] * direction
        residual = residual - step_size[:, None, None] * applied
        if iteration + 1 < ITERS:
            norm_next = square_total(residual)
            direction = residual + (norm_next / norm_now)[:, None, None] * direction
            norm_now = norm_next
    return (solution, residual)


def solution(mesh):
    placed = (
        P(None, ("band", "lon"), None),
        P(("band", "lon"), None),
        P(None, ("band", "lon"), None),
        P(("band", "lon"), None, None),
        P(("band", "lon"), None, None, None),
        P(("band", "lon"), None, None),
        P(("band", "lon"), None, None, None),
        P(("band", "lon"), None),
        P(("band", "lon"), None),
        P(("band", "lon"), None),
        P(("band", "lon")),
    )
    return jax.shard_map(
        on_device,
        mesh=mesh,
        in_specs=placed,
        out_specs=(P(None, ("band", "lon"), None), P(None, ("band", "lon"), None)),
        check_vma=False,
    )
```

profile of v0, /device:TPU:1, one launch (start us, length us, event | category | flops | bytes accessed | tf_op | source)
XLA Modules:
  0.0 555.7 jit_solution(6584740147777887504)
XLA Ops:
  1.7 3.0 collective-permute-start.2
  4.7 4.4 collective-permute-start.3
  13.5 3.6 collective-permute-start.1
  20.4 20.6 %all_gather.6 = f32[16,32,64]{2,0,1:T(8,128)} all-gather(f32[16,2,64]{2,0,1:T(8,128)S(1)} %copy.56), channel_id=1, replica_groups=mesh['band'=16,'lon'=32] {'band'}, dimensions={1}, use_global_device_ids=true | all-gather | bytes 139264 | tf_op jit(solution)/shard_map/all_gather | solution.py:110
  46.6 98.0 %while.12 = (s32[]{:T(128)}, f32[16,5,256,256]{3,2,1,0:T(8,128)}, f32[16,3,256]{2,1,0:T(4,128)}, s32[16,5]{1,0:T(8,128)S(1)}, f32[3,20,256]{2,0,1:T(4,128)S(1)},...) while((s32[]{:T(128)}, f32[16,5,256,256]{3,2,1,0:T(8,128)}, f32[16,3,256]{2,1,0:T(4,128)}, ...), condition=%wide.region_3.4_spmd, body=%wide.region_2.3_spmd.sunk | while | flops 4588563 | bytes 1434957 | solution.py:78
  50.1 2.8 multiply_dynamic-update-slice_fusion.2
  56.2 2.8 multiply_dynamic-update-slice_fusion.2
  62.3 2.8 multiply_dynamic-update-slice_fusion.2
  68.4 2.8 multiply_dynamic-update-slice_fusion.2
  74.5 2.8 multiply_dynamic-update-slice_fusion.2
  80.6 2.8 multiply_dynamic-update-slice_fusion.2
  86.7 2.9 multiply_dynamic-update-slice_fusion.2
  92.9 2.8 multiply_dynamic-update-slice_fusion.2
  99.0 2.8 multiply_dynamic-update-slice_fusion.2
  105.1 2.9 multiply_dynamic-update-slice_fusion.2
  111.3 2.8 multiply_dynamic-update-slice_fusion.2
  117.3 2.8 multiply_dynamic-update-slice_fusion.2
  123.5 2.8 multiply_dynamic-update-slice_fusion.2
  129.6 2.9 multiply_dynamic-update-slice_fusion.2
  135.7 2.8 multiply_dynamic-update-slice_fusion.2
  141.8 2.8 multiply_dynamic-update-slice_fusion.2
  146.2 2.5 gather_fusion.2
  148.7 2.9 convolution_bitcast_fusion.9
  155.8 21.5 %fusion.6 = f32[16,16,256]{2,0,1:T(8,128)S(1)} fusion(f32[16,16,5,256]{3,0,2,1:T(8,128)} %bitcast.154, f32[16,5,256,256]{3,2,1,0:T(8,128)} %get-tuple-element.79, f32[16,256]{1,0:T(8,128)S(1)} %copy-done.23, f32[16,16,256]{2,1,0:T(8,128)S(1)} %copy-done.1), kind=kOutput, calls=%fused_computation.28 | convolution fusion | flops 1006764032 | bytes 22822912 | tf_op jit(solution)/shard_map/lspq,mlsq->mlp/dot_general | solution.py:102
  178.1 107.3 %all-reduce = (f32[16]{0:T(128)S(1)}, f32[16]{0:T(128)S(1)}) all-reduce(f32[16]{0:T(128)S(1)} %copy-done.33, f32[16]{0:T(128)S(1)} %get-tuple-element.120), channel_id=1, replica_groups=mesh['band'=16,'lon'=32] {'band','lon'}, use_global_device_ids=true, to_apply=%region_1.2 | all-reduce | flops 32 | bytes 256 | tf_op jit(solution)/shard_map/psum | solution.py:88
  285.7 100.1 %psum.30 = f32[16]{0:T(128)S(1)} all-reduce(f32[16]{0:T(128)S(1)} %multiply_reduce_fusion.1), channel_id=1, replica_groups=mesh['band'=16,'lon'=32] {'band','lon'}, use_global_device_ids=true, to_apply=%region_7.8 | all-reduce | flops 16 | bytes 128 | tf_op jit(solution)/shard_map/psum | solution.py:88
  389.8 17.5 %all_gather.7 = f32[16,32,64]{2,0,1:T(8,128)S(1)} all-gather(f32[16,2,64]{2,0,1:T(8,128)S(1)} %copy.64), channel_id=1, replica_groups=mesh['band'=16,'lon'=32] {'band'}, dimensions={1}, use_global_device_ids=true | all-gather | bytes 139264 | tf_op jit(solution)/shard_map/all_gather | solution.py:110
  409.1 5.9 %collective-permute-start.4 = (f32[16,6,320]{2,0,1:T(8,128)}, f32[16,6,320]{2,0,1:T(8,128)S(1)}, u32[]{:S(2)}, u32[]{:S(2)}) collective-permute-start(f32[16,6,320]{2,0,1:T(8,128)} %get-tuple-element.110), channel_id=1, source_target_pairs={{0,1},{1,2},{2,3},{3,4},{4,5},{5,6},{6,7},{7,8},{8,9},{9,10},{10,1... | collective-permute-start | bytes 368648 | tf_op jit(solution)/shard_map/ppermute | solution.py:24
  417.5 2.7 collective-permute-done.5
  423.2 3.6 convolution_bitcast_fusion.6
  428.6 21.5 %fusion.5 = f32[16,16,256]{2,0,1:T(8,128)S(1)} fusion(f32[16,16,5,256]{3,0,2,1:T(8,128)} %bitcast.153, f32[16,5,256,256]{3,2,1,0:T(8,128)} %get-tuple-element.79, f32[16,16,256]{2,0,1:T(8,128)S(1)} %multiply_add_fusion.1, f32[16,256]{1,0:T(8,128)S(1)} %copy-done.23), kind=kOutput, calls=%fused_computation.26 | convolution fusion | flops 1006764032 | bytes 22822912 | tf_op jit(solution)/shard_map/lspq,mlsq->mlp/dot_general | solution.py:102
  451.8 102.0 %psum.31 = f32[16]{0:T(128)S(1)} all-reduce(f32[16]{0:T(128)S(1)} %get-tuple-element.122), channel_id=1, replica_groups=mesh['band'=16,'lon'=32] {'band','lon'}, use_global_device_ids=true, to_apply=%region_9.10 | all-reduce | flops 16 | bytes 128 | tf_op jit(solution)/shard_map/psum | solution.py:123
  (317 shorter events, 89.7 us)
Async XLA Ops:
  0.6 148.0 %copy-start = (f32[16,4,64,64]{3,2,1,0:T(8,128)S(1)}, f32[16,4,64,64]{3,2,1,0:T(8,128)}, u32[]{:S(2)}) copy-start(f32[16,4,64,64]{3,2,1,0:T(8,128)} %param.17) | copy-start | bytes 3145732
  1.7 43.5 %collective-permute-start.2 = (f32[3,2,256]{2,0,1:T(4,128)S(1)}, f32[3,2,256]{2,0,1:T(4,128)S(1)}, u32[]{:S(2)}, u32[]{:S(2)}) collective-permute-start(f32[3,2,256]{2,0,1:T(4,128)S(1)} %get-tuple-element.116), channel_id=1, source_target_pairs={{0,1},{1,2},{2,3},{3,4},{4,5},{5,6},{6,7},{7,8},{8,9},{9,10},{10,1... | collective-permute-start | bytes 18440 | tf_op jit(solution)/shard_map/ppermute | solution.py:24
  4.7 12.3 %copy-start.1 = (f32[16,16,256]{2,1,0:T(8,128)S(1)}, f32[16,16,256]{2,1,0:T(8,128)}, u32[]{:S(2)}) copy-start(f32[16,16,256]{2,1,0:T(8,128)} %param.13) | copy-start | bytes 786436
  4.7 41.0 %collective-permute-start.3 = (f32[3,2,256]{2,0,1:T(4,128)S(1)}, f32[3,2,256]{2,0,1:T(4,128)}, u32[]{:S(2)}, u32[]{:S(2)}) collective-permute-start(f32[3,2,256]{2,0,1:T(4,128)S(1)} %get-tuple-element.117), channel_id=1, source_target_pairs={{1,0},{2,1},{3,2},{4,3},{5,4},{6,5},{7,6},{8,7},{9,8},{10,9},{11,1... | collective-permute-start | bytes 18440 | tf_op jit(solution)/shard_map/ppermute | solution.py:26
  10.2 7.6 %copy-start.30 = (s32[16,5]{0,1:T(8,128)S(1)}, s32[16,5]{0,1:T(8,128)}, u32[]{:S(2)}) copy-start(s32[16,5]{0,1:T(8,128)} %param.20) | copy-start | bytes 964
  10.3 7.7 %copy-start.32 = (s32[2,2]{1,0:T(2,128)S(1)}, s32[2,2]{1,0:T(2,128)}, u32[]{:S(2)}) copy-start(s32[2,2]{1,0:T(2,128)} %param.22) | copy-start | bytes 52
  10.3 7.8 %copy-start.31 = (s32[16,4]{0,1:T(4,128)S(1)}, s32[16,4]{0,1:T(4,128)}, u32[]{:S(2)}) copy-start(s32[16,4]{0,1:T(4,128)} %param.21) | copy-start | bytes 772
  10.3 9.4 %copy-start.4 = (f32[16,64,64]{2,1,0:T(8,128)S(1)}, f32[16,64,64]{2,1,0:T(8,128)}, u32[]{:S(2)}) copy-start(f32[16,64,64]{2,1,0:T(8,128)} %param.18) | copy-start | bytes 786436
  10.3 9.9 %copy-start.25 = (s32[16]{0:T(128)S(1)}, s32[16]{0:T(128)}, u32[]{:S(2)}) copy-start(s32[16]{0:T(128)} %param.23) | copy-start | bytes 196
  12.7 131.9 %copy-start.7 = (f32[16,16,64]{2,0,1:T(8,128)}, f32[16,16,64]{2,0,1:T(8,128)S(1)}, u32[]{:S(2)}) copy-start(f32[16,16,64]{2,0,1:T(8,128)S(1)} %convolution_bitcast_fusion.11) | copy-start | bytes 196612
  13.5 131.1 %collective-permute-start = (f32[16,6,320]{2,0,1:T(8,128)}, f32[16,6,320]{2,0,1:T(8,128)S(1)}, u32[]{:S(2)}, u32[]{:S(2)}) collective-permute-start(f32[16,6,320]{2,0,1:T(8,128)} %get-tuple-element.112), channel_id=1, source_target_pairs={{0,1},{1,2},{2,3},{3,4},{4,5},{5,6},{6,7},{7,8},{8,9},{9,10},{10,1... | collective-permute-start | bytes 368648 | tf_op jit(solution)/shard_map/ppermute | solution.py:24
  13.5 131.1 %collective-permute-start.1 = (f32[16,6,320]{2,0,1:T(8,128)}, f32[16,6,320]{2,0,1:T(8,128)}, u32[]{:S(2)}, u32[]{:S(2)}) collective-permute-start(f32[16,6,320]{2,0,1:T(8,128)} %get-tuple-element.113), channel_id=1, source_target_pairs={{1,0},{2,1},{3,2},{4,3},{5,4},{6,5},{7,6},{8,7},{9,8},{10,9},{11,1... | collective-permute-start | bytes 368648 | tf_op jit(solution)/shard_map/ppermute | solution.py:26
  18.0 28.6 %copy-start.24 = (s32[1024]{0:T(1024)}, s32[1024]{0:T(1024)S(1)}, u32[]{:S(2)}) copy-start(s32[1024]{0:T(1024)S(1)} %pad_clamp_fusion.1) | copy-start | bytes 12292
  95.7 3.2 copy-start.27
  108.0 3.2 copy-start.27
  138.5 3.2 copy-start.27
  144.6 6.9 %copy-start.11 = (f32[16,6,320]{2,0,1:T(8,128)}, f32[16,6,320]{2,0,1:T(8,128)S(1)}, u32[]{:S(2)}) copy-start(f32[16,6,320]{2,0,1:T(8,128)S(1)} %collective-permute-done) | copy-start | bytes 368644
  148.7 4.5 copy-start.8
  155.8 21.5 %copy-start.2 = (f32[16,256,64]{1,2,0:T(8,128)S(1)}, f32[16,256,64]{1,2,0:T(8,128)}, u32[]{:S(2)}) copy-start(f32[16,256,64]{1,2,0:T(8,128)} %param.16) | copy-start | bytes 3145732
  155.8 21.5 %copy-start.16 = (f32[16,16,64]{2,0,1:T(8,128)S(1)}, f32[16,16,64]{2,0,1:T(8,128)}, u32[]{:S(2)}) copy-start(f32[16,16,64]{2,0,1:T(8,128)} %fusion.8) | copy-start | bytes 196612
  178.1 210.1 %copy-start.5 = (f32[16,16,256]{2,0,1:T(8,128)}, f32[16,16,256]{2,0,1:T(8,128)S(1)}, u32[]{:S(2)}) copy-start(f32[16,16,256]{2,0,1:T(8,128)S(1)} %get-tuple-element.121) | copy-start | bytes 786436
  386.0 3.6 copy-start.26
  388.9 32.8 %copy-start.21 = (s32[1024]{0:T(1024)S(1)}, s32[1024]{0:T(1024)}, u32[]{:S(2)}) copy-start(s32[1024]{0:T(1024)} %pad_clamp_fusion.2) | copy-start | bytes 12292
  409.1 8.3 %collective-permute-start.4 = (f32[16,6,320]{2,0,1:T(8,128)}, f32[16,6,320]{2,0,1:T(8,128)S(1)}, u32[]{:S(2)}, u32[]{:S(2)}) collective-permute-start(f32[16,6,320]{2,0,1:T(8,128)} %get-tuple-element.110), channel_id=1, source_target_pairs={{0,1},{1,2},{2,3},{3,4},{4,5},{5,6},{6,7},{7,8},{8,9},{9,10},{10,1... | collective-permute-start | bytes 368648 | tf_op jit(solution)/shard_map/ppermute | solution.py:24
  415.0 5.1 collective-permute-start.5
  423.2 3.6 copy-start.10
  423.2 3.6 copy-start.13
  423.2 3.6 copy-start.15
  428.6 21.5 %copy-start.18 = (f32[16,16,64]{2,1,0:T(8,128)S(1)}, f32[16,16,64]{2,1,0:T(8,128)}, u32[]{:S(2)}) copy-start(f32[16,16,64]{2,1,0:T(8,128)} %convolution_bitcast_fusion.4) | copy-start | bytes 196612
  428.6 21.5 %copy-start.19 = (f32[16,16,64]{2,1,0:T(8,128)S(1)}, f32[16,16,64]{2,1,0:T(8,128)}, u32[]{:S(2)}) copy-start(f32[16,16,64]{2,1,0:T(8,128)} %convolution_bitcast_fusion.6) | copy-start | bytes 196612
  428.6 22.4 %copy-start.3 = (f32[16,256,64]{1,2,0:T(8,128)S(1)}, f32[16,256,64]{1,2,0:T(8,128)}, u32[]{:S(2)}) copy-start(f32[16,256,64]{1,2,0:T(8,128)} %param.16) | copy-start | bytes 3145732
  450.1 103.7 %copy-start.6 = (f32[16,16,256]{2,0,1:T(8,128)S(1)}, f32[16,16,256]{2,0,1:T(8,128)}, u32[]{:S(2)}) copy-start(f32[16,16,256]{2,0,1:T(8,128)} %copy-done.5) | copy-start | bytes 786436
  (38 other events, 103.1 us)
where the time goes:
time: 558 us; the launch traced here: 556 us
  blocking collectives  347 us (62%)
  local copies, waits for them, and re-layouts  67.1 us (12%)
  matrix products  63.6 us (11%)
  other arithmetic  54.6 us (10%)
  starting transfers between devices  16.9 us (3%)
    psum x2, blocking collectives, square_total(): return lax.psum(jnp.sum(vector * vector, axis=(1, 2)), ('band', 'lon'))  207 us
    psum x1, blocking collectives, on_device(): lax.psum(jnp.sum(direction * applied, axis=(1, 2)), ('band', 'lon'))  102 us
    dynamic_update_slice x16, other arithmetic, on_device(): lax.map(leaf_blocks, (jnp.transpose(position, (1, 0, 2)), near_rows, near...  45.3 us
    dot_general x2, matrix products, on_device(): jnp.einsum('lspq,mlsq->mlp', near_blocks, rim_values[:, near_rows], preci...  42.9 us
    all_gather x2, blocking collectives, on_device(): band_coeffs = lax.all_gather(panel_coeffs, 'band', axis=1, tiled=True)  38 us
    slice x16, local copies, waits for them, and re-layouts, matern_block(): rows_pos[component][None, :, None] - cols_pos[component][:, None, :]  22 us
    mul x16, local copies, waits for them, and re-layouts, leaf_blocks(): matern_block(rows_pos, cols_pos, length_scale) * slot_mask[:, None, None]  20 us
  transfers between devices with their start and end apart: 6, of which 2 were waited for; matrix products, arithmetic and copies ran while one was open for 20% of the time, Pallas kernels for 0%

commit v1 on v0

--- a/solution.py
+++ b/solution.py
@@ -28,6 +28,21 @@
             axis=dim,
         )
     return cells
+
+
+def all_sum(vector, axes):
+    for axis in axes:
+        count = lax.axis_size(axis)
+        if count & (count - 1):
+            vector = lax.psum(vector, axis)
+            continue
+        stride = 1
+        while stride < count:
+            vector = vector + lax.ppermute(
+                vector, axis, [(i, i ^ stride) for i in range(count)]
+            )
+            stride *= 2
+    return vector
 
 
 def matern_block(rows_pos, cols_pos, length_scale):
@@ -75,8 +90,8 @@
         cols_pos = rim_pos[:, rows_index]
         return matern_block(rows_pos, cols_pos, length_scale) * slot_mask[:, None, None]
 
-    near_blocks = lax.map(
-        leaf_blocks, (jnp.transpose(position, (1, 0, 2)), near_rows, near_valid.astype(jnp.float32))
+    near_blocks = jax.vmap(lambda *leaf: leaf_blocks(leaf))(
+        jnp.transpose(position, (1, 0, 2)), near_rows, near_valid.astype(jnp.float32)
     )
     band_slot = panel_list // (lon_count * panel_count)
     gathered_rows = band_slot * panel_count + panel_list % panel_count
@@ -85,13 +100,9 @@
     )
 
     def square_total(vector):
-        return lax.psum(jnp.sum(vector * vector, axis=(1, 2)), ("band", "lon"))
+        return all_sum(jnp.sum(vector * vector, axis=(1, 2)), ("lon", "band"))
 
-    solution = jnp.zeros_like(sky_maps)
-    residual = sky_maps
-    direction = sky_maps
-    norm_now = square_total(residual)
-    for iteration in range(ITERS):
+    def covariance_apply(direction):
         coeffs = jnp.einsum("lpr,mlp->mlr", leaf_basis, direction, precision=HIGHEST_PRECISION)
         joined = jnp.concatenate([direction, coeffs], axis=2)
         rim_joined = extended(joined, (("lon", 1),), REACH)
@@ -119,14 +130,24 @@
             "lab,mlb->mla", transfer, downward, precision=HIGHEST_PRECISION
         )
         far_part = jnp.einsum("lpr,mlr->mlp", leaf_basis, leaf_far, precision=HIGHEST_PRECISION)
-        applied = noise_var[None] * direction + near_part + far_part
-        curvature_sum = lax.psum(jnp.sum(direction * applied, axis=(1, 2)), ("band", "lon"))
+        return noise_var[None] * direction + near_part + far_part
+
+    solution = jnp.zeros_like(sky_maps)
+    residual = sky_maps
+    direction = sky_maps
+    norm_now = square_total(residual)
+    applied = covariance_apply(direction)
+    for iteration in range(ITERS):
+        curvature_sum = all_sum(jnp.sum(direction * applied, axis=(1, 2)), ("lon", "band"))
         step_size = norm_now / curvature_sum
         solution = solution + step_size[:, None, None] * direction
         residual = residual - step_size[:, None, None] * applied
         if iteration + 1 < ITERS:
             norm_next = square_total(residual)
-            direction = residual + (norm_next / norm_now)[:, None, None] * direction
+            applied_residual = covariance_apply(residual)
+            ratio = (norm_next / norm_now)[:, None, None]
+            direction = residual + ratio * direction
+            applied = applied_residual + ratio * applied
             norm_now = norm_next
     return (solution, residual)
 

time: 558 us -> 394 us (0.71)
  the two profiles are of different devices: /device:TPU:1 before, /device:TPU:32 now
where the time goes in v1:
time: 394 us; the launch traced here: 392 us
  starting transfers between devices  140 us (36%)
  waiting for transfers between devices  85.8 us (22%)
  matrix products  85 us (22%)
  blocking collectives  44.7 us (11%)
  local copies, waits for them, and re-layouts  20.7 us (5%)
  other arithmetic  13.6 us (3%)
    ppermute x36, starting transfers between devices, all_sum(): lax.ppermute(vector, axis, [(i, i ^ stride) for i in range(count)])  133 us
    ppermute x36, waiting for transfers between devices, all_sum(): lax.ppermute(vector, axis, [(i, i ^ stride) for i in range(count)])  85.7 us
    dot_general x2, matrix products, covariance_apply(): jnp.einsum('lspq,mlsq->mlp', near_blocks, rim_values[:, near_rows], preci...  66.9 us
    all_gather x2, blocking collectives, covariance_apply(): band_coeffs = lax.all_gather(panel_coeffs, 'band', axis=1, tiled=True)  44.7 us
  transfers between devices with their start and end apart: 42, of which 26 were waited for; matrix products, arithmetic and copies ran while one was open for 17% of the time, Pallas kernels for 0%

profile of v1, /device:TPU:32, one launch (start us, length us, event | category | flops | bytes accessed | tf_op | source)
XLA Modules:
  0.0 391.8 jit_solution(15250787226746953187)
XLA Ops:
  6.4 5.1 %collective-permute-start.12 = (f32[3,2,256]{2,0,1:T(4,128)}, f32[3,2,256]{2,0,1:T(4,128)}, u32[]{:S(2)}, u32[]{:S(2)}) collective-permute-start(f32[3,2,256]{2,0,1:T(4,128)} %get-tuple-element.24), channel_id=1, source_target_pairs={{1,0},{2,1},{3,2},{4,3},{5,4},{6,5},{7,6},{8,7},{9,8},{10,9},{11,1... | collective-permute-start | bytes 18440 | tf_op jit(solution)/shard_map/ppermute | solution.py:26
  21.0 20.7 %all_gather.6 = f32[16,32,64]{2,0,1:T(8,128)S(1)} all-gather(f32[16,2,64]{2,0,1:T(8,128)S(1)} %copy.55), channel_id=1, replica_groups=mesh['band'=16,'lon'=32] {'band'}, dimensions={1}, use_global_device_ids=true | all-gather | bytes 139264 | tf_op jit(solution)/shard_map/all_gather | solution.py:121
  44.9 10.6 %collective-permute-start.1 = (f32[16]{0:T(128)S(1)}, f32[16]{0:T(128)S(1)}, u32[]{:S(2)}, u32[]{:S(2)}) collective-permute-start(f32[16]{0:T(128)S(1)} %add.208), channel_id=1, source_target_pairs={{0,2},{1,3},{2,0},{3,1},{4,6},{5,7},{6,4},{7,5},{8,10},{9,11},{10,... | collective-permute-start | bytes 200 | tf_op jit(solution)/shard_map/ppermute | solution.py:41
  59.5 3.8 collective-permute-done.2
  67.1 5.5 %collective-permute-done.3 = f32[16]{0:T(128)S(1)} collective-permute-done((f32[16]{0:T(128)S(1)}, f32[16]{0:T(128)S(1)}, u32[]{:S(2)}, u32[]{:S(2)}) %collective-permute-start.3) | collective-permute-done | bytes 96 | tf_op jit(solution)/shard_map/ppermute | solution.py:41
  73.2 9.1 %collective-permute-start.4 = (f32[16]{0:T(128)}, f32[16]{0:T(128)}, u32[]{:S(2)}, u32[]{:S(2)}) collective-permute-start(f32[16]{0:T(128)} %add.211), channel_id=1, source_target_pairs={{0,16},{1,17},{2,18},{3,19},{4,20},{5,21},{6,22},{7,23},{8,24},{9,... | collective-permute-start | bytes 200 | tf_op jit(solution)/shard_map/ppermute | solution.py:41
  94.0 32.2 %fusion.27 = f32[16,16,256]{2,0,1:T(8,128)S(1)} fusion(f32[16,16,5,256]{3,0,2,1:T(8,128)S(1)} %bitcast.127, f32[16,5]{1,0:T(8,128)S(1)} %copy-done.39, f32[16,5,256]{2,1,0:T(8,128)S(1)} %copy-done.26, f32[16,256]{1,0:T(8,128)S(1)} %copy-done.32, f32[16,5,256]{2,1,0:T(8,128)S(1)} %copy-done.25, f32[16,256]{1,0:T(8,128)S(1)} %copy-done.34, ...), kind=kOutput, calls=%fused_computation.37 | convolution fusion | flops 1080164352 | bytes 2146624 | tf_op jit(solution)/shard_map/lspq,mlsq->mlp/dot_general | solution.py:113
  130.1 3.9 collective-permute-start.14
  139.5 4.0 %collective-permute-done.15 = f32[16]{0:T(128)S(1)} collective-permute-done((f32[16]{0:T(128)S(1)}, f32[16]{0:T(128)S(1)}, u32[]{:S(2)}, u32[]{:S(2)}) %collective-permute-start.15) | collective-permute-done | bytes 96 | tf_op jit(solution)/shard_map/ppermute | solution.py:41
  143.5 4.3 %collective-permute-start.16 = (f32[16]{0:T(128)S(1)}, f32[16]{0:T(128)S(1)}, u32[]{:S(2)}, u32[]{:S(2)}) collective-permute-start(f32[16]{0:T(128)S(1)} %add.240), channel_id=1, source_target_pairs={{0,8},{1,9},{2,10},{3,11},{4,12},{5,13},{6,14},{7,15},{8,0},{9,1},... | collective-permute-start | bytes 200 | tf_op jit(solution)/shard_map/ppermute | solution.py:41
  147.8 4.6 %collective-permute-start.6 = (f32[16]{0:T(128)S(1)}, f32[16]{0:T(128)S(1)}, u32[]{:S(2)}, u32[]{:S(2)}) collective-permute-start(f32[16]{0:T(128)S(1)} %add.213), channel_id=1, source_target_pairs={{0,64},{32,96},{64,0},{96,32},{128,192},{160,224},{192,128},{224,1... | collective-permute-start | bytes 200 | tf_op jit(solution)/shard_map/ppermute | solution.py:41
  152.9 5.5 %collective-permute-start.17 = (f32[16]{0:T(128)S(1)}, f32[16]{0:T(128)S(1)}, u32[]{:S(2)}, u32[]{:S(2)}) collective-permute-start(f32[16]{0:T(128)S(1)} %add.241), channel_id=1, source_target_pairs={{0,16},{1,17},{2,18},{3,19},{4,20},{5,21},{6,22},{7,23},{8,24},{9,... | collective-permute-start | bytes 200 | tf_op jit(solution)/shard_map/ppermute | solution.py:41
  158.4 8.6 %collective-permute-done.17 = f32[16]{0:T(128)S(1)} collective-permute-done((f32[16]{0:T(128)S(1)}, f32[16]{0:T(128)S(1)}, u32[]{:S(2)}, u32[]{:S(2)}) %collective-permute-start.17) | collective-permute-done | bytes 96 | tf_op jit(solution)/shard_map/ppermute | solution.py:41
  172.9 4.1 %collective-permute-start.19 = (f32[16]{0:T(128)S(1)}, f32[16]{0:T(128)S(1)}, u32[]{:S(2)}, u32[]{:S(2)}) collective-permute-start(f32[16]{0:T(128)S(1)} %add.243), channel_id=1, source_target_pairs={{0,64},{32,96},{64,0},{96,32},{128,192},{160,224},{192,128},{224,1... | collective-permute-start | bytes 200 | tf_op jit(solution)/shard_map/ppermute | solution.py:41
  182.6 4.6 %collective-permute-start.8 = (f32[16]{0:T(128)S(1)}, f32[16]{0:T(128)S(1)}, u32[]{:S(2)}, u32[]{:S(2)}) collective-permute-start(f32[16]{0:T(128)S(1)} %add.215), channel_id=1, source_target_pairs={{0,256},{32,288},{64,320},{96,352},{128,384},{160,416},{192,448},{... | collective-permute-start | bytes 200 | tf_op jit(solution)/shard_map/ppermute | solution.py:41
  190.0 4.1 %collective-permute-done.21 = f32[16]{0:T(128)S(1)} collective-permute-done((f32[16]{0:T(128)S(1)}, f32[16]{0:T(128)S(1)}, u32[]{:S(2)}, u32[]{:S(2)}) %collective-permute-start.21) | collective-permute-done | bytes 96 | tf_op jit(solution)/shard_map/ppermute | solution.py:41
  200.8 3.2 collective-permute-done.23
  206.0 24.0 %all_gather.7 = f32[16,32,64]{2,0,1:T(8,128)} all-gather(f32[16,2,64]{2,0,1:T(8,128)S(1)} %copy.63), channel_id=1, replica_groups=mesh['band'=16,'lon'=32] {'band'}, dimensions={1}, use_global_device_ids=true | all-gather | bytes 139264 | tf_op jit(solution)/shard_map/all_gather | solution.py:121
  229.9 4.6 %collective-permute-start.25 = (f32[16]{0:T(128)S(1)}, f32[16]{0:T(128)}, u32[]{:S(2)}, u32[]{:S(2)}) collective-permute-start(f32[16]{0:T(128)S(1)} %add.249), channel_id=1, source_target_pairs={{0,8},{1,9},{2,10},{3,11},{4,12},{5,13},{6,14},{7,15},{8,0},{9,1},... | collective-permute-start | bytes 200 | tf_op jit(solution)/shard_map/ppermute | solution.py:41
  239.9 5.5 %collective-permute-start.26 = (f32[16]{0:T(128)S(1)}, f32[16]{0:T(128)S(1)}, u32[]{:S(2)}, u32[]{:S(2)}) collective-permute-start(f32[16]{0:T(128)S(1)} %add.250), channel_id=1, source_target_pairs={{0,16},{1,17},{2,18},{3,19},{4,20},{5,21},{6,22},{7,23},{8,24},{9,... | collective-permute-start | bytes 200 | tf_op jit(solution)/shard_map/ppermute | solution.py:41
  246.5 7.5 %collective-permute-done.26 = f32[16]{0:T(128)S(1)} collective-permute-done((f32[16]{0:T(128)S(1)}, f32[16]{0:T(128)S(1)}, u32[]{:S(2)}, u32[]{:S(2)}) %collective-permute-start.26) | collective-permute-done | bytes 96 | tf_op jit(solution)/shard_map/ppermute | solution.py:41
  259.5 4.1 %collective-permute-start.28 = (f32[16]{0:T(128)S(1)}, f32[16]{0:T(128)S(1)}, u32[]{:S(2)}, u32[]{:S(2)}) collective-permute-start(f32[16]{0:T(128)S(1)} %add.252), channel_id=1, source_target_pairs={{0,64},{32,96},{64,0},{96,32},{128,192},{160,224},{192,128},{224,1... | collective-permute-start | bytes 200 | tf_op jit(solution)/shard_map/ppermute | solution.py:41
  271.8 4.0 %collective-permute-start.30 = (f32[16]{0:T(128)S(1)}, f32[16]{0:T(128)S(1)}, u32[]{:S(2)}, u32[]{:S(2)}) collective-permute-start(f32[16]{0:T(128)S(1)} %add.254), channel_id=1, source_target_pairs={{0,256},{32,288},{64,320},{96,352},{128,384},{160,416},{192,448},{... | collective-permute-start | bytes 200 | tf_op jit(solution)/shard_map/ppermute | solution.py:41
  283.8 3.6 convolution_bitcast_fusion.4
  290.2 34.7 %fusion.26 = f32[16,16,256]{2,0,1:T(8,128)S(1)} fusion(f32[16,16,5,256]{3,0,2,1:T(8,128)} %bitcast.128, f32[16,5]{1,0:T(8,128)S(1)} %copy-done.40, f32[16,5,256]{2,1,0:T(8,128)} %get-tuple-element.18, f32[16,256]{1,0:T(8,128)S(1)} %copy-done.33, f32[16,5,256]{2,1,0:T(8,128)} %get-tuple-element.17, f32[16,256]{1,0:T(8,128)S(1)} %copy-done.35, ...), kind=kOutput, calls=%fused_computation.36 | convolution fusion | flops 1080164352 | bytes 2146624 | tf_op jit(solution)/shard_map/lspq,mlsq->mlp/dot_general | solution.py:113
  335.3 4.7 %collective-permute-start.35 = (f32[16]{0:T(128)S(1)}, f32[16]{0:T(128)S(1)}, u32[]{:S(2)}, u32[]{:S(2)}) collective-permute-start(f32[16]{0:T(128)S(1)} %add.263), channel_id=1, source_target_pairs={{0,4},{1,5},{2,6},{3,7},{4,0},{5,1},{6,2},{7,3},{8,12},{9,13},{10,... | collective-permute-start | bytes 200 | tf_op jit(solution)/shard_map/ppermute | solution.py:41
  341.6 4.4 %collective-permute-start.36 = (f32[16]{0:T(128)S(1)}, f32[16]{0:T(128)S(1)}, u32[]{:S(2)}, u32[]{:S(2)}) collective-permute-start(f32[16]{0:T(128)S(1)} %add.264), channel_id=1, source_target_pairs={{0,8},{1,9},{2,10},{3,11},{4,12},{5,13},{6,14},{7,15},{8,0},{9,1},... | collective-permute-start | bytes 200 | tf_op jit(solution)/shard_map/ppermute | solution.py:41
  346.0 4.9 %collective-permute-done.36 = f32[16]{0:T(128)S(1)} collective-permute-done((f32[16]{0:T(128)S(1)}, f32[16]{0:T(128)S(1)}, u32[]{:S(2)}, u32[]{:S(2)}) %collective-permute-start.36) | collective-permute-done | bytes 96 | tf_op jit(solution)/shard_map/ppermute | solution.py:41
  350.9 5.5 %collective-permute-start.37 = (f32[16]{0:T(128)S(1)}, f32[16]{0:T(128)S(1)}, u32[]{:S(2)}, u32[]{:S(2)}) collective-permute-start(f32[16]{0:T(128)S(1)} %add.265), channel_id=1, source_target_pairs={{0,16},{1,17},{2,18},{3,19},{4,20},{5,21},{6,22},{7,23},{8,24},{9,... | collective-permute-start | bytes 200 | tf_op jit(solution)/shard_map/ppermute | solution.py:41
  356.4 8.7 %collective-permute-done.37 = f32[16]{0:T(128)S(1)} collective-permute-done((f32[16]{0:T(128)S(1)}, f32[16]{0:T(128)S(1)}, u32[]{:S(2)}, u32[]{:S(2)}) %collective-permute-start.37) | collective-permute-done | bytes 96 | tf_op jit(solution)/shard_map/ppermute | solution.py:41
  370.5 3.9 %collective-permute-start.39 = (f32[16]{0:T(128)S(1)}, f32[16]{0:T(128)S(1)}, u32[]{:S(2)}, u32[]{:S(2)}) collective-permute-start(f32[16]{0:T(128)S(1)} %add.267), channel_id=1, source_target_pairs={{0,64},{32,96},{64,0},{96,32},{128,192},{160,224},{192,128},{224,1... | collective-permute-start | bytes 200 | tf_op jit(solution)/shard_map/ppermute | solution.py:41
  382.9 3.8 collective-permute-start.41
  (236 shorter events, 132.4 us)
Async XLA Ops:
  2.5 41.7 %collective-permute-start = (f32[16]{0:T(128)}, f32[16]{0:T(128)}, u32[]{:S(2)}, u32[]{:S(2)}) collective-permute-start(f32[16]{0:T(128)} %multiply_reduce_fusion.3), channel_id=1, source_target_pairs={{0,1},{1,0},{2,3},{3,2},{4,5},{5,4},{6,7},{7,6},{8,9},{9,8},{10,11... | collective-permute-start | bytes 200 | tf_op jit(solution)/shard_map/ppermute | solution.py:41
  5.9 76.4 %collective-permute-start.11 = (f32[3,2,256]{2,0,1:T(4,128)}, f32[3,2,256]{2,0,1:T(4,128)}, u32[]{:S(2)}, u32[]{:S(2)}) collective-permute-start(f32[3,2,256]{2,0,1:T(4,128)} %get-tuple-element.23), channel_id=1, source_target_pairs={{0,1},{1,2},{2,3},{3,4},{4,5},{5,6},{6,7},{7,8},{8,9},{9,10},{10,1... | collective-permute-start | bytes 18440 | tf_op jit(solution)/shard_map/ppermute | solution.py:24
  6.4 75.9 %collective-permute-start.12 = (f32[3,2,256]{2,0,1:T(4,128)}, f32[3,2,256]{2,0,1:T(4,128)}, u32[]{:S(2)}, u32[]{:S(2)}) collective-permute-start(f32[3,2,256]{2,0,1:T(4,128)} %get-tuple-element.24), channel_id=1, source_target_pairs={{1,0},{2,1},{3,2},{4,3},{5,4},{6,5},{7,6},{8,7},{9,8},{10,9},{11,1... | collective-permute-start | bytes 18440 | tf_op jit(solution)/shard_map/ppermute | solution.py:26
  15.7 69.2 %collective-permute-start.9 = (f32[16,6,320]{2,0,1:T(8,128)}, f32[16,6,320]{2,0,1:T(8,128)}, u32[]{:S(2)}, u32[]{:S(2)}) collective-permute-start(f32[16,6,320]{2,0,1:T(8,128)} %get-tuple-element.19), channel_id=1, source_target_pairs={{0,1},{1,2},{2,3},{3,4},{4,5},{5,6},{6,7},{7,8},{8,9},{9,10},{10,1... | collective-permute-start | bytes 368648 | tf_op jit(solution)/shard_map/ppermute | solution.py:24
  15.7 69.2 %collective-permute-start.10 = (f32[16,6,320]{2,0,1:T(8,128)}, f32[16,6,320]{2,0,1:T(8,128)}, u32[]{:S(2)}, u32[]{:S(2)}) collective-permute-start(f32[16,6,320]{2,0,1:T(8,128)} %get-tuple-element.20), channel_id=1, source_target_pairs={{1,0},{2,1},{3,2},{4,3},{5,4},{6,5},{7,6},{8,7},{9,8},{10,9},{11,1... | collective-permute-start | bytes 368648 | tf_op jit(solution)/shard_map/ppermute | solution.py:26
  44.9 12.1 %collective-permute-start.1 = (f32[16]{0:T(128)S(1)}, f32[16]{0:T(128)S(1)}, u32[]{:S(2)}, u32[]{:S(2)}) collective-permute-start(f32[16]{0:T(128)S(1)} %add.208), channel_id=1, source_target_pairs={{0,2},{1,3},{2,0},{3,1},{4,6},{5,7},{6,4},{7,5},{8,10},{9,11},{10,... | collective-permute-start | bytes 200 | tf_op jit(solution)/shard_map/ppermute | solution.py:41
  57.0 6.3 %collective-permute-start.2 = (f32[16]{0:T(128)S(1)}, f32[16]{0:T(128)S(1)}, u32[]{:S(2)}, u32[]{:S(2)}) collective-permute-start(f32[16]{0:T(128)S(1)} %add.209), channel_id=1, source_target_pairs={{0,4},{1,5},{2,6},{3,7},{4,0},{5,1},{6,2},{7,3},{8,12},{9,13},{10,... | collective-permute-start | bytes 200 | tf_op jit(solution)/shard_map/ppermute | solution.py:41
  63.3 9.3 %collective-permute-start.3 = (f32[16]{0:T(128)S(1)}, f32[16]{0:T(128)S(1)}, u32[]{:S(2)}, u32[]{:S(2)}) collective-permute-start(f32[16]{0:T(128)S(1)} %add.210), channel_id=1, source_target_pairs={{0,8},{1,9},{2,10},{3,11},{4,12},{5,13},{6,14},{7,15},{8,0},{9,1},... | collective-permute-start | bytes 200 | tf_op jit(solution)/shard_map/ppermute | solution.py:41
  73.2 55.8 %collective-permute-start.4 = (f32[16]{0:T(128)}, f32[16]{0:T(128)}, u32[]{:S(2)}, u32[]{:S(2)}) collective-permute-start(f32[16]{0:T(128)} %add.211), channel_id=1, source_target_pairs={{0,16},{1,17},{2,18},{3,19},{4,20},{5,21},{6,22},{7,23},{8,24},{9,... | collective-permute-start | bytes 200 | tf_op jit(solution)/shard_map/ppermute | solution.py:41
  130.1 7.0 %collective-permute-start.14 = (f32[16]{0:T(128)S(1)}, f32[16]{0:T(128)S(1)}, u32[]{:S(2)}, u32[]{:S(2)}) collective-permute-start(f32[16]{0:T(128)S(1)} %add.238), channel_id=1, source_target_pairs={{0,2},{1,3},{2,0},{3,1},{4,6},{5,7},{6,4},{7,5},{8,10},{9,11},{10,... | collective-permute-start | bytes 200 | tf_op jit(solution)/shard_map/ppermute | solution.py:41
  137.2 6.3 %collective-permute-start.15 = (f32[16]{0:T(128)S(1)}, f32[16]{0:T(128)S(1)}, u32[]{:S(2)}, u32[]{:S(2)}) collective-permute-start(f32[16]{0:T(128)S(1)} %add.239), channel_id=1, source_target_pairs={{0,4},{1,5},{2,6},{3,7},{4,0},{5,1},{6,2},{7,3},{8,12},{9,13},{10,... | collective-permute-start | bytes 200 | tf_op jit(solution)/shard_map/ppermute | solution.py:41
  143.5 9.3 %collective-permute-start.16 = (f32[16]{0:T(128)S(1)}, f32[16]{0:T(128)S(1)}, u32[]{:S(2)}, u32[]{:S(2)}) collective-permute-start(f32[16]{0:T(128)S(1)} %add.240), channel_id=1, source_target_pairs={{0,8},{1,9},{2,10},{3,11},{4,12},{5,13},{6,14},{7,15},{8,0},{9,1},... | collective-permute-start | bytes 200 | tf_op jit(solution)/shard_map/ppermute | solution.py:41
  147.8 10.5 %collective-permute-start.6 = (f32[16]{0:T(128)S(1)}, f32[16]{0:T(128)S(1)}, u32[]{:S(2)}, u32[]{:S(2)}) collective-permute-start(f32[16]{0:T(128)S(1)} %add.213), channel_id=1, source_target_pairs={{0,64},{32,96},{64,0},{96,32},{128,192},{160,224},{192,128},{224,1... | collective-permute-start | bytes 200 | tf_op jit(solution)/shard_map/ppermute | solution.py:41
  152.9 14.1 %collective-permute-start.17 = (f32[16]{0:T(128)S(1)}, f32[16]{0:T(128)S(1)}, u32[]{:S(2)}, u32[]{:S(2)}) collective-permute-start(f32[16]{0:T(128)S(1)} %add.241), channel_id=1, source_target_pairs={{0,16},{1,17},{2,18},{3,19},{4,20},{5,21},{6,22},{7,23},{8,24},{9,... | collective-permute-start | bytes 200 | tf_op jit(solution)/shard_map/ppermute | solution.py:41
  167.0 5.8 %collective-permute-start.18 = (f32[16]{0:T(128)S(1)}, f32[16]{0:T(128)S(1)}, u32[]{:S(2)}, u32[]{:S(2)}) collective-permute-start(f32[16]{0:T(128)S(1)} %add.242), channel_id=1, source_target_pairs={{0,32},{32,0},{64,96},{96,64},{128,160},{160,128},{192,224},{224,1... | collective-permute-start | bytes 200 | tf_op jit(solution)/shard_map/ppermute | solution.py:41
  169.7 7.3 %collective-permute-start.7 = (f32[16]{0:T(128)S(1)}, f32[16]{0:T(128)S(1)}, u32[]{:S(2)}, u32[]{:S(2)}) collective-permute-start(f32[16]{0:T(128)S(1)} %add.214), channel_id=1, source_target_pairs={{0,128},{32,160},{64,192},{96,224},{128,0},{160,32},{192,64},{224,... | collective-permute-start | bytes 200 | tf_op jit(solution)/shard_map/ppermute | solution.py:41
  172.9 6.9 %collective-permute-start.19 = (f32[16]{0:T(128)S(1)}, f32[16]{0:T(128)S(1)}, u32[]{:S(2)}, u32[]{:S(2)}) collective-permute-start(f32[16]{0:T(128)S(1)} %add.243), channel_id=1, source_target_pairs={{0,64},{32,96},{64,0},{96,32},{128,192},{160,224},{192,128},{224,1... | collective-permute-start | bytes 200 | tf_op jit(solution)/shard_map/ppermute | solution.py:41
  179.8 7.3 %collective-permute-start.20 = (f32[16]{0:T(128)S(1)}, f32[16]{0:T(128)S(1)}, u32[]{:S(2)}, u32[]{:S(2)}) collective-permute-start(f32[16]{0:T(128)S(1)} %add.244), channel_id=1, source_target_pairs={{0,128},{32,160},{64,192},{96,224},{128,0},{160,32},{192,64},{224,... | collective-permute-start | bytes 200 | tf_op jit(solution)/shard_map/ppermute | solution.py:41
  182.6 7.4 %collective-permute-start.8 = (f32[16]{0:T(128)S(1)}, f32[16]{0:T(128)S(1)}, u32[]{:S(2)}, u32[]{:S(2)}) collective-permute-start(f32[16]{0:T(128)S(1)} %add.215), channel_id=1, source_target_pairs={{0,256},{32,288},{64,320},{96,352},{128,384},{160,416},{192,448},{... | collective-permute-start | bytes 200 | tf_op jit(solution)/shard_map/ppermute | solution.py:41
  187.2 6.9 %collective-permute-start.21 = (f32[16]{0:T(128)S(1)}, f32[16]{0:T(128)S(1)}, u32[]{:S(2)}, u32[]{:S(2)}) collective-permute-start(f32[16]{0:T(128)S(1)} %add.245), channel_id=1, source_target_pairs={{0,256},{32,288},{64,320},{96,352},{128,384},{160,416},{192,448},{... | collective-permute-start | bytes 200 | tf_op jit(solution)/shard_map/ppermute | solution.py:41
  198.6 5.4 %collective-permute-start.23 = (f32[16]{0:T(128)S(1)}, f32[16]{0:T(128)S(1)}, u32[]{:S(2)}, u32[]{:S(2)}) collective-permute-start(f32[16]{0:T(128)S(1)} %add.247), channel_id=1, source_target_pairs={{0,2},{1,3},{2,0},{3,1},{4,6},{5,7},{6,4},{7,5},{8,10},{9,11},{10,... | collective-permute-start | bytes 200 | tf_op jit(solution)/shard_map/ppermute | solution.py:41
  204.0 25.9 %collective-permute-start.24 = (f32[16]{0:T(128)S(1)}, f32[16]{0:T(128)S(1)}, u32[]{:S(2)}, u32[]{:S(2)}) collective-permute-start(f32[16]{0:T(128)S(1)} %add.248), channel_id=1, source_target_pairs={{0,4},{1,5},{2,6},{3,7},{4,0},{5,1},{6,2},{7,3},{8,12},{9,13},{10,... | collective-permute-start | bytes 200 | tf_op jit(solution)/shard_map/ppermute | solution.py:41
  229.9 9.3 %collective-permute-start.25 = (f32[16]{0:T(128)S(1)}, f32[16]{0:T(128)}, u32[]{:S(2)}, u32[]{:S(2)}) collective-permute-start(f32[16]{0:T(128)S(1)} %add.249), channel_id=1, source_target_pairs={{0,8},{1,9},{2,10},{3,11},{4,12},{5,13},{6,14},{7,15},{8,0},{9,1},... | collective-permute-start | bytes 200 | tf_op jit(solution)/shard_map/ppermute | solution.py:41
  239.9 14.1 %collective-permute-start.26 = (f32[16]{0:T(128)S(1)}, f32[16]{0:T(128)S(1)}, u32[]{:S(2)}, u32[]{:S(2)}) collective-permute-start(f32[16]{0:T(128)S(1)} %add.250), channel_id=1, source_target_pairs={{0,16},{1,17},{2,18},{3,19},{4,20},{5,21},{6,22},{7,23},{8,24},{9,... | collective-permute-start | bytes 200 | tf_op jit(solution)/shard_map/ppermute | solution.py:41
  259.5 6.9 %collective-permute-start.28 = (f32[16]{0:T(128)S(1)}, f32[16]{0:T(128)S(1)}, u32[]{:S(2)}, u32[]{:S(2)}) collective-permute-start(f32[16]{0:T(128)S(1)} %add.252), channel_id=1, source_target_pairs={{0,64},{32,96},{64,0},{96,32},{128,192},{160,224},{192,128},{224,1... | collective-permute-start | bytes 200 | tf_op jit(solution)/shard_map/ppermute | solution.py:41
  269.1 10.2 %collective-permute-start.31 = (f32[16,6,320]{2,0,1:T(8,128)S(1)}, f32[16,6,320]{2,0,1:T(8,128)S(1)}, u32[]{:S(2)}, u32[]{:S(2)}) collective-permute-start(f32[16,6,320]{2,0,1:T(8,128)S(1)} %get-tuple-element.14), channel_id=1, source_target_pairs={{0,1},{1,2},{2,3},{3,4},{4,5},{5,6},{6,7},{7,8},{8,9},{9,10},{10,1... | collective-permute-start | bytes 368648 | tf_op jit(solution)/shard_map/ppermute | solution.py:24
  271.8 6.9 %collective-permute-start.30 = (f32[16]{0:T(128)S(1)}, f32[16]{0:T(128)S(1)}, u32[]{:S(2)}, u32[]{:S(2)}) collective-permute-start(f32[16]{0:T(128)S(1)} %add.254), channel_id=1, source_target_pairs={{0,256},{32,288},{64,320},{96,352},{128,384},{160,416},{192,448},{... | collective-permute-start | bytes 200 | tf_op jit(solution)/shard_map/ppermute | solution.py:41
  335.3 6.3 %collective-permute-start.35 = (f32[16]{0:T(128)S(1)}, f32[16]{0:T(128)S(1)}, u32[]{:S(2)}, u32[]{:S(2)}) collective-permute-start(f32[16]{0:T(128)S(1)} %add.263), channel_id=1, source_target_pairs={{0,4},{1,5},{2,6},{3,7},{4,0},{5,1},{6,2},{7,3},{8,12},{9,13},{10,... | collective-permute-start | bytes 200 | tf_op jit(solution)/shard_map/ppermute | solution.py:41
  341.6 9.3 %collective-permute-start.36 = (f32[16]{0:T(128)S(1)}, f32[16]{0:T(128)S(1)}, u32[]{:S(2)}, u32[]{:S(2)}) collective-permute-start(f32[16]{0:T(128)S(1)} %add.264), channel_id=1, source_target_pairs={{0,8},{1,9},{2,10},{3,11},{4,12},{5,13},{6,14},{7,15},{8,0},{9,1},... | collective-permute-start | bytes 200 | tf_op jit(solution)/shard_map/ppermute | solution.py:41
  350.9 14.1 %collective-permute-start.37 = (f32[16]{0:T(128)S(1)}, f32[16]{0:T(128)S(1)}, u32[]{:S(2)}, u32[]{:S(2)}) collective-permute-start(f32[16]{0:T(128)S(1)} %add.265), channel_id=1, source_target_pairs={{0,16},{1,17},{2,18},{3,19},{4,20},{5,21},{6,22},{7,23},{8,24},{9,... | collective-permute-start | bytes 200 | tf_op jit(solution)/shard_map/ppermute | solution.py:41
  370.5 6.9 %collective-permute-start.39 = (f32[16]{0:T(128)S(1)}, f32[16]{0:T(128)S(1)}, u32[]{:S(2)}, u32[]{:S(2)}) collective-permute-start(f32[16]{0:T(128)S(1)} %add.267), channel_id=1, source_target_pairs={{0,64},{32,96},{64,0},{96,32},{128,192},{160,224},{192,128},{224,1... | collective-permute-start | bytes 200 | tf_op jit(solution)/shard_map/ppermute | solution.py:41
  382.9 6.9 %collective-permute-start.41 = (f32[16]{0:T(128)S(1)}, f32[16]{0:T(128)S(1)}, u32[]{:S(2)}, u32[]{:S(2)}) collective-permute-start(f32[16]{0:T(128)S(1)} %add.269), channel_id=1, source_target_pairs={{0,256},{32,288},{64,320},{96,352},{128,384},{160,416},{192,448},{... | collective-permute-start | bytes 200 | tf_op jit(solution)/shard_map/ppermute | solution.py:41
  (54 other events, 1091.4 us)

commit v2 on v1

--- a/solution.py
+++ b/solution.py
@@ -99,9 +99,6 @@
         jnp.float32
     )
 
-    def square_total(vector):
-        return all_sum(jnp.sum(vector * vector, axis=(1, 2)), ("lon", "band"))
-
     def covariance_apply(direction):
         coeffs = jnp.einsum("lpr,mlp->mlr", leaf_basis, direction, precision=HIGHEST_PRECISION)
         joined = jnp.concatenate([direction, coeffs], axis=2)
@@ -132,23 +129,31 @@
         far_part = jnp.einsum("lpr,mlr->mlp", leaf_basis, leaf_far, precision=HIGHEST_PRECISION)
         return noise_var[None] * direction + near_part + far_part
 
-    solution = jnp.zeros_like(sky_maps)
-    residual = sky_maps
+    def total(*products):
+        sums = jnp.stack([jnp.sum(product, axis=(1, 2)) for product in products])
+        return all_sum(sums, ("lon", "band"))
+
+    assert ITERS == 2
     direction = sky_maps
-    norm_now = square_total(residual)
     applied = covariance_apply(direction)
-    for iteration in range(ITERS):
-        curvature_sum = all_sum(jnp.sum(direction * applied, axis=(1, 2)), ("lon", "band"))
-        step_size = norm_now / curvature_sum
-        solution = solution + step_size[:, None, None] * direction
-        residual = residual - step_size[:, None, None] * applied
-        if iteration + 1 < ITERS:
-            norm_next = square_total(residual)
-            applied_residual = covariance_apply(residual)
-            ratio = (norm_next / norm_now)[:, None, None]
-            direction = residual + ratio * direction
-            applied = applied_residual + ratio * applied
-            norm_now = norm_next
+    applied_twice = covariance_apply(applied)
+    norm_now, curvature_sum = total(direction * direction, direction * applied)
+    step_size = (norm_now / curvature_sum)[:, None, None]
+    solution = step_size * direction
+    residual = direction - step_size * applied
+    applied_residual = applied - step_size * applied_twice
+    norm_next, residual_curv, cross_one, cross_two = total(
+        residual * residual,
+        residual * applied_residual,
+        residual * applied,
+        direction * applied_residual,
+    )
+    ratio = norm_next / norm_now
+    next_curv = residual_curv + ratio * (cross_one + cross_two) + ratio * ratio * curvature_sum
+    ratio = ratio[:, None, None]
+    step_next = (norm_next / next_curv)[:, None, None]
+    solution = solution + step_next * (residual + ratio * direction)
+    residual = residual - step_next * (applied_residual + ratio * applied)
     return (solution, residual)
 
 

time: 394 us -> 298 us (0.76)
  starting transfers between devices: 140 us -> 87.9 us
  waiting for transfers between devices: 85.8 us -> 41.4 us
  other arithmetic: 13.6 us -> 7.81 us
  blocking collectives: 44.7 us -> 48.8 us
    ppermute x36 -> x18, starting transfers between devices: 133 us -> 82.2 us  [all_sum(): lax.ppermute(vector, axis, [(i, i ^ stride) for i in range(count)])]
    ppermute x36 -> x18, waiting for transfers between devices: 85.7 us -> 41.4 us  [all_sum(): lax.ppermute(vector, axis, [(i, i ^ stride) for i in range(count)])]
    all_gather x2, blocking collectives: 44.7 us -> 48.8 us  [covariance_apply(): band_coeffs = lax.all_gather(panel_coeffs, 'band', axis=1, tiled=True)]
  transfers between devices with their start and end apart: 42 -> 24, of which waited for: 26 -> 17; matrix products, arithmetic and copies ran while one was open for 17% -> 8% of each run, Pallas kernels for 0% -> 0%
where the time goes in v2:
time: 298 us; the launch traced here: 297 us
  starting transfers between devices  87.9 us (29%)
  matrix products  86.3 us (29%)
  blocking collectives  48.8 us (16%)
  waiting for transfers between devices  41.4 us (14%)
  local copies, waits for them, and re-layouts  23.4 us (8%)
  other arithmetic  7.81 us (3%)
    ppermute x18, starting transfers between devices, all_sum(): lax.ppermute(vector, axis, [(i, i ^ stride) for i in range(count)])  82.2 us
    dot_general x2, matrix products, covariance_apply(): jnp.einsum('lspq,mlsq->mlp', near_blocks, rim_values[:, near_rows], preci...  66.7 us
    all_gather x2, blocking collectives, covariance_apply(): band_coeffs = lax.all_gather(panel_coeffs, 'band', axis=1, tiled=True)  48.8 us
    ppermute x18, waiting for transfers between devices, all_sum(): lax.ppermute(vector, axis, [(i, i ^ stride) for i in range(count)])  41.4 us
    dot_general x2, matrix products, covariance_apply(): jnp.einsum('lsab,mlsb->mla', leaf_couple, rim_coeffs[:, far_rows], precis...  6.54 us
  transfers between devices with their start and end apart: 24, of which 17 were waited for; matrix products, arithmetic and copies ran while one was open for 8% of the time, Pallas kernels for 0%

profile of v2, /device:TPU:32, one launch (start us, length us, event | category | flops | bytes accessed | tf_op | source)
XLA Modules:
  0.0 297.0 jit_solution(15449280280194295112)
XLA Ops:
  5.2 2.4 convolution_bitcast_fusion.9
  8.7 3.5 %collective-permute-start.1 = (f32[16,6,320]{2,0,1:T(8,128)}, f32[16,6,320]{2,0,1:T(8,128)}, u32[]{:S(2)}, u32[]{:S(2)}) collective-permute-start(f32[16,6,320]{2,0,1:T(8,128)} %get-tuple-element.22), channel_id=1, source_target_pairs={{1,0},{2,1},{3,2},{4,3},{5,4},{6,5},{7,6},{8,7},{9,8},{10,9},{11,1... | collective-permute-start | bytes 368648 | tf_op jit(solution)/shard_map/ppermute | solution.py:26
  16.8 23.9 %all_gather.6 = f32[16,32,64]{2,0,1:T(8,128)} all-gather(f32[16,2,64]{2,0,1:T(8,128)S(1)} %copy.57), channel_id=1, replica_groups=mesh['band'=16,'lon'=32] {'band'}, dimensions={1}, use_global_device_ids=true | all-gather | bytes 139264 | tf_op jit(solution)/shard_map/all_gather | solution.py:118
  54.7 3.0 convolution_bitcast_fusion.7
  58.7 32.3 %fusion.29 = f32[16,16,256]{2,0,1:T(8,128)S(1)} fusion(f32[16,16,5,256]{3,0,2,1:T(8,128)S(1)} %bitcast.160, f32[16,5]{1,0:T(8,128)S(1)} %copy-done.40, f32[16,5,256]{2,1,0:T(8,128)S(1)} %copy-done.28, f32[16,256]{1,0:T(8,128)S(1)} %copy-done.34, f32[16,5,256]{2,1,0:T(8,128)S(1)} %copy-done.27, f32[16,256]{1,0:T(8,128)S(1)} %copy-done.36, ...), kind=kOutput, calls=%fused_computation.39 | convolution fusion | flops 1080164352 | bytes 2146624 | tf_op jit(solution)/shard_map/lspq,mlsq->mlp/dot_general | solution.py:110
  94.9 10.4 %collective-permute-start.5 = (f32[2,16]{1,0:T(2,128)S(1)}, f32[2,16]{1,0:T(2,128)S(1)}, u32[]{:S(2)}, u32[]{:S(2)}) collective-permute-start(f32[2,16]{1,0:T(2,128)S(1)} %fusion.64), channel_id=1, source_target_pairs={{0,2},{1,3},{2,0},{3,1},{4,6},{5,7},{6,4},{7,5},{8,10},{9,11},{10,... | collective-permute-start | bytes 392 | tf_op jit(solution)/shard_map/ppermute | solution.py:41
  109.0 4.2 %collective-permute-done.6 = f32[2,16]{1,0:T(2,128)S(1)} collective-permute-done((f32[2,16]{1,0:T(2,128)S(1)}, f32[2,16]{1,0:T(2,128)S(1)}, u32[]{:S(2)}, u32[]{:S(2)}) %collective-permute-start.6) | collective-permute-done | bytes 160 | tf_op jit(solution)/shard_map/ppermute | solution.py:41
  113.8 3.1 %collective-permute-start.7 = (f32[2,16]{1,0:T(2,128)}, f32[2,16]{1,0:T(2,128)}, u32[]{:S(2)}, u32[]{:S(2)}) collective-permute-start(f32[2,16]{1,0:T(2,128)} %add.201), channel_id=1, source_target_pairs={{0,8},{1,9},{2,10},{3,11},{4,12},{5,13},{6,14},{7,15},{8,0},{9,1},... | collective-permute-start | bytes 392 | tf_op jit(solution)/shard_map/ppermute | solution.py:41
  116.9 25.0 %all_gather.7 = f32[16,32,64]{2,0,1:T(8,128)} all-gather(f32[16,2,64]{2,0,1:T(8,128)S(1)} %copy.64), channel_id=1, replica_groups=mesh['band'=16,'lon'=32] {'band'}, dimensions={1}, use_global_device_ids=true | all-gather | bytes 139264 | tf_op jit(solution)/shard_map/all_gather | solution.py:118
  144.8 10.9 %collective-permute-start.8 = (f32[2,16]{1,0:T(2,128)S(1)}, f32[2,16]{1,0:T(2,128)S(1)}, u32[]{:S(2)}, u32[]{:S(2)}) collective-permute-start(f32[2,16]{1,0:T(2,128)S(1)} %add.202), channel_id=1, source_target_pairs={{0,16},{1,17},{2,18},{3,19},{4,20},{5,21},{6,22},{7,23},{8,24},{9,... | collective-permute-start | bytes 392 | tf_op jit(solution)/shard_map/ppermute | solution.py:41
  162.1 2.4 collective-permute-done.9
  164.5 3.5 %collective-permute-start.10 = (f32[2,16]{1,0:T(2,128)S(1)}, f32[2,16]{1,0:T(2,128)S(1)}, u32[]{:S(2)}, u32[]{:S(2)}) collective-permute-start(f32[2,16]{1,0:T(2,128)S(1)} %add.204), channel_id=1, source_target_pairs={{0,64},{32,96},{64,0},{96,32},{128,192},{160,224},{192,128},{224,1... | collective-permute-start | bytes 392 | tf_op jit(solution)/shard_map/ppermute | solution.py:41
  168.0 3.4 %collective-permute-done.10 = f32[2,16]{1,0:T(2,128)S(1)} collective-permute-done((f32[2,16]{1,0:T(2,128)S(1)}, f32[2,16]{1,0:T(2,128)S(1)}, u32[]{:S(2)}, u32[]{:S(2)}) %collective-permute-start.10) | collective-permute-done | bytes 160 | tf_op jit(solution)/shard_map/ppermute | solution.py:41
  173.8 3.1 %collective-permute-done.11 = f32[2,16]{1,0:T(2,128)S(1)} collective-permute-done((f32[2,16]{1,0:T(2,128)S(1)}, f32[2,16]{1,0:T(2,128)S(1)}, u32[]{:S(2)}, u32[]{:S(2)}) %collective-permute-start.11) | collective-permute-done | bytes 160 | tf_op jit(solution)/shard_map/ppermute | solution.py:41
  176.9 3.7 %collective-permute-start.12 = (f32[2,16]{1,0:T(2,128)S(1)}, f32[2,16]{1,0:T(2,128)S(1)}, u32[]{:S(2)}, u32[]{:S(2)}) collective-permute-start(f32[2,16]{1,0:T(2,128)S(1)} %add.206), channel_id=1, source_target_pairs={{0,256},{32,288},{64,320},{96,352},{128,384},{160,416},{192,448},{... | collective-permute-start | bytes 392 | tf_op jit(solution)/shard_map/ppermute | solution.py:41
  180.6 3.3 %collective-permute-done.12 = f32[2,16]{1,0:T(2,128)S(1)} collective-permute-done((f32[2,16]{1,0:T(2,128)S(1)}, f32[2,16]{1,0:T(2,128)S(1)}, u32[]{:S(2)}, u32[]{:S(2)}) %collective-permute-start.12) | collective-permute-done | bytes 160 | tf_op jit(solution)/shard_map/ppermute | solution.py:41
  188.8 3.6 %convolution_bitcast_fusion.4 = f32[16,16,64]{2,1,0:T(8,128)} fusion(f32[16,16,4,64]{3,0,2,1:T(8,128)} %bitcast.162, f32[16,4,64,64]{3,2,1,0:T(8,128)S(1)} %copy-done), kind=kOutput, calls=%fused_computation.44 | convolution fusion | flops 50331648 | bytes 1376256 | tf_op jit(solution)/shard_map/lsab,mlsb->mla/dot_general | solution.py:113
  194.4 34.4 %fusion.28 = f32[16,16,256]{2,0,1:T(8,128)S(1)} fusion(f32[16,16,5,256]{3,0,2,1:T(8,128)} %bitcast.161, f32[16,5]{1,0:T(8,128)S(1)} %copy-done.40, f32[16,5,256]{2,1,0:T(8,128)} %get-tuple-element.20, f32[16,256]{1,0:T(8,128)S(1)} %copy-done.35, f32[16,5,256]{2,1,0:T(8,128)} %get-tuple-element.19, f32[16,256]{1,0:T(8,128)S(1)} %copy-done.37, ...), kind=kOutput, calls=%fused_computation.38 | convolution fusion | flops 1080164352 | bytes 2146624 | tf_op jit(solution)/shard_map/lspq,mlsq->mlp/dot_general | solution.py:110
  233.8 3.9 %collective-permute-start.16 = (f32[4,16]{1,0:T(4,128)S(1)}, f32[4,16]{1,0:T(4,128)S(1)}, u32[]{:S(2)}, u32[]{:S(2)}) collective-permute-start(f32[4,16]{1,0:T(4,128)S(1)} %fusion.65), channel_id=1, source_target_pairs={{0,2},{1,3},{2,0},{3,1},{4,6},{5,7},{6,4},{7,5},{8,10},{9,11},{10,... | collective-permute-start | bytes 776 | tf_op jit(solution)/shard_map/ppermute | solution.py:41
  239.3 5.7 %collective-permute-start.17 = (f32[4,16]{1,0:T(4,128)S(1)}, f32[4,16]{1,0:T(4,128)S(1)}, u32[]{:S(2)}, u32[]{:S(2)}) collective-permute-start(f32[4,16]{1,0:T(4,128)S(1)} %fusion.91), channel_id=1, source_target_pairs={{0,4},{1,5},{2,6},{3,7},{4,0},{5,1},{6,2},{7,3},{8,12},{9,13},{10,... | collective-permute-start | bytes 776 | tf_op jit(solution)/shard_map/ppermute | solution.py:41
  246.6 6.7 %collective-permute-start.18 = (f32[4,16]{1,0:T(4,128)S(1)}, f32[4,16]{1,0:T(4,128)S(1)}, u32[]{:S(2)}, u32[]{:S(2)}) collective-permute-start(f32[4,16]{1,0:T(4,128)S(1)} %add.214), channel_id=1, source_target_pairs={{0,8},{1,9},{2,10},{3,11},{4,12},{5,13},{6,14},{7,15},{8,0},{9,1},... | collective-permute-start | bytes 776 | tf_op jit(solution)/shard_map/ppermute | solution.py:41
  253.3 2.6 collective-permute-done.18
  256.0 10.0 %collective-permute-start.19 = (f32[4,16]{1,0:T(4,128)S(1)}, f32[4,16]{1,0:T(4,128)S(1)}, u32[]{:S(2)}, u32[]{:S(2)}) collective-permute-start(f32[4,16]{1,0:T(4,128)S(1)} %add.215), channel_id=1, source_target_pairs={{0,16},{1,17},{2,18},{3,19},{4,20},{5,21},{6,22},{7,23},{8,24},{9,... | collective-permute-start | bytes 776 | tf_op jit(solution)/shard_map/ppermute | solution.py:41
  266.0 4.1 %collective-permute-done.19 = f32[4,16]{1,0:T(4,128)S(1)} collective-permute-done((f32[4,16]{1,0:T(4,128)S(1)}, f32[4,16]{1,0:T(4,128)S(1)}, u32[]{:S(2)}, u32[]{:S(2)}) %collective-permute-start.19) | collective-permute-done | bytes 288 | tf_op jit(solution)/shard_map/ppermute | solution.py:41
  270.1 3.1 %collective-permute-start.20 = (f32[4,16]{1,0:T(4,128)S(1)}, f32[4,16]{1,0:T(4,128)S(1)}, u32[]{:S(2)}, u32[]{:S(2)}) collective-permute-start(f32[4,16]{1,0:T(4,128)S(1)} %add.216), channel_id=1, source_target_pairs={{0,32},{32,0},{64,96},{96,64},{128,160},{160,128},{192,224},{224,1... | collective-permute-start | bytes 776 | tf_op jit(solution)/shard_map/ppermute | solution.py:41
  273.2 2.4 collective-permute-done.20
  275.6 4.4 %collective-permute-start.21 = (f32[4,16]{1,0:T(4,128)S(1)}, f32[4,16]{1,0:T(4,128)S(1)}, u32[]{:S(2)}, u32[]{:S(2)}) collective-permute-start(f32[4,16]{1,0:T(4,128)S(1)} %add.217), channel_id=1, source_target_pairs={{0,64},{32,96},{64,0},{96,32},{128,192},{160,224},{192,128},{224,1... | collective-permute-start | bytes 776 | tf_op jit(solution)/shard_map/ppermute | solution.py:41
  280.1 2.5 collective-permute-done.21
  282.6 2.5 collective-permute-start.22
  285.1 3.0 %collective-permute-done.22 = f32[4,16]{1,0:T(4,128)S(1)} collective-permute-done((f32[4,16]{1,0:T(4,128)S(1)}, f32[4,16]{1,0:T(4,128)S(1)}, u32[]{:S(2)}, u32[]{:S(2)}) %collective-permute-start.22) | collective-permute-done | bytes 288 | tf_op jit(solution)/shard_map/ppermute | solution.py:41
  288.1 4.0 %collective-permute-start.23 = (f32[4,16]{1,0:T(4,128)S(1)}, f32[4,16]{1,0:T(4,128)S(1)}, u32[]{:S(2)}, u32[]{:S(2)}) collective-permute-start(f32[4,16]{1,0:T(4,128)S(1)} %add.219), channel_id=1, source_target_pairs={{0,256},{32,288},{64,320},{96,352},{128,384},{160,416},{192,448},{... | collective-permute-start | bytes 776 | tf_op jit(solution)/shard_map/ppermute | solution.py:41
  292.0 3.0 %collective-permute-done.23 = f32[4,16]{1,0:T(4,128)S(1)} collective-permute-done((f32[4,16]{1,0:T(4,128)S(1)}, f32[4,16]{1,0:T(4,128)S(1)}, u32[]{:S(2)}, u32[]{:S(2)}) %collective-permute-start.23) | collective-permute-done | bytes 288 | tf_op jit(solution)/shard_map/ppermute | solution.py:41
  (192 shorter events, 61.6 us)
Async XLA Ops:
  0.6 54.0 %copy-start = (f32[16,4,64,64]{3,2,1,0:T(8,128)S(1)}, f32[16,4,64,64]{3,2,1,0:T(8,128)}, u32[]{:S(2)}) copy-start(f32[16,4,64,64]{3,2,1,0:T(8,128)} %param.15) | copy-start | bytes 3145732
  2.3 43.1 %collective-permute-start.2 = (f32[3,2,256]{2,0,1:T(4,128)}, f32[3,2,256]{2,0,1:T(4,128)}, u32[]{:S(2)}, u32[]{:S(2)}) collective-permute-start(f32[3,2,256]{2,0,1:T(4,128)} %get-tuple-element.23), channel_id=1, source_target_pairs={{0,1},{1,2},{2,3},{3,4},{4,5},{5,6},{6,7},{7,8},{8,9},{9,10},{10,1... | collective-permute-start | bytes 18440 | tf_op jit(solution)/shard_map/ppermute | solution.py:24
  2.3 40.0 %copy-start.21 = (f32[2,2,64,64]{3,2,1,0:T(8,128)S(1)}, f32[2,2,64,64]{3,2,1,0:T(8,128)}, u32[]{:S(2)}) copy-start(f32[2,2,64,64]{3,2,1,0:T(8,128)} %param.17) | copy-start | bytes 196612
  2.3 43.1 %collective-permute-start.3 = (f32[3,2,256]{2,0,1:T(4,128)}, f32[3,2,256]{2,0,1:T(4,128)}, u32[]{:S(2)}, u32[]{:S(2)}) collective-permute-start(f32[3,2,256]{2,0,1:T(4,128)} %get-tuple-element.24), channel_id=1, source_target_pairs={{1,0},{2,1},{3,2},{4,3},{5,4},{6,5},{7,6},{8,7},{9,8},{10,9},{11,1... | collective-permute-start | bytes 18440 | tf_op jit(solution)/shard_map/ppermute | solution.py:26
  8.4 41.1 %collective-permute-start = (f32[16,6,320]{2,0,1:T(8,128)}, f32[16,6,320]{2,0,1:T(8,128)S(1)}, u32[]{:S(2)}, u32[]{:S(2)}) collective-permute-start(f32[16,6,320]{2,0,1:T(8,128)} %get-tuple-element.21), channel_id=1, source_target_pairs={{0,1},{1,2},{2,3},{3,4},{4,5},{5,6},{6,7},{7,8},{8,9},{9,10},{10,1... | collective-permute-start | bytes 368648 | tf_op jit(solution)/shard_map/ppermute | solution.py:24
  8.7 40.8 %collective-permute-start.1 = (f32[16,6,320]{2,0,1:T(8,128)}, f32[16,6,320]{2,0,1:T(8,128)}, u32[]{:S(2)}, u32[]{:S(2)}) collective-permute-start(f32[16,6,320]{2,0,1:T(8,128)} %get-tuple-element.22), channel_id=1, source_target_pairs={{1,0},{2,1},{3,2},{4,3},{5,4},{6,5},{7,6},{8,7},{9,8},{10,9},{11,1... | collective-permute-start | bytes 368648 | tf_op jit(solution)/shard_map/ppermute | solution.py:26
  14.0 36.6 %copy-start.23 = (s32[1024]{0:T(1024)}, s32[1024]{0:T(1024)S(1)}, u32[]{:S(2)}) copy-start(s32[1024]{0:T(1024)S(1)} %pad_clamp_fusion.2) | copy-start | bytes 12292
  91.8 94.6 %copy-start.2 = (f32[16,16,256]{2,0,1:T(8,128)}, f32[16,16,256]{2,0,1:T(8,128)S(1)}, u32[]{:S(2)}) copy-start(f32[16,16,256]{2,0,1:T(8,128)S(1)} %get-tuple-element.29) | copy-start | bytes 786436
  91.9 3.0 %collective-permute-start.4 = (f32[2,16]{1,0:T(2,128)S(1)}, f32[2,16]{1,0:T(2,128)S(1)}, u32[]{:S(2)}, u32[]{:S(2)}) collective-permute-start(f32[2,16]{1,0:T(2,128)S(1)} %pad_maximum_fusion.14), channel_id=1, source_target_pairs={{0,1},{1,0},{2,3},{3,2},{4,5},{5,4},{6,7},{7,6},{8,9},{9,8},{10,11... | collective-permute-start | bytes 392 | tf_op jit(solution)/shard_map/ppermute | solution.py:41
  93.8 92.7 %copy-start.30 = (s32[1024]{0:T(1024)S(1)}, s32[1024]{0:T(1024)}, u32[]{:S(2)}) copy-start(s32[1024]{0:T(1024)} %copy-done.29) | copy-start | bytes 12292
  94.7 94.0 %copy-start.13 = (f32[16,16,64]{2,0,1:T(8,128)}, f32[16,16,64]{2,0,1:T(8,128)S(1)}, u32[]{:S(2)}) copy-start(f32[16,16,64]{2,0,1:T(8,128)S(1)} %convolution_bitcast_fusion.8) | copy-start | bytes 196612
  94.9 11.9 %collective-permute-start.5 = (f32[2,16]{1,0:T(2,128)S(1)}, f32[2,16]{1,0:T(2,128)S(1)}, u32[]{:S(2)}, u32[]{:S(2)}) collective-permute-start(f32[2,16]{1,0:T(2,128)S(1)} %fusion.64), channel_id=1, source_target_pairs={{0,2},{1,3},{2,0},{3,1},{4,6},{5,7},{6,4},{7,5},{8,10},{9,11},{10,... | collective-permute-start | bytes 392 | tf_op jit(solution)/shard_map/ppermute | solution.py:41
  106.8 6.4 %collective-permute-start.6 = (f32[2,16]{1,0:T(2,128)S(1)}, f32[2,16]{1,0:T(2,128)S(1)}, u32[]{:S(2)}, u32[]{:S(2)}) collective-permute-start(f32[2,16]{1,0:T(2,128)S(1)} %fusion.92), channel_id=1, source_target_pairs={{0,4},{1,5},{2,6},{3,7},{4,0},{5,1},{6,2},{7,3},{8,12},{9,13},{10,... | collective-permute-start | bytes 392 | tf_op jit(solution)/shard_map/ppermute | solution.py:41
  113.8 30.3 %collective-permute-start.7 = (f32[2,16]{1,0:T(2,128)}, f32[2,16]{1,0:T(2,128)}, u32[]{:S(2)}, u32[]{:S(2)}) collective-permute-start(f32[2,16]{1,0:T(2,128)} %add.201), channel_id=1, source_target_pairs={{0,8},{1,9},{2,10},{3,11},{4,12},{5,13},{6,14},{7,15},{8,0},{9,1},... | collective-permute-start | bytes 392 | tf_op jit(solution)/shard_map/ppermute | solution.py:41
  144.8 14.2 %collective-permute-start.8 = (f32[2,16]{1,0:T(2,128)S(1)}, f32[2,16]{1,0:T(2,128)S(1)}, u32[]{:S(2)}, u32[]{:S(2)}) collective-permute-start(f32[2,16]{1,0:T(2,128)S(1)} %add.202), channel_id=1, source_target_pairs={{0,16},{1,17},{2,18},{3,19},{4,20},{5,21},{6,22},{7,23},{8,24},{9,... | collective-permute-start | bytes 392 | tf_op jit(solution)/shard_map/ppermute | solution.py:41
  159.0 5.5 %collective-permute-start.9 = (f32[2,16]{1,0:T(2,128)S(1)}, f32[2,16]{1,0:T(2,128)S(1)}, u32[]{:S(2)}, u32[]{:S(2)}) collective-permute-start(f32[2,16]{1,0:T(2,128)S(1)} %add.203), channel_id=1, source_target_pairs={{0,32},{32,0},{64,96},{96,64},{128,160},{160,128},{192,224},{224,1... | collective-permute-start | bytes 392 | tf_op jit(solution)/shard_map/ppermute | solution.py:41
  164.5 7.0 %collective-permute-start.10 = (f32[2,16]{1,0:T(2,128)S(1)}, f32[2,16]{1,0:T(2,128)S(1)}, u32[]{:S(2)}, u32[]{:S(2)}) collective-permute-start(f32[2,16]{1,0:T(2,128)S(1)} %add.204), channel_id=1, source_target_pairs={{0,64},{32,96},{64,0},{96,32},{128,192},{160,224},{192,128},{224,1... | collective-permute-start | bytes 392 | tf_op jit(solution)/shard_map/ppermute | solution.py:41
  171.4 5.5 %collective-permute-start.11 = (f32[2,16]{1,0:T(2,128)S(1)}, f32[2,16]{1,0:T(2,128)S(1)}, u32[]{:S(2)}, u32[]{:S(2)}) collective-permute-start(f32[2,16]{1,0:T(2,128)S(1)} %add.205), channel_id=1, source_target_pairs={{0,128},{32,160},{64,192},{96,224},{128,0},{160,32},{192,64},{224,... | collective-permute-start | bytes 392 | tf_op jit(solution)/shard_map/ppermute | solution.py:41
  173.8 10.1 %collective-permute-start.13 = (f32[16,6,320]{2,0,1:T(8,128)S(1)}, f32[16,6,320]{2,0,1:T(8,128)S(1)}, u32[]{:S(2)}, u32[]{:S(2)}) collective-permute-start(f32[16,6,320]{2,0,1:T(8,128)S(1)} %get-tuple-element.16), channel_id=1, source_target_pairs={{0,1},{1,2},{2,3},{3,4},{4,5},{5,6},{6,7},{7,8},{8,9},{9,10},{10,1... | collective-permute-start | bytes 368648 | tf_op jit(solution)/shard_map/ppermute | solution.py:24
  176.9 7.0 %collective-permute-start.12 = (f32[2,16]{1,0:T(2,128)S(1)}, f32[2,16]{1,0:T(2,128)S(1)}, u32[]{:S(2)}, u32[]{:S(2)}) collective-permute-start(f32[2,16]{1,0:T(2,128)S(1)} %add.206), channel_id=1, source_target_pairs={{0,256},{32,288},{64,320},{96,352},{128,384},{160,416},{192,448},{... | collective-permute-start | bytes 392 | tf_op jit(solution)/shard_map/ppermute | solution.py:41
  180.5 3.9 %collective-permute-start.14 = (f32[16,6,320]{2,0,1:T(8,128)S(1)}, f32[16,6,320]{2,0,1:T(8,128)S(1)}, u32[]{:S(2)}, u32[]{:S(2)}) collective-permute-start(f32[16,6,320]{2,0,1:T(8,128)S(1)} %get-tuple-element.17), channel_id=1, source_target_pairs={{1,0},{2,1},{3,2},{4,3},{5,4},{6,5},{7,6},{8,7},{9,8},{10,9},{11,1... | collective-permute-start | bytes 368648 | tf_op jit(solution)/shard_map/ppermute | solution.py:26
  194.3 35.4 %copy-start.4 = (f32[16,16,256]{2,0,1:T(8,128)S(1)}, f32[16,16,256]{2,0,1:T(8,128)}, u32[]{:S(2)}) copy-start(f32[16,16,256]{2,0,1:T(8,128)} %copy-done.2) | copy-start | bytes 786436
  228.9 66.2 %copy-start.42 = (f32[2,16]{1,0:T(2,128)S(1)}, f32[2,16]{1,0:T(2,128)}, u32[]{:S(2)}) copy-start(f32[2,16]{1,0:T(2,128)} %copy-done.41) | copy-start | bytes 388
  230.7 3.1 %collective-permute-start.15 = (f32[4,16]{1,0:T(4,128)S(1)}, f32[4,16]{1,0:T(4,128)S(1)}, u32[]{:S(2)}, u32[]{:S(2)}) collective-permute-start(f32[4,16]{1,0:T(4,128)S(1)} %pad_maximum_fusion.13), channel_id=1, source_target_pairs={{0,1},{1,0},{2,3},{3,2},{4,5},{5,4},{6,7},{7,6},{8,9},{9,8},{10,11... | collective-permute-start | bytes 776 | tf_op jit(solution)/shard_map/ppermute | solution.py:41
  233.8 5.5 %collective-permute-start.16 = (f32[4,16]{1,0:T(4,128)S(1)}, f32[4,16]{1,0:T(4,128)S(1)}, u32[]{:S(2)}, u32[]{:S(2)}) collective-permute-start(f32[4,16]{1,0:T(4,128)S(1)} %fusion.65), channel_id=1, source_target_pairs={{0,2},{1,3},{2,0},{3,1},{4,6},{5,7},{6,4},{7,5},{8,10},{9,11},{10,... | collective-permute-start | bytes 776 | tf_op jit(solution)/shard_map/ppermute | solution.py:41
  239.3 7.3 %collective-permute-start.17 = (f32[4,16]{1,0:T(4,128)S(1)}, f32[4,16]{1,0:T(4,128)S(1)}, u32[]{:S(2)}, u32[]{:S(2)}) collective-permute-start(f32[4,16]{1,0:T(4,128)S(1)} %fusion.91), channel_id=1, source_target_pairs={{0,4},{1,5},{2,6},{3,7},{4,0},{5,1},{6,2},{7,3},{8,12},{9,13},{10,... | collective-permute-start | bytes 776 | tf_op jit(solution)/shard_map/ppermute | solution.py:41
  246.6 9.4 %collective-permute-start.18 = (f32[4,16]{1,0:T(4,128)S(1)}, f32[4,16]{1,0:T(4,128)S(1)}, u32[]{:S(2)}, u32[]{:S(2)}) collective-permute-start(f32[4,16]{1,0:T(4,128)S(1)} %add.214), channel_id=1, source_target_pairs={{0,8},{1,9},{2,10},{3,11},{4,12},{5,13},{6,14},{7,15},{8,0},{9,1},... | collective-permute-start | bytes 776 | tf_op jit(solution)/shard_map/ppermute | solution.py:41
  256.0 14.2 %collective-permute-start.19 = (f32[4,16]{1,0:T(4,128)S(1)}, f32[4,16]{1,0:T(4,128)S(1)}, u32[]{:S(2)}, u32[]{:S(2)}) collective-permute-start(f32[4,16]{1,0:T(4,128)S(1)} %add.215), channel_id=1, source_target_pairs={{0,16},{1,17},{2,18},{3,19},{4,20},{5,21},{6,22},{7,23},{8,24},{9,... | collective-permute-start | bytes 776 | tf_op jit(solution)/shard_map/ppermute | solution.py:41
  270.1 5.5 %collective-permute-start.20 = (f32[4,16]{1,0:T(4,128)S(1)}, f32[4,16]{1,0:T(4,128)S(1)}, u32[]{:S(2)}, u32[]{:S(2)}) collective-permute-start(f32[4,16]{1,0:T(4,128)S(1)} %add.216), channel_id=1, source_target_pairs={{0,32},{32,0},{64,96},{96,64},{128,160},{160,128},{192,224},{224,1... | collective-permute-start | bytes 776 | tf_op jit(solution)/shard_map/ppermute | solution.py:41
  275.6 7.0 %collective-permute-start.21 = (f32[4,16]{1,0:T(4,128)S(1)}, f32[4,16]{1,0:T(4,128)S(1)}, u32[]{:S(2)}, u32[]{:S(2)}) collective-permute-start(f32[4,16]{1,0:T(4,128)S(1)} %add.217), channel_id=1, source_target_pairs={{0,64},{32,96},{64,0},{96,32},{128,192},{160,224},{192,128},{224,1... | collective-permute-start | bytes 776 | tf_op jit(solution)/shard_map/ppermute | solution.py:41
  282.6 5.5 %collective-permute-start.22 = (f32[4,16]{1,0:T(4,128)S(1)}, f32[4,16]{1,0:T(4,128)S(1)}, u32[]{:S(2)}, u32[]{:S(2)}) collective-permute-start(f32[4,16]{1,0:T(4,128)S(1)} %add.218), channel_id=1, source_target_pairs={{0,128},{32,160},{64,192},{96,224},{128,0},{160,32},{192,64},{224,... | collective-permute-start | bytes 776 | tf_op jit(solution)/shard_map/ppermute | solution.py:41
  288.1 7.0 %collective-permute-start.23 = (f32[4,16]{1,0:T(4,128)S(1)}, f32[4,16]{1,0:T(4,128)S(1)}, u32[]{:S(2)}, u32[]{:S(2)}) collective-permute-start(f32[4,16]{1,0:T(4,128)S(1)} %add.219), channel_id=1, source_target_pairs={{0,256},{32,288},{64,320},{96,352},{128,384},{160,416},{192,448},{... | collective-permute-start | bytes 776 | tf_op jit(solution)/shard_map/ppermute | solution.py:41
  (39 other events, 424.9 us)

commit v3 on v2

--- a/solution.py
+++ b/solution.py
@@ -30,18 +30,15 @@
     return cells
 
 
+def gathered(vector, axis):
+    count = lax.axis_size(axis)
+    copies = jnp.broadcast_to(vector[None], (count,) + vector.shape)
+    return lax.all_to_all(copies, axis, 0, 0, tiled=False)
+
+
 def all_sum(vector, axes):
     for axis in axes:
-        count = lax.axis_size(axis)
-        if count & (count - 1):
-            vector = lax.psum(vector, axis)
-            continue
-        stride = 1
-        while stride < count:
-            vector = vector + lax.ppermute(
-                vector, axis, [(i, i ^ stride) for i in range(count)]
-            )
-            stride *= 2
+        vector = jnp.sum(gathered(vector, axis), axis=0)
     return vector
 
 
@@ -115,7 +112,9 @@
         )
         upward = jnp.einsum("lab,mla->mlb", transfer, coeffs, precision=HIGHEST_PRECISION)
         panel_coeffs = jnp.einsum("lk,mlb->mkb", membership, upward, precision=HIGHEST_PRECISION)
-        band_coeffs = lax.all_gather(panel_coeffs, "band", axis=1, tiled=True)
+        band_coeffs = jnp.swapaxes(gathered(panel_coeffs, "band"), 0, 1).reshape(
+            panel_coeffs.shape[0], -1, panel_coeffs.shape[2]
+        )
         panel_far = jnp.einsum(
             "ksab,mksb->mka",
             panel_couple,

time: 298 us -> 220 us (0.74)
  the two profiles are of different devices: /device:TPU:32 before, /device:TPU:1 now
where the time goes in v3:
time: 220 us; the launch traced here: 219 us
  matrix products  88.3 us (40%)
  starting transfers between devices  42.9 us (20%)
  blocking collectives  29.5 us (13%)
  local copies, waits for them, and re-layouts  24.4 us (11%)
  other arithmetic  17.1 us (8%)
  waiting for transfers between devices  15.1 us (7%)
    dot_general x2, matrix products, covariance_apply(): jnp.einsum('lspq,mlsq->mlp', near_blocks, rim_values[:, near_rows], preci...  66.7 us
    all_to_all x2, blocking collectives, gathered(): return lax.all_to_all(copies, axis, 0, 0, tiled=False)  29.5 us
    all_to_all x4, starting transfers between devices, gathered(): return lax.all_to_all(copies, axis, 0, 0, tiled=False)  27.9 us
    all_to_all x4, waiting for transfers between devices, gathered(): return lax.all_to_all(copies, axis, 0, 0, tiled=False)  15.1 us
    ppermute x3, starting transfers between devices, extended(): lax.ppermute(head, axis, [((i + 1) % count, i) for i in range(count)])  9.64 us
    unnamed x94, local copies, waits for them, and re-layouts  8.28 us
    dot_general x2, matrix products, covariance_apply(): jnp.einsum('lsab,mlsb->mla', leaf_couple, rim_coeffs[:, far_rows], precis...  6.52 us
    ppermute x3, starting transfers between devices, extended(): lax.ppermute(tail, axis, [(i, (i + 1) % count) for i in range(count)])  5.38 us
  transfers between devices with their start and end apart: 10, of which 3 were waited for; matrix products, arithmetic and copies ran while one was open for 15% of the time, Pallas kernels for 0%

profile of v3, /device:TPU:1, one launch (start us, length us, event | category | flops | bytes accessed | tf_op | source)
XLA Modules:
  0.0 218.6 jit_solution(10291585088330408136)
XLA Ops:
  1.7 3.0 %collective-permute-start.2 = (f32[3,2,256]{2,0,1:T(4,128)S(1)}, f32[3,2,256]{2,0,1:T(4,128)S(1)}, u32[]{:S(2)}, u32[]{:S(2)}) collective-permute-start(f32[3,2,256]{2,0,1:T(4,128)S(1)} %get-tuple-element.25), channel_id=1, source_target_pairs={{0,1},{1,2},{2,3},{3,4},{4,5},{5,6},{6,7},{7,8},{8,9},{9,10},{10,1... | collective-permute-start | bytes 18440 | tf_op jit(solution)/shard_map/ppermute | solution.py:24
  4.7 3.9 %collective-permute-start.3 = (f32[3,2,256]{2,0,1:T(4,128)S(1)}, f32[3,2,256]{2,0,1:T(4,128)S(1)}, u32[]{:S(2)}, u32[]{:S(2)}) collective-permute-start(f32[3,2,256]{2,0,1:T(4,128)S(1)} %get-tuple-element.26), channel_id=1, source_target_pairs={{1,0},{2,1},{3,2},{4,3},{5,4},{6,5},{7,6},{8,7},{9,8},{10,9},{11,1... | collective-permute-start | bytes 18440 | tf_op jit(solution)/shard_map/ppermute | solution.py:26
  8.6 2.4 %convolution_bitcast_fusion.9 = f32[16,16,64]{2,0,1:T(8,128)S(1)} fusion(f32[16,256,64]{1,2,0:T(8,128)} %param.14, f32[16,16,256]{2,1,0:T(8,128)} %param.11), kind=kOutput, calls=%fused_computation.51 | convolution fusion | flops 50331648 | bytes 1376256 | tf_op jit(solution)/shard_map/lpr,mlp->mlr/dot_general | solution.py:100
  11.0 1.6 convolution_bitcast_fusion.6
  13.7 4.2 %all-to-all-start = ((f32[16,1,2048]{2,1,0:T(1,128)}), f32[16,1,2048]{2,1,0:T(1,128)}, u32[]{:S(2)}, u32[]{:S(2)}) async-start(f32[16,1,2048]{2,1,0:T(1,128)} %reshape.155), calls=%async_computation | async-start | bytes 262144 | tf_op jit(solution)/shard_map/all_to_all | solution.py:36
  19.6 5.7 %collective-permute-start.1 = (f32[16,6,320]{2,0,1:T(8,128)}, f32[16,6,320]{2,0,1:T(8,128)}, u32[]{:S(2)}, u32[]{:S(2)}) collective-permute-start(f32[16,6,320]{2,0,1:T(8,128)} %get-tuple-element.24), channel_id=1, source_target_pairs={{1,0},{2,1},{3,2},{4,3},{5,4},{6,5},{7,6},{8,7},{9,8},{10,9},{11,1... | collective-permute-start | bytes 368648 | tf_op jit(solution)/shard_map/ppermute | solution.py:26
  31.2 1.8 reduce
  34.0 1.6 convolution_bitcast_fusion.5
  36.4 1.9 gather_fusion
  39.1 1.4 gather_fusion.2
  40.6 3.0 %convolution_bitcast_fusion.7 = f32[16,16,64]{2,1,0:T(8,128)S(1)} fusion(f32[16,16,4,64]{3,0,2,1:T(8,128)} %bitcast.175, f32[16,4,64,64]{3,2,1,0:T(8,128)S(1)} %copy-done), kind=kOutput, calls=%fused_computation.49 | convolution fusion | flops 50331648 | bytes 1376256 | tf_op jit(solution)/shard_map/lsab,mlsb->mla/dot_general | solution.py:110
  44.7 32.3 %fusion.29 = f32[16,16,256]{2,0,1:T(8,128)S(1)} fusion(f32[16,16,5,256]{3,0,2,1:T(8,128)S(1)} %bitcast.172, f32[16,5]{1,0:T(8,128)S(1)} %copy-done.34, f32[16,5,256]{2,1,0:T(8,128)S(1)} %copy-done.22, f32[16,256]{1,0:T(8,128)S(1)} %copy-done.28, f32[16,5,256]{2,1,0:T(8,128)S(1)} %copy-done.21, f32[16,256]{1,0:T(8,128)S(1)} %copy-done.30, ...), kind=kOutput, calls=%fused_computation.39 | convolution fusion | flops 1080164352 | bytes 2146624 | tf_op jit(solution)/shard_map/lspq,mlsq->mlp/dot_general | solution.py:107
  78.5 12.2 %all-to-all-start.1 = ((f32[32,2,16]{2,1,0:T(2,128)}), f32[32,2,16]{2,1,0:T(2,128)}, u32[]{:S(2)}, u32[]{:S(2)}) async-start(f32[32,2,16]{2,1,0:T(2,128)} %broadcast_in_dim.34), calls=%async_computation.1 | async-start | bytes 65536 | tf_op jit(solution)/shard_map/all_to_all | solution.py:36
  91.7 1.6 convolution_bitcast_fusion.3
  94.3 8.6 %all-to-all-done.1 = f32[32,2,16]{2,1,0:T(2,128)} async-done(((f32[32,2,16]{2,1,0:T(2,128)}), f32[32,2,16]{2,1,0:T(2,128)}, u32[]{:S(2)}, u32[]{:S(2)}) %all-to-all-start.1) | async-done | bytes 4128 | tf_op jit(solution)/shard_map/all_to_all | solution.py:36
  105.6 6.9 %all-to-all-start.2 = ((f32[16,2,16]{2,1,0:T(2,128)}), f32[16,2,16]{2,1,0:T(2,128)}, u32[]{:S(2)}, u32[]{:S(2)}) async-start(f32[16,2,16]{2,1,0:T(2,128)} %broadcast_in_dim.35), calls=%async_computation.2 | async-start | bytes 32768 | tf_op jit(solution)/shard_map/all_to_all | solution.py:36
  113.2 1.8 reshape.157
  115.0 1.6 collective-permute-start.4
  116.6 2.4 %all-to-all-done.2 = f32[16,2,16]{2,1,0:T(2,128)} async-done(((f32[16,2,16]{2,1,0:T(2,128)}), f32[16,2,16]{2,1,0:T(2,128)}, u32[]{:S(2)}, u32[]{:S(2)}) %all-to-all-start.2) | async-done | bytes 2080 | tf_op jit(solution)/shard_map/all_to_all | solution.py:36
  119.0 4.6 %all-to-all-start.3 = ((f32[16,1,2048]{2,1,0:T(1,128)}), f32[16,1,2048]{2,1,0:T(1,128)}, u32[]{:S(2)}, u32[]{:S(2)}) async-start(f32[16,1,2048]{2,1,0:T(1,128)} %reshape.157), calls=%async_computation.3 | async-start | bytes 262144 | tf_op jit(solution)/shard_map/all_to_all | solution.py:36
  126.2 4.1 %all-to-all-done.3 = f32[16,1,2048]{2,1,0:T(1,128)} async-done(((f32[16,1,2048]{2,1,0:T(1,128)}), f32[16,1,2048]{2,1,0:T(1,128)}, u32[]{:S(2)}, u32[]{:S(2)}) %all-to-all-start.3) | async-done | bytes 131104 | tf_op jit(solution)/shard_map/all_to_all | solution.py:36
  130.3 2.5 %reduce.1 = f32[16,2048]{1,0:T(8,128)} reduce(f32[16,1,2048]{2,1,0:T(1,128)} %all-to-all-done.3, f32[]{:T(128)} %broadcast.94), dimensions={1}, to_apply=%all_to_all.21.reduce_sub_computation | reduce | bytes 262148 | tf_op jit(solution)/shard_map/all_to_all | solution.py:36
  132.8 1.7 reshape.158
  134.5 2.2 %gather_fusion.6 = f32[4,16,64]{2,1,0:T(8,128)} fusion(f32[16,32,64]{2,0,1:T(8,128)} %bitcast.178, s32[1024]{0:T(1024)} %pad_clamp_fusion), kind=kCustom, calls=%fused_computation.6 | custom fusion | bytes 32784 | tf_op jit(solution)/shard_map/gather | solution.py:121
  138.8 1.5 pad_maximum_fusion.2
  140.3 2.3 %gather_fusion.5 = f32[64,16,64]{2,1,0:T(8,128)} fusion(f32[16,28,64]{2,0,1:T(8,128)} %pad_maximum_fusion.2, s32[1024]{0:T(1024)S(1)} %copy-done.24), kind=kCustom, calls=%fused_computation.5 | custom fusion | bytes 524544 | tf_op jit(solution)/shard_map/gather | solution.py:111
  142.7 3.6 %convolution_bitcast_fusion.4 = f32[16,16,64]{2,1,0:T(8,128)} fusion(f32[16,16,4,64]{3,0,2,1:T(8,128)} %bitcast.174, f32[16,4,64,64]{3,2,1,0:T(8,128)S(1)} %copy-done), kind=kOutput, calls=%fused_computation.44 | convolution fusion | flops 50331648 | bytes 1376256 | tf_op jit(solution)/shard_map/lsab,mlsb->mla/dot_general | solution.py:110
  147.1 1.8 gather_fusion.4
  148.9 34.5 %fusion.28 = f32[16,16,256]{2,0,1:T(8,128)S(1)} fusion(f32[16,16,5,256]{3,0,2,1:T(8,128)} %bitcast.173, f32[16,5]{1,0:T(8,128)S(1)} %copy-done.34, f32[16,5,256]{2,1,0:T(8,128)} %get-tuple-element.22, f32[16,256]{1,0:T(8,128)S(1)} %copy-done.29, f32[16,5,256]{2,1,0:T(8,128)} %get-tuple-element.21, f32[16,256]{1,0:T(8,128)S(1)} %copy-done.31, ...), kind=kOutput, calls=%fused_computation.38 | convolution fusion | flops 1080164352 | bytes 2146624 | tf_op jit(solution)/shard_map/lspq,mlsq->mlp/dot_general | solution.py:107
  184.4 1.6 multiply_reduce_fusion.3
  186.0 19.9 %all_to_all.30 = f32[32,4,16]{2,1,0:T(4,128)S(1)} all-to-all(f32[32,4,16]{2,1,0:T(4,128)S(1)} %broadcast_in_dim.37), channel_id=1, replica_groups=mesh['band'=16,'lon'=32] {'lon'}, dimensions={0} | all-to-all | bytes 16384 | tf_op jit(solution)/shard_map/all_to_all | solution.py:36
  206.0 9.6 %all_to_all.31 = f32[16,4,16]{2,1,0:T(4,128)S(1)} all-to-all(f32[16,4,16]{2,1,0:T(4,128)S(1)} %broadcast_in_dim.38), channel_id=1, replica_groups=mesh['band'=16,'lon'=32] {'band'}, dimensions={0} | all-to-all | bytes 8192 | tf_op jit(solution)/shard_map/all_to_all | solution.py:36
  (153 shorter events, 29.6 us)
Async XLA Ops:
  0.6 40.0 %copy-start = (f32[16,4,64,64]{3,2,1,0:T(8,128)S(1)}, f32[16,4,64,64]{3,2,1,0:T(8,128)}, u32[]{:S(2)}) copy-start(f32[16,4,64,64]{3,2,1,0:T(8,128)} %param.15) | copy-start | bytes 3145732
  0.6 17.2 %copy-start.5 = (f32[16,16,256]{2,1,0:T(8,128)S(1)}, f32[16,16,256]{2,1,0:T(8,128)}, u32[]{:S(2)}) copy-start(f32[16,16,256]{2,1,0:T(8,128)} %param.11) | copy-start | bytes 786436
  0.7 11.9 %copy-start.32 = (s32[16]{0:T(128)S(1)}, s32[16]{0:T(128)}, u32[]{:S(2)}) copy-start(s32[16]{0:T(128)} %param.21) | copy-start | bytes 196
  1.7 27.3 %collective-permute-start.2 = (f32[3,2,256]{2,0,1:T(4,128)S(1)}, f32[3,2,256]{2,0,1:T(4,128)S(1)}, u32[]{:S(2)}, u32[]{:S(2)}) collective-permute-start(f32[3,2,256]{2,0,1:T(4,128)S(1)} %get-tuple-element.25), channel_id=1, source_target_pairs={{0,1},{1,2},{2,3},{3,4},{4,5},{5,6},{6,7},{7,8},{8,9},{9,10},{10,1... | collective-permute-start | bytes 18440 | tf_op jit(solution)/shard_map/ppermute | solution.py:24
  4.7 21.3 %copy-start.25 = (s32[16,5]{0,1:T(8,128)S(1)}, s32[16,5]{0,1:T(8,128)}, u32[]{:S(2)}) copy-start(s32[16,5]{0,1:T(8,128)} %param.18) | copy-start | bytes 964
  4.7 21.3 %copy-start.39 = (s32[2,2]{1,0:T(2,128)S(1)}, s32[2,2]{1,0:T(2,128)}, u32[]{:S(2)}) copy-start(s32[2,2]{1,0:T(2,128)} %param.20) | copy-start | bytes 52
  4.7 21.4 %copy-start.37 = (s32[16,4]{0,1:T(4,128)S(1)}, s32[16,4]{0,1:T(4,128)}, u32[]{:S(2)}) copy-start(s32[16,4]{0,1:T(4,128)} %param.19) | copy-start | bytes 772
  4.7 22.4 %copy-start.19 = (f32[3,16,256]{2,1,0:T(8,128)S(1)}, f32[3,16,256]{2,1,0:T(8,128)}, u32[]{:S(2)}) copy-start(f32[3,16,256]{2,1,0:T(8,128)} %param.13) | copy-start | bytes 147460
  4.7 24.3 %collective-permute-start.3 = (f32[3,2,256]{2,0,1:T(4,128)S(1)}, f32[3,2,256]{2,0,1:T(4,128)S(1)}, u32[]{:S(2)}, u32[]{:S(2)}) collective-permute-start(f32[3,2,256]{2,0,1:T(4,128)S(1)} %get-tuple-element.26), channel_id=1, source_target_pairs={{1,0},{2,1},{3,2},{4,3},{5,4},{6,5},{7,6},{8,7},{9,8},{10,9},{11,1... | collective-permute-start | bytes 18440 | tf_op jit(solution)/shard_map/ppermute | solution.py:26
  13.7 16.9 %all-to-all-start = ((f32[16,1,2048]{2,1,0:T(1,128)}), f32[16,1,2048]{2,1,0:T(1,128)}, u32[]{:S(2)}, u32[]{:S(2)}) async-start(f32[16,1,2048]{2,1,0:T(1,128)} %reshape.155), calls=%async_computation | async-start | bytes 262144 | tf_op jit(solution)/shard_map/all_to_all | solution.py:36
  18.1 15.7 %copy-start.15 = (f32[2,2,64,64]{3,2,1,0:T(8,128)S(1)}, f32[2,2,64,64]{3,2,1,0:T(8,128)}, u32[]{:S(2)}) copy-start(f32[2,2,64,64]{3,2,1,0:T(8,128)} %param.17) | copy-start | bytes 196612
  18.8 16.8 %collective-permute-start = (f32[16,6,320]{2,0,1:T(8,128)}, f32[16,6,320]{2,0,1:T(8,128)S(1)}, u32[]{:S(2)}, u32[]{:S(2)}) collective-permute-start(f32[16,6,320]{2,0,1:T(8,128)} %get-tuple-element.23), channel_id=1, source_target_pairs={{0,1},{1,2},{2,3},{3,4},{4,5},{5,6},{6,7},{7,8},{8,9},{9,10},{10,1... | collective-permute-start | bytes 368648 | tf_op jit(solution)/shard_map/ppermute | solution.py:24
  19.6 16.0 %collective-permute-start.1 = (f32[16,6,320]{2,0,1:T(8,128)}, f32[16,6,320]{2,0,1:T(8,128)}, u32[]{:S(2)}, u32[]{:S(2)}) collective-permute-start(f32[16,6,320]{2,0,1:T(8,128)} %get-tuple-element.24), channel_id=1, source_target_pairs={{1,0},{2,1},{3,2},{4,3},{5,4},{6,5},{7,6},{8,7},{9,8},{10,9},{11,1... | collective-permute-start | bytes 368648 | tf_op jit(solution)/shard_map/ppermute | solution.py:26
  44.6 32.3 %copy-start.1 = (f32[16,256,64]{1,2,0:T(8,128)S(1)}, f32[16,256,64]{1,2,0:T(8,128)}, u32[]{:S(2)}) copy-start(f32[16,256,64]{1,2,0:T(8,128)} %param.14) | copy-start | bytes 3145732
  44.6 32.3 %copy-start.6 = (f32[16,16,256]{2,1,0:T(8,128)S(1)}, f32[16,16,256]{2,1,0:T(8,128)}, u32[]{:S(2)}) copy-start(f32[16,16,256]{2,1,0:T(8,128)} %param.11) | copy-start | bytes 786436
  44.6 33.2 %copy-start.36 = (f32[16]{0:T(128)S(1)}, f32[16]{0:T(128)}, u32[]{:S(2)}) copy-start(f32[16]{0:T(128)} %multiply_reduce_fusion.5) | copy-start | bytes 196
  76.9 16.4 %copy-start.33 = (s32[16]{0:T(128)S(1)}, s32[16]{0:T(128)}, u32[]{:S(2)}) copy-start(s32[16]{0:T(128)} %param.21) | copy-start | bytes 196
  77.8 61.0 %copy-start.2 = (f32[16,16,256]{2,0,1:T(8,128)}, f32[16,16,256]{2,0,1:T(8,128)S(1)}, u32[]{:S(2)}) copy-start(f32[16,16,256]{2,0,1:T(8,128)S(1)} %get-tuple-element.31) | copy-start | bytes 786436
  78.5 24.4 %all-to-all-start.1 = ((f32[32,2,16]{2,1,0:T(2,128)}), f32[32,2,16]{2,1,0:T(2,128)}, u32[]{:S(2)}, u32[]{:S(2)}) async-start(f32[32,2,16]{2,1,0:T(2,128)} %broadcast_in_dim.34), calls=%async_computation.1 | async-start | bytes 65536 | tf_op jit(solution)/shard_map/all_to_all | solution.py:36
  91.7 48.7 %copy-start.11 = (f32[16,16,64]{2,0,1:T(8,128)}, f32[16,16,64]{2,0,1:T(8,128)S(1)}, u32[]{:S(2)}) copy-start(f32[16,16,64]{2,0,1:T(8,128)S(1)} %convolution_bitcast_fusion.8) | copy-start | bytes 196612
  93.3 47.0 %copy-start.24 = (s32[1024]{0:T(1024)S(1)}, s32[1024]{0:T(1024)}, u32[]{:S(2)}) copy-start(s32[1024]{0:T(1024)} %pad_clamp_fusion.1) | copy-start | bytes 12292
  105.6 13.4 %all-to-all-start.2 = ((f32[16,2,16]{2,1,0:T(2,128)}), f32[16,2,16]{2,1,0:T(2,128)}, u32[]{:S(2)}, u32[]{:S(2)}) async-start(f32[16,2,16]{2,1,0:T(2,128)} %broadcast_in_dim.35), calls=%async_computation.2 | async-start | bytes 32768 | tf_op jit(solution)/shard_map/all_to_all | solution.py:36
  115.0 23.8 %collective-permute-start.4 = (f32[16,6,320]{2,0,1:T(8,128)}, f32[16,6,320]{2,0,1:T(8,128)}, u32[]{:S(2)}, u32[]{:S(2)}) collective-permute-start(f32[16,6,320]{2,0,1:T(8,128)} %get-tuple-element.18), channel_id=1, source_target_pairs={{0,1},{1,2},{2,3},{3,4},{4,5},{5,6},{6,7},{7,8},{8,9},{9,10},{10,1... | collective-permute-start | bytes 368648 | tf_op jit(solution)/shard_map/ppermute | solution.py:24
  116.6 22.2 %collective-permute-start.5 = (f32[16,6,320]{2,0,1:T(8,128)}, f32[16,6,320]{2,0,1:T(8,128)}, u32[]{:S(2)}, u32[]{:S(2)}) collective-permute-start(f32[16,6,320]{2,0,1:T(8,128)} %get-tuple-element.19), channel_id=1, source_target_pairs={{1,0},{2,1},{3,2},{4,3},{5,4},{6,5},{7,6},{8,7},{9,8},{10,9},{11,1... | collective-permute-start | bytes 368648 | tf_op jit(solution)/shard_map/ppermute | solution.py:26
  119.0 11.3 %all-to-all-start.3 = ((f32[16,1,2048]{2,1,0:T(1,128)}), f32[16,1,2048]{2,1,0:T(1,128)}, u32[]{:S(2)}, u32[]{:S(2)}) async-start(f32[16,1,2048]{2,1,0:T(1,128)} %reshape.157), calls=%async_computation.3 | async-start | bytes 262144 | tf_op jit(solution)/shard_map/all_to_all | solution.py:36
  148.9 34.5 %copy-start.9 = (f32[16,64,64]{2,1,0:T(8,128)S(1)}, f32[16,64,64]{2,1,0:T(8,128)}, u32[]{:S(2)}) copy-start(f32[16,64,64]{2,1,0:T(8,128)} %param.16) | copy-start | bytes 786436
  148.9 34.5 %copy-start.13 = (f32[16,16,64]{2,1,0:T(8,128)S(1)}, f32[16,16,64]{2,1,0:T(8,128)}, u32[]{:S(2)}) copy-start(f32[16,16,64]{2,1,0:T(8,128)} %convolution_bitcast_fusion.2) | copy-start | bytes 196612
  148.9 34.5 %copy-start.16 = (f32[16,16,64]{2,1,0:T(8,128)S(1)}, f32[16,16,64]{2,1,0:T(8,128)}, u32[]{:S(2)}) copy-start(f32[16,16,64]{2,1,0:T(8,128)} %convolution_bitcast_fusion.4) | copy-start | bytes 196612
  148.9 35.4 %copy-start.4 = (f32[16,16,256]{2,0,1:T(8,128)S(1)}, f32[16,16,256]{2,0,1:T(8,128)}, u32[]{:S(2)}) copy-start(f32[16,16,256]{2,0,1:T(8,128)} %copy-done.2) | copy-start | bytes 786436
  148.9 35.4 %copy-start.7 = (f32[16,16,256]{2,1,0:T(8,128)S(1)}, f32[16,16,256]{2,1,0:T(8,128)}, u32[]{:S(2)}) copy-start(f32[16,16,256]{2,1,0:T(8,128)} %param.11) | copy-start | bytes 786436
  148.9 35.4 %copy-start.38 = (f32[16]{0:T(128)S(1)}, f32[16]{0:T(128)}, u32[]{:S(2)}) copy-start(f32[16]{0:T(128)} %bitcast_divide_fusion.1) | copy-start | bytes 196
  183.4 32.2 %copy-start.35 = (f32[2,16]{1,0:T(2,128)S(1)}, f32[2,16]{1,0:T(2,128)}, u32[]{:S(2)}) copy-start(f32[2,16]{1,0:T(2,128)} %reduce_sum.93) | copy-start | bytes 388
  (20 other events, 70.0 us)

commit v4 on v3

--- a/solution.py
+++ b/solution.py
@@ -42,13 +42,13 @@
     return vector
 
 
-def matern_block(rows_pos, cols_pos, length_scale):
-    squared = jnp.zeros((cols_pos.shape[1], rows_pos.shape[1], cols_pos.shape[2]), jnp.float32)
+def matern_shape(rows_pos, cols_pos, length_scale):
+    squared = None
     for component in range(3):
         offset = rows_pos[component][None, :, None] - cols_pos[component][:, None, :]
-        squared = squared + offset * offset
-    scaled = ROOT_THREE * jnp.sqrt(squared) / length_scale
-    return AMPLITUDE * (1.0 + scaled) * jnp.exp(-scaled)
+        squared = offset * offset if squared is None else squared + offset * offset
+    scaled = jnp.sqrt(squared) * (ROOT_THREE / length_scale)
+    return (1.0 + scaled) * jnp.exp(-scaled)
 
 
 def on_device(
@@ -82,14 +82,11 @@
     far_rows = rim_index(far_list, REACH)
     rim_pos = extended(position, (("lon", 1),), near_depth)
 
-    def leaf_blocks(inputs):
-        rows_pos, rows_index, slot_mask = inputs
-        cols_pos = rim_pos[:, rows_index]
-        return matern_block(rows_pos, cols_pos, length_scale) * slot_mask[:, None, None]
+    def leaf_blocks(rows_pos, rows_index):
+        return matern_shape(rows_pos, rim_pos[:, rows_index], length_scale)
 
-    near_blocks = jax.vmap(lambda *leaf: leaf_blocks(leaf))(
-        jnp.transpose(position, (1, 0, 2)), near_rows, near_valid.astype(jnp.float32)
-    )
+    near_blocks = jax.vmap(leaf_blocks)(jnp.transpose(position, (1, 0, 2)), near_rows)
+    slot_scale = AMPLITUDE * near_valid.astype(jnp.float32)
     band_slot = panel_list // (lon_count * panel_count)
     gathered_rows = band_slot * panel_count + panel_list % panel_count
     membership = (leaf_panel[:, None] == jnp.arange(panel_count, dtype=jnp.int32)[None, :]).astype(
@@ -104,8 +101,9 @@
             :, REACH - near_depth : REACH + local_leaves + near_depth, :pixel_count
         ]
         rim_coeffs = rim_joined[:, :, pixel_count:]
+        near_values = rim_values[:, near_rows] * slot_scale[None, :, :, None]
         near_part = jnp.einsum(
-            "lspq,mlsq->mlp", near_blocks, rim_values[:, near_rows], precision=HIGHEST_PRECISION
+            "lspq,mlsq->mlp", near_blocks, near_values, precision=lax.Precision.HIGH
         )
         leaf_far = jnp.einsum(
             "lsab,mlsb->mla", leaf_couple, rim_coeffs[:, far_rows], precision=HIGHEST_PRECISION

time: 220 us -> 201 us (0.914)
  matrix products: 88.3 us -> 69.1 us
    dot_general x2, matrix products: 66.7 us -> 47.6 us  [covariance_apply(): jnp.einsum('lspq,mlsq->mlp', near_blocks, near_values, precision=lax.Prec...]
  transfers between devices with their start and end apart: 10 -> 10, of which waited for: 3 -> 3; matrix products, arithmetic and copies ran while one was open for 15% -> 17% of each run, Pallas kernels for 0% -> 0%
where the time goes in v4:
time: 201 us; the launch traced here: 199 us
  matrix products  69.1 us (34%)
  starting transfers between devices  42.9 us (21%)
  blocking collectives  29.5 us (15%)
  local copies, waits for them, and re-layouts  24.4 us (12%)
  other arithmetic  17.1 us (9%)
  waiting for transfers between devices  15.1 us (8%)
    dot_general x2, matrix products, covariance_apply(): jnp.einsum('lspq,mlsq->mlp', near_blocks, near_values, precision=lax.Prec...  47.6 us
    all_to_all x2, blocking collectives, gathered(): return lax.all_to_all(copies, axis, 0, 0, tiled=False)  29.5 us
    all_to_all x4, starting transfers between devices, gathered(): return lax.all_to_all(copies, axis, 0, 0, tiled=False)  27.9 us
    all_to_all x4, waiting for transfers between devices, gathered(): return lax.all_to_all(copies, axis, 0, 0, tiled=False)  15.1 us
    ppermute x3, starting transfers between devices, extended(): lax.ppermute(head, axis, [((i + 1) % count, i) for i in range(count)])  9.64 us
    unnamed x94, local copies, waits for them, and re-layouts  8.28 us
    dot_general x2, matrix products, covariance_apply(): jnp.einsum('lsab,mlsb->mla', leaf_couple, rim_coeffs[:, far_rows], precis...  6.52 us
    ppermute x3, starting transfers between devices, extended(): lax.ppermute(tail, axis, [(i, (i + 1) % count) for i in range(count)])  5.38 us
  transfers between devices with their start and end apart: 10, of which 3 were waited for; matrix products, arithmetic and copies ran while one was open for 17% of the time, Pallas kernels for 0%

profile of v4, /device:TPU:1, one launch (start us, length us, event | category | flops | bytes accessed | tf_op | source)
XLA Modules:
  0.0 199.4 jit_solution(14793443736013807012)
XLA Ops:
  1.7 3.0 %collective-permute-start.2 = (f32[3,2,256]{2,0,1:T(4,128)S(1)}, f32[3,2,256]{2,0,1:T(4,128)S(1)}, u32[]{:S(2)}, u32[]{:S(2)}) collective-permute-start(f32[3,2,256]{2,0,1:T(4,128)S(1)} %get-tuple-element.25), channel_id=1, source_target_pairs={{0,1},{1,2},{2,3},{3,4},{4,5},{5,6},{6,7},{7,8},{8,9},{9,10},{10,1... | collective-permute-start | bytes 18440 | tf_op jit(solution)/shard_map/ppermute | solution.py:24
  4.7 3.9 %collective-permute-start.3 = (f32[3,2,256]{2,0,1:T(4,128)S(1)}, f32[3,2,256]{2,0,1:T(4,128)S(1)}, u32[]{:S(2)}, u32[]{:S(2)}) collective-permute-start(f32[3,2,256]{2,0,1:T(4,128)S(1)} %get-tuple-element.26), channel_id=1, source_target_pairs={{1,0},{2,1},{3,2},{4,3},{5,4},{6,5},{7,6},{8,7},{9,8},{10,9},{11,1... | collective-permute-start | bytes 18440 | tf_op jit(solution)/shard_map/ppermute | solution.py:26
  8.6 2.4 %convolution_bitcast_fusion.9 = f32[16,16,64]{2,0,1:T(8,128)S(1)} fusion(f32[16,256,64]{1,2,0:T(8,128)} %param.14, f32[16,16,256]{2,1,0:T(8,128)} %param.11), kind=kOutput, calls=%fused_computation.51 | convolution fusion | flops 50331648 | bytes 1376256 | tf_op jit(solution)/shard_map/lpr,mlp->mlr/dot_general | solution.py:97
  11.0 1.6 convolution_bitcast_fusion.6
  13.7 4.2 %all-to-all-start = ((f32[16,1,2048]{2,1,0:T(1,128)}), f32[16,1,2048]{2,1,0:T(1,128)}, u32[]{:S(2)}, u32[]{:S(2)}) async-start(f32[16,1,2048]{2,1,0:T(1,128)} %reshape.155), calls=%async_computation | async-start | bytes 262144 | tf_op jit(solution)/shard_map/all_to_all | solution.py:36
  19.6 5.7 %collective-permute-start.1 = (f32[16,6,320]{2,0,1:T(8,128)}, f32[16,6,320]{2,0,1:T(8,128)}, u32[]{:S(2)}, u32[]{:S(2)}) collective-permute-start(f32[16,6,320]{2,0,1:T(8,128)} %get-tuple-element.21), channel_id=1, source_target_pairs={{1,0},{2,1},{3,2},{4,3},{5,4},{6,5},{7,6},{8,7},{9,8},{10,9},{11,1... | collective-permute-start | bytes 368648 | tf_op jit(solution)/shard_map/ppermute | solution.py:26
  31.2 1.8 reduce
  34.0 1.6 convolution_bitcast_fusion.5
  36.4 1.9 gather_fusion
  39.1 1.4 gather_fusion.2
  40.6 3.0 %convolution_bitcast_fusion.7 = f32[16,16,64]{2,1,0:T(8,128)S(1)} fusion(f32[16,16,4,64]{3,0,2,1:T(8,128)} %bitcast.183, f32[16,4,64,64]{3,2,1,0:T(8,128)S(1)} %copy-done), kind=kOutput, calls=%fused_computation.49 | convolution fusion | flops 50331648 | bytes 1376256 | tf_op jit(solution)/shard_map/lsab,mlsb->mla/dot_general | solution.py:108
  44.7 24.6 %fusion.35 = f32[16,16,256]{2,0,1:T(8,128)S(1)} fusion(f32[16,5,256]{2,1,0:T(8,128)S(1)} %copy-done.22, f32[16,256]{1,0:T(8,128)S(1)} %copy-done.28, f32[16,5,256]{2,1,0:T(8,128)S(1)} %copy-done.21, f32[16,256]{1,0:T(8,128)S(1)} %copy-done.30, f32[16,5,256]{2,1,0:T(8,128)S(1)} %copy-done.20, f32[16,256]{1,0:T(8,128)S(1)} %copy-done.26, ...), kind=kOutput, calls=%fused_computation.39 | convolution fusion | flops 566689792 | bytes 2146624 | tf_op jit(solution)/shard_map/lspq,mlsq->mlp/dot_general | solution.py:105
  70.8 12.2 %all-to-all-start.1 = ((f32[32,2,16]{2,1,0:T(2,128)}), f32[32,2,16]{2,1,0:T(2,128)}, u32[]{:S(2)}, u32[]{:S(2)}) async-start(f32[32,2,16]{2,1,0:T(2,128)} %broadcast_in_dim.34), calls=%async_computation.1 | async-start | bytes 65536 | tf_op jit(solution)/shard_map/all_to_all | solution.py:36
  84.0 1.6 convolution_bitcast_fusion.3
  86.6 8.6 %all-to-all-done.1 = f32[32,2,16]{2,1,0:T(2,128)} async-done(((f32[32,2,16]{2,1,0:T(2,128)}), f32[32,2,16]{2,1,0:T(2,128)}, u32[]{:S(2)}, u32[]{:S(2)}) %all-to-all-start.1) | async-done | bytes 4128 | tf_op jit(solution)/shard_map/all_to_all | solution.py:36
  97.8 6.9 %all-to-all-start.2 = ((f32[16,2,16]{2,1,0:T(2,128)}), f32[16,2,16]{2,1,0:T(2,128)}, u32[]{:S(2)}, u32[]{:S(2)}) async-start(f32[16,2,16]{2,1,0:T(2,128)} %broadcast_in_dim.35), calls=%async_computation.2 | async-start | bytes 32768 | tf_op jit(solution)/shard_map/all_to_all | solution.py:36
  105.5 1.8 reshape.157
  107.3 1.6 collective-permute-start.4
  108.9 2.4 %all-to-all-done.2 = f32[16,2,16]{2,1,0:T(2,128)} async-done(((f32[16,2,16]{2,1,0:T(2,128)}), f32[16,2,16]{2,1,0:T(2,128)}, u32[]{:S(2)}, u32[]{:S(2)}) %all-to-all-start.2) | async-done | bytes 2080 | tf_op jit(solution)/shard_map/all_to_all | solution.py:36
  111.3 4.6 %all-to-all-start.3 = ((f32[16,1,2048]{2,1,0:T(1,128)}), f32[16,1,2048]{2,1,0:T(1,128)}, u32[]{:S(2)}, u32[]{:S(2)}) async-start(f32[16,1,2048]{2,1,0:T(1,128)} %reshape.157), calls=%async_computation.3 | async-start | bytes 262144 | tf_op jit(solution)/shard_map/all_to_all | solution.py:36
  118.5 4.1 %all-to-all-done.3 = f32[16,1,2048]{2,1,0:T(1,128)} async-done(((f32[16,1,2048]{2,1,0:T(1,128)}), f32[16,1,2048]{2,1,0:T(1,128)}, u32[]{:S(2)}, u32[]{:S(2)}) %all-to-all-start.3) | async-done | bytes 131104 | tf_op jit(solution)/shard_map/all_to_all | solution.py:36
  122.6 2.5 %reduce.1 = f32[16,2048]{1,0:T(8,128)} reduce(f32[16,1,2048]{2,1,0:T(1,128)} %all-to-all-done.3, f32[]{:T(128)} %broadcast.107), dimensions={1}, to_apply=%all_to_all.21.reduce_sub_computation | reduce | bytes 262148 | tf_op jit(solution)/shard_map/all_to_all | solution.py:36
  125.1 1.7 reshape.158
  126.8 2.2 %gather_fusion.6 = f32[4,16,64]{2,1,0:T(8,128)} fusion(f32[16,32,64]{2,0,1:T(8,128)} %bitcast.186, s32[1024]{0:T(1024)} %pad_clamp_fusion), kind=kCustom, calls=%fused_computation.6 | custom fusion | bytes 32784 | tf_op jit(solution)/shard_map/gather | solution.py:119
  131.1 1.5 pad_maximum_fusion.2
  132.6 2.3 %gather_fusion.5 = f32[64,16,64]{2,1,0:T(8,128)} fusion(f32[16,28,64]{2,0,1:T(8,128)} %pad_maximum_fusion.2, s32[1024]{0:T(1024)S(1)} %copy-done.24), kind=kCustom, calls=%fused_computation.5 | custom fusion | bytes 524544 | tf_op jit(solution)/shard_map/gather | solution.py:109
  135.0 3.6 %convolution_bitcast_fusion.4 = f32[16,16,64]{2,1,0:T(8,128)} fusion(f32[16,16,4,64]{3,0,2,1:T(8,128)} %bitcast.182, f32[16,4,64,64]{3,2,1,0:T(8,128)S(1)} %copy-done), kind=kOutput, calls=%fused_computation.44 | convolution fusion | flops 50331648 | bytes 1376256 | tf_op jit(solution)/shard_map/lsab,mlsb->mla/dot_general | solution.py:108
  139.4 1.8 gather_fusion.4
  141.2 23.0 %fusion.32 = f32[16,16,256]{2,0,1:T(8,128)S(1)} fusion(f32[16,5,256]{2,1,0:T(8,128)} %get-tuple-element.24, f32[16,256]{1,0:T(8,128)S(1)} %copy-done.29, f32[16,5,256]{2,1,0:T(8,128)} %get-tuple-element.23, f32[16,256]{1,0:T(8,128)S(1)} %copy-done.31, f32[16,5,256]{2,1,0:T(8,128)} %get-tuple-element.22, f32[16,256]{1,0:T(8,128)S(1)} %copy-done.27, ...), kind=kOutput, calls=%fused_computation.38 | convolution fusion | flops 566689792 | bytes 2146624 | tf_op jit(solution)/shard_map/lspq,mlsq->mlp/dot_general | solution.py:105
  165.2 1.6 multiply_reduce_fusion.3
  166.9 19.9 %all_to_all.30 = f32[32,4,16]{2,1,0:T(4,128)S(1)} all-to-all(f32[32,4,16]{2,1,0:T(4,128)S(1)} %broadcast_in_dim.37), channel_id=1, replica_groups=mesh['band'=16,'lon'=32] {'lon'}, dimensions={0} | all-to-all | bytes 16384 | tf_op jit(solution)/shard_map/all_to_all | solution.py:36
  186.8 9.6 %all_to_all.31 = f32[16,4,16]{2,1,0:T(4,128)S(1)} all-to-all(f32[16,4,16]{2,1,0:T(4,128)S(1)} %broadcast_in_dim.38), channel_id=1, replica_groups=mesh['band'=16,'lon'=32] {'band'}, dimensions={0} | all-to-all | bytes 8192 | tf_op jit(solution)/shard_map/all_to_all | solution.py:36
  (153 shorter events, 29.6 us)
Async XLA Ops:
  0.6 40.0 %copy-start = (f32[16,4,64,64]{3,2,1,0:T(8,128)S(1)}, f32[16,4,64,64]{3,2,1,0:T(8,128)}, u32[]{:S(2)}) copy-start(f32[16,4,64,64]{3,2,1,0:T(8,128)} %param.15) | copy-start | bytes 3145732
  0.6 17.2 %copy-start.5 = (f32[16,16,256]{2,1,0:T(8,128)S(1)}, f32[16,16,256]{2,1,0:T(8,128)}, u32[]{:S(2)}) copy-start(f32[16,16,256]{2,1,0:T(8,128)} %param.11) | copy-start | bytes 786436
  0.7 11.9 %copy-start.32 = (s32[16]{0:T(128)S(1)}, s32[16]{0:T(128)}, u32[]{:S(2)}) copy-start(s32[16]{0:T(128)} %param.21) | copy-start | bytes 196
  1.7 27.3 %collective-permute-start.2 = (f32[3,2,256]{2,0,1:T(4,128)S(1)}, f32[3,2,256]{2,0,1:T(4,128)S(1)}, u32[]{:S(2)}, u32[]{:S(2)}) collective-permute-start(f32[3,2,256]{2,0,1:T(4,128)S(1)} %get-tuple-element.25), channel_id=1, source_target_pairs={{0,1},{1,2},{2,3},{3,4},{4,5},{5,6},{6,7},{7,8},{8,9},{9,10},{10,1... | collective-permute-start | bytes 18440 | tf_op jit(solution)/shard_map/ppermute | solution.py:24
  4.7 21.3 %copy-start.25 = (s32[16,5]{0,1:T(8,128)S(1)}, s32[16,5]{0,1:T(8,128)}, u32[]{:S(2)}) copy-start(s32[16,5]{0,1:T(8,128)} %param.18) | copy-start | bytes 964
  4.7 21.3 %copy-start.39 = (s32[2,2]{1,0:T(2,128)S(1)}, s32[2,2]{1,0:T(2,128)}, u32[]{:S(2)}) copy-start(s32[2,2]{1,0:T(2,128)} %param.20) | copy-start | bytes 52
  4.7 21.4 %copy-start.37 = (s32[16,4]{0,1:T(4,128)S(1)}, s32[16,4]{0,1:T(4,128)}, u32[]{:S(2)}) copy-start(s32[16,4]{0,1:T(4,128)} %param.19) | copy-start | bytes 772
  4.7 22.4 %copy-start.19 = (f32[3,16,256]{2,1,0:T(8,128)S(1)}, f32[3,16,256]{2,1,0:T(8,128)}, u32[]{:S(2)}) copy-start(f32[3,16,256]{2,1,0:T(8,128)} %param.13) | copy-start | bytes 147460
  4.7 24.3 %collective-permute-start.3 = (f32[3,2,256]{2,0,1:T(4,128)S(1)}, f32[3,2,256]{2,0,1:T(4,128)S(1)}, u32[]{:S(2)}, u32[]{:S(2)}) collective-permute-start(f32[3,2,256]{2,0,1:T(4,128)S(1)} %get-tuple-element.26), channel_id=1, source_target_pairs={{1,0},{2,1},{3,2},{4,3},{5,4},{6,5},{7,6},{8,7},{9,8},{10,9},{11,1... | collective-permute-start | bytes 18440 | tf_op jit(solution)/shard_map/ppermute | solution.py:26
  13.7 16.9 %all-to-all-start = ((f32[16,1,2048]{2,1,0:T(1,128)}), f32[16,1,2048]{2,1,0:T(1,128)}, u32[]{:S(2)}, u32[]{:S(2)}) async-start(f32[16,1,2048]{2,1,0:T(1,128)} %reshape.155), calls=%async_computation | async-start | bytes 262144 | tf_op jit(solution)/shard_map/all_to_all | solution.py:36
  18.1 15.7 %copy-start.15 = (f32[2,2,64,64]{3,2,1,0:T(8,128)S(1)}, f32[2,2,64,64]{3,2,1,0:T(8,128)}, u32[]{:S(2)}) copy-start(f32[2,2,64,64]{3,2,1,0:T(8,128)} %param.17) | copy-start | bytes 196612
  18.8 16.8 %collective-permute-start = (f32[16,6,320]{2,0,1:T(8,128)}, f32[16,6,320]{2,0,1:T(8,128)S(1)}, u32[]{:S(2)}, u32[]{:S(2)}) collective-permute-start(f32[16,6,320]{2,0,1:T(8,128)} %get-tuple-element.20), channel_id=1, source_target_pairs={{0,1},{1,2},{2,3},{3,4},{4,5},{5,6},{6,7},{7,8},{8,9},{9,10},{10,1... | collective-permute-start | bytes 368648 | tf_op jit(solution)/shard_map/ppermute | solution.py:24
  19.6 16.0 %collective-permute-start.1 = (f32[16,6,320]{2,0,1:T(8,128)}, f32[16,6,320]{2,0,1:T(8,128)}, u32[]{:S(2)}, u32[]{:S(2)}) collective-permute-start(f32[16,6,320]{2,0,1:T(8,128)} %get-tuple-element.21), channel_id=1, source_target_pairs={{1,0},{2,1},{3,2},{4,3},{5,4},{6,5},{7,6},{8,7},{9,8},{10,9},{11,1... | collective-permute-start | bytes 368648 | tf_op jit(solution)/shard_map/ppermute | solution.py:26
  44.6 24.6 %copy-start.1 = (f32[16,256,64]{1,2,0:T(8,128)S(1)}, f32[16,256,64]{1,2,0:T(8,128)}, u32[]{:S(2)}) copy-start(f32[16,256,64]{1,2,0:T(8,128)} %param.14) | copy-start | bytes 3145732
  44.6 24.6 %copy-start.6 = (f32[16,16,256]{2,1,0:T(8,128)S(1)}, f32[16,16,256]{2,1,0:T(8,128)}, u32[]{:S(2)}) copy-start(f32[16,16,256]{2,1,0:T(8,128)} %param.11) | copy-start | bytes 786436
  44.6 25.4 %copy-start.36 = (f32[16]{0:T(128)S(1)}, f32[16]{0:T(128)}, u32[]{:S(2)}) copy-start(f32[16]{0:T(128)} %multiply_reduce_fusion.5) | copy-start | bytes 196
  69.2 16.4 %copy-start.33 = (s32[16]{0:T(128)S(1)}, s32[16]{0:T(128)}, u32[]{:S(2)}) copy-start(s32[16]{0:T(128)} %param.21) | copy-start | bytes 196
  70.1 61.0 %copy-start.2 = (f32[16,16,256]{2,0,1:T(8,128)}, f32[16,16,256]{2,0,1:T(8,128)S(1)}, u32[]{:S(2)}) copy-start(f32[16,16,256]{2,0,1:T(8,128)S(1)} %get-tuple-element.31) | copy-start | bytes 786436
  70.8 24.4 %all-to-all-start.1 = ((f32[32,2,16]{2,1,0:T(2,128)}), f32[32,2,16]{2,1,0:T(2,128)}, u32[]{:S(2)}, u32[]{:S(2)}) async-start(f32[32,2,16]{2,1,0:T(2,128)} %broadcast_in_dim.34), calls=%async_computation.1 | async-start | bytes 65536 | tf_op jit(solution)/shard_map/all_to_all | solution.py:36
  84.0 48.7 %copy-start.11 = (f32[16,16,64]{2,0,1:T(8,128)}, f32[16,16,64]{2,0,1:T(8,128)S(1)}, u32[]{:S(2)}) copy-start(f32[16,16,64]{2,0,1:T(8,128)S(1)} %convolution_bitcast_fusion.8) | copy-start | bytes 196612
  85.6 47.0 %copy-start.24 = (s32[1024]{0:T(1024)S(1)}, s32[1024]{0:T(1024)}, u32[]{:S(2)}) copy-start(s32[1024]{0:T(1024)} %pad_clamp_fusion.1) | copy-start | bytes 12292
  97.8 13.4 %all-to-all-start.2 = ((f32[16,2,16]{2,1,0:T(2,128)}), f32[16,2,16]{2,1,0:T(2,128)}, u32[]{:S(2)}, u32[]{:S(2)}) async-start(f32[16,2,16]{2,1,0:T(2,128)} %broadcast_in_dim.35), calls=%async_computation.2 | async-start | bytes 32768 | tf_op jit(solution)/shard_map/all_to_all | solution.py:36
  107.3 23.8 %collective-permute-start.4 = (f32[16,6,320]{2,0,1:T(8,128)}, f32[16,6,320]{2,0,1:T(8,128)}, u32[]{:S(2)}, u32[]{:S(2)}) collective-permute-start(f32[16,6,320]{2,0,1:T(8,128)} %get-tuple-element.18), channel_id=1, source_target_pairs={{0,1},{1,2},{2,3},{3,4},{4,5},{5,6},{6,7},{7,8},{8,9},{9,10},{10,1... | collective-permute-start | bytes 368648 | tf_op jit(solution)/shard_map/ppermute | solution.py:24
  108.9 22.2 %collective-permute-start.5 = (f32[16,6,320]{2,0,1:T(8,128)}, f32[16,6,320]{2,0,1:T(8,128)}, u32[]{:S(2)}, u32[]{:S(2)}) collective-permute-start(f32[16,6,320]{2,0,1:T(8,128)} %get-tuple-element.19), channel_id=1, source_target_pairs={{1,0},{2,1},{3,2},{4,3},{5,4},{6,5},{7,6},{8,7},{9,8},{10,9},{11,1... | collective-permute-start | bytes 368648 | tf_op jit(solution)/shard_map/ppermute | solution.py:26
  111.3 11.3 %all-to-all-start.3 = ((f32[16,1,2048]{2,1,0:T(1,128)}), f32[16,1,2048]{2,1,0:T(1,128)}, u32[]{:S(2)}, u32[]{:S(2)}) async-start(f32[16,1,2048]{2,1,0:T(1,128)} %reshape.157), calls=%async_computation.3 | async-start | bytes 262144 | tf_op jit(solution)/shard_map/all_to_all | solution.py:36
  141.2 23.1 %copy-start.9 = (f32[16,64,64]{2,1,0:T(8,128)S(1)}, f32[16,64,64]{2,1,0:T(8,128)}, u32[]{:S(2)}) copy-start(f32[16,64,64]{2,1,0:T(8,128)} %param.16) | copy-start | bytes 786436
  141.2 23.1 %copy-start.13 = (f32[16,16,64]{2,1,0:T(8,128)S(1)}, f32[16,16,64]{2,1,0:T(8,128)}, u32[]{:S(2)}) copy-start(f32[16,16,64]{2,1,0:T(8,128)} %convolution_bitcast_fusion.2) | copy-start | bytes 196612
  141.2 23.1 %copy-start.16 = (f32[16,16,64]{2,1,0:T(8,128)S(1)}, f32[16,16,64]{2,1,0:T(8,128)}, u32[]{:S(2)}) copy-start(f32[16,16,64]{2,1,0:T(8,128)} %convolution_bitcast_fusion.4) | copy-start | bytes 196612
  141.2 24.0 %copy-start.4 = (f32[16,16,256]{2,0,1:T(8,128)S(1)}, f32[16,16,256]{2,0,1:T(8,128)}, u32[]{:S(2)}) copy-start(f32[16,16,256]{2,0,1:T(8,128)} %copy-done.2) | copy-start | bytes 786436
  141.2 24.0 %copy-start.7 = (f32[16,16,256]{2,1,0:T(8,128)S(1)}, f32[16,16,256]{2,1,0:T(8,128)}, u32[]{:S(2)}) copy-start(f32[16,16,256]{2,1,0:T(8,128)} %param.11) | copy-start | bytes 786436
  141.2 24.0 %copy-start.38 = (f32[16]{0:T(128)S(1)}, f32[16]{0:T(128)}, u32[]{:S(2)}) copy-start(f32[16]{0:T(128)} %bitcast_divide_fusion.1) | copy-start | bytes 196
  164.3 32.2 %copy-start.35 = (f32[2,16]{1,0:T(2,128)S(1)}, f32[2,16]{1,0:T(2,128)}, u32[]{:S(2)}) copy-start(f32[2,16]{1,0:T(2,128)} %reduce_sum.93) | copy-start | bytes 388
  (20 other events, 70.0 us)

commit v5 on v4

--- a/solution.py
+++ b/solution.py
@@ -45,7 +45,7 @@
 def matern_shape(rows_pos, cols_pos, length_scale):
     squared = None
     for component in range(3):
-        offset = rows_pos[component][None, :, None] - cols_pos[component][:, None, :]
+        offset = rows_pos[component][:, :, None] - cols_pos[component][:, None, :]
         squared = offset * offset if squared is None else squared + offset * offset
     scaled = jnp.sqrt(squared) * (ROOT_THREE / length_scale)
     return (1.0 + scaled) * jnp.exp(-scaled)
@@ -82,11 +82,23 @@
     far_rows = rim_index(far_list, REACH)
     rim_pos = extended(position, (("lon", 1),), near_depth)
 
-    def leaf_blocks(rows_pos, rows_index):
-        return matern_shape(rows_pos, rim_pos[:, rows_index], length_scale)
-
-    near_blocks = jax.vmap(leaf_blocks)(jnp.transpose(position, (1, 0, 2)), near_rows)
-    slot_scale = AMPLITUDE * near_valid.astype(jnp.float32)
+    same_blocks = matern_shape(
+        rim_pos[:, near_depth : near_depth + local_leaves],
+        rim_pos[:, near_depth : near_depth + local_leaves],
+        length_scale,
+    )
+    step_blocks = [
+        matern_shape(
+            rim_pos[:, near_depth - step : near_depth + local_leaves],
+            rim_pos[:, near_depth : near_depth + local_leaves + step],
+            length_scale,
+        )
+        for step in range(1, near_depth + 1)
+    ]
+    step_range = jnp.arange(-near_depth, near_depth + 1, dtype=jnp.int32)
+    targets = jnp.arange(local_leaves, dtype=jnp.int32)[:, None] + near_depth + step_range[None, :]
+    matches = (near_rows[:, :, None] == targets[:, None, :]) & near_valid[:, :, None]
+    offset_scale = AMPLITUDE * jnp.sum(matches.astype(jnp.float32), axis=1)
     band_slot = panel_list // (lon_count * panel_count)
     gathered_rows = band_slot * panel_count + panel_list % panel_count
     membership = (leaf_panel[:, None] == jnp.arange(panel_count, dtype=jnp.int32)[None, :]).astype(
@@ -101,10 +113,25 @@
             :, REACH - near_depth : REACH + local_leaves + near_depth, :pixel_count
         ]
         rim_coeffs = rim_joined[:, :, pixel_count:]
-        near_values = rim_values[:, near_rows] * slot_scale[None, :, :, None]
+
+        def offset_values(step):
+            start = near_depth + step
+            values = rim_values[:, start : start + local_leaves]
+            return values * offset_scale[None, :, step + near_depth, None]
+
         near_part = jnp.einsum(
-            "lspq,mlsq->mlp", near_blocks, near_values, precision=lax.Precision.HIGH
-        )
+            "ipq,miq->mip", same_blocks, offset_values(0), precision=lax.Precision.HIGH
+        )
+        for step in range(1, near_depth + 1):
+            blocks = step_blocks[step - 1]
+            ahead = blocks[step : step + local_leaves]
+            behind = blocks[:local_leaves]
+            near_part = near_part + jnp.einsum(
+                "ipq,miq->mip", ahead, offset_values(step), precision=lax.Precision.HIGH
+            )
+            near_part = near_part + jnp.einsum(
+                "iqp,miq->mip", behind, offset_values(-step), precision=lax.Precision.HIGH
+            )
         leaf_far = jnp.einsum(
             "lsab,mlsb->mla", leaf_couple, rim_coeffs[:, far_rows], precision=HIGHEST_PRECISION
         )

time: 201 us -> 187 us (0.930)
  matrix products: 69.1 us -> 57.6 us
  local copies, waits for them, and re-layouts: 24.4 us -> 19.9 us
  starting transfers between devices: 42.9 us -> 39.2 us
  other arithmetic: 17.1 us -> 20.4 us
    dot_general x2 -> x10, matrix products: 47.6 us -> 33.4 us  [the longest x4 12.5 us: covariance_apply(): jnp.einsum('ipq,miq->mip', ahead, offset_values(step), precision=lax.Prec...]
    mul x1 -> x3, other arithmetic: 0.01 us -> 9.72 us  [the longest x2 9.71 us: matern_shape(): return (1.0 + scaled) * jnp.exp(-scaled)]
    ppermute x3, starting transfers between devices: 5.38 us -> 0.01 us  [extended(): lax.ppermute(tail, axis, [(i, (i + 1) % count) for i in range(count)])]
    gather x4 -> x0, local copies, waits for them, and re-layouts: 4.47 us -> none  [the longest x2 3.64 us: covariance_apply(): near_values = rim_values[:, near_rows] * slot_scale[None, :, :, None]]
    ppermute x3, starting transfers between devices: 9.64 us -> 13.7 us  [extended(): lax.ppermute(head, axis, [((i + 1) % count, i) for i in range(count)])]
    all_to_all x4, starting transfers between devices: 27.9 us -> 25.5 us  [gathered(): return lax.all_to_all(copies, axis, 0, 0, tiled=False)]
    dot_general x2, matrix products: 1.83 us -> 4.02 us  [covariance_apply(): jnp.einsum('lab,mlb->mla', transfer, downward, precision=HIGHEST_PRECISION)]
    unnamed x94 -> x98, local copies, waits for them, and re-layouts: 8.28 us -> 10 us
  transfers between devices with their start and end apart: 10 -> 10, of which waited for: 3 -> 2; matrix products, arithmetic and copies ran while one was open for 17% -> 25% of each run, Pallas kernels for 0% -> 0%
where the time goes in v5:
time: 187 us; the launch traced here: 185 us
  matrix products  57.6 us (31%)
  starting transfers between devices  39.2 us (21%)
  blocking collectives  31.5 us (17%)
  other arithmetic  20.4 us (11%)
  local copies, waits for them, and re-layouts  19.9 us (11%)
  waiting for transfers between devices  15.1 us (8%)
    all_to_all x2, blocking collectives, gathered(): return lax.all_to_all(copies, axis, 0, 0, tiled=False)  31.5 us
    all_to_all x4, starting transfers between devices, gathered(): return lax.all_to_all(copies, axis, 0, 0, tiled=False)  25.5 us
    all_to_all x4, waiting for transfers between devices, gathered(): return lax.all_to_all(copies, axis, 0, 0, tiled=False)  15.1 us
    ppermute x3, starting transfers between devices, extended(): lax.ppermute(head, axis, [((i + 1) % count, i) for i in range(count)])  13.7 us
    dot_general x4, matrix products, covariance_apply(): jnp.einsum('ipq,miq->mip', ahead, offset_values(step), precision=lax.Prec...  12.5 us
    dot_general x2, matrix products, covariance_apply(): jnp.einsum('ipq,miq->mip', same_blocks, offset_values(0), precision=lax.P...  11.3 us
    unnamed x98, local copies, waits for them, and re-layouts  10 us
    mul x2, other arithmetic, matern_shape(): return (1.0 + scaled) * jnp.exp(-scaled)  9.71 us
  transfers between devices with their start and end apart: 10, of which 2 were waited for; matrix products, arithmetic and copies ran while one was open for 25% of the time, Pallas kernels for 0%

profile of v5, /device:TPU:1, one launch (start us, length us, event | category | flops | bytes accessed | tf_op | source)
XLA Modules:
  0.0 185.0 jit_solution(14082538362721928812)
XLA Ops:
  1.6 6.9 %collective-permute-start.2 = (f32[3,2,256]{2,1,0:T(2,128)S(1)}, f32[3,2,256]{2,1,0:T(2,128)S(1)}, u32[]{:S(2)}, u32[]{:S(2)}) collective-permute-start(f32[3,2,256]{2,1,0:T(2,128)S(1)} %get-tuple-element.38), channel_id=1, source_target_pairs={{1,0},{2,1},{3,2},{4,3},{5,4},{6,5},{7,6},{8,7},{9,8},{10,9},{11,1... | collective-permute-start | bytes 18440 | tf_op jit(solution)/shard_map/ppermute | solution.py:26
  9.6 2.4 %convolution_bitcast_fusion.9 = f32[16,16,64]{2,0,1:T(8,128)S(1)} fusion(f32[16,256,64]{1,2,0:T(8,128)} %param.14, f32[16,16,256]{2,1,0:T(8,128)} %param.11), kind=kOutput, calls=%fused_computation.70 | convolution fusion | flops 50331648 | bytes 1376256 | tf_op jit(solution)/shard_map/lpr,mlp->mlr/dot_general | solution.py:109
  12.7 3.6 %collective-permute-start = (f32[16,6,320]{2,0,1:T(8,128)}, f32[16,6,320]{2,0,1:T(8,128)}, u32[]{:S(2)}, u32[]{:S(2)}) collective-permute-start(f32[16,6,320]{2,0,1:T(8,128)} %get-tuple-element.20), channel_id=1, source_target_pairs={{1,0},{2,1},{3,2},{4,3},{5,4},{6,5},{7,6},{8,7},{9,8},{10,9},{11,1... | collective-permute-start | bytes 368648 | tf_op jit(solution)/shard_map/ppermute | solution.py:26
  19.6 6.8 %all-to-all-start = ((f32[16,1,2048]{2,1,0:T(1,128)}), f32[16,1,2048]{2,1,0:T(1,128)S(1)}, u32[]{:S(2)}, u32[]{:S(2)}) async-start(f32[16,1,2048]{2,1,0:T(1,128)} %reshape.173), calls=%async_computation | async-start | bytes 262144 | tf_op jit(solution)/shard_map/all_to_all | solution.py:36
  28.8 5.7 %fusion.17 = f32[16,16,256]{2,1,0:T(8,128)} fusion(f32[16,256]{1,0:T(8,128)S(1)} %get-tuple-element.35, f32[16,256]{1,0:T(8,128)S(1)} %get-tuple-element.36, f32[16,256]{1,0:T(8,128)S(1)} %get-tuple-element.34, f32[16]{0:T(128)S(1)} %get-tuple-element.43, f32[16,16,256]{2,1,0:T(8,128)S(1)} %copy-done.3), kind=kOutput, calls=%fused_computation.24 | convolution fusion | flops 113311744 | bytes 573504 | tf_op jit(solution)/shard_map/ipq,miq->mip/dot_general | solution.py:122
  35.2 5.2 %exponential_multiply_fusion = f32[18,256,256]{2,1,0:T(8,128)} fusion(f32[18,256]{1,0:T(8,128)S(1)} %get-tuple-element.26, f32[18,256]{1,0:T(8,128)S(1)} %get-tuple-element.32, f32[18,256]{1,0:T(8,128)S(1)} %get-tuple-element.27, f32[18,256]{1,0:T(8,128)S(1)} %get-tuple-element.33, f32[18,256]{1,0:T(8,128)S(1)} %get-tuple-element.25, ...), kind=kLoop, calls=%fused_computation.4 | loop fusion | flops 14155776 | bytes 4829184 | tf_op jit(solution)/shard_map/mul | solution.py:51
  40.3 4.5 %exponential_multiply_fusion.1 = f32[17,256,256]{2,1,0:T(8,128)} fusion(f32[17,256]{1,0:T(8,128)S(1)} %get-tuple-element.23, f32[17,256]{1,0:T(8,128)S(1)} %get-tuple-element.30, f32[17,256]{1,0:T(8,128)S(1)} %get-tuple-element.24, f32[17,256]{1,0:T(8,128)S(1)} %get-tuple-element.29, f32[17,256]{1,0:T(8,128)S(1)} %get-tuple-element.22, ...), kind=kLoop, calls=%fused_computation.5 | loop fusion | flops 13369344 | bytes 4560896 | tf_op jit(solution)/shard_map/mul | solution.py:51
  46.1 1.8 reduce
  48.7 1.6 gather_fusion.1
  51.5 1.6 convolution_bitcast_fusion.5
  56.1 3.0 %convolution_bitcast_fusion.7 = f32[16,16,64]{2,1,0:T(8,128)S(1)} fusion(f32[16,16,4,64]{3,0,2,1:T(8,128)} %bitcast.188, f32[16,4,64,64]{3,2,1,0:T(8,128)S(1)} %copy-done), kind=kOutput, calls=%fused_computation.68 | convolution fusion | flops 50331648 | bytes 1376256 | tf_op jit(solution)/shard_map/lsab,mlsb->mla/dot_general | solution.py:135
  59.1 2.2 %fusion.75 = f32[16,16,64]{2,0,1:T(8,128)S(1)} fusion(f32[16,16,64]{2,1,0:T(8,128)S(1)} %convolution_bitcast_fusion.7, f32[16,64,64]{2,1,0:T(8,128)} %param.16, f32[16,16,64]{2,1,0:T(8,128)} %convolution_bitcast_fusion.5), kind=kOutput, calls=%fused_computation.65 | convolution fusion | flops 12599296 | bytes 458752 | tf_op jit(solution)/shard_map/lab,mlb->mla/dot_general | solution.py:150
  61.4 4.0 %fusion.6 = f32[16,16,256]{2,1,0:T(8,128)S(1)} fusion(f32[18,256,256]{2,1,0:T(8,128)} %exponential_multiply_fusion, f32[16,6,320]{2,0,1:T(8,128)} %collective-permute-done, f32[16,16,64]{2,0,1:T(8,128)S(1)} %convolution_bitcast_fusion.9, f32[16,16,256]{2,0,1:T(8,128)S(1)} %copy.72, f32[16]{0:T(128)S(1)} %copy-done.27), kind=kOutput, calls=%fused_computation.13 | convolution fusion | flops 100859904 | bytes 4931648 | tf_op jit(solution)/shard_map/ipq,miq->mip/dot_general | solution.py:129
  68.1 2.7 %fusion.71 = f32[16,16,256]{2,0,1:T(8,128)S(1)} fusion(f32[16,16,256]{2,1,0:T(8,128)S(1)} %fusion.2, f32[16,16,256]{2,1,0:T(8,128)S(1)} %fusion.6, f32[16,16,256]{2,1,0:T(8,128)S(1)} %fusion.10, f32[16,16,256]{2,1,0:T(8,128)S(1)} %copy-done.13, f32[17,256,256]{2,1,0:T(8,128)S(1)} %bitcast.182, f32[16,6,320]{2,0,1:T(8,128)} %collective-permute-done, ...), kind=kOutput, calls=%fused_computation.58 | convolution fusion | flops 101253120 | bytes 6234176 | tf_op jit(solution)/shard_map/ipq,miq->mip/dot_general | solution.py:129
  74.0 5.6 %fusion.16 = f32[16,16,256]{2,1,0:T(8,128)} fusion(f32[16,256]{1,0:T(8,128)S(1)} %copy-done.20, f32[16,256]{1,0:T(8,128)S(1)} %copy-done.22, f32[16,256]{1,0:T(8,128)S(1)} %copy-done.18, f32[16,16,256]{2,0,1:T(8,128)S(1)} %get-tuple-element.45, f32[16]{0:T(128)S(1)} %copy-done.37), kind=kOutput, calls=%fused_computation.23 | convolution fusion | flops 113311744 | bytes 573504 | tf_op jit(solution)/shard_map/ipq,miq->mip/dot_general | solution.py:122
  79.6 3.2 %collective-permute-start.4 = (f32[16,6,320]{2,0,1:T(8,128)}, f32[16,6,320]{2,0,1:T(8,128)S(1)}, u32[]{:S(2)}, u32[]{:S(2)}) collective-permute-start(f32[16,6,320]{2,0,1:T(8,128)} %get-tuple-element.18), channel_id=1, source_target_pairs={{1,0},{2,1},{3,2},{4,3},{5,4},{6,5},{7,6},{8,7},{9,8},{10,9},{11,1... | collective-permute-start | bytes 368648 | tf_op jit(solution)/shard_map/ppermute | solution.py:26
  83.5 7.9 %all-to-all-start.1 = ((f32[32,2,16]{2,1,0:T(2,128)}), f32[32,2,16]{2,1,0:T(2,128)}, u32[]{:S(2)}, u32[]{:S(2)}) async-start(f32[32,2,16]{2,1,0:T(2,128)} %broadcast_in_dim.31), calls=%async_computation.1 | async-start | bytes 65536 | tf_op jit(solution)/shard_map/all_to_all | solution.py:36
  92.3 11.3 %all-to-all-done.1 = f32[32,2,16]{2,1,0:T(2,128)} async-done(((f32[32,2,16]{2,1,0:T(2,128)}), f32[32,2,16]{2,1,0:T(2,128)}, u32[]{:S(2)}, u32[]{:S(2)}) %all-to-all-start.1) | async-done | bytes 4128 | tf_op jit(solution)/shard_map/all_to_all | solution.py:36
  105.0 6.7 %all-to-all-start.2 = ((f32[16,2,16]{2,1,0:T(2,128)}), f32[16,2,16]{2,1,0:T(2,128)S(1)}, u32[]{:S(2)}, u32[]{:S(2)}) async-start(f32[16,2,16]{2,1,0:T(2,128)} %broadcast_in_dim.32), calls=%async_computation.2 | async-start | bytes 32768 | tf_op jit(solution)/shard_map/all_to_all | solution.py:36
  112.4 1.8 reshape.175
  114.2 3.8 %all-to-all-done.2 = f32[16,2,16]{2,1,0:T(2,128)S(1)} async-done(((f32[16,2,16]{2,1,0:T(2,128)}), f32[16,2,16]{2,1,0:T(2,128)S(1)}, u32[]{:S(2)}, u32[]{:S(2)}) %all-to-all-start.2) | async-done | bytes 2080 | tf_op jit(solution)/shard_map/all_to_all | solution.py:36
  118.0 4.2 %all-to-all-start.3 = ((f32[16,1,2048]{2,1,0:T(1,128)}), f32[16,1,2048]{2,1,0:T(1,128)}, u32[]{:S(2)}, u32[]{:S(2)}) async-start(f32[16,1,2048]{2,1,0:T(1,128)} %reshape.175), calls=%async_computation.3 | async-start | bytes 262144 | tf_op jit(solution)/shard_map/all_to_all | solution.py:36
  125.9 3.5 %convolution_bitcast_fusion.4 = f32[16,16,64]{2,1,0:T(8,128)} fusion(f32[16,16,4,64]{3,0,2,1:T(8,128)} %bitcast.187, f32[16,4,64,64]{3,2,1,0:T(8,128)S(1)} %copy-done), kind=kOutput, calls=%fused_computation.63 | convolution fusion | flops 50331648 | bytes 1376256 | tf_op jit(solution)/shard_map/lsab,mlsb->mla/dot_general | solution.py:135
  129.4 1.8 reduce.1
  132.0 1.6 gather_fusion.3
  135.7 1.8 fusion.74
  137.6 3.5 %fusion.8 = f32[16,16,256]{2,1,0:T(8,128)S(1)} fusion(f32[17,256,256]{2,1,0:T(8,128)} %exponential_multiply_fusion.1, f32[16,6,320]{2,0,1:T(8,128)} %collective-permute-done.5, f32[16,16,64]{2,0,1:T(8,128)S(1)} %convolution_bitcast_fusion.8, f32[16,16,256]{2,0,1:T(8,128)S(1)} %get-tuple-element.45, f32[16]{0:T(128)} %get-tuple-element.42), kind=kOutput, calls=%fused_computation.15 | convolution fusion | flops 100859904 | bytes 4932096 | tf_op jit(solution)/shard_map/iqp,miq->mip/dot_general | solution.py:132
  141.2 4.0 %fusion.4 = f32[16,16,256]{2,1,0:T(8,128)S(1)} fusion(f32[18,256,256]{2,1,0:T(8,128)} %exponential_multiply_fusion, f32[16,6,320]{2,0,1:T(8,128)S(1)} %copy-done.9, f32[16,16,64]{2,0,1:T(8,128)S(1)} %convolution_bitcast_fusion.8, f32[16,16,256]{2,0,1:T(8,128)S(1)} %get-tuple-element.45, f32[16]{0:T(128)S(1)} %copy-done.28), kind=kOutput, calls=%fused_computation.11 | convolution fusion | flops 100859904 | bytes 4907072 | tf_op jit(solution)/shard_map/ipq,miq->mip/dot_general | solution.py:129
  145.2 3.4 %fusion = f32[16,16,256]{2,1,0:T(8,128)S(1)} fusion(f32[18,256,256]{2,1,0:T(8,128)} %exponential_multiply_fusion, f32[16,6,320]{2,0,1:T(8,128)} %collective-permute-done.5, f32[16,16,64]{2,0,1:T(8,128)S(1)} %convolution_bitcast_fusion.8, f32[16,16,256]{2,0,1:T(8,128)S(1)} %get-tuple-element.45, f32[16]{0:T(128)S(1)} %copy-done.26), kind=kOutput, calls=%fused_computation.7 | convolution fusion | flops 100859904 | bytes 4931648 | tf_op jit(solution)/shard_map/iqp,miq->mip/dot_general | solution.py:132
  148.6 1.9 %fusion.62 = f32[16,16,256]{2,0,1:T(8,128)S(1)} fusion(f32[16,16,256]{2,1,0:T(8,128)S(1)} %fusion, f32[16,16,256]{2,1,0:T(8,128)S(1)} %fusion.4, f32[16,16,256]{2,1,0:T(8,128)S(1)} %fusion.8, f32[16,16,256]{2,1,0:T(8,128)S(1)} %copy-done.12, f32[17,256,256]{2,1,0:T(8,128)S(1)} %bitcast.184, f32[16,6,320]{2,0,1:T(8,128)S(1)} %copy-done.9, ...), kind=kOutput, calls=%fused_computation.55 | convolution fusion | flops 101253120 | bytes 6234176 | tf_op jit(solution)/shard_map/ipq,miq->mip/dot_general | solution.py:129
  151.5 19.0 %all_to_all.30 = f32[32,4,16]{2,1,0:T(4,128)S(1)} all-to-all(f32[32,4,16]{2,1,0:T(4,128)S(1)} %broadcast_in_dim.34), channel_id=1, replica_groups=mesh['band'=16,'lon'=32] {'lon'}, dimensions={0} | all-to-all | bytes 16384 | tf_op jit(solution)/shard_map/all_to_all | solution.py:36
  170.5 12.5 %all_to_all.31 = f32[16,4,16]{2,1,0:T(4,128)S(1)} all-to-all(f32[16,4,16]{2,1,0:T(4,128)S(1)} %broadcast_in_dim.35), channel_id=1, replica_groups=mesh['band'=16,'lon'=32] {'band'}, dimensions={0} | all-to-all | bytes 8192 | tf_op jit(solution)/shard_map/all_to_all | solution.py:36
  (168 shorter events, 34.2 us)
Async XLA Ops:
  0.6 55.5 %copy-start = (f32[16,4,64,64]{3,2,1,0:T(8,128)S(1)}, f32[16,4,64,64]{3,2,1,0:T(8,128)}, u32[]{:S(2)}) copy-start(f32[16,4,64,64]{3,2,1,0:T(8,128)} %param.15) | copy-start | bytes 3145732
  0.6 25.7 %copy-start.10 = (f32[3,16,256]{2,1,0:T(8,128)S(1)}, f32[3,16,256]{2,1,0:T(8,128)}, u32[]{:S(2)}) copy-start(f32[3,16,256]{2,1,0:T(8,128)} %param.13) | copy-start | bytes 147460
  0.7 25.8 %copy-start.3 = (f32[16,16,256]{2,1,0:T(8,128)S(1)}, f32[16,16,256]{2,1,0:T(8,128)}, u32[]{:S(2)}) copy-start(f32[16,16,256]{2,1,0:T(8,128)} %param.11) | copy-start | bytes 786436
  0.7 25.7 %copy-start.16 = (s32[16,5]{0,1:T(8,128)S(1)}, s32[16,5]{0,1:T(8,128)}, u32[]{:S(2)}) copy-start(s32[16,5]{0,1:T(8,128)} %param.18) | copy-start | bytes 964
  0.7 27.2 %copy-start.33 = (s32[16,4]{0,1:T(4,128)S(1)}, s32[16,4]{0,1:T(4,128)}, u32[]{:S(2)}) copy-start(s32[16,4]{0,1:T(4,128)} %param.19) | copy-start | bytes 772
  0.7 28.0 %copy-start.35 = (s32[2,2]{1,0:T(2,128)S(1)}, s32[2,2]{1,0:T(2,128)}, u32[]{:S(2)}) copy-start(s32[2,2]{1,0:T(2,128)} %param.20) | copy-start | bytes 52
  1.6 33.5 %collective-permute-start.2 = (f32[3,2,256]{2,1,0:T(2,128)S(1)}, f32[3,2,256]{2,1,0:T(2,128)S(1)}, u32[]{:S(2)}, u32[]{:S(2)}) collective-permute-start(f32[3,2,256]{2,1,0:T(2,128)S(1)} %get-tuple-element.38), channel_id=1, source_target_pairs={{1,0},{2,1},{3,2},{4,3},{5,4},{6,5},{7,6},{8,7},{9,8},{10,9},{11,1... | collective-permute-start | bytes 18440 | tf_op jit(solution)/shard_map/ppermute | solution.py:26
  8.5 26.6 %collective-permute-start.1 = (f32[3,2,256]{2,1,0:T(2,128)S(1)}, f32[3,2,256]{2,1,0:T(2,128)S(1)}, u32[]{:S(2)}, u32[]{:S(2)}) collective-permute-start(f32[3,2,256]{2,1,0:T(2,128)S(1)} %get-tuple-element.37), channel_id=1, source_target_pairs={{0,1},{1,2},{2,3},{3,4},{4,5},{5,6},{6,7},{7,8},{8,9},{9,10},{10,1... | collective-permute-start | bytes 18440 | tf_op jit(solution)/shard_map/ppermute | solution.py:24
  12.7 40.4 %collective-permute-start.3 = (f32[16,6,320]{2,0,1:T(8,128)}, f32[16,6,320]{2,0,1:T(8,128)S(1)}, u32[]{:S(2)}, u32[]{:S(2)}) collective-permute-start(f32[16,6,320]{2,0,1:T(8,128)} %get-tuple-element.21), channel_id=1, source_target_pairs={{0,1},{1,2},{2,3},{3,4},{4,5},{5,6},{6,7},{7,8},{8,9},{9,10},{10,1... | collective-permute-start | bytes 368648 | tf_op jit(solution)/shard_map/ppermute | solution.py:24
  12.7 41.0 %collective-permute-start = (f32[16,6,320]{2,0,1:T(8,128)}, f32[16,6,320]{2,0,1:T(8,128)}, u32[]{:S(2)}, u32[]{:S(2)}) collective-permute-start(f32[16,6,320]{2,0,1:T(8,128)} %get-tuple-element.20), channel_id=1, source_target_pairs={{1,0},{2,1},{3,2},{4,3},{5,4},{6,5},{7,6},{8,7},{9,8},{10,9},{11,1... | collective-permute-start | bytes 368648 | tf_op jit(solution)/shard_map/ppermute | solution.py:26
  19.6 25.3 %all-to-all-start = ((f32[16,1,2048]{2,1,0:T(1,128)}), f32[16,1,2048]{2,1,0:T(1,128)S(1)}, u32[]{:S(2)}, u32[]{:S(2)}) async-start(f32[16,1,2048]{2,1,0:T(1,128)} %reshape.173), calls=%async_computation | async-start | bytes 262144 | tf_op jit(solution)/shard_map/all_to_all | solution.py:36
  26.5 8.0 %copy-start.17 = (f32[16,256]{1,0:T(8,128)}, f32[16,256]{1,0:T(8,128)S(1)}, u32[]{:S(2)}) copy-start(f32[16,256]{1,0:T(8,128)S(1)} %get-tuple-element.34) | copy-start | bytes 49156
  26.5 8.0 %copy-start.19 = (f32[16,256]{1,0:T(8,128)}, f32[16,256]{1,0:T(8,128)S(1)}, u32[]{:S(2)}) copy-start(f32[16,256]{1,0:T(8,128)S(1)} %get-tuple-element.35) | copy-start | bytes 49156
  26.5 8.0 %copy-start.21 = (f32[16,256]{1,0:T(8,128)}, f32[16,256]{1,0:T(8,128)S(1)}, u32[]{:S(2)}) copy-start(f32[16,256]{1,0:T(8,128)S(1)} %get-tuple-element.36) | copy-start | bytes 49156
  40.3 25.0 %slice-start.4 = ((s8[4718592]{0:T(1024)(128)(4,1)}), s8[524288]{0:T(1024)(128)(4,1)S(1)}, s32[]{:S(2)}) async-start(s8[4718592]{0:T(1024)(128)(4,1)} %bitcast.185), calls=%async_computation.10 | async-start | bytes 1048576
  48.7 12.6 %copy-start.27 = (f32[16]{0:T(128)S(1)}, f32[16]{0:T(128)}, u32[]{:S(2)}) copy-start(f32[16]{0:T(128)} %get-tuple-element.41) | copy-start | bytes 196
  56.1 9.2 %slice-start.5 = ((s8[4718592]{0:T(1024)(128)(4,1)}), s8[4194304]{0:T(1024)(128)(4,1)S(1)}, s32[]{:S(2)}) async-start(s8[4718592]{0:T(1024)(128)(4,1)} %bitcast.185), calls=%async_computation.11 | async-start | bytes 8388608
  56.1 9.2 %copy-start.7 = (f32[16,6,320]{2,0,1:T(8,128)S(1)}, f32[16,6,320]{2,0,1:T(8,128)}, u32[]{:S(2)}) copy-start(f32[16,6,320]{2,0,1:T(8,128)} %copy-done.6) | copy-start | bytes 368644
  56.1 9.2 %copy-start.25 = (f32[16]{0:T(128)S(1)}, f32[16]{0:T(128)}, u32[]{:S(2)}) copy-start(f32[16]{0:T(128)} %get-tuple-element.40) | copy-start | bytes 196
  59.1 7.5 %slice-start = ((s8[4456448]{0:T(1024)(128)(4,1)}), s8[4194304]{0:T(1024)(128)(4,1)S(1)}, s32[]{:S(2)}) async-start(s8[4456448]{0:T(1024)(128)(4,1)} %bitcast.181), calls=%async_computation.6 | async-start | bytes 8388608
  74.0 8.9 %copy-start.32 = (f32[16]{0:T(128)S(1)}, f32[16]{0:T(128)}, u32[]{:S(2)}) copy-start(f32[16]{0:T(128)} %multiply_reduce_fusion.5) | copy-start | bytes 196
  79.6 56.1 %copy-start.5 = (f32[16,64,64]{2,1,0:T(8,128)S(1)}, f32[16,64,64]{2,1,0:T(8,128)}, u32[]{:S(2)}) copy-start(f32[16,64,64]{2,1,0:T(8,128)} %param.16) | copy-start | bytes 786436
  79.6 43.1 %collective-permute-start.4 = (f32[16,6,320]{2,0,1:T(8,128)}, f32[16,6,320]{2,0,1:T(8,128)S(1)}, u32[]{:S(2)}, u32[]{:S(2)}) collective-permute-start(f32[16,6,320]{2,0,1:T(8,128)} %get-tuple-element.18), channel_id=1, source_target_pairs={{1,0},{2,1},{3,2},{4,3},{5,4},{6,5},{7,6},{8,7},{9,8},{10,9},{11,1... | collective-permute-start | bytes 368648 | tf_op jit(solution)/shard_map/ppermute | solution.py:26
  82.9 40.6 %collective-permute-start.5 = (f32[16,6,320]{2,0,1:T(8,128)}, f32[16,6,320]{2,0,1:T(8,128)}, u32[]{:S(2)}, u32[]{:S(2)}) collective-permute-start(f32[16,6,320]{2,0,1:T(8,128)} %get-tuple-element.19), channel_id=1, source_target_pairs={{0,1},{1,2},{2,3},{3,4},{4,5},{5,6},{6,7},{7,8},{8,9},{9,10},{10,1... | collective-permute-start | bytes 368648 | tf_op jit(solution)/shard_map/ppermute | solution.py:24
  83.5 20.0 %all-to-all-start.1 = ((f32[32,2,16]{2,1,0:T(2,128)}), f32[32,2,16]{2,1,0:T(2,128)}, u32[]{:S(2)}, u32[]{:S(2)}) async-start(f32[32,2,16]{2,1,0:T(2,128)} %broadcast_in_dim.31), calls=%async_computation.1 | async-start | bytes 65536 | tf_op jit(solution)/shard_map/all_to_all | solution.py:36
  105.0 13.0 %all-to-all-start.2 = ((f32[16,2,16]{2,1,0:T(2,128)}), f32[16,2,16]{2,1,0:T(2,128)S(1)}, u32[]{:S(2)}, u32[]{:S(2)}) async-start(f32[16,2,16]{2,1,0:T(2,128)} %broadcast_in_dim.32), calls=%async_computation.2 | async-start | bytes 32768 | tf_op jit(solution)/shard_map/all_to_all | solution.py:36
  118.0 11.4 %all-to-all-start.3 = ((f32[16,1,2048]{2,1,0:T(1,128)}), f32[16,1,2048]{2,1,0:T(1,128)}, u32[]{:S(2)}, u32[]{:S(2)}) async-start(f32[16,1,2048]{2,1,0:T(1,128)} %reshape.175), calls=%async_computation.3 | async-start | bytes 262144 | tf_op jit(solution)/shard_map/all_to_all | solution.py:36
  125.9 15.3 %copy-start.9 = (f32[16,6,320]{2,0,1:T(8,128)S(1)}, f32[16,6,320]{2,0,1:T(8,128)}, u32[]{:S(2)}) copy-start(f32[16,6,320]{2,0,1:T(8,128)} %copy-done.8) | copy-start | bytes 368644
  132.0 9.1 %copy-start.28 = (f32[16]{0:T(128)S(1)}, f32[16]{0:T(128)}, u32[]{:S(2)}) copy-start(f32[16]{0:T(128)} %get-tuple-element.41) | copy-start | bytes 196
  137.6 7.6 %copy-start.26 = (f32[16]{0:T(128)S(1)}, f32[16]{0:T(128)}, u32[]{:S(2)}) copy-start(f32[16]{0:T(128)} %get-tuple-element.40) | copy-start | bytes 196
  137.6 11.0 %slice-start.2 = ((s8[4456448]{0:T(1024)(128)(4,1)}), s8[4194304]{0:T(1024)(128)(4,1)S(1)}, s32[]{:S(2)}) async-start(s8[4456448]{0:T(1024)(128)(4,1)} %bitcast.183), calls=%async_computation.8 | async-start | bytes 8388608
  148.6 34.4 %copy-start.31 = (f32[2,16]{1,0:T(2,128)S(1)}, f32[2,16]{1,0:T(2,128)}, u32[]{:S(2)}) copy-start(f32[2,16]{1,0:T(2,128)} %copy-done.30) | copy-start | bytes 388
  (22 other events, 92.8 us)

commit v6 on v5

--- a/solution.py
+++ b/solution.py
@@ -105,7 +105,7 @@
         jnp.float32
     )
 
-    def covariance_apply(direction):
+    def covariance_local(direction):
         coeffs = jnp.einsum("lpr,mlp->mlr", leaf_basis, direction, precision=HIGHEST_PRECISION)
         joined = jnp.concatenate([direction, coeffs], axis=2)
         rim_joined = extended(joined, (("lon", 1),), REACH)
@@ -137,9 +137,16 @@
         )
         upward = jnp.einsum("lab,mla->mlb", transfer, coeffs, precision=HIGHEST_PRECISION)
         panel_coeffs = jnp.einsum("lk,mlb->mkb", membership, upward, precision=HIGHEST_PRECISION)
-        band_coeffs = jnp.swapaxes(gathered(panel_coeffs, "band"), 0, 1).reshape(
+        return direction, near_part, leaf_far, panel_coeffs
+
+    def band_layout(band_panels, panel_coeffs):
+        stacked = band_panels.reshape((band_panels.shape[0],) + panel_coeffs.shape)
+        return jnp.swapaxes(stacked, 0, 1).reshape(
             panel_coeffs.shape[0], -1, panel_coeffs.shape[2]
         )
+
+    def covariance_finish(local, band_coeffs):
+        direction, near_part, leaf_far, panel_coeffs = local
         panel_far = jnp.einsum(
             "ksab,mksb->mka",
             panel_couple,
@@ -153,6 +160,12 @@
         far_part = jnp.einsum("lpr,mlr->mlp", leaf_basis, leaf_far, precision=HIGHEST_PRECISION)
         return noise_var[None] * direction + near_part + far_part
 
+    def covariance_apply(direction):
+        local = covariance_local(direction)
+        panel_coeffs = local[3]
+        band_panels = gathered(panel_coeffs.reshape(-1), "band")
+        return covariance_finish(local, band_layout(band_panels, panel_coeffs))
+
     def total(*products):
         sums = jnp.stack([jnp.sum(product, axis=(1, 2)) for product in products])
         return all_sum(sums, ("lon", "band"))
@@ -160,8 +173,21 @@
     assert ITERS == 2
     direction = sky_maps
     applied = covariance_apply(direction)
-    applied_twice = covariance_apply(applied)
-    norm_now, curvature_sum = total(direction * direction, direction * applied)
+    applied_local = covariance_local(applied)
+    first_sums = jnp.stack(
+        [jnp.sum(product, axis=(1, 2)) for product in (direction * direction, direction * applied)]
+    )
+    first_sums = all_sum(first_sums, ("lon",))
+    panel_coeffs = applied_local[3]
+    payload = jnp.concatenate([panel_coeffs.reshape(-1), first_sums.reshape(-1)])
+    band_payload = gathered(payload, "band")
+    panel_size = panel_coeffs.size
+    norm_now, curvature_sum = jnp.sum(band_payload[:, panel_size:], axis=0).reshape(
+        first_sums.shape
+    )
+    applied_twice = covariance_finish(
+        applied_local, band_layout(band_payload[:, :panel_size], panel_coeffs)
+    )
     step_size = (norm_now / curvature_sum)[:, None, None]
     solution = step_size * direction
     residual = direction - step_size * applied

time: 187 us -> 171 us (0.914)
  waiting for transfers between devices: 15.1 us -> 10.2 us
  other arithmetic: 20.4 us -> 15.7 us
  matrix products: 57.6 us -> 54.2 us
  starting transfers between devices: 39.2 us -> 36.1 us
    all_to_all x4 -> x3, waiting for transfers between devices: 15.1 us -> 10.2 us  [gathered(): return lax.all_to_all(copies, axis, 0, 0, tiled=False)]
    unnamed x98 -> x83, local copies, waits for them, and re-layouts: 10 us -> 6.05 us
    dot_general x26, matrix products: 57.6 us -> 54.2 us  [the longest x4 11.7 us: covariance_local(): jnp.einsum('ipq,miq->mip', ahead, offset_values(step), precision=lax.Prec...]
    all_to_all x2 -> x1, other arithmetic: 3.64 us -> 0.31 us  [gathered(): return lax.all_to_all(copies, axis, 0, 0, tiled=False)]
    ppermute x3, starting transfers between devices: 13.7 us -> 10.4 us  [extended(): lax.ppermute(head, axis, [((i + 1) % count, i) for i in range(count)])]
    transpose x2, local copies, waits for them, and re-layouts: 0.01 us -> 2.38 us  [band_layout(): jnp.swapaxes(stacked, 0, 1)]
    all_to_all x4 -> x3, starting transfers between devices: 25.5 us -> 24 us  [gathered(): return lax.all_to_all(copies, axis, 0, 0, tiled=False)]
  transfers between devices with their start and end apart: 10 -> 9, of which waited for: 2 -> 1; matrix products, arithmetic and copies ran while one was open for 25% -> 31% of each run, Pallas kernels for 0% -> 0%
where the time goes in v6:
time: 171 us; the launch traced here: 169 us
  matrix products  54.2 us (32%)
  starting transfers between devices  36.1 us (21%)
  blocking collectives  30.4 us (18%)
  local copies, waits for them, and re-layouts  21.3 us (12%)
  other arithmetic  15.7 us (9%)
  waiting for transfers between devices  10.2 us (6%)
    all_to_all x2, blocking collectives, gathered(): return lax.all_to_all(copies, axis, 0, 0, tiled=False)  30.4 us
    all_to_all x3, starting transfers between devices, gathered(): return lax.all_to_all(copies, axis, 0, 0, tiled=False)  24 us
    dot_general x4, matrix products, covariance_local(): jnp.einsum('ipq,miq->mip', ahead, offset_values(step), precision=lax.Prec...  11.7 us
    dot_general x2, matrix products, covariance_local(): jnp.einsum('ipq,miq->mip', same_blocks, offset_values(0), precision=lax.P...  11.3 us
    ppermute x3, starting transfers between devices, extended(): lax.ppermute(head, axis, [((i + 1) % count, i) for i in range(count)])  10.4 us
    all_to_all x3, waiting for transfers between devices, gathered(): return lax.all_to_all(copies, axis, 0, 0, tiled=False)  10.2 us
    mul x2, other arithmetic, matern_shape(): return (1.0 + scaled) * jnp.exp(-scaled)  9.75 us
    dot_general x4, matrix products, covariance_local(): jnp.einsum('iqp,miq->mip', behind, offset_values(-step), precision=lax.Pr...  9.56 us
  transfers between devices with their start and end apart: 9, of which 1 were waited for; matrix products, arithmetic and copies ran while one was open for 31% of the time, Pallas kernels for 0%

profile of v6, /device:TPU:1, one launch (start us, length us, event | category | flops | bytes accessed | tf_op | source)
XLA Modules:
  0.0 169.1 jit_solution(13854825874918584384)
XLA Ops:
  1.6 6.9 %collective-permute-start.2 = (f32[3,2,256]{2,1,0:T(2,128)S(1)}, f32[3,2,256]{2,1,0:T(2,128)S(1)}, u32[]{:S(2)}, u32[]{:S(2)}) collective-permute-start(f32[3,2,256]{2,1,0:T(2,128)S(1)} %get-tuple-element.42), channel_id=1, source_target_pairs={{1,0},{2,1},{3,2},{4,3},{5,4},{6,5},{7,6},{8,7},{9,8},{10,9},{11,1... | collective-permute-start | bytes 18440 | tf_op jit(solution)/shard_map/ppermute | solution.py:26
  9.6 2.4 %convolution_bitcast_fusion.9 = f32[16,16,64]{2,0,1:T(8,128)S(1)} fusion(f32[16,256,64]{1,2,0:T(8,128)} %param.14, f32[16,16,256]{2,1,0:T(8,128)} %param.11), kind=kOutput, calls=%fused_computation.70 | convolution fusion | flops 50331648 | bytes 1376256 | tf_op jit(solution)/shard_map/lpr,mlp->mlr/dot_general | solution.py:109
  12.7 3.6 %collective-permute-start = (f32[16,6,320]{2,0,1:T(8,128)}, f32[16,6,320]{2,0,1:T(8,128)}, u32[]{:S(2)}, u32[]{:S(2)}) collective-permute-start(f32[16,6,320]{2,0,1:T(8,128)} %get-tuple-element.24), channel_id=1, source_target_pairs={{1,0},{2,1},{3,2},{4,3},{5,4},{6,5},{7,6},{8,7},{9,8},{10,9},{11,1... | collective-permute-start | bytes 368648 | tf_op jit(solution)/shard_map/ppermute | solution.py:26
  16.3 1.6 convolution_bitcast_fusion.6
  19.5 6.8 %all-to-all-start = ((f32[16,1,2048]{2,1,0:T(1,128)}), f32[16,1,2048]{2,1,0:T(1,128)S(1)}, u32[]{:S(2)}, u32[]{:S(2)}) async-start(f32[16,1,2048]{2,1,0:T(1,128)} %broadcast_in_dim.30), calls=%async_computation | async-start | bytes 262144 | tf_op jit(solution)/shard_map/all_to_all | solution.py:36
  31.6 5.7 %fusion.17 = f32[16,16,256]{2,1,0:T(8,128)} fusion(f32[16,256]{1,0:T(8,128)S(1)} %get-tuple-element.39, f32[16,256]{1,0:T(8,128)S(1)} %get-tuple-element.40, f32[16,256]{1,0:T(8,128)S(1)} %get-tuple-element.38, f32[16]{0:T(128)S(1)} %get-tuple-element.47, f32[16,16,256]{2,1,0:T(8,128)S(1)} %copy-done.2), kind=kOutput, calls=%fused_computation.24 | convolution fusion | flops 113311744 | bytes 573504 | tf_op jit(solution)/shard_map/ipq,miq->mip/dot_general | solution.py:122
  38.0 5.2 %exponential_multiply_fusion = f32[18,256,256]{2,1,0:T(8,128)} fusion(f32[18,256]{1,0:T(8,128)S(1)} %get-tuple-element.30, f32[18,256]{1,0:T(8,128)S(1)} %get-tuple-element.36, f32[18,256]{1,0:T(8,128)S(1)} %get-tuple-element.31, f32[18,256]{1,0:T(8,128)S(1)} %get-tuple-element.37, f32[18,256]{1,0:T(8,128)S(1)} %get-tuple-element.29, ...), kind=kLoop, calls=%fused_computation.4 | loop fusion | flops 14155776 | bytes 4829184 | tf_op jit(solution)/shard_map/mul | solution.py:51
  43.2 4.6 %exponential_multiply_fusion.1 = f32[17,256,256]{2,1,0:T(8,128)} fusion(f32[17,256]{1,0:T(8,128)S(1)} %get-tuple-element.27, f32[17,256]{1,0:T(8,128)S(1)} %get-tuple-element.34, f32[17,256]{1,0:T(8,128)S(1)} %get-tuple-element.28, f32[17,256]{1,0:T(8,128)S(1)} %get-tuple-element.33, f32[17,256]{1,0:T(8,128)S(1)} %get-tuple-element.26, ...), kind=kLoop, calls=%fused_computation.5 | loop fusion | flops 13369344 | bytes 4560896 | tf_op jit(solution)/shard_map/mul | solution.py:51
  49.0 1.7 copy.111
  50.6 1.6 gather_fusion.1
  53.4 1.6 convolution_bitcast_fusion.5
  56.5 1.6 gather_fusion
  58.0 3.0 %convolution_bitcast_fusion.7 = f32[16,16,64]{2,1,0:T(8,128)S(1)} fusion(f32[16,16,4,64]{3,0,2,1:T(8,128)} %bitcast.174, f32[16,4,64,64]{3,2,1,0:T(8,128)S(1)} %copy-done), kind=kOutput, calls=%fused_computation.68 | convolution fusion | flops 50331648 | bytes 1376256 | tf_op jit(solution)/shard_map/lsab,mlsb->mla/dot_general | solution.py:135
  61.0 2.2 %fusion.75 = f32[16,16,64]{2,0,1:T(8,128)S(1)} fusion(f32[16,16,64]{2,1,0:T(8,128)S(1)} %convolution_bitcast_fusion.7, f32[16,64,64]{2,1,0:T(8,128)} %param.16, f32[16,16,64]{2,1,0:T(8,128)} %convolution_bitcast_fusion.5), kind=kOutput, calls=%fused_computation.65 | convolution fusion | flops 12599296 | bytes 458752 | tf_op jit(solution)/shard_map/lab,mlb->mla/dot_general | solution.py:157
  63.3 3.4 %fusion.2 = f32[16,16,256]{2,1,0:T(8,128)S(1)} fusion(f32[18,256,256]{2,1,0:T(8,128)} %exponential_multiply_fusion, f32[16,6,320]{2,0,1:T(8,128)} %copy-done.5, f32[16,16,64]{2,0,1:T(8,128)S(1)} %convolution_bitcast_fusion.9, f32[16,16,256]{2,0,1:T(8,128)S(1)} %copy.105, f32[16]{0:T(128)S(1)} %copy-done.27), kind=kOutput, calls=%fused_computation.9 | convolution fusion | flops 100859904 | bytes 4931648 | tf_op jit(solution)/shard_map/iqp,miq->mip/dot_general | solution.py:132
  66.8 2.5 %fusion.6 = f32[16,16,256]{2,1,0:T(8,128)S(1)} fusion(f32[18,256,256]{2,1,0:T(8,128)S(1)} %bitcast.172, f32[16,6,320]{2,0,1:T(8,128)} %collective-permute-done, f32[16,16,64]{2,0,1:T(8,128)S(1)} %convolution_bitcast_fusion.9, f32[16,16,256]{2,0,1:T(8,128)S(1)} %copy.105, f32[16]{0:T(128)S(1)} %copy-done.26), kind=kOutput, calls=%fused_computation.13 | convolution fusion | flops 100859904 | bytes 4973056 | tf_op jit(solution)/shard_map/ipq,miq->mip/dot_general | solution.py:129
  70.8 2.7 %fusion.71 = f32[16,16,256]{2,0,1:T(8,128)S(1)} fusion(f32[16,16,256]{2,1,0:T(8,128)S(1)} %fusion.2, f32[16,16,256]{2,1,0:T(8,128)S(1)} %fusion.6, f32[16,16,256]{2,1,0:T(8,128)S(1)} %fusion.10, f32[16,16,256]{2,1,0:T(8,128)S(1)} %copy-done.12, f32[17,256,256]{2,1,0:T(8,128)S(1)} %bitcast.168, f32[16,6,320]{2,0,1:T(8,128)} %collective-permute-done, ...), kind=kOutput, calls=%fused_computation.58 | convolution fusion | flops 101253120 | bytes 6234176 | tf_op jit(solution)/shard_map/ipq,miq->mip/dot_general | solution.py:129
  76.6 5.6 %fusion.16 = f32[16,16,256]{2,1,0:T(8,128)} fusion(f32[16,256]{1,0:T(8,128)S(1)} %copy-done.20, f32[16,256]{1,0:T(8,128)S(1)} %copy-done.22, f32[16,256]{1,0:T(8,128)S(1)} %copy-done.18, f32[16,16,256]{2,0,1:T(8,128)S(1)} %get-tuple-element.49, f32[16]{0:T(128)S(1)} %copy-done.32), kind=kOutput, calls=%fused_computation.23 | convolution fusion | flops 113311744 | bytes 573504 | tf_op jit(solution)/shard_map/ipq,miq->mip/dot_general | solution.py:122
  82.9 10.3 %all-to-all-start.1 = ((f32[32,2,16]{2,1,0:T(2,128)}), f32[32,2,16]{2,1,0:T(2,128)S(1)}, u32[]{:S(2)}, u32[]{:S(2)}) async-start(f32[32,2,16]{2,1,0:T(2,128)} %broadcast_in_dim.32), calls=%async_computation.1 | async-start | bytes 65536 | tf_op jit(solution)/shard_map/all_to_all | solution.py:36
  93.2 1.6 collective-permute-start.5
  95.1 10.2 %all-to-all-done.1 = f32[32,2,16]{2,1,0:T(2,128)S(1)} async-done(((f32[32,2,16]{2,1,0:T(2,128)}), f32[32,2,16]{2,1,0:T(2,128)S(1)}, u32[]{:S(2)}, u32[]{:S(2)}) %all-to-all-start.1) | async-done | bytes 4128 | tf_op jit(solution)/shard_map/all_to_all | solution.py:36
  106.2 7.0 %all-to-all-start.2 = ((f32[16,1,2080]{2,1,0:T(1,128)}), f32[16,1,2080]{2,1,0:T(1,128)}, u32[]{:S(2)}, u32[]{:S(2)}) async-start(f32[16,1,2080]{2,1,0:T(1,128)} %broadcast_in_dim.33), calls=%async_computation.2 | async-start | bytes 278528 | tf_op jit(solution)/shard_map/all_to_all | solution.py:36
  113.9 1.4 gather_fusion.2
  115.3 3.5 %fusion = f32[16,16,256]{2,1,0:T(8,128)S(1)} fusion(f32[18,256,256]{2,1,0:T(8,128)} %exponential_multiply_fusion, f32[16,6,320]{2,0,1:T(8,128)} %copy-done.7, f32[16,16,64]{2,0,1:T(8,128)S(1)} %convolution_bitcast_fusion.8, f32[16,16,256]{2,0,1:T(8,128)S(1)} %get-tuple-element.49, f32[16]{0:T(128)} %get-tuple-element.44), kind=kOutput, calls=%fused_computation.7 | convolution fusion | flops 100859904 | bytes 4932096 | tf_op jit(solution)/shard_map/iqp,miq->mip/dot_general | solution.py:132
  118.9 4.0 %fusion.4 = f32[16,16,256]{2,1,0:T(8,128)S(1)} fusion(f32[18,256,256]{2,1,0:T(8,128)} %exponential_multiply_fusion, f32[16,6,320]{2,0,1:T(8,128)S(1)} %collective-permute-done.4, f32[16,16,64]{2,0,1:T(8,128)S(1)} %convolution_bitcast_fusion.8, f32[16,16,256]{2,0,1:T(8,128)S(1)} %get-tuple-element.49, f32[16]{0:T(128)} %get-tuple-element.45), kind=kOutput, calls=%fused_computation.11 | convolution fusion | flops 100859904 | bytes 4907520 | tf_op jit(solution)/shard_map/ipq,miq->mip/dot_general | solution.py:129
  124.1 2.5 %fusion.62 = f32[16,16,256]{2,0,1:T(8,128)} fusion(f32[16,16,256]{2,1,0:T(8,128)S(1)} %fusion, f32[16,16,256]{2,1,0:T(8,128)S(1)} %fusion.4, f32[16,16,256]{2,1,0:T(8,128)S(1)} %fusion.8, f32[16,16,256]{2,1,0:T(8,128)S(1)} %copy-done.13, f32[17,256,256]{2,1,0:T(8,128)S(1)} %bitcast.170, f32[16,6,320]{2,0,1:T(8,128)S(1)} %collective-permute-done.4, ...), kind=kOutput, calls=%fused_computation.55 | convolution fusion | flops 101253120 | bytes 6234176 | tf_op jit(solution)/shard_map/ipq,miq->mip/dot_general | solution.py:129
  126.6 1.8 %convolution_bitcast_fusion.3 = f32[16,16,64]{2,1,0:T(8,128)S(1)} fusion(f32[16,16,4,64]{3,0,2,1:T(8,128)S(1)} %bitcast.173, f32[16,4,64,64]{3,2,1,0:T(8,128)S(1)} %copy-done), kind=kOutput, calls=%fused_computation.62 | convolution fusion | flops 50331648 | bytes 1376256 | tf_op jit(solution)/shard_map/lsab,mlsb->mla/dot_general | solution.py:135
  130.4 1.6 gather_fusion.3
  132.5 2.0 %fusion.74 = f32[16,16,64]{2,0,1:T(8,128)S(1)} fusion(f32[16,16,64]{2,1,0:T(8,128)S(1)} %convolution_bitcast_fusion.3, f32[16,64,64]{2,1,0:T(8,128)} %param.16, f32[16,16,64]{2,1,0:T(8,128)S(1)} %convolution_bitcast_fusion.2), kind=kOutput, calls=%fused_computation.60 | convolution fusion | flops 12599296 | bytes 458752 | tf_op jit(solution)/shard_map/lab,mlb->mla/dot_general | solution.py:157
  134.5 2.1 %multiply_reduce_fusion.3 = (f32[16]{0:T(128)S(1)}, f32[16]{0:T(128)S(1)}, f32[16]{0:T(128)S(1)}, f32[16]{0:T(128)S(1)}, f32[16,16,256]{2,0,1:T(8,128)S(1)}) fusion(f32[16,16,256]{2,0,1:T(8,128)S(1)} %get-tuple-element.49, f32[16]{0:T(128)S(1)} %slice_divide_fusion, f32[16,16,256]{2,1,0:T(8,128)S(1)} %copy-done.2, f32[16,16,256]{2,0,1:T(8,128)S(1)} %copy-done.9, ...), kind=kOutput, calls=%fused_computation.117 | convolution fusion | flops 51183552 | bytes 2163008 | tf_op jit(solution)/shard_map/lpr,mlr->mlp/dot_general | solution.py:160
  136.6 17.2 %all_to_all.30 = f32[32,4,16]{2,1,0:T(4,128)S(1)} all-to-all(f32[32,4,16]{2,1,0:T(4,128)S(1)} %broadcast_in_dim.34), channel_id=1, replica_groups=mesh['band'=16,'lon'=32] {'lon'}, dimensions={0} | all-to-all | bytes 16384 | tf_op jit(solution)/shard_map/all_to_all | solution.py:36
  153.9 13.2 %all_to_all.31 = f32[16,4,16]{2,1,0:T(4,128)S(1)} all-to-all(f32[16,4,16]{2,1,0:T(4,128)S(1)} %broadcast_in_dim.35), channel_id=1, replica_groups=mesh['band'=16,'lon'=32] {'band'}, dimensions={0} | all-to-all | bytes 8192 | tf_op jit(solution)/shard_map/all_to_all | solution.py:36
  (157 shorter events, 27.0 us)
Async XLA Ops:
  0.6 57.4 %copy-start = (f32[16,4,64,64]{3,2,1,0:T(8,128)S(1)}, f32[16,4,64,64]{3,2,1,0:T(8,128)}, u32[]{:S(2)}) copy-start(f32[16,4,64,64]{3,2,1,0:T(8,128)} %param.15) | copy-start | bytes 3145732
  0.6 28.6 %copy-start.2 = (f32[16,16,256]{2,1,0:T(8,128)S(1)}, f32[16,16,256]{2,1,0:T(8,128)}, u32[]{:S(2)}) copy-start(f32[16,16,256]{2,1,0:T(8,128)} %param.11) | copy-start | bytes 786436
  0.7 29.4 %copy-start.16 = (s32[16,5]{0,1:T(8,128)S(1)}, s32[16,5]{0,1:T(8,128)}, u32[]{:S(2)}) copy-start(s32[16,5]{0,1:T(8,128)} %param.18) | copy-start | bytes 964
  0.7 30.0 %copy-start.29 = (s32[16,4]{0,1:T(4,128)S(1)}, s32[16,4]{0,1:T(4,128)}, u32[]{:S(2)}) copy-start(s32[16,4]{0,1:T(4,128)} %param.19) | copy-start | bytes 772
  0.7 30.8 %copy-start.30 = (s32[2,2]{1,0:T(2,128)S(1)}, s32[2,2]{1,0:T(2,128)}, u32[]{:S(2)}) copy-start(s32[2,2]{1,0:T(2,128)} %param.20) | copy-start | bytes 52
  1.6 36.3 %collective-permute-start.2 = (f32[3,2,256]{2,1,0:T(2,128)S(1)}, f32[3,2,256]{2,1,0:T(2,128)S(1)}, u32[]{:S(2)}, u32[]{:S(2)}) collective-permute-start(f32[3,2,256]{2,1,0:T(2,128)S(1)} %get-tuple-element.42), channel_id=1, source_target_pairs={{1,0},{2,1},{3,2},{4,3},{5,4},{6,5},{7,6},{8,7},{9,8},{10,9},{11,1... | collective-permute-start | bytes 18440 | tf_op jit(solution)/shard_map/ppermute | solution.py:26
  8.5 29.5 %collective-permute-start.1 = (f32[3,2,256]{2,1,0:T(2,128)S(1)}, f32[3,2,256]{2,1,0:T(2,128)S(1)}, u32[]{:S(2)}, u32[]{:S(2)}) collective-permute-start(f32[3,2,256]{2,1,0:T(2,128)S(1)} %get-tuple-element.41), channel_id=1, source_target_pairs={{0,1},{1,2},{2,3},{3,4},{4,5},{5,6},{6,7},{7,8},{8,9},{9,10},{10,1... | collective-permute-start | bytes 18440 | tf_op jit(solution)/shard_map/ppermute | solution.py:24
  12.7 42.3 %collective-permute-start.3 = (f32[16,6,320]{2,0,1:T(8,128)}, f32[16,6,320]{2,0,1:T(8,128)S(1)}, u32[]{:S(2)}, u32[]{:S(2)}) collective-permute-start(f32[16,6,320]{2,0,1:T(8,128)} %get-tuple-element.25), channel_id=1, source_target_pairs={{0,1},{1,2},{2,3},{3,4},{4,5},{5,6},{6,7},{7,8},{8,9},{9,10},{10,1... | collective-permute-start | bytes 368648 | tf_op jit(solution)/shard_map/ppermute | solution.py:24
  12.7 42.9 %collective-permute-start = (f32[16,6,320]{2,0,1:T(8,128)}, f32[16,6,320]{2,0,1:T(8,128)}, u32[]{:S(2)}, u32[]{:S(2)}) collective-permute-start(f32[16,6,320]{2,0,1:T(8,128)} %get-tuple-element.24), channel_id=1, source_target_pairs={{1,0},{2,1},{3,2},{4,3},{5,4},{6,5},{7,6},{8,7},{9,8},{10,9},{11,1... | collective-permute-start | bytes 368648 | tf_op jit(solution)/shard_map/ppermute | solution.py:26
  19.5 28.2 %all-to-all-start = ((f32[16,1,2048]{2,1,0:T(1,128)}), f32[16,1,2048]{2,1,0:T(1,128)S(1)}, u32[]{:S(2)}, u32[]{:S(2)}) async-start(f32[16,1,2048]{2,1,0:T(1,128)} %broadcast_in_dim.30), calls=%async_computation | async-start | bytes 262144 | tf_op jit(solution)/shard_map/all_to_all | solution.py:36
  29.3 8.0 %copy-start.17 = (f32[16,256]{1,0:T(8,128)}, f32[16,256]{1,0:T(8,128)S(1)}, u32[]{:S(2)}) copy-start(f32[16,256]{1,0:T(8,128)S(1)} %get-tuple-element.38) | copy-start | bytes 49156
  29.3 8.0 %copy-start.19 = (f32[16,256]{1,0:T(8,128)}, f32[16,256]{1,0:T(8,128)S(1)}, u32[]{:S(2)}) copy-start(f32[16,256]{1,0:T(8,128)S(1)} %get-tuple-element.39) | copy-start | bytes 49156
  29.3 8.0 %copy-start.21 = (f32[16,256]{1,0:T(8,128)}, f32[16,256]{1,0:T(8,128)S(1)}, u32[]{:S(2)}) copy-start(f32[16,256]{1,0:T(8,128)S(1)} %get-tuple-element.40) | copy-start | bytes 49156
  30.7 6.6 %copy-start.31 = (f32[16]{0:T(128)}, f32[16]{0:T(128)S(1)}, u32[]{:S(2)}) copy-start(f32[16]{0:T(128)S(1)} %get-tuple-element.47) | copy-start | bytes 196
  31.6 6.4 %copy-start.10 = (f32[3,16,256]{2,1,0:T(8,128)S(1)}, f32[3,16,256]{2,1,0:T(8,128)}, u32[]{:S(2)}) copy-start(f32[3,16,256]{2,1,0:T(8,128)} %param.13) | copy-start | bytes 147460
  48.1 18.6 %slice-start.4 = ((s8[4718592]{0:T(1024)(128)(4,1)}), s8[524288]{0:T(1024)(128)(4,1)S(1)}, s32[]{:S(2)}) async-start(s8[4718592]{0:T(1024)(128)(4,1)} %bitcast.171), calls=%async_computation.9 | async-start | bytes 1048576
  49.0 14.3 %copy-start.27 = (f32[16]{0:T(128)S(1)}, f32[16]{0:T(128)}, u32[]{:S(2)}) copy-start(f32[16]{0:T(128)} %get-tuple-element.44) | copy-start | bytes 196
  58.0 8.7 %slice-start.5 = ((s8[4718592]{0:T(1024)(128)(4,1)}), s8[4194304]{0:T(1024)(128)(4,1)S(1)}, s32[]{:S(2)}) async-start(s8[4718592]{0:T(1024)(128)(4,1)} %bitcast.171), calls=%async_computation.10 | async-start | bytes 8388608
  58.0 8.7 %copy-start.26 = (f32[16]{0:T(128)S(1)}, f32[16]{0:T(128)}, u32[]{:S(2)}) copy-start(f32[16]{0:T(128)} %get-tuple-element.45) | copy-start | bytes 196
  61.0 8.3 %slice-start = ((s8[4456448]{0:T(1024)(128)(4,1)}), s8[4194304]{0:T(1024)(128)(4,1)S(1)}, s32[]{:S(2)}) async-start(s8[4456448]{0:T(1024)(128)(4,1)} %bitcast.167), calls=%async_computation.5 | async-start | bytes 8388608
  63.2 6.1 %slice-start.1 = ((s8[4456448]{0:T(1024)(128)(4,1)}), s8[262144]{0:T(1024)(128)(4,1)S(1)}, s32[]{:S(2)}) async-start(s8[4456448]{0:T(1024)(128)(4,1)} %bitcast.167), calls=%async_computation.6 | async-start | bytes 524288
  63.2 6.1 %copy-start.6 = (f32[16,6,320]{2,0,1:T(8,128)S(1)}, f32[16,6,320]{2,0,1:T(8,128)}, u32[]{:S(2)}) copy-start(f32[16,6,320]{2,0,1:T(8,128)} %copy-done.5) | copy-start | bytes 368644
  76.6 18.2 %copy-start.23 = (s32[16]{0:T(128)S(1)}, s32[16]{0:T(128)}, u32[]{:S(2)}) copy-start(s32[16]{0:T(128)} %param.21) | copy-start | bytes 196
  76.6 37.2 %copy-start.14 = (s32[1024]{0:T(1024)S(1)}, s32[1024]{0:T(1024)}, u32[]{:S(2)}) copy-start(s32[1024]{0:T(1024)} %pad_clamp_fusion.1) | copy-start | bytes 12292
  82.9 22.4 %all-to-all-start.1 = ((f32[32,2,16]{2,1,0:T(2,128)}), f32[32,2,16]{2,1,0:T(2,128)S(1)}, u32[]{:S(2)}, u32[]{:S(2)}) async-start(f32[32,2,16]{2,1,0:T(2,128)} %broadcast_in_dim.32), calls=%async_computation.1 | async-start | bytes 65536 | tf_op jit(solution)/shard_map/all_to_all | solution.py:36
  93.2 20.0 %collective-permute-start.5 = (f32[16,6,320]{2,0,1:T(8,128)}, f32[16,6,320]{2,0,1:T(8,128)S(1)}, u32[]{:S(2)}, u32[]{:S(2)}) collective-permute-start(f32[16,6,320]{2,0,1:T(8,128)} %get-tuple-element.23), channel_id=1, source_target_pairs={{0,1},{1,2},{2,3},{3,4},{4,5},{5,6},{6,7},{7,8},{8,9},{9,10},{10,1... | collective-permute-start | bytes 368648 | tf_op jit(solution)/shard_map/ppermute | solution.py:24
  94.8 18.3 %collective-permute-start.4 = (f32[16,6,320]{2,0,1:T(8,128)S(1)}, f32[16,6,320]{2,0,1:T(8,128)S(1)}, u32[]{:S(2)}, u32[]{:S(2)}) collective-permute-start(f32[16,6,320]{2,0,1:T(8,128)S(1)} %get-tuple-element.22), channel_id=1, source_target_pairs={{1,0},{2,1},{3,2},{4,3},{5,4},{6,5},{7,6},{8,7},{9,8},{10,9},{11,1... | collective-permute-start | bytes 368648 | tf_op jit(solution)/shard_map/ppermute | solution.py:26
  106.2 22.2 %all-to-all-start.2 = ((f32[16,1,2080]{2,1,0:T(1,128)}), f32[16,1,2080]{2,1,0:T(1,128)}, u32[]{:S(2)}, u32[]{:S(2)}) async-start(f32[16,1,2080]{2,1,0:T(1,128)} %broadcast_in_dim.33), calls=%async_computation.2 | async-start | bytes 278528 | tf_op jit(solution)/shard_map/all_to_all | solution.py:36
  113.9 9.0 %slice-start.2 = ((s8[4456448]{0:T(1024)(128)(4,1)}), s8[262144]{0:T(1024)(128)(4,1)S(1)}, s32[]{:S(2)}) async-start(s8[4456448]{0:T(1024)(128)(4,1)} %bitcast.169), calls=%async_computation.7 | async-start | bytes 524288
  115.3 7.5 %slice-start.3 = ((s8[4456448]{0:T(1024)(128)(4,1)}), s8[4194304]{0:T(1024)(128)(4,1)S(1)}, s32[]{:S(2)}) async-start(s8[4456448]{0:T(1024)(128)(4,1)} %bitcast.169), calls=%async_computation.8 | async-start | bytes 8388608
  115.3 7.6 %copy-start.8 = (f32[16,6,320]{2,0,1:T(8,128)S(1)}, f32[16,6,320]{2,0,1:T(8,128)}, u32[]{:S(2)}) copy-start(f32[16,6,320]{2,0,1:T(8,128)} %copy-done.7) | copy-start | bytes 368644
  126.6 7.9 %copy-start.9 = (f32[16,16,256]{2,0,1:T(8,128)S(1)}, f32[16,16,256]{2,0,1:T(8,128)}, u32[]{:S(2)}) copy-start(f32[16,16,256]{2,0,1:T(8,128)} %fusion.62) | copy-start | bytes 786436
  (16 other events, 68.8 us)

commit v7 on v6

--- a/solution.py
+++ b/solution.py
@@ -14,20 +14,28 @@
 AMPLITUDE = 0.02
 
 
-def extended(cells, sides, width):
-    for axis, dim in sides:
-        count = lax.axis_size(axis)
-        head = lax.slice_in_dim(cells, 0, width, axis=dim)
-        tail = lax.slice_in_dim(cells, cells.shape[dim] - width, cells.shape[dim], axis=dim)
-        cells = jnp.concatenate(
-            [
-                lax.ppermute(tail, axis, [(i, (i + 1) % count) for i in range(count)]),
-                cells,
-                lax.ppermute(head, axis, [((i + 1) % count, i) for i in range(count)]),
-            ],
-            axis=dim,
-        )
-    return cells
+def extended_together(items, axis):
+    count = lax.axis_size(axis)
+    heads = [lax.slice_in_dim(cells, 0, width, axis=dim) for cells, dim, width in items]
+    tails = [
+        lax.slice_in_dim(cells, cells.shape[dim] - width, cells.shape[dim], axis=dim)
+        for cells, dim, width in items
+    ]
+
+    def moved(parts, pairs):
+        flat = lax.ppermute(jnp.concatenate([part.reshape(-1) for part in parts]), axis, pairs)
+        pieces, start = [], 0
+        for part in parts:
+            pieces.append(flat[start : start + part.size].reshape(part.shape))
+            start += part.size
+        return pieces
+
+    from_before = moved(tails, [(i, (i + 1) % count) for i in range(count)])
+    from_after = moved(heads, [((i + 1) % count, i) for i in range(count)])
+    return [
+        jnp.concatenate([before, cells, after], axis=dim)
+        for (cells, dim, _), before, after in zip(items, from_before, from_after)
+    ]
 
 
 def gathered(vector, axis):
@@ -80,21 +88,23 @@
     near_valid = near_list >= 0
     near_rows = rim_index(jnp.where(near_valid, near_list, near_list[:, :1]), near_depth)
     far_rows = rim_index(far_list, REACH)
-    rim_pos = extended(position, (("lon", 1),), near_depth)
-
-    same_blocks = matern_shape(
-        rim_pos[:, near_depth : near_depth + local_leaves],
-        rim_pos[:, near_depth : near_depth + local_leaves],
-        length_scale,
-    )
-    step_blocks = [
-        matern_shape(
-            rim_pos[:, near_depth - step : near_depth + local_leaves],
-            rim_pos[:, near_depth : near_depth + local_leaves + step],
+
+    def near_blocks(rim_pos):
+        same_blocks = matern_shape(
+            rim_pos[:, near_depth : near_depth + local_leaves],
+            rim_pos[:, near_depth : near_depth + local_leaves],
             length_scale,
         )
-        for step in range(1, near_depth + 1)
-    ]
+        step_blocks = [
+            matern_shape(
+                rim_pos[:, near_depth - step : near_depth + local_leaves],
+                rim_pos[:, near_depth : near_depth + local_leaves + step],
+                length_scale,
+            )
+            for step in range(1, near_depth + 1)
+        ]
+        return same_blocks, step_blocks
+
     step_range = jnp.arange(-near_depth, near_depth + 1, dtype=jnp.int32)
     targets = jnp.arange(local_leaves, dtype=jnp.int32)[:, None] + near_depth + step_range[None, :]
     matches = (near_rows[:, :, None] == targets[:, None, :]) & near_valid[:, :, None]
@@ -105,10 +115,17 @@
         jnp.float32
     )
 
-    def covariance_local(direction):
+    def covariance_local(direction, blocks=None):
         coeffs = jnp.einsum("lpr,mlp->mlr", leaf_basis, direction, precision=HIGHEST_PRECISION)
         joined = jnp.concatenate([direction, coeffs], axis=2)
-        rim_joined = extended(joined, (("lon", 1),), REACH)
+        items = [(joined, 1, REACH)]
+        if blocks is None:
+            items.append((position, 1, near_depth))
+        rims = extended_together(items, "lon")
+        rim_joined = rims[0]
+        if blocks is None:
+            blocks = near_blocks(rims[1])
+        same_blocks, step_blocks = blocks
         rim_values = rim_joined[
             :, REACH - near_depth : REACH + local_leaves + near_depth, :pixel_count
         ]
@@ -123,9 +140,9 @@
             "ipq,miq->mip", same_blocks, offset_values(0), precision=lax.Precision.HIGH
         )
         for step in range(1, near_depth + 1):
-            blocks = step_blocks[step - 1]
-            ahead = blocks[step : step + local_leaves]
-            behind = blocks[:local_leaves]
+            step_block = step_blocks[step - 1]
+            ahead = step_block[step : step + local_leaves]
+            behind = step_block[:local_leaves]
             near_part = near_part + jnp.einsum(
                 "ipq,miq->mip", ahead, offset_values(step), precision=lax.Precision.HIGH
             )
@@ -137,7 +154,7 @@
         )
         upward = jnp.einsum("lab,mla->mlb", transfer, coeffs, precision=HIGHEST_PRECISION)
         panel_coeffs = jnp.einsum("lk,mlb->mkb", membership, upward, precision=HIGHEST_PRECISION)
-        return direction, near_part, leaf_far, panel_coeffs
+        return (direction, near_part, leaf_far, panel_coeffs), blocks
 
     def band_layout(band_panels, panel_coeffs):
         stacked = band_panels.reshape((band_panels.shape[0],) + panel_coeffs.shape)
@@ -161,10 +178,10 @@
         return noise_var[None] * direction + near_part + far_part
 
     def covariance_apply(direction):
-        local = covariance_local(direction)
+        local, blocks = covariance_local(direction)
         panel_coeffs = local[3]
         band_panels = gathered(panel_coeffs.reshape(-1), "band")
-        return covariance_finish(local, band_layout(band_panels, panel_coeffs))
+        return covariance_finish(local, band_layout(band_panels, panel_coeffs)), blocks
 
     def total(*products):
         sums = jnp.stack([jnp.sum(product, axis=(1, 2)) for product in products])
@@ -172,8 +189,8 @@
 
     assert ITERS == 2
     direction = sky_maps
-    applied = covariance_apply(direction)
-    applied_local = covariance_local(applied)
+    applied, blocks = covariance_apply(direction)
+    applied_local, _ = covariance_local(applied, blocks)
     first_sums = jnp.stack(
         [jnp.sum(product, axis=(1, 2)) for product in (direction * direction, direction * applied)]
     )

time: 171 us -> 197 us (1.15)
  local copies, waits for them, and re-layouts: 21.3 us -> 39.3 us
  other arithmetic: 15.7 us -> 20.7 us
  matrix products: 54.2 us -> 58.4 us
    reshape x0 -> x14, local copies, waits for them, and re-layouts: none -> 11 us  [the longest x8 7.98 us: moved(): pieces.append(flat[start:start + part.size].reshape(part.shape))]
    slice x1 -> x11, local copies, waits for them, and re-layouts: 0.91 us -> 7.31 us  [the longest x6 4.52 us: moved(): pieces.append(flat[start:start + part.size].reshape(part.shape))]
    concatenate x2 -> x6, other arithmetic: 0.86 us -> 6.13 us  [the longest x2 3.12 us: moved(): jnp.concatenate([part.reshape(-1) for part in parts])]
    all_to_all x3, starting transfers between devices: 24 us -> 20.4 us  [gathered(): return lax.all_to_all(copies, axis, 0, 0, tiled=False)]
    sub x2, other arithmetic: 0.02 us -> 2.99 us  [matern_shape(): offset = rows_pos[component][:, :, None] - cols_pos[component][:, None, :]]
    ppermute x6 -> x4, starting transfers between devices: 12.1 us -> 13.8 us  [moved(): lax.ppermute(jnp.concatenate([part.reshape(-1) for part in parts]), axis,...]
    unnamed x83 -> x87, local copies, waits for them, and re-layouts: 6.05 us -> 5.34 us
  transfers between devices with their start and end apart: 9 -> 7, of which waited for: 1 -> 1; matrix products, arithmetic and copies ran while one was open for 31% -> 25% of each run, Pallas kernels for 0% -> 0%
where the time goes in v7:
time: 197 us; the launch traced here: 195 us
  matrix products  58.4 us (30%)
  local copies, waits for them, and re-layouts  39.3 us (20%)
  starting transfers between devices  34.2 us (17%)
  blocking collectives  30.2 us (15%)
  other arithmetic  20.7 us (11%)
  waiting for transfers between devices  10.9 us (6%)
    all_to_all x2, blocking collectives, gathered(): return lax.all_to_all(copies, axis, 0, 0, tiled=False)  30.2 us
    all_to_all x3, starting transfers between devices, gathered(): return lax.all_to_all(copies, axis, 0, 0, tiled=False)  20.4 us
    ppermute x4, starting transfers between devices, moved(): lax.ppermute(jnp.concatenate([part.reshape(-1) for part in parts]), axis,...  13.8 us
    dot_general x4, matrix products, covariance_local(): jnp.einsum('ipq,miq->mip', ahead, offset_values(step), precision=lax.Prec...  13.3 us
    dot_general x2, matrix products, covariance_local(): jnp.einsum('ipq,miq->mip', same_blocks, offset_values(0), precision=lax.P...  11.3 us
    dot_general x4, matrix products, covariance_local(): jnp.einsum('iqp,miq->mip', behind, offset_values(-step), precision=lax.Pr...  11.2 us
    all_to_all x3, waiting for transfers between devices, gathered(): return lax.all_to_all(copies, axis, 0, 0, tiled=False)  10.9 us
    reshape x8, local copies, waits for them, and re-layouts, moved(): pieces.append(flat[start:start + part.size].reshape(part.shape))  7.98 us
  transfers between devices with their start and end apart: 7, of which 1 were waited for; matrix products, arithmetic and copies ran while one was open for 25% of the time, Pallas kernels for 0%

profile of v7, /device:TPU:1, one launch (start us, length us, event | category | flops | bytes accessed | tf_op | source)
XLA Modules:
  0.0 195.1 jit_solution(3686655683827876736)
XLA Ops:
  2.0 2.4 %convolution_bitcast_fusion.9 = f32[16,16,64]{2,0,1:T(8,128)S(1)} fusion(f32[16,256,64]{1,2,0:T(8,128)} %param.14, f32[16,16,256]{2,1,0:T(8,128)} %param.11), kind=kOutput, calls=%fused_computation.70 | convolution fusion | flops 50331648 | bytes 1376256 | tf_op jit(solution)/shard_map/lpr,mlp->mlr/dot_general | solution.py:119
  6.6 1.6 pad_maximum_fusion.22
  8.2 6.9 %collective-permute-start = (f32[32256]{0:T(1024)}, f32[32256]{0:T(1024)}, u32[]{:S(2)}, u32[]{:S(2)}) collective-permute-start(f32[32256]{0:T(1024)} %pad_maximum_fusion.22), channel_id=1, source_target_pairs={{1,0},{2,1},{3,2},{4,3},{5,4},{6,5},{7,6},{8,7},{9,8},{10,9},{11,1... | collective-permute-start | bytes 387080 | tf_op jit(solution)/shard_map/ppermute | solution.py:26
  16.8 1.6 pad_maximum_fusion.23
  19.9 3.7 %all-to-all-start = ((f32[16,1,2048]{2,1,0:T(1,128)}), f32[16,1,2048]{2,1,0:T(1,128)S(1)}, u32[]{:S(2)}, u32[]{:S(2)}) async-start(f32[16,1,2048]{2,1,0:T(1,128)} %broadcast_in_dim.30), calls=%async_computation | async-start | bytes 262144 | tf_op jit(solution)/shard_map/all_to_all | solution.py:44
  26.6 5.7 %fusion.17 = f32[16,16,256]{2,1,0:T(8,128)} fusion(f32[16,256]{1,0:T(8,128)S(1)} %get-tuple-element.39, f32[16,256]{1,0:T(8,128)S(1)} %get-tuple-element.40, f32[16,256]{1,0:T(8,128)S(1)} %get-tuple-element.38, f32[16]{0:T(128)S(1)} %get-tuple-element.47, f32[16,16,256]{2,1,0:T(8,128)S(1)} %copy-done.4), kind=kOutput, calls=%fused_computation.24 | convolution fusion | flops 113311744 | bytes 573504 | tf_op jit(solution)/shard_map/ipq,miq->mip/dot_general | solution.py:139
  53.2 2.9 %convolution_bitcast_fusion.7 = f32[16,16,64]{2,1,0:T(8,128)S(1)} fusion(f32[16,16,4,64]{3,0,2,1:T(8,128)} %bitcast.172, f32[16,4,64,64]{3,2,1,0:T(8,128)S(1)} %copy-done), kind=kOutput, calls=%fused_computation.68 | convolution fusion | flops 50331648 | bytes 1376256 | tf_op jit(solution)/shard_map/lsab,mlsb->mla/dot_general | solution.py:152
  56.1 1.8 fusion.83
  57.9 1.9 convolution_bitcast_fusion.1
  59.9 4.1 %exponential_multiply_fusion.1 = f32[17,256,256]{2,1,0:T(8,128)S(1)} fusion(f32[17,256]{1,0:T(8,128)} %get-tuple-element.59, f32[17,256]{1,0:T(8,128)} %get-tuple-element.34, f32[17,256]{1,0:T(8,128)} %get-tuple-element.58, f32[17,256]{1,0:T(8,128)} %get-tuple-element.33, f32[17,256]{1,0:T(8,128)} %get-tuple-element.60, f32[17,256]{1,0:T(8,128)} %get-tuple-element.32), kind=kLoop, calls=%fused_computation.5 | loop fusion | flops 13369344 | bytes 4560896 | tf_op jit(solution)/shard_map/mul | solution.py:59
  65.5 3.7 %exponential_multiply_fusion = f32[18,256,256]{2,1,0:T(8,128)S(1)} fusion(f32[18,256]{1,0:T(8,128)S(1)} %copy-done.19, f32[18,256]{1,0:T(8,128)S(1)} %copy-done.16, f32[18,256]{1,0:T(8,128)S(1)} %copy-done.18, f32[18,256]{1,0:T(8,128)S(1)} %copy-done.17, f32[18,256]{1,0:T(8,128)S(1)} %copy-done.20, f32[18,256]{1,0:T(8,128)S(1)} %copy-done.15), kind=kLoop, calls=%fused_computation.4 | loop fusion | flops 14155776 | bytes 4829184 | tf_op jit(solution)/shard_map/mul | solution.py:59
  69.3 1.9 fusion.6
  71.2 1.9 fusion.40
  73.1 2.1 %multiply_reduce_fusion.4 = (f32[16]{0:T(128)}, f32[16,16,256]{2,0,1:T(8,128)S(1)}) fusion(f32[16,16,256]{2,1,0:T(8,128)S(1)} %copy-done.4, f32[16,16,256]{2,0,1:T(8,128)S(1)} %convolution_bitcast_fusion.1, f32[16,16,256]{2,1,0:T(8,128)S(1)} %fusion.40, f32[18,256,256]{2,1,0:T(8,128)S(1)} %exponential_multiply_fusion, f32[16,6,320]{2,0,1:T(8,128)S(1)} %copy-done.8, ...), kind=kOutput, calls=%fused_computation.119 | convolution fusion | flops 101253104 | bytes 6062656 | tf_op jit(solution)/shard_map/iqp,miq->mip/dot_general | solution.py:149
  76.2 5.6 %fusion.16 = f32[16,16,256]{2,1,0:T(8,128)} fusion(f32[16,256]{1,0:T(8,128)S(1)} %copy-done.27, f32[16,256]{1,0:T(8,128)S(1)} %copy-done.29, f32[16,256]{1,0:T(8,128)S(1)} %copy-done.25, f32[16,16,256]{2,0,1:T(8,128)S(1)} %get-tuple-element.49, f32[16]{0:T(128)S(1)} %copy-done.40), kind=kOutput, calls=%fused_computation.23 | convolution fusion | flops 113311744 | bytes 573504 | tf_op jit(solution)/shard_map/ipq,miq->mip/dot_general | solution.py:139
  86.3 6.9 %collective-permute-start.2 = (f32[30720]{0:T(1024)}, f32[30720]{0:T(1024)}, u32[]{:S(2)}, u32[]{:S(2)}) collective-permute-start(f32[30720]{0:T(1024)} %reshape.166), channel_id=1, source_target_pairs={{1,0},{2,1},{3,2},{4,3},{5,4},{6,5},{7,6},{8,7},{9,8},{10,9},{11,1... | collective-permute-start | bytes 368648 | tf_op jit(solution)/shard_map/ppermute | solution.py:26
  93.8 9.8 %all-to-all-start.1 = ((f32[32,2,16]{2,1,0:T(2,128)}), f32[32,2,16]{2,1,0:T(2,128)S(1)}, u32[]{:S(2)}, u32[]{:S(2)}) async-start(f32[32,2,16]{2,1,0:T(2,128)} %broadcast_in_dim.32), calls=%async_computation.1 | async-start | bytes 65536 | tf_op jit(solution)/shard_map/all_to_all | solution.py:44
  104.8 10.9 %all-to-all-done.1 = f32[32,2,16]{2,1,0:T(2,128)S(1)} async-done(((f32[32,2,16]{2,1,0:T(2,128)}), f32[32,2,16]{2,1,0:T(2,128)S(1)}, u32[]{:S(2)}, u32[]{:S(2)}) %all-to-all-start.1) | async-done | bytes 4128 | tf_op jit(solution)/shard_map/all_to_all | solution.py:44
  116.6 7.0 %all-to-all-start.2 = ((f32[16,1,2080]{2,1,0:T(1,128)}), f32[16,1,2080]{2,1,0:T(1,128)}, u32[]{:S(2)}, u32[]{:S(2)}) async-start(f32[16,1,2080]{2,1,0:T(1,128)} %broadcast_in_dim.33), calls=%async_computation.2 | async-start | bytes 278528 | tf_op jit(solution)/shard_map/all_to_all | solution.py:44
  123.6 1.7 reshape.169
  126.3 4.1 %fusion.8 = f32[16,16,256]{2,1,0:T(8,128)} fusion(f32[17,256,256]{2,1,0:T(8,128)} %copy-done.1, f32[16,6,320]{2,0,1:T(8,128)S(1)} %copy.176, f32[16,16,64]{2,0,1:T(8,128)S(1)} %convolution_bitcast_fusion.8, f32[16,16,256]{2,0,1:T(8,128)S(1)} %get-tuple-element.49, f32[16]{0:T(128)S(1)} %copy-done.36), kind=kOutput, calls=%fused_computation.15 | convolution fusion | flops 100859904 | bytes 4907072 | tf_op jit(solution)/shard_map/iqp,miq->mip/dot_general | solution.py:149
  130.4 1.7 reshape.167
  133.1 4.7 %fusion.4 = f32[16,16,256]{2,1,0:T(8,128)} fusion(f32[18,256,256]{2,1,0:T(8,128)} %copy-done.2, f32[16,6,320]{2,0,1:T(8,128)S(1)} %copy.174, f32[16,16,64]{2,0,1:T(8,128)S(1)} %convolution_bitcast_fusion.8, f32[16,16,256]{2,0,1:T(8,128)S(1)} %get-tuple-element.49, f32[16]{0:T(128)S(1)} %copy-done.34), kind=kOutput, calls=%fused_computation.11 | convolution fusion | flops 100859904 | bytes 4907072 | tf_op jit(solution)/shard_map/ipq,miq->mip/dot_general | solution.py:146
  140.0 4.9 %fusion.49 = f32[16,16,256]{2,1,0:T(8,128)} fusion(f32[16,16,256]{2,1,0:T(8,128)} %fusion.4, f32[16,16,256]{2,1,0:T(8,128)} %fusion.8, f32[16,16,256]{2,1,0:T(8,128)} %fusion.16, f32[17,256,256]{2,1,0:T(8,128)} %copy-done.1, f32[16,6,320]{2,0,1:T(8,128)} %copy-done.11, f32[16,16,64]{2,0,1:T(8,128)S(1)} %convolution_bitcast_fusion.8, ...), kind=kOutput, calls=%fused_computation.46 | convolution fusion | flops 101056512 | bytes 5718080 | tf_op jit(solution)/shard_map/ipq,miq->mip/dot_general | solution.py:146
  144.9 2.5 %convolution_bitcast_fusion.3 = f32[16,16,64]{2,1,0:T(8,128)} fusion(f32[16,16,4,64]{3,0,2,1:T(8,128)S(1)} %bitcast.171, f32[16,4,64,64]{3,2,1,0:T(8,128)S(1)} %copy-done), kind=kOutput, calls=%fused_computation.62 | convolution fusion | flops 50331648 | bytes 1376256 | tf_op jit(solution)/shard_map/lsab,mlsb->mla/dot_general | solution.py:152
  149.0 1.8 reshape.170
  150.8 1.7 copy.179
  155.4 1.8 fusion.82
  157.2 1.9 convolution_bitcast_fusion
  159.2 3.6 %multiply_reduce_fusion.3 = (f32[16]{0:T(128)S(1)}, f32[16]{0:T(128)S(1)}, f32[16]{0:T(128)S(1)}, f32[16]{0:T(128)S(1)}, f32[16,16,256]{2,0,1:T(8,128)S(1)}) fusion(f32[16,16,256]{2,0,1:T(8,128)S(1)} %get-tuple-element.49, f32[16]{0:T(128)S(1)} %slice_divide_fusion, f32[16,16,256]{2,1,0:T(8,128)S(1)} %copy-done.4, ...), kind=kOutput, calls=%fused_computation.117 | convolution fusion | flops 101908416 | bytes 6063360 | tf_op jit(solution)/shard_map/iqp,miq->mip/dot_general | solution.py:149
  162.8 17.1 %all_to_all.30 = f32[32,4,16]{2,1,0:T(4,128)S(1)} all-to-all(f32[32,4,16]{2,1,0:T(4,128)S(1)} %broadcast_in_dim.34), channel_id=1, replica_groups=mesh['band'=16,'lon'=32] {'lon'}, dimensions={0} | all-to-all | bytes 16384 | tf_op jit(solution)/shard_map/all_to_all | solution.py:44
  179.9 13.1 %all_to_all.31 = f32[16,4,16]{2,1,0:T(4,128)S(1)} all-to-all(f32[16,4,16]{2,1,0:T(4,128)S(1)} %broadcast_in_dim.35), channel_id=1, replica_groups=mesh['band'=16,'lon'=32] {'band'}, dimensions={0} | all-to-all | bytes 8192 | tf_op jit(solution)/shard_map/all_to_all | solution.py:44
  (177 shorter events, 51.1 us)
Async XLA Ops:
  0.6 52.6 %copy-start = (f32[16,4,64,64]{3,2,1,0:T(8,128)S(1)}, f32[16,4,64,64]{3,2,1,0:T(8,128)}, u32[]{:S(2)}) copy-start(f32[16,4,64,64]{3,2,1,0:T(8,128)} %param.15) | copy-start | bytes 3145732
  0.6 26.0 %copy-start.4 = (f32[16,16,256]{2,1,0:T(8,128)S(1)}, f32[16,16,256]{2,1,0:T(8,128)}, u32[]{:S(2)}) copy-start(f32[16,16,256]{2,1,0:T(8,128)} %param.11) | copy-start | bytes 786436
  0.7 23.0 %copy-start.13 = (f32[3,16,256]{2,1,0:T(8,128)S(1)}, f32[3,16,256]{2,1,0:T(8,128)}, u32[]{:S(2)}) copy-start(f32[3,16,256]{2,1,0:T(8,128)} %param.13) | copy-start | bytes 147460
  0.7 17.7 %copy-start.5 = (f32[16,64,64]{2,1,0:T(8,128)S(1)}, f32[16,64,64]{2,1,0:T(8,128)}, u32[]{:S(2)}) copy-start(f32[16,64,64]{2,1,0:T(8,128)} %param.16) | copy-start | bytes 786436
  0.7 18.2 %copy-start.30 = (s32[16]{0:T(128)S(1)}, s32[16]{0:T(128)}, u32[]{:S(2)}) copy-start(s32[16]{0:T(128)} %param.21) | copy-start | bytes 196
  0.7 23.6 %copy-start.23 = (s32[16,5]{0,1:T(8,128)S(1)}, s32[16,5]{0,1:T(8,128)}, u32[]{:S(2)}) copy-start(s32[16,5]{0,1:T(8,128)} %param.18) | copy-start | bytes 964
  8.2 31.3 %collective-permute-start = (f32[32256]{0:T(1024)}, f32[32256]{0:T(1024)}, u32[]{:S(2)}, u32[]{:S(2)}) collective-permute-start(f32[32256]{0:T(1024)} %pad_maximum_fusion.22), channel_id=1, source_target_pairs={{1,0},{2,1},{3,2},{4,3},{5,4},{6,5},{7,6},{8,7},{9,8},{10,9},{11,1... | collective-permute-start | bytes 387080 | tf_op jit(solution)/shard_map/ppermute | solution.py:26
  18.3 21.8 %collective-permute-start.1 = (f32[32256]{0:T(1024)}, f32[32256]{0:T(1024)}, u32[]{:S(2)}, u32[]{:S(2)}) collective-permute-start(f32[32256]{0:T(1024)} %pad_maximum_fusion.23), channel_id=1, source_target_pairs={{0,1},{1,2},{2,3},{3,4},{4,5},{5,6},{6,7},{7,8},{8,9},{9,10},{10,1... | collective-permute-start | bytes 387080 | tf_op jit(solution)/shard_map/ppermute | solution.py:26
  19.9 13.2 %all-to-all-start = ((f32[16,1,2048]{2,1,0:T(1,128)}), f32[16,1,2048]{2,1,0:T(1,128)S(1)}, u32[]{:S(2)}, u32[]{:S(2)}) async-start(f32[16,1,2048]{2,1,0:T(1,128)} %broadcast_in_dim.30), calls=%async_computation | async-start | bytes 262144 | tf_op jit(solution)/shard_map/all_to_all | solution.py:44
  24.3 8.0 %copy-start.24 = (f32[16,256]{1,0:T(8,128)}, f32[16,256]{1,0:T(8,128)S(1)}, u32[]{:S(2)}) copy-start(f32[16,256]{1,0:T(8,128)S(1)} %get-tuple-element.38) | copy-start | bytes 49156
  24.3 8.0 %copy-start.26 = (f32[16,256]{1,0:T(8,128)}, f32[16,256]{1,0:T(8,128)S(1)}, u32[]{:S(2)}) copy-start(f32[16,256]{1,0:T(8,128)S(1)} %get-tuple-element.39) | copy-start | bytes 49156
  24.3 8.0 %copy-start.28 = (f32[16,256]{1,0:T(8,128)}, f32[16,256]{1,0:T(8,128)S(1)}, u32[]{:S(2)}) copy-start(f32[16,256]{1,0:T(8,128)S(1)} %get-tuple-element.40) | copy-start | bytes 49156
  53.2 10.8 %copy-start.8 = (f32[16,6,320]{2,0,1:T(8,128)S(1)}, f32[16,6,320]{2,0,1:T(8,128)}, u32[]{:S(2)}) copy-start(f32[16,6,320]{2,0,1:T(8,128)} %copy.160) | copy-start | bytes 368644
  53.2 10.8 %copy-start.35 = (f32[16]{0:T(128)S(1)}, f32[16]{0:T(128)}, u32[]{:S(2)}) copy-start(f32[16]{0:T(128)} %get-tuple-element.45) | copy-start | bytes 196
  59.8 5.6 %copy-start.15 = (f32[18,256]{1,0:T(8,128)S(1)}, f32[18,256]{1,0:T(8,128)}, u32[]{:S(2)}) copy-start(f32[18,256]{1,0:T(8,128)} %get-tuple-element.35) | copy-start | bytes 55300
  59.8 5.6 %copy-start.16 = (f32[18,256]{1,0:T(8,128)S(1)}, f32[18,256]{1,0:T(8,128)}, u32[]{:S(2)}) copy-start(f32[18,256]{1,0:T(8,128)} %get-tuple-element.36) | copy-start | bytes 55300
  59.8 5.6 %copy-start.17 = (f32[18,256]{1,0:T(8,128)S(1)}, f32[18,256]{1,0:T(8,128)}, u32[]{:S(2)}) copy-start(f32[18,256]{1,0:T(8,128)} %get-tuple-element.37) | copy-start | bytes 55300
  64.0 7.2 %copy-start.1 = (f32[17,256,256]{2,1,0:T(8,128)}, f32[17,256,256]{2,1,0:T(8,128)S(1)}, u32[]{:S(2)}) copy-start(f32[17,256,256]{2,1,0:T(8,128)S(1)} %exponential_multiply_fusion.1) | copy-start | bytes 13369348
  65.5 5.7 %copy-start.14 = (f32[16,16,256]{2,1,0:T(8,128)S(1)}, f32[16,16,256]{2,1,0:T(8,128)}, u32[]{:S(2)}) copy-start(f32[16,16,256]{2,1,0:T(8,128)} %fusion.17) | copy-start | bytes 786436
  65.5 5.7 %copy-start.31 = (f32[16]{0:T(128)S(1)}, f32[16]{0:T(128)}, u32[]{:S(2)}) copy-start(f32[16]{0:T(128)} %get-tuple-element.46) | copy-start | bytes 196
  76.2 17.0 %copy-start.37 = (f32[16]{0:T(128)S(1)}, f32[16]{0:T(128)}, u32[]{:S(2)}) copy-start(f32[16]{0:T(128)} %multiply_reduce_fusion.5) | copy-start | bytes 196
  76.2 17.0 %copy-start.38 = (f32[16]{0:T(128)S(1)}, f32[16]{0:T(128)}, u32[]{:S(2)}) copy-start(f32[16]{0:T(128)} %get-tuple-element.48) | copy-start | bytes 196
  81.8 44.4 %copy-start.36 = (f32[16]{0:T(128)S(1)}, f32[16]{0:T(128)}, u32[]{:S(2)}) copy-start(f32[16]{0:T(128)} %get-tuple-element.45) | copy-start | bytes 196
  83.7 49.3 %copy-start.34 = (f32[16]{0:T(128)S(1)}, f32[16]{0:T(128)}, u32[]{:S(2)}) copy-start(f32[16]{0:T(128)} %get-tuple-element.44) | copy-start | bytes 196
  84.5 39.1 %collective-permute-start.3 = (f32[30720]{0:T(1024)}, f32[30720]{0:T(1024)}, u32[]{:S(2)}, u32[]{:S(2)}) collective-permute-start(f32[30720]{0:T(1024)} %reshape.168), channel_id=1, source_target_pairs={{0,1},{1,2},{2,3},{3,4},{4,5},{5,6},{6,7},{7,8},{8,9},{9,10},{10,1... | collective-permute-start | bytes 368648 | tf_op jit(solution)/shard_map/ppermute | solution.py:26
  86.3 44.1 %collective-permute-start.2 = (f32[30720]{0:T(1024)}, f32[30720]{0:T(1024)}, u32[]{:S(2)}, u32[]{:S(2)}) collective-permute-start(f32[30720]{0:T(1024)} %reshape.166), channel_id=1, source_target_pairs={{1,0},{2,1},{3,2},{4,3},{5,4},{6,5},{7,6},{8,7},{9,8},{10,9},{11,1... | collective-permute-start | bytes 368648 | tf_op jit(solution)/shard_map/ppermute | solution.py:26
  93.8 21.9 %all-to-all-start.1 = ((f32[32,2,16]{2,1,0:T(2,128)}), f32[32,2,16]{2,1,0:T(2,128)S(1)}, u32[]{:S(2)}, u32[]{:S(2)}) async-start(f32[32,2,16]{2,1,0:T(2,128)} %broadcast_in_dim.32), calls=%async_computation.1 | async-start | bytes 65536 | tf_op jit(solution)/shard_map/all_to_all | solution.py:44
  116.6 30.8 %all-to-all-start.2 = ((f32[16,1,2080]{2,1,0:T(1,128)}), f32[16,1,2080]{2,1,0:T(1,128)}, u32[]{:S(2)}, u32[]{:S(2)}) async-start(f32[16,1,2080]{2,1,0:T(1,128)} %broadcast_in_dim.33), calls=%async_computation.2 | async-start | bytes 278528 | tf_op jit(solution)/shard_map/all_to_all | solution.py:44
  126.3 6.8 %copy-start.6 = (f32[16,6,320]{2,0,1:T(8,128)}, f32[16,6,320]{2,0,1:T(8,128)S(1)}, u32[]{:S(2)}) copy-start(f32[16,6,320]{2,0,1:T(8,128)S(1)} %copy.176) | copy-start | bytes 368644
  130.4 9.6 %copy-start.32 = (f32[16]{0:T(128)S(1)}, f32[16]{0:T(128)}, u32[]{:S(2)}) copy-start(f32[16]{0:T(128)} %get-tuple-element.46) | copy-start | bytes 196
  144.9 14.2 %copy-start.7 = (f32[16,6,320]{2,0,1:T(8,128)S(1)}, f32[16,6,320]{2,0,1:T(8,128)}, u32[]{:S(2)}) copy-start(f32[16,6,320]{2,0,1:T(8,128)} %copy-done.6) | copy-start | bytes 368644
  144.9 14.2 %copy-start.22 = (f32[16,256]{1,0:T(8,128)S(1)}, f32[16,256]{1,0:T(8,128)}, u32[]{:S(2)}) copy-start(f32[16,256]{1,0:T(8,128)} %param.12) | copy-start | bytes 49156
  (16 other events, 61.4 us)

commit v8 on v6

--- a/solution.py
+++ b/solution.py
@@ -9,7 +9,7 @@
 ITERS = 2
 
 
-HIGHEST_PRECISION = lax.Precision.HIGHEST
+MATMUL_PRECISION = lax.Precision.HIGH
 ROOT_THREE = math.sqrt(3.0)
 AMPLITUDE = 0.02
 
@@ -106,7 +106,7 @@
     )
 
     def covariance_local(direction):
-        coeffs = jnp.einsum("lpr,mlp->mlr", leaf_basis, direction, precision=HIGHEST_PRECISION)
+        coeffs = jnp.einsum("lpr,mlp->mlr", leaf_basis, direction, precision=MATMUL_PRECISION)
         joined = jnp.concatenate([direction, coeffs], axis=2)
         rim_joined = extended(joined, (("lon", 1),), REACH)
         rim_values = rim_joined[
@@ -120,23 +120,23 @@
             return values * offset_scale[None, :, step + near_depth, None]
 
         near_part = jnp.einsum(
-            "ipq,miq->mip", same_blocks, offset_values(0), precision=lax.Precision.HIGH
+            "ipq,miq->mip", same_blocks, offset_values(0), precision=MATMUL_PRECISION
         )
         for step in range(1, near_depth + 1):
             blocks = step_blocks[step - 1]
             ahead = blocks[step : step + local_leaves]
             behind = blocks[:local_leaves]
             near_part = near_part + jnp.einsum(
-                "ipq,miq->mip", ahead, offset_values(step), precision=lax.Precision.HIGH
+                "ipq,miq->mip", ahead, offset_values(step), precision=MATMUL_PRECISION
             )
             near_part = near_part + jnp.einsum(
-                "iqp,miq->mip", behind, offset_values(-step), precision=lax.Precision.HIGH
+                "iqp,miq->mip", behind, offset_values(-step), precision=MATMUL_PRECISION
             )
         leaf_far = jnp.einsum(
-            "lsab,mlsb->mla", leaf_couple, rim_coeffs[:, far_rows], precision=HIGHEST_PRECISION
-        )
-        upward = jnp.einsum("lab,mla->mlb", transfer, coeffs, precision=HIGHEST_PRECISION)
-        panel_coeffs = jnp.einsum("lk,mlb->mkb", membership, upward, precision=HIGHEST_PRECISION)
+            "lsab,mlsb->mla", leaf_couple, rim_coeffs[:, far_rows], precision=MATMUL_PRECISION
+        )
+        upward = jnp.einsum("lab,mla->mlb", transfer, coeffs, precision=MATMUL_PRECISION)
+        panel_coeffs = jnp.einsum("lk,mlb->mkb", membership, upward, precision=MATMUL_PRECISION)
         return direction, near_part, leaf_far, panel_coeffs
 
     def band_layout(band_panels, panel_coeffs):
@@ -151,13 +151,13 @@
             "ksab,mksb->mka",
             panel_couple,
             band_coeffs[:, gathered_rows],
-            precision=HIGHEST_PRECISION,
-        )
-        downward = jnp.einsum("lk,mkb->mlb", membership, panel_far, precision=HIGHEST_PRECISION)
+            precision=MATMUL_PRECISION,
+        )
+        downward = jnp.einsum("lk,mkb->mlb", membership, panel_far, precision=MATMUL_PRECISION)
         leaf_far = leaf_far + jnp.einsum(
-            "lab,mlb->mla", transfer, downward, precision=HIGHEST_PRECISION
-        )
-        far_part = jnp.einsum("lpr,mlr->mlp", leaf_basis, leaf_far, precision=HIGHEST_PRECISION)
+            "lab,mlb->mla", transfer, downward, precision=MATMUL_PRECISION
+        )
+        far_part = jnp.einsum("lpr,mlr->mlp", leaf_basis, leaf_far, precision=MATMUL_PRECISION)
         return noise_var[None] * direction + near_part + far_part
 
     def covariance_apply(direction):

time: 171 us -> 166 us (0.971)
  matrix products: 54.2 us -> 49.8 us
    dot_general x22, matrix products: 48 us -> 45.5 us  [the longest x4 11.7 us: covariance_local(): jnp.einsum('ipq,miq->mip', ahead, offset_values(step), precision=MATMUL_P...]
    dot_general x2, matrix products: 4.8 us -> 3.03 us  [covariance_local(): jnp.einsum('lsab,mlsb->mla', leaf_couple, rim_coeffs[:, far_rows], precis...]
  transfers between devices with their start and end apart: 9 -> 9, of which waited for: 1 -> 1; matrix products, arithmetic and copies ran while one was open for 31% -> 30% of each run, Pallas kernels for 0% -> 0%
where the time goes in v8:
time: 166 us; the launch traced here: 165 us
  matrix products  49.8 us (30%)
  starting transfers between devices  35.9 us (22%)
  blocking collectives  30.4 us (18%)
  local copies, waits for them, and re-layouts  21.3 us (13%)
  other arithmetic  15.7 us (9%)
  waiting for transfers between devices  10.2 us (6%)
    all_to_all x2, blocking collectives, gathered(): return lax.all_to_all(copies, axis, 0, 0, tiled=False)  30.4 us
    all_to_all x3, starting transfers between devices, gathered(): return lax.all_to_all(copies, axis, 0, 0, tiled=False)  23.8 us
    dot_general x4, matrix products, covariance_local(): jnp.einsum('ipq,miq->mip', ahead, offset_values(step), precision=MATMUL_P...  11.7 us
    dot_general x2, matrix products, covariance_local(): jnp.einsum('ipq,miq->mip', same_blocks, offset_values(0), precision=MATMU...  11.5 us
    ppermute x3, starting transfers between devices, extended(): lax.ppermute(head, axis, [((i + 1) % count, i) for i in range(count)])  10.4 us
    all_to_all x3, waiting for transfers between devices, gathered(): return lax.all_to_all(copies, axis, 0, 0, tiled=False)  10.2 us
    mul x2, other arithmetic, matern_shape(): return (1.0 + scaled) * jnp.exp(-scaled)  9.75 us
    dot_general x4, matrix products, covariance_local(): jnp.einsum('iqp,miq->mip', behind, offset_values(-step), precision=MATMUL...  9.56 us
  transfers between devices with their start and end apart: 9, of which 1 were waited for; matrix products, arithmetic and copies ran while one was open for 30% of the time, Pallas kernels for 0%

profile of v8, /device:TPU:1, one launch (start us, length us, event | category | flops | bytes accessed | tf_op | source)
XLA Modules:
  0.0 164.5 jit_solution(12767512542158903822)
XLA Ops:
  1.6 6.9 %collective-permute-start.2 = (f32[3,2,256]{2,1,0:T(2,128)S(1)}, f32[3,2,256]{2,1,0:T(2,128)S(1)}, u32[]{:S(2)}, u32[]{:S(2)}) collective-permute-start(f32[3,2,256]{2,1,0:T(2,128)S(1)} %get-tuple-element.42), channel_id=1, source_target_pairs={{1,0},{2,1},{3,2},{4,3},{5,4},{6,5},{7,6},{8,7},{9,8},{10,9},{11,1... | collective-permute-start | bytes 18440 | tf_op jit(solution)/shard_map/ppermute | solution.py:26
  9.6 1.9 %convolution_bitcast_fusion.9 = f32[16,16,64]{2,0,1:T(8,128)S(1)} fusion(f32[16,256,64]{1,2,0:T(8,128)} %param.14, f32[16,16,256]{2,1,0:T(8,128)} %param.11), kind=kOutput, calls=%fused_computation.70 | convolution fusion | flops 25165824 | bytes 1376256 | tf_op jit(solution)/shard_map/lpr,mlp->mlr/dot_general | solution.py:109
  12.3 3.6 %collective-permute-start = (f32[16,6,320]{2,0,1:T(8,128)}, f32[16,6,320]{2,0,1:T(8,128)}, u32[]{:S(2)}, u32[]{:S(2)}) collective-permute-start(f32[16,6,320]{2,0,1:T(8,128)} %get-tuple-element.24), channel_id=1, source_target_pairs={{1,0},{2,1},{3,2},{4,3},{5,4},{6,5},{7,6},{8,7},{9,8},{10,9},{11,1... | collective-permute-start | bytes 368648 | tf_op jit(solution)/shard_map/ppermute | solution.py:26
  15.8 1.4 convolution_bitcast_fusion.6
  18.8 6.8 %all-to-all-start = ((f32[16,1,2048]{2,1,0:T(1,128)}), f32[16,1,2048]{2,1,0:T(1,128)S(1)}, u32[]{:S(2)}, u32[]{:S(2)}) async-start(f32[16,1,2048]{2,1,0:T(1,128)} %broadcast_in_dim.30), calls=%async_computation | async-start | bytes 262144 | tf_op jit(solution)/shard_map/all_to_all | solution.py:36
  30.9 5.7 %fusion.17 = f32[16,16,256]{2,1,0:T(8,128)} fusion(f32[16,256]{1,0:T(8,128)S(1)} %get-tuple-element.39, f32[16,256]{1,0:T(8,128)S(1)} %get-tuple-element.40, f32[16,256]{1,0:T(8,128)S(1)} %get-tuple-element.38, f32[16]{0:T(128)S(1)} %get-tuple-element.47, f32[16,16,256]{2,1,0:T(8,128)S(1)} %copy-done.2), kind=kOutput, calls=%fused_computation.24 | convolution fusion | flops 113311744 | bytes 573504 | tf_op jit(solution)/shard_map/ipq,miq->mip/dot_general | solution.py:122
  37.3 5.2 %exponential_multiply_fusion = f32[18,256,256]{2,1,0:T(8,128)} fusion(f32[18,256]{1,0:T(8,128)S(1)} %get-tuple-element.30, f32[18,256]{1,0:T(8,128)S(1)} %get-tuple-element.36, f32[18,256]{1,0:T(8,128)S(1)} %get-tuple-element.31, f32[18,256]{1,0:T(8,128)S(1)} %get-tuple-element.37, f32[18,256]{1,0:T(8,128)S(1)} %get-tuple-element.29, ...), kind=kLoop, calls=%fused_computation.4 | loop fusion | flops 14155776 | bytes 4829184 | tf_op jit(solution)/shard_map/mul | solution.py:51
  42.5 4.6 %exponential_multiply_fusion.1 = f32[17,256,256]{2,1,0:T(8,128)} fusion(f32[17,256]{1,0:T(8,128)S(1)} %get-tuple-element.27, f32[17,256]{1,0:T(8,128)S(1)} %get-tuple-element.34, f32[17,256]{1,0:T(8,128)S(1)} %get-tuple-element.28, f32[17,256]{1,0:T(8,128)S(1)} %get-tuple-element.33, f32[17,256]{1,0:T(8,128)S(1)} %get-tuple-element.26, ...), kind=kLoop, calls=%fused_computation.5 | loop fusion | flops 13369344 | bytes 4560896 | tf_op jit(solution)/shard_map/mul | solution.py:51
  48.3 1.7 %copy.111 = f32[16,16,2,64]{3,0,2,1:T(8,128)} copy(f32[16,16,2,64]{3,2,0,1:T(2,128)} %bitcast.175) | data formatting | bytes 262144 | tf_op jit(solution)/shard_map/transpose | solution.py:144
  49.9 1.6 gather_fusion.1
  52.6 1.5 convolution_bitcast_fusion.5
  55.7 1.6 gather_fusion
  57.3 2.1 %convolution_bitcast_fusion.7 = f32[16,16,64]{2,1,0:T(8,128)S(1)} fusion(f32[16,16,4,64]{3,0,2,1:T(8,128)} %bitcast.174, f32[16,4,64,64]{3,2,1,0:T(8,128)S(1)} %copy-done), kind=kOutput, calls=%fused_computation.68 | convolution fusion | flops 25165824 | bytes 1376256 | tf_op jit(solution)/shard_map/lsab,mlsb->mla/dot_general | solution.py:135
  59.4 1.8 %fusion.75 = f32[16,16,64]{2,0,1:T(8,128)S(1)} fusion(f32[16,16,64]{2,1,0:T(8,128)S(1)} %convolution_bitcast_fusion.7, f32[16,64,64]{2,1,0:T(8,128)} %param.16, f32[16,16,64]{2,1,0:T(8,128)} %convolution_bitcast_fusion.5), kind=kOutput, calls=%fused_computation.65 | convolution fusion | flops 6307840 | bytes 458752 | tf_op jit(solution)/shard_map/lab,mlb->mla/dot_general | solution.py:157
  61.2 3.4 %fusion.2 = f32[16,16,256]{2,1,0:T(8,128)S(1)} fusion(f32[18,256,256]{2,1,0:T(8,128)} %exponential_multiply_fusion, f32[16,6,320]{2,0,1:T(8,128)} %copy-done.5, f32[16,16,64]{2,0,1:T(8,128)S(1)} %convolution_bitcast_fusion.9, f32[16,16,256]{2,0,1:T(8,128)S(1)} %copy.105, f32[16]{0:T(128)S(1)} %copy-done.27), kind=kOutput, calls=%fused_computation.9 | convolution fusion | flops 100859904 | bytes 4931648 | tf_op jit(solution)/shard_map/iqp,miq->mip/dot_general | solution.py:132
  64.7 2.5 %fusion.6 = f32[16,16,256]{2,1,0:T(8,128)S(1)} fusion(f32[18,256,256]{2,1,0:T(8,128)S(1)} %bitcast.172, f32[16,6,320]{2,0,1:T(8,128)} %collective-permute-done, f32[16,16,64]{2,0,1:T(8,128)S(1)} %convolution_bitcast_fusion.9, f32[16,16,256]{2,0,1:T(8,128)S(1)} %copy.105, f32[16]{0:T(128)S(1)} %copy-done.26), kind=kOutput, calls=%fused_computation.13 | convolution fusion | flops 100859904 | bytes 4973056 | tf_op jit(solution)/shard_map/ipq,miq->mip/dot_general | solution.py:129
  67.3 1.4 fusion.10
  68.8 2.7 %fusion.71 = f32[16,16,256]{2,0,1:T(8,128)S(1)} fusion(f32[16,16,256]{2,1,0:T(8,128)S(1)} %fusion.2, f32[16,16,256]{2,1,0:T(8,128)S(1)} %fusion.6, f32[16,16,256]{2,1,0:T(8,128)S(1)} %fusion.10, f32[16,16,256]{2,1,0:T(8,128)S(1)} %copy-done.12, f32[17,256,256]{2,1,0:T(8,128)S(1)} %bitcast.168, f32[16,6,320]{2,0,1:T(8,128)} %collective-permute-done, ...), kind=kOutput, calls=%fused_computation.58 | convolution fusion | flops 101253120 | bytes 6234176 | tf_op jit(solution)/shard_map/ipq,miq->mip/dot_general | solution.py:129
  73.8 5.8 %fusion.16 = f32[16,16,256]{2,1,0:T(8,128)} fusion(f32[16,256]{1,0:T(8,128)S(1)} %copy-done.20, f32[16,256]{1,0:T(8,128)S(1)} %copy-done.22, f32[16,256]{1,0:T(8,128)S(1)} %copy-done.18, f32[16,16,256]{2,0,1:T(8,128)S(1)} %get-tuple-element.49, f32[16]{0:T(128)S(1)} %copy-done.32), kind=kOutput, calls=%fused_computation.23 | convolution fusion | flops 113311744 | bytes 573504 | tf_op jit(solution)/shard_map/ipq,miq->mip/dot_general | solution.py:122
  80.2 10.1 %all-to-all-start.1 = ((f32[32,2,16]{2,1,0:T(2,128)}), f32[32,2,16]{2,1,0:T(2,128)S(1)}, u32[]{:S(2)}, u32[]{:S(2)}) async-start(f32[32,2,16]{2,1,0:T(2,128)} %broadcast_in_dim.32), calls=%async_computation.1 | async-start | bytes 65536 | tf_op jit(solution)/shard_map/all_to_all | solution.py:36
  90.3 1.6 collective-permute-start.5
  92.2 10.2 %all-to-all-done.1 = f32[32,2,16]{2,1,0:T(2,128)S(1)} async-done(((f32[32,2,16]{2,1,0:T(2,128)}), f32[32,2,16]{2,1,0:T(2,128)S(1)}, u32[]{:S(2)}, u32[]{:S(2)}) %all-to-all-start.1) | async-done | bytes 4128 | tf_op jit(solution)/shard_map/all_to_all | solution.py:36
  103.2 7.0 %all-to-all-start.2 = ((f32[16,1,2080]{2,1,0:T(1,128)}), f32[16,1,2080]{2,1,0:T(1,128)}, u32[]{:S(2)}, u32[]{:S(2)}) async-start(f32[16,1,2080]{2,1,0:T(1,128)} %broadcast_in_dim.33), calls=%async_computation.2 | async-start | bytes 278528 | tf_op jit(solution)/shard_map/all_to_all | solution.py:36
  110.9 1.4 gather_fusion.2
  112.4 3.5 %fusion = f32[16,16,256]{2,1,0:T(8,128)S(1)} fusion(f32[18,256,256]{2,1,0:T(8,128)} %exponential_multiply_fusion, f32[16,6,320]{2,0,1:T(8,128)} %copy-done.7, f32[16,16,64]{2,0,1:T(8,128)S(1)} %convolution_bitcast_fusion.8, f32[16,16,256]{2,0,1:T(8,128)S(1)} %get-tuple-element.49, f32[16]{0:T(128)} %get-tuple-element.44), kind=kOutput, calls=%fused_computation.7 | convolution fusion | flops 100859904 | bytes 4932096 | tf_op jit(solution)/shard_map/iqp,miq->mip/dot_general | solution.py:132
  115.9 4.0 %fusion.4 = f32[16,16,256]{2,1,0:T(8,128)S(1)} fusion(f32[18,256,256]{2,1,0:T(8,128)} %exponential_multiply_fusion, f32[16,6,320]{2,0,1:T(8,128)S(1)} %collective-permute-done.4, f32[16,16,64]{2,0,1:T(8,128)S(1)} %convolution_bitcast_fusion.8, f32[16,16,256]{2,0,1:T(8,128)S(1)} %get-tuple-element.49, f32[16]{0:T(128)} %get-tuple-element.45), kind=kOutput, calls=%fused_computation.11 | convolution fusion | flops 100859904 | bytes 4907520 | tf_op jit(solution)/shard_map/ipq,miq->mip/dot_general | solution.py:129
  121.2 2.5 %fusion.62 = f32[16,16,256]{2,0,1:T(8,128)} fusion(f32[16,16,256]{2,1,0:T(8,128)S(1)} %fusion, f32[16,16,256]{2,1,0:T(8,128)S(1)} %fusion.4, f32[16,16,256]{2,1,0:T(8,128)S(1)} %fusion.8, f32[16,16,256]{2,1,0:T(8,128)S(1)} %copy-done.13, f32[17,256,256]{2,1,0:T(8,128)S(1)} %bitcast.170, f32[16,6,320]{2,0,1:T(8,128)S(1)} %collective-permute-done.4, ...), kind=kOutput, calls=%fused_computation.55 | convolution fusion | flops 101253120 | bytes 6234176 | tf_op jit(solution)/shard_map/ipq,miq->mip/dot_general | solution.py:129
  126.5 1.6 gather_fusion.3
  128.6 1.6 fusion.74
  130.2 1.8 %multiply_reduce_fusion.3 = (f32[16]{0:T(128)S(1)}, f32[16]{0:T(128)S(1)}, f32[16]{0:T(128)S(1)}, f32[16]{0:T(128)S(1)}, f32[16,16,256]{2,0,1:T(8,128)S(1)}) fusion(f32[16,16,256]{2,0,1:T(8,128)S(1)} %get-tuple-element.49, f32[16]{0:T(128)S(1)} %slice_divide_fusion, f32[16,16,256]{2,1,0:T(8,128)S(1)} %copy-done.2, f32[16,16,256]{2,0,1:T(8,128)S(1)} %copy-done.9, ...), kind=kOutput, calls=%fused_computation.117 | convolution fusion | flops 26017728 | bytes 2163008 | tf_op jit(solution)/shard_map/lpr,mlr->mlp/dot_general | solution.py:160
  132.0 17.2 %all_to_all.30 = f32[32,4,16]{2,1,0:T(4,128)S(1)} all-to-all(f32[32,4,16]{2,1,0:T(4,128)S(1)} %broadcast_in_dim.34), channel_id=1, replica_groups=mesh['band'=16,'lon'=32] {'lon'}, dimensions={0} | all-to-all | bytes 16384 | tf_op jit(solution)/shard_map/all_to_all | solution.py:36
  149.3 13.2 %all_to_all.31 = f32[16,4,16]{2,1,0:T(4,128)S(1)} all-to-all(f32[16,4,16]{2,1,0:T(4,128)S(1)} %broadcast_in_dim.35), channel_id=1, replica_groups=mesh['band'=16,'lon'=32] {'band'}, dimensions={0} | all-to-all | bytes 8192 | tf_op jit(solution)/shard_map/all_to_all | solution.py:36
  (157 shorter events, 25.5 us)
Async XLA Ops:
  0.6 56.6 %copy-start = (f32[16,4,64,64]{3,2,1,0:T(8,128)S(1)}, f32[16,4,64,64]{3,2,1,0:T(8,128)}, u32[]{:S(2)}) copy-start(f32[16,4,64,64]{3,2,1,0:T(8,128)} %param.15) | copy-start | bytes 3145732
  0.6 27.9 %copy-start.2 = (f32[16,16,256]{2,1,0:T(8,128)S(1)}, f32[16,16,256]{2,1,0:T(8,128)}, u32[]{:S(2)}) copy-start(f32[16,16,256]{2,1,0:T(8,128)} %param.11) | copy-start | bytes 786436
  0.7 28.7 %copy-start.16 = (s32[16,5]{0,1:T(8,128)S(1)}, s32[16,5]{0,1:T(8,128)}, u32[]{:S(2)}) copy-start(s32[16,5]{0,1:T(8,128)} %param.18) | copy-start | bytes 964
  0.7 29.3 %copy-start.29 = (s32[16,4]{0,1:T(4,128)S(1)}, s32[16,4]{0,1:T(4,128)}, u32[]{:S(2)}) copy-start(s32[16,4]{0,1:T(4,128)} %param.19) | copy-start | bytes 772
  0.7 30.1 %copy-start.30 = (s32[2,2]{1,0:T(2,128)S(1)}, s32[2,2]{1,0:T(2,128)}, u32[]{:S(2)}) copy-start(s32[2,2]{1,0:T(2,128)} %param.20) | copy-start | bytes 52
  1.6 35.6 %collective-permute-start.2 = (f32[3,2,256]{2,1,0:T(2,128)S(1)}, f32[3,2,256]{2,1,0:T(2,128)S(1)}, u32[]{:S(2)}, u32[]{:S(2)}) collective-permute-start(f32[3,2,256]{2,1,0:T(2,128)S(1)} %get-tuple-element.42), channel_id=1, source_target_pairs={{1,0},{2,1},{3,2},{4,3},{5,4},{6,5},{7,6},{8,7},{9,8},{10,9},{11,1... | collective-permute-start | bytes 18440 | tf_op jit(solution)/shard_map/ppermute | solution.py:26
  8.5 28.8 %collective-permute-start.1 = (f32[3,2,256]{2,1,0:T(2,128)S(1)}, f32[3,2,256]{2,1,0:T(2,128)S(1)}, u32[]{:S(2)}, u32[]{:S(2)}) collective-permute-start(f32[3,2,256]{2,1,0:T(2,128)S(1)} %get-tuple-element.41), channel_id=1, source_target_pairs={{0,1},{1,2},{2,3},{3,4},{4,5},{5,6},{6,7},{7,8},{8,9},{9,10},{10,1... | collective-permute-start | bytes 18440 | tf_op jit(solution)/shard_map/ppermute | solution.py:24
  12.3 41.9 %collective-permute-start.3 = (f32[16,6,320]{2,0,1:T(8,128)}, f32[16,6,320]{2,0,1:T(8,128)S(1)}, u32[]{:S(2)}, u32[]{:S(2)}) collective-permute-start(f32[16,6,320]{2,0,1:T(8,128)} %get-tuple-element.25), channel_id=1, source_target_pairs={{0,1},{1,2},{2,3},{3,4},{4,5},{5,6},{6,7},{7,8},{8,9},{9,10},{10,1... | collective-permute-start | bytes 368648 | tf_op jit(solution)/shard_map/ppermute | solution.py:24
  12.3 42.6 %collective-permute-start = (f32[16,6,320]{2,0,1:T(8,128)}, f32[16,6,320]{2,0,1:T(8,128)}, u32[]{:S(2)}, u32[]{:S(2)}) collective-permute-start(f32[16,6,320]{2,0,1:T(8,128)} %get-tuple-element.24), channel_id=1, source_target_pairs={{1,0},{2,1},{3,2},{4,3},{5,4},{6,5},{7,6},{8,7},{9,8},{10,9},{11,1... | collective-permute-start | bytes 368648 | tf_op jit(solution)/shard_map/ppermute | solution.py:26
  18.8 28.2 %all-to-all-start = ((f32[16,1,2048]{2,1,0:T(1,128)}), f32[16,1,2048]{2,1,0:T(1,128)S(1)}, u32[]{:S(2)}, u32[]{:S(2)}) async-start(f32[16,1,2048]{2,1,0:T(1,128)} %broadcast_in_dim.30), calls=%async_computation | async-start | bytes 262144 | tf_op jit(solution)/shard_map/all_to_all | solution.py:36
  28.6 8.0 %copy-start.17 = (f32[16,256]{1,0:T(8,128)}, f32[16,256]{1,0:T(8,128)S(1)}, u32[]{:S(2)}) copy-start(f32[16,256]{1,0:T(8,128)S(1)} %get-tuple-element.38) | copy-start | bytes 49156
  28.6 8.0 %copy-start.19 = (f32[16,256]{1,0:T(8,128)}, f32[16,256]{1,0:T(8,128)S(1)}, u32[]{:S(2)}) copy-start(f32[16,256]{1,0:T(8,128)S(1)} %get-tuple-element.39) | copy-start | bytes 49156
  28.6 8.0 %copy-start.21 = (f32[16,256]{1,0:T(8,128)}, f32[16,256]{1,0:T(8,128)S(1)}, u32[]{:S(2)}) copy-start(f32[16,256]{1,0:T(8,128)S(1)} %get-tuple-element.40) | copy-start | bytes 49156
  30.0 6.6 %copy-start.31 = (f32[16]{0:T(128)}, f32[16]{0:T(128)S(1)}, u32[]{:S(2)}) copy-start(f32[16]{0:T(128)S(1)} %get-tuple-element.47) | copy-start | bytes 196
  30.9 6.4 %copy-start.10 = (f32[3,16,256]{2,1,0:T(8,128)S(1)}, f32[3,16,256]{2,1,0:T(8,128)}, u32[]{:S(2)}) copy-start(f32[3,16,256]{2,1,0:T(8,128)} %param.13) | copy-start | bytes 147460
  47.4 17.3 %slice-start.4 = ((s8[4718592]{0:T(1024)(128)(4,1)}), s8[524288]{0:T(1024)(128)(4,1)S(1)}, s32[]{:S(2)}) async-start(s8[4718592]{0:T(1024)(128)(4,1)} %bitcast.171), calls=%async_computation.9 | async-start | bytes 1048576
  48.3 12.9 %copy-start.27 = (f32[16]{0:T(128)S(1)}, f32[16]{0:T(128)}, u32[]{:S(2)}) copy-start(f32[16]{0:T(128)} %get-tuple-element.44) | copy-start | bytes 196
  57.3 7.4 %slice-start.5 = ((s8[4718592]{0:T(1024)(128)(4,1)}), s8[4194304]{0:T(1024)(128)(4,1)S(1)}, s32[]{:S(2)}) async-start(s8[4718592]{0:T(1024)(128)(4,1)} %bitcast.171), calls=%async_computation.10 | async-start | bytes 8388608
  57.3 7.4 %copy-start.26 = (f32[16]{0:T(128)S(1)}, f32[16]{0:T(128)}, u32[]{:S(2)}) copy-start(f32[16]{0:T(128)} %get-tuple-element.45) | copy-start | bytes 196
  59.4 7.9 %slice-start = ((s8[4456448]{0:T(1024)(128)(4,1)}), s8[4194304]{0:T(1024)(128)(4,1)S(1)}, s32[]{:S(2)}) async-start(s8[4456448]{0:T(1024)(128)(4,1)} %bitcast.167), calls=%async_computation.5 | async-start | bytes 8388608
  61.2 6.1 %slice-start.1 = ((s8[4456448]{0:T(1024)(128)(4,1)}), s8[262144]{0:T(1024)(128)(4,1)S(1)}, s32[]{:S(2)}) async-start(s8[4456448]{0:T(1024)(128)(4,1)} %bitcast.167), calls=%async_computation.6 | async-start | bytes 524288
  61.2 6.1 %copy-start.6 = (f32[16,6,320]{2,0,1:T(8,128)S(1)}, f32[16,6,320]{2,0,1:T(8,128)}, u32[]{:S(2)}) copy-start(f32[16,6,320]{2,0,1:T(8,128)} %copy-done.5) | copy-start | bytes 368644
  73.7 18.2 %copy-start.23 = (s32[16]{0:T(128)S(1)}, s32[16]{0:T(128)}, u32[]{:S(2)}) copy-start(s32[16]{0:T(128)} %param.21) | copy-start | bytes 196
  73.7 37.2 %copy-start.14 = (s32[1024]{0:T(1024)S(1)}, s32[1024]{0:T(1024)}, u32[]{:S(2)}) copy-start(s32[1024]{0:T(1024)} %pad_clamp_fusion.1) | copy-start | bytes 12292
  80.2 22.2 %all-to-all-start.1 = ((f32[32,2,16]{2,1,0:T(2,128)}), f32[32,2,16]{2,1,0:T(2,128)S(1)}, u32[]{:S(2)}, u32[]{:S(2)}) async-start(f32[32,2,16]{2,1,0:T(2,128)} %broadcast_in_dim.32), calls=%async_computation.1 | async-start | bytes 65536 | tf_op jit(solution)/shard_map/all_to_all | solution.py:36
  90.3 20.0 %collective-permute-start.5 = (f32[16,6,320]{2,0,1:T(8,128)}, f32[16,6,320]{2,0,1:T(8,128)S(1)}, u32[]{:S(2)}, u32[]{:S(2)}) collective-permute-start(f32[16,6,320]{2,0,1:T(8,128)} %get-tuple-element.23), channel_id=1, source_target_pairs={{0,1},{1,2},{2,3},{3,4},{4,5},{5,6},{6,7},{7,8},{8,9},{9,10},{10,1... | collective-permute-start | bytes 368648 | tf_op jit(solution)/shard_map/ppermute | solution.py:24
  91.9 18.3 %collective-permute-start.4 = (f32[16,6,320]{2,0,1:T(8,128)S(1)}, f32[16,6,320]{2,0,1:T(8,128)S(1)}, u32[]{:S(2)}, u32[]{:S(2)}) collective-permute-start(f32[16,6,320]{2,0,1:T(8,128)S(1)} %get-tuple-element.22), channel_id=1, source_target_pairs={{1,0},{2,1},{3,2},{4,3},{5,4},{6,5},{7,6},{8,7},{9,8},{10,9},{11,1... | collective-permute-start | bytes 368648 | tf_op jit(solution)/shard_map/ppermute | solution.py:26
  103.2 21.3 %all-to-all-start.2 = ((f32[16,1,2080]{2,1,0:T(1,128)}), f32[16,1,2080]{2,1,0:T(1,128)}, u32[]{:S(2)}, u32[]{:S(2)}) async-start(f32[16,1,2080]{2,1,0:T(1,128)} %broadcast_in_dim.33), calls=%async_computation.2 | async-start | bytes 278528 | tf_op jit(solution)/shard_map/all_to_all | solution.py:36
  110.9 9.0 %slice-start.2 = ((s8[4456448]{0:T(1024)(128)(4,1)}), s8[262144]{0:T(1024)(128)(4,1)S(1)}, s32[]{:S(2)}) async-start(s8[4456448]{0:T(1024)(128)(4,1)} %bitcast.169), calls=%async_computation.7 | async-start | bytes 524288
  112.4 7.5 %slice-start.3 = ((s8[4456448]{0:T(1024)(128)(4,1)}), s8[4194304]{0:T(1024)(128)(4,1)S(1)}, s32[]{:S(2)}) async-start(s8[4456448]{0:T(1024)(128)(4,1)} %bitcast.169), calls=%async_computation.8 | async-start | bytes 8388608
  112.4 7.6 %copy-start.8 = (f32[16,6,320]{2,0,1:T(8,128)S(1)}, f32[16,6,320]{2,0,1:T(8,128)}, u32[]{:S(2)}) copy-start(f32[16,6,320]{2,0,1:T(8,128)} %copy-done.7) | copy-start | bytes 368644
  123.6 6.5 %copy-start.9 = (f32[16,16,256]{2,0,1:T(8,128)S(1)}, f32[16,16,256]{2,0,1:T(8,128)}, u32[]{:S(2)}) copy-start(f32[16,16,256]{2,0,1:T(8,128)} %fusion.62) | copy-start | bytes 786436
  (16 other events, 64.2 us)

commit v9 on v8

--- a/solution.py
+++ b/solution.py
@@ -163,6 +163,7 @@
     def covariance_apply(direction):
         local = covariance_local(direction)
         panel_coeffs = local[3]
+        _, panel_coeffs = lax.optimization_barrier(((same_blocks, step_blocks), panel_coeffs))
         band_panels = gathered(panel_coeffs.reshape(-1), "band")
         return covariance_finish(local, band_layout(band_panels, panel_coeffs))
 

time: 166 us -> 173 us (1.042)
  matrix products: 49.8 us -> 54.6 us
  other arithmetic: 15.7 us -> 19.6 us
    unnamed x83 -> x75, local copies, waits for them, and re-layouts: 6.06 us -> 5.42 us
  transfers between devices with their start and end apart: 9 -> 9, of which waited for: 1 -> 1; matrix products, arithmetic and copies ran while one was open for 30% -> 37% of each run, Pallas kernels for 0% -> 0%
where the time goes in v9:
time: 173 us; the launch traced here: 171 us
  matrix products  54.6 us (32%)
  starting transfers between devices  35.9 us (21%)
  blocking collectives  30.4 us (18%)
  local copies, waits for them, and re-layouts  19.8 us (11%)
  other arithmetic  19.6 us (11%)
  waiting for transfers between devices  9.43 us (5%)
    all_to_all x2, blocking collectives, gathered(): return lax.all_to_all(copies, axis, 0, 0, tiled=False)  30.4 us
    all_to_all x3, starting transfers between devices, gathered(): return lax.all_to_all(copies, axis, 0, 0, tiled=False)  23.8 us
    dot_general x2, matrix products, covariance_local(): jnp.einsum('ipq,miq->mip', same_blocks, offset_values(0), precision=MATMU...  12.8 us
    dot_general x4, matrix products, covariance_local(): jnp.einsum('ipq,miq->mip', ahead, offset_values(step), precision=MATMUL_P...  10.8 us
    ppermute x3, starting transfers between devices, extended(): lax.ppermute(head, axis, [((i + 1) % count, i) for i in range(count)])  10.4 us
    dot_general x4, matrix products, covariance_local(): jnp.einsum('iqp,miq->mip', behind, offset_values(-step), precision=MATMUL...  10.2 us
    mul x2, other arithmetic, matern_shape(): return (1.0 + scaled) * jnp.exp(-scaled)  9.79 us
    all_to_all x3, waiting for transfers between devices, gathered(): return lax.all_to_all(copies, axis, 0, 0, tiled=False)  9.42 us
  transfers between devices with their start and end apart: 9, of which 1 were waited for; matrix products, arithmetic and copies ran while one was open for 37% of the time, Pallas kernels for 0%

profile of v9, /device:TPU:1, one launch (start us, length us, event | category | flops | bytes accessed | tf_op | source)
XLA Modules:
  0.0 170.9 jit_solution(11259443047890669984)
XLA Ops:
  1.6 6.9 %collective-permute-start.2 = (f32[3,2,256]{2,1,0:T(2,128)S(1)}, f32[3,2,256]{2,1,0:T(2,128)S(1)}, u32[]{:S(2)}, u32[]{:S(2)}) collective-permute-start(f32[3,2,256]{2,1,0:T(2,128)S(1)} %get-tuple-element.44), channel_id=1, source_target_pairs={{1,0},{2,1},{3,2},{4,3},{5,4},{6,5},{7,6},{8,7},{9,8},{10,9},{11,1... | collective-permute-start | bytes 18440 | tf_op jit(solution)/shard_map/ppermute | solution.py:26
  9.5 1.9 %convolution_bitcast_fusion.9 = f32[16,16,64]{2,0,1:T(8,128)S(1)} fusion(f32[16,256,64]{1,2,0:T(8,128)} %param.14, f32[16,16,256]{2,1,0:T(8,128)} %param.11), kind=kOutput, calls=%fused_computation.54 | convolution fusion | flops 25165824 | bytes 1376256 | tf_op jit(solution)/shard_map/lpr,mlp->mlr/dot_general | solution.py:109
  12.2 3.6 %collective-permute-start = (f32[16,6,320]{2,0,1:T(8,128)S(1)}, f32[16,6,320]{2,0,1:T(8,128)S(1)}, u32[]{:S(2)}, u32[]{:S(2)}) collective-permute-start(f32[16,6,320]{2,0,1:T(8,128)S(1)} %get-tuple-element.26), channel_id=1, source_target_pairs={{1,0},{2,1},{3,2},{4,3},{5,4},{6,5},{7,6},{8,7},{9,8},{10,9},{11,1... | collective-permute-start | bytes 368648 | tf_op jit(solution)/shard_map/ppermute | solution.py:26
  18.7 1.7 multiply_reduce_fusion.5
  25.6 6.2 %fusion.17 = f32[16,16,256]{2,1,0:T(8,128)} fusion(f32[16,256]{1,0:T(8,128)S(1)} %get-tuple-element.41, f32[16,256]{1,0:T(8,128)S(1)} %get-tuple-element.42, f32[16,256]{1,0:T(8,128)S(1)} %get-tuple-element.40, f32[16]{0:T(128)S(1)} %get-tuple-element.49, f32[16,16,256]{2,1,0:T(8,128)} %param.11), kind=kOutput, calls=%fused_computation.24 | convolution fusion | flops 113311744 | bytes 573504 | tf_op jit(solution)/shard_map/ipq,miq->mip/dot_general | solution.py:122
  32.4 5.2 %exponential_multiply_fusion = f32[18,256,256]{2,1,0:T(8,128)} fusion(f32[18,256]{1,0:T(8,128)S(1)} %get-tuple-element.32, f32[18,256]{1,0:T(8,128)S(1)} %get-tuple-element.38, f32[18,256]{1,0:T(8,128)S(1)} %get-tuple-element.33, f32[18,256]{1,0:T(8,128)S(1)} %get-tuple-element.39, f32[18,256]{1,0:T(8,128)S(1)} %get-tuple-element.31, ...), kind=kLoop, calls=%fused_computation.4 | loop fusion | flops 14155776 | bytes 4829184 | tf_op jit(solution)/shard_map/mul | solution.py:51
  37.6 4.6 %exponential_multiply_fusion.1 = f32[17,256,256]{2,1,0:T(8,128)} fusion(f32[17,256]{1,0:T(8,128)S(1)} %get-tuple-element.29, f32[17,256]{1,0:T(8,128)S(1)} %get-tuple-element.36, f32[17,256]{1,0:T(8,128)S(1)} %get-tuple-element.30, f32[17,256]{1,0:T(8,128)S(1)} %get-tuple-element.35, f32[17,256]{1,0:T(8,128)S(1)} %get-tuple-element.28, ...), kind=kLoop, calls=%fused_computation.5 | loop fusion | flops 13369344 | bytes 4560896 | tf_op jit(solution)/shard_map/mul | solution.py:51
  43.0 6.8 %all-to-all-start = ((f32[16,1,2048]{2,1,0:T(1,128)}), f32[16,1,2048]{2,1,0:T(1,128)}, u32[]{:S(2)}, u32[]{:S(2)}) async-start(f32[16,1,2048]{2,1,0:T(1,128)} %broadcast_in_dim.30), calls=%async_computation | async-start | bytes 262144 | tf_op jit(solution)/shard_map/all_to_all | solution.py:36
  49.9 1.4 gather_fusion
  51.4 3.5 %fusion.2 = f32[16,16,256]{2,1,0:T(8,128)S(1)} fusion(f32[18,256,256]{2,1,0:T(8,128)} %exponential_multiply_fusion, f32[16,6,320]{2,0,1:T(8,128)S(1)} %collective-permute-done.3, f32[16,16,64]{2,0,1:T(8,128)S(1)} %convolution_bitcast_fusion.9, f32[16,16,256]{2,0,1:T(8,128)S(1)} %copy.105, f32[16]{0:T(128)S(1)} %get-tuple-element.46), kind=kOutput, calls=%fused_computation.9 | convolution fusion | flops 100859904 | bytes 4907072 | tf_op jit(solution)/shard_map/iqp,miq->mip/dot_general | solution.py:132
  55.0 1.9 %fusion.6 = f32[16,16,256]{2,1,0:T(8,128)S(1)} fusion(f32[18,256,256]{2,1,0:T(8,128)S(1)} %copy-done.1, f32[16,6,320]{2,0,1:T(8,128)S(1)} %collective-permute-done, f32[16,16,64]{2,0,1:T(8,128)S(1)} %convolution_bitcast_fusion.9, f32[16,16,256]{2,0,1:T(8,128)S(1)} %copy.105, f32[16]{0:T(128)S(1)} %get-tuple-element.47), kind=kOutput, calls=%fused_computation.13 | convolution fusion | flops 100859904 | bytes 4997632 | tf_op jit(solution)/shard_map/ipq,miq->mip/dot_general | solution.py:129
  58.1 2.5 %fusion.55 = f32[16,16,256]{2,0,1:T(8,128)} fusion(f32[16,16,256]{2,1,0:T(8,128)S(1)} %fusion.2, f32[16,16,256]{2,1,0:T(8,128)S(1)} %fusion.6, f32[16,16,256]{2,1,0:T(8,128)S(1)} %fusion.10, f32[16,16,256]{2,1,0:T(8,128)S(1)} %copy-done.10, f32[17,256,256]{2,1,0:T(8,128)S(1)} %bitcast.168, f32[16,6,320]{2,0,1:T(8,128)S(1)} %collective-permute-done, ...), kind=kOutput, calls=%fused_computation.42 | convolution fusion | flops 101253120 | bytes 6234176 | tf_op jit(solution)/shard_map/ipq,miq->mip/dot_general | solution.py:129
  60.6 1.6 convolution_bitcast_fusion.7
  64.4 1.6 gather_fusion.1
  69.4 1.8 %multiply_reduce_fusion.4 = (f32[16]{0:T(128)S(1)}, f32[16,16,256]{2,0,1:T(8,128)S(1)}) fusion(f32[16,16,256]{2,1,0:T(8,128)S(1)} %copy-done.2, f32[16,16,256]{2,0,1:T(8,128)S(1)} %copy-done.8, f32[16,16,64]{2,0,1:T(8,128)S(1)} %fusion.59, f32[16,256,64]{1,2,0:T(8,128)} %param.14), kind=kOutput, calls=%fused_computation.103 | convolution fusion | flops 25362416 | bytes 1900608 | tf_op jit(solution)/shard_map/lpr,mlr->mlp/dot_general | solution.py:160
  71.2 1.7 %convolution_bitcast_fusion.8 = f32[16,16,64]{2,0,1:T(8,128)S(1)} fusion(f32[16,16,256]{2,0,1:T(8,128)S(1)} %get-tuple-element.51, f32[16,256,64]{1,2,0:T(8,128)} %param.14), kind=kOutput, calls=%fused_computation.53 | convolution fusion | flops 25165824 | bytes 1376256 | tf_op jit(solution)/shard_map/lpr,mlp->mlr/dot_general | solution.py:109
  74.7 6.6 %fusion.16 = f32[16,16,256]{2,1,0:T(8,128)} fusion(f32[16,256]{1,0:T(8,128)} %copy-done.17, f32[16,256]{1,0:T(8,128)} %copy-done.18, f32[16,256]{1,0:T(8,128)} %copy-done.16, f32[16,16,256]{2,0,1:T(8,128)S(1)} %get-tuple-element.51, f32[16]{0:T(128)S(1)} %copy-done.30), kind=kOutput, calls=%fused_computation.23 | convolution fusion | flops 113311744 | bytes 573504 | tf_op jit(solution)/shard_map/ipq,miq->mip/dot_general | solution.py:122
  81.9 10.0 %all-to-all-start.1 = ((f32[32,2,16]{2,1,0:T(2,128)}), f32[32,2,16]{2,1,0:T(2,128)S(1)}, u32[]{:S(2)}, u32[]{:S(2)}) async-start(f32[32,2,16]{2,1,0:T(2,128)} %broadcast_in_dim.32), calls=%async_computation.1 | async-start | bytes 65536 | tf_op jit(solution)/shard_map/all_to_all | solution.py:36
  92.0 1.6 collective-permute-start.5
  94.8 9.4 %all-to-all-done.1 = f32[32,2,16]{2,1,0:T(2,128)S(1)} async-done(((f32[32,2,16]{2,1,0:T(2,128)}), f32[32,2,16]{2,1,0:T(2,128)S(1)}, u32[]{:S(2)}, u32[]{:S(2)}) %all-to-all-start.1) | async-done | bytes 4128 | tf_op jit(solution)/shard_map/all_to_all | solution.py:36
  105.1 6.9 %all-to-all-start.2 = ((f32[16,1,2080]{2,1,0:T(1,128)}), f32[16,1,2080]{2,1,0:T(1,128)}, u32[]{:S(2)}, u32[]{:S(2)}) async-start(f32[16,1,2080]{2,1,0:T(1,128)} %broadcast_in_dim.33), calls=%async_computation.2 | async-start | bytes 278528 | tf_op jit(solution)/shard_map/all_to_all | solution.py:36
  112.7 1.5 pad_maximum_fusion.12
  114.2 2.4 %gather_fusion.2 = f32[64,16,64]{2,1,0:T(8,128)} fusion(f32[16,28,64]{2,0,1:T(8,128)} %pad_maximum_fusion.12, s32[1024]{0:T(1024)S(1)} %copy-done.13), kind=kCustom, calls=%fused_computation.2 | custom fusion | bytes 524544 | tf_op jit(solution)/shard_map/gather | solution.py:136
  116.6 3.5 %fusion = f32[16,16,256]{2,1,0:T(8,128)S(1)} fusion(f32[18,256,256]{2,1,0:T(8,128)} %exponential_multiply_fusion, f32[16,6,320]{2,0,1:T(8,128)} %collective-permute-done.5, f32[16,16,64]{2,0,1:T(8,128)S(1)} %convolution_bitcast_fusion.8, f32[16,16,256]{2,0,1:T(8,128)S(1)} %get-tuple-element.51, f32[16]{0:T(128)S(1)} %copy-done.27), kind=kOutput, calls=%fused_computation.7 | convolution fusion | flops 100859904 | bytes 4931648 | tf_op jit(solution)/shard_map/iqp,miq->mip/dot_general | solution.py:132
  120.2 4.0 %fusion.4 = f32[16,16,256]{2,1,0:T(8,128)S(1)} fusion(f32[18,256,256]{2,1,0:T(8,128)} %exponential_multiply_fusion, f32[16,6,320]{2,0,1:T(8,128)S(1)} %copy-done.7, f32[16,16,64]{2,0,1:T(8,128)S(1)} %convolution_bitcast_fusion.8, f32[16,16,256]{2,0,1:T(8,128)S(1)} %get-tuple-element.51, f32[16]{0:T(128)S(1)} %copy-done.25), kind=kOutput, calls=%fused_computation.11 | convolution fusion | flops 100859904 | bytes 4907072 | tf_op jit(solution)/shard_map/ipq,miq->mip/dot_general | solution.py:129
  124.2 1.9 %fusion.8 = f32[16,16,256]{2,1,0:T(8,128)S(1)} fusion(f32[17,256,256]{2,1,0:T(8,128)S(1)} %bitcast.170, f32[16,6,320]{2,0,1:T(8,128)} %collective-permute-done.5, f32[16,16,64]{2,0,1:T(8,128)S(1)} %convolution_bitcast_fusion.8, f32[16,16,256]{2,0,1:T(8,128)S(1)} %get-tuple-element.51, f32[16]{0:T(128)S(1)} %copy-done.23), kind=kOutput, calls=%fused_computation.15 | convolution fusion | flops 100859904 | bytes 4973056 | tf_op jit(solution)/shard_map/iqp,miq->mip/dot_general | solution.py:132
  126.1 2.5 %fusion.46 = f32[16,16,256]{2,0,1:T(8,128)} fusion(f32[16,16,256]{2,1,0:T(8,128)S(1)} %fusion, f32[16,16,256]{2,1,0:T(8,128)S(1)} %fusion.4, f32[16,16,256]{2,1,0:T(8,128)S(1)} %fusion.8, f32[16,16,256]{2,1,0:T(8,128)S(1)} %copy-done.11, f32[17,256,256]{2,1,0:T(8,128)S(1)} %bitcast.170, f32[16,6,320]{2,0,1:T(8,128)S(1)} %copy-done.7, ...), kind=kOutput, calls=%fused_computation.39 | convolution fusion | flops 101253120 | bytes 6234176 | tf_op jit(solution)/shard_map/ipq,miq->mip/dot_general | solution.py:129
  128.6 1.6 convolution_bitcast_fusion.3
  132.1 1.6 gather_fusion.3
  136.5 1.9 %multiply_reduce_fusion.3 = (f32[16]{0:T(128)S(1)}, f32[16]{0:T(128)S(1)}, f32[16]{0:T(128)S(1)}, f32[16]{0:T(128)S(1)}, f32[16,16,256]{2,0,1:T(8,128)S(1)}) fusion(f32[16,16,256]{2,0,1:T(8,128)S(1)} %get-tuple-element.51, f32[16]{0:T(128)S(1)} %slice_divide_fusion, f32[16,16,256]{2,1,0:T(8,128)S(1)} %copy-done.2, f32[16,16,256]{2,0,1:T(8,128)} %fusion.46, ...), kind=kOutput, calls=%fused_computation.101 | convolution fusion | flops 26017728 | bytes 2163008 | tf_op jit(solution)/shard_map/lpr,mlr->mlp/dot_general | solution.py:160
  138.5 17.2 %all_to_all.30 = f32[32,4,16]{2,1,0:T(4,128)S(1)} all-to-all(f32[32,4,16]{2,1,0:T(4,128)S(1)} %broadcast_in_dim.34), channel_id=1, replica_groups=mesh['band'=16,'lon'=32] {'lon'}, dimensions={0} | all-to-all | bytes 16384 | tf_op jit(solution)/shard_map/all_to_all | solution.py:36
  155.7 13.1 %all_to_all.31 = f32[16,4,16]{2,1,0:T(4,128)S(1)} all-to-all(f32[16,4,16]{2,1,0:T(4,128)S(1)} %broadcast_in_dim.35), channel_id=1, replica_groups=mesh['band'=16,'lon'=32] {'band'}, dimensions={0} | all-to-all | bytes 8192 | tf_op jit(solution)/shard_map/all_to_all | solution.py:36
  (148 shorter events, 31.1 us)
Async XLA Ops:
  0.6 60.0 %copy-start = (f32[16,4,64,64]{3,2,1,0:T(8,128)S(1)}, f32[16,4,64,64]{3,2,1,0:T(8,128)}, u32[]{:S(2)}) copy-start(f32[16,4,64,64]{3,2,1,0:T(8,128)} %param.15) | copy-start | bytes 3145732
  1.6 30.8 %collective-permute-start.2 = (f32[3,2,256]{2,1,0:T(2,128)S(1)}, f32[3,2,256]{2,1,0:T(2,128)S(1)}, u32[]{:S(2)}, u32[]{:S(2)}) collective-permute-start(f32[3,2,256]{2,1,0:T(2,128)S(1)} %get-tuple-element.44), channel_id=1, source_target_pairs={{1,0},{2,1},{3,2},{4,3},{5,4},{6,5},{7,6},{8,7},{9,8},{10,9},{11,1... | collective-permute-start | bytes 18440 | tf_op jit(solution)/shard_map/ppermute | solution.py:26
  8.4 23.9 %collective-permute-start.1 = (f32[3,2,256]{2,1,0:T(2,128)S(1)}, f32[3,2,256]{2,1,0:T(2,128)S(1)}, u32[]{:S(2)}, u32[]{:S(2)}) collective-permute-start(f32[3,2,256]{2,1,0:T(2,128)S(1)} %get-tuple-element.43), channel_id=1, source_target_pairs={{0,1},{1,2},{2,3},{3,4},{4,5},{5,6},{6,7},{7,8},{8,9},{9,10},{10,1... | collective-permute-start | bytes 18440 | tf_op jit(solution)/shard_map/ppermute | solution.py:24
  12.2 37.7 %collective-permute-start.3 = (f32[16,6,320]{2,0,1:T(8,128)}, f32[16,6,320]{2,0,1:T(8,128)S(1)}, u32[]{:S(2)}, u32[]{:S(2)}) collective-permute-start(f32[16,6,320]{2,0,1:T(8,128)} %get-tuple-element.27), channel_id=1, source_target_pairs={{0,1},{1,2},{2,3},{3,4},{4,5},{5,6},{6,7},{7,8},{8,9},{9,10},{10,1... | collective-permute-start | bytes 368648 | tf_op jit(solution)/shard_map/ppermute | solution.py:24
  12.2 37.7 %collective-permute-start = (f32[16,6,320]{2,0,1:T(8,128)S(1)}, f32[16,6,320]{2,0,1:T(8,128)S(1)}, u32[]{:S(2)}, u32[]{:S(2)}) collective-permute-start(f32[16,6,320]{2,0,1:T(8,128)S(1)} %get-tuple-element.26), channel_id=1, source_target_pairs={{1,0},{2,1},{3,2},{4,3},{5,4},{6,5},{7,6},{8,7},{9,8},{10,9},{11,1... | collective-permute-start | bytes 368648 | tf_op jit(solution)/shard_map/ppermute | solution.py:26
  18.7 13.1 %copy-start.16 = (f32[16,256]{1,0:T(8,128)}, f32[16,256]{1,0:T(8,128)S(1)}, u32[]{:S(2)}) copy-start(f32[16,256]{1,0:T(8,128)S(1)} %get-tuple-element.40) | copy-start | bytes 49156
  18.7 13.1 %copy-start.17 = (f32[16,256]{1,0:T(8,128)}, f32[16,256]{1,0:T(8,128)S(1)}, u32[]{:S(2)}) copy-start(f32[16,256]{1,0:T(8,128)S(1)} %get-tuple-element.41) | copy-start | bytes 49156
  18.7 13.1 %copy-start.18 = (f32[16,256]{1,0:T(8,128)}, f32[16,256]{1,0:T(8,128)S(1)}, u32[]{:S(2)}) copy-start(f32[16,256]{1,0:T(8,128)S(1)} %get-tuple-element.42) | copy-start | bytes 49156
  21.6 10.1 %copy-start.29 = (f32[16]{0:T(128)}, f32[16]{0:T(128)S(1)}, u32[]{:S(2)}) copy-start(f32[16]{0:T(128)S(1)} %get-tuple-element.49) | copy-start | bytes 196
  21.6 29.7 %copy-start.26 = (f32[16]{0:T(128)}, f32[16]{0:T(128)S(1)}, u32[]{:S(2)}) copy-start(f32[16]{0:T(128)S(1)} %get-tuple-element.46) | copy-start | bytes 196
  21.6 33.2 %copy-start.24 = (f32[16]{0:T(128)}, f32[16]{0:T(128)S(1)}, u32[]{:S(2)}) copy-start(f32[16]{0:T(128)S(1)} %get-tuple-element.47) | copy-start | bytes 196
  21.6 35.2 %copy-start.22 = (f32[16]{0:T(128)}, f32[16]{0:T(128)S(1)}, u32[]{:S(2)}) copy-start(f32[16]{0:T(128)S(1)} %get-tuple-element.48) | copy-start | bytes 196
  22.5 27.4 %copy-start.12 = (s32[1024]{0:T(1024)}, s32[1024]{0:T(1024)S(1)}, u32[]{:S(2)}) copy-start(s32[1024]{0:T(1024)S(1)} %pad_clamp_fusion.1) | copy-start | bytes 12292
  25.5 6.8 %copy-start.9 = (f32[3,16,256]{2,1,0:T(8,128)S(1)}, f32[3,16,256]{2,1,0:T(8,128)}, u32[]{:S(2)}) copy-start(f32[3,16,256]{2,1,0:T(8,128)} %param.13) | copy-start | bytes 147460
  43.0 19.2 %all-to-all-start = ((f32[16,1,2048]{2,1,0:T(1,128)}), f32[16,1,2048]{2,1,0:T(1,128)}, u32[]{:S(2)}, u32[]{:S(2)}) async-start(f32[16,1,2048]{2,1,0:T(1,128)} %broadcast_in_dim.30), calls=%async_computation | async-start | bytes 262144 | tf_op jit(solution)/shard_map/all_to_all | solution.py:36
  49.9 6.9 %slice-start = ((s8[4456448]{0:T(1024)(128)(4,1)}), s8[262144]{0:T(1024)(128)(4,1)S(1)}, s32[]{:S(2)}) async-start(s8[4456448]{0:T(1024)(128)(4,1)} %bitcast.167), calls=%async_computation.5 | async-start | bytes 524288
  58.1 9.8 %copy-start.3 = (f32[16,64,64]{2,1,0:T(8,128)S(1)}, f32[16,64,64]{2,1,0:T(8,128)}, u32[]{:S(2)}) copy-start(f32[16,64,64]{2,1,0:T(8,128)} %param.16) | copy-start | bytes 786436
  60.6 8.8 %copy-start.2 = (f32[16,16,256]{2,1,0:T(8,128)S(1)}, f32[16,16,256]{2,1,0:T(8,128)}, u32[]{:S(2)}) copy-start(f32[16,16,256]{2,1,0:T(8,128)} %param.11) | copy-start | bytes 786436
  60.6 8.8 %copy-start.8 = (f32[16,16,256]{2,0,1:T(8,128)S(1)}, f32[16,16,256]{2,0,1:T(8,128)}, u32[]{:S(2)}) copy-start(f32[16,16,256]{2,0,1:T(8,128)} %fusion.55) | copy-start | bytes 786436
  62.2 12.5 %copy-start.30 = (f32[16]{0:T(128)S(1)}, f32[16]{0:T(128)}, u32[]{:S(2)}) copy-start(f32[16]{0:T(128)} %copy-done.29) | copy-start | bytes 196
  74.7 6.6 %copy-start.28 = (f32[16]{0:T(128)S(1)}, f32[16]{0:T(128)}, u32[]{:S(2)}) copy-start(f32[16]{0:T(128)} %multiply_reduce_fusion.5) | copy-start | bytes 196
  74.7 18.9 %copy-start.19 = (s32[16]{0:T(128)S(1)}, s32[16]{0:T(128)}, u32[]{:S(2)}) copy-start(s32[16]{0:T(128)} %param.21) | copy-start | bytes 196
  74.7 39.5 %copy-start.13 = (s32[1024]{0:T(1024)S(1)}, s32[1024]{0:T(1024)}, u32[]{:S(2)}) copy-start(s32[1024]{0:T(1024)} %copy-done.12) | copy-start | bytes 12292
  74.7 41.9 %copy-start.27 = (f32[16]{0:T(128)S(1)}, f32[16]{0:T(128)}, u32[]{:S(2)}) copy-start(f32[16]{0:T(128)} %copy-done.26) | copy-start | bytes 196
  81.3 38.8 %copy-start.25 = (f32[16]{0:T(128)S(1)}, f32[16]{0:T(128)}, u32[]{:S(2)}) copy-start(f32[16]{0:T(128)} %copy-done.24) | copy-start | bytes 196
  81.9 22.3 %all-to-all-start.1 = ((f32[32,2,16]{2,1,0:T(2,128)}), f32[32,2,16]{2,1,0:T(2,128)S(1)}, u32[]{:S(2)}, u32[]{:S(2)}) async-start(f32[32,2,16]{2,1,0:T(2,128)} %broadcast_in_dim.32), calls=%async_computation.1 | async-start | bytes 65536 | tf_op jit(solution)/shard_map/all_to_all | solution.py:36
  92.0 20.0 %collective-permute-start.5 = (f32[16,6,320]{2,0,1:T(8,128)}, f32[16,6,320]{2,0,1:T(8,128)}, u32[]{:S(2)}, u32[]{:S(2)}) collective-permute-start(f32[16,6,320]{2,0,1:T(8,128)} %get-tuple-element.25), channel_id=1, source_target_pairs={{0,1},{1,2},{2,3},{3,4},{4,5},{5,6},{6,7},{7,8},{8,9},{9,10},{10,1... | collective-permute-start | bytes 368648 | tf_op jit(solution)/shard_map/ppermute | solution.py:24
  93.6 18.4 %collective-permute-start.4 = (f32[16,6,320]{2,0,1:T(8,128)}, f32[16,6,320]{2,0,1:T(8,128)S(1)}, u32[]{:S(2)}, u32[]{:S(2)}) collective-permute-start(f32[16,6,320]{2,0,1:T(8,128)} %get-tuple-element.24), channel_id=1, source_target_pairs={{1,0},{2,1},{3,2},{4,3},{5,4},{6,5},{7,6},{8,7},{9,8},{10,9},{11,1... | collective-permute-start | bytes 368648 | tf_op jit(solution)/shard_map/ppermute | solution.py:26
  105.1 25.1 %all-to-all-start.2 = ((f32[16,1,2080]{2,1,0:T(1,128)}), f32[16,1,2080]{2,1,0:T(1,128)}, u32[]{:S(2)}, u32[]{:S(2)}) async-start(f32[16,1,2080]{2,1,0:T(1,128)} %broadcast_in_dim.33), calls=%async_computation.2 | async-start | bytes 278528 | tf_op jit(solution)/shard_map/all_to_all | solution.py:36
  114.2 10.0 %slice-start.2 = ((s8[4456448]{0:T(1024)(128)(4,1)}), s8[262144]{0:T(1024)(128)(4,1)S(1)}, s32[]{:S(2)}) async-start(s8[4456448]{0:T(1024)(128)(4,1)} %bitcast.169), calls=%async_computation.7 | async-start | bytes 524288
  116.6 7.6 %slice-start.3 = ((s8[4456448]{0:T(1024)(128)(4,1)}), s8[4194304]{0:T(1024)(128)(4,1)S(1)}, s32[]{:S(2)}) async-start(s8[4456448]{0:T(1024)(128)(4,1)} %bitcast.169), calls=%async_computation.8 | async-start | bytes 8388608
  116.6 7.6 %copy-start.23 = (f32[16]{0:T(128)S(1)}, f32[16]{0:T(128)}, u32[]{:S(2)}) copy-start(f32[16]{0:T(128)} %copy-done.22) | copy-start | bytes 196
  (12 other events, 45.7 us)

commit v10 on v8

--- a/solution.py
+++ b/solution.py
@@ -168,7 +168,7 @@
 
     def total(*products):
         sums = jnp.stack([jnp.sum(product, axis=(1, 2)) for product in products])
-        return all_sum(sums, ("lon", "band"))
+        return all_sum(sums, ("band", "lon"))
 
     assert ITERS == 2
     direction = sky_maps

time: 166 us -> 167 us (level)
  no operation moved by 1% of the time
where the time goes in v10:
time: 167 us; the launch traced here: 166 us
  matrix products  49.8 us (30%)
  starting transfers between devices  35.9 us (21%)
  blocking collectives  31.8 us (19%)
  local copies, waits for them, and re-layouts  21.3 us (13%)
  other arithmetic  15.7 us (9%)
  waiting for transfers between devices  10.2 us (6%)
    all_to_all x2, blocking collectives, gathered(): return lax.all_to_all(copies, axis, 0, 0, tiled=False)  31.8 us
    all_to_all x3, starting transfers between devices, gathered(): return lax.all_to_all(copies, axis, 0, 0, tiled=False)  23.8 us
    dot_general x4, matrix products, covariance_local(): jnp.einsum('ipq,miq->mip', ahead, offset_values(step), precision=MATMUL_P...  11.7 us
    dot_general x2, matrix products, covariance_local(): jnp.einsum('ipq,miq->mip', same_blocks, offset_values(0), precision=MATMU...  11.5 us
    ppermute x3, starting transfers between devices, extended(): lax.ppermute(head, axis, [((i + 1) % count, i) for i in range(count)])  10.4 us
    all_to_all x3, waiting for transfers between devices, gathered(): return lax.all_to_all(copies, axis, 0, 0, tiled=False)  10.2 us
    mul x2, other arithmetic, matern_shape(): return (1.0 + scaled) * jnp.exp(-scaled)  9.75 us
    dot_general x4, matrix products, covariance_local(): jnp.einsum('iqp,miq->mip', behind, offset_values(-step), precision=MATMUL...  9.56 us
  transfers between devices with their start and end apart: 9, of which 1 were waited for; matrix products, arithmetic and copies ran while one was open for 30% of the time, Pallas kernels for 0%

profile of v10, /device:TPU:1, one launch (start us, length us, event | category | flops | bytes accessed | tf_op | source)
XLA Modules:
  0.0 165.9 jit_solution(7855417094078901794)
XLA Ops:
  1.6 6.9 %collective-permute-start.2 = (f32[3,2,256]{2,1,0:T(2,128)S(1)}, f32[3,2,256]{2,1,0:T(2,128)S(1)}, u32[]{:S(2)}, u32[]{:S(2)}) collective-permute-start(f32[3,2,256]{2,1,0:T(2,128)S(1)} %get-tuple-element.42), channel_id=1, source_target_pairs={{1,0},{2,1},{3,2},{4,3},{5,4},{6,5},{7,6},{8,7},{9,8},{10,9},{11,1... | collective-permute-start | bytes 18440 | tf_op jit(solution)/shard_map/ppermute | solution.py:26
  9.6 1.9 %convolution_bitcast_fusion.9 = f32[16,16,64]{2,0,1:T(8,128)S(1)} fusion(f32[16,256,64]{1,2,0:T(8,128)} %param.14, f32[16,16,256]{2,1,0:T(8,128)} %param.11), kind=kOutput, calls=%fused_computation.70 | convolution fusion | flops 25165824 | bytes 1376256 | tf_op jit(solution)/shard_map/lpr,mlp->mlr/dot_general | solution.py:109
  12.3 3.6 %collective-permute-start = (f32[16,6,320]{2,0,1:T(8,128)}, f32[16,6,320]{2,0,1:T(8,128)}, u32[]{:S(2)}, u32[]{:S(2)}) collective-permute-start(f32[16,6,320]{2,0,1:T(8,128)} %get-tuple-element.24), channel_id=1, source_target_pairs={{1,0},{2,1},{3,2},{4,3},{5,4},{6,5},{7,6},{8,7},{9,8},{10,9},{11,1... | collective-permute-start | bytes 368648 | tf_op jit(solution)/shard_map/ppermute | solution.py:26
  15.8 1.4 convolution_bitcast_fusion.6
  18.8 6.8 %all-to-all-start = ((f32[16,1,2048]{2,1,0:T(1,128)}), f32[16,1,2048]{2,1,0:T(1,128)S(1)}, u32[]{:S(2)}, u32[]{:S(2)}) async-start(f32[16,1,2048]{2,1,0:T(1,128)} %broadcast_in_dim.30), calls=%async_computation | async-start | bytes 262144 | tf_op jit(solution)/shard_map/all_to_all | solution.py:36
  30.9 5.7 %fusion.17 = f32[16,16,256]{2,1,0:T(8,128)} fusion(f32[16,256]{1,0:T(8,128)S(1)} %get-tuple-element.39, f32[16,256]{1,0:T(8,128)S(1)} %get-tuple-element.40, f32[16,256]{1,0:T(8,128)S(1)} %get-tuple-element.38, f32[16]{0:T(128)S(1)} %get-tuple-element.47, f32[16,16,256]{2,1,0:T(8,128)S(1)} %copy-done.2), kind=kOutput, calls=%fused_computation.24 | convolution fusion | flops 113311744 | bytes 573504 | tf_op jit(solution)/shard_map/ipq,miq->mip/dot_general | solution.py:122
  37.3 5.2 %exponential_multiply_fusion = f32[18,256,256]{2,1,0:T(8,128)} fusion(f32[18,256]{1,0:T(8,128)S(1)} %get-tuple-element.30, f32[18,256]{1,0:T(8,128)S(1)} %get-tuple-element.36, f32[18,256]{1,0:T(8,128)S(1)} %get-tuple-element.31, f32[18,256]{1,0:T(8,128)S(1)} %get-tuple-element.37, f32[18,256]{1,0:T(8,128)S(1)} %get-tuple-element.29, ...), kind=kLoop, calls=%fused_computation.4 | loop fusion | flops 14155776 | bytes 4829184 | tf_op jit(solution)/shard_map/mul | solution.py:51
  42.5 4.6 %exponential_multiply_fusion.1 = f32[17,256,256]{2,1,0:T(8,128)} fusion(f32[17,256]{1,0:T(8,128)S(1)} %get-tuple-element.27, f32[17,256]{1,0:T(8,128)S(1)} %get-tuple-element.34, f32[17,256]{1,0:T(8,128)S(1)} %get-tuple-element.28, f32[17,256]{1,0:T(8,128)S(1)} %get-tuple-element.33, f32[17,256]{1,0:T(8,128)S(1)} %get-tuple-element.26, ...), kind=kLoop, calls=%fused_computation.5 | loop fusion | flops 13369344 | bytes 4560896 | tf_op jit(solution)/shard_map/mul | solution.py:51
  48.3 1.7 %copy.111 = f32[16,16,2,64]{3,0,2,1:T(8,128)} copy(f32[16,16,2,64]{3,2,0,1:T(2,128)} %bitcast.175) | data formatting | bytes 262144 | tf_op jit(solution)/shard_map/transpose | solution.py:144
  49.9 1.6 gather_fusion.1
  52.6 1.5 convolution_bitcast_fusion.5
  55.7 1.6 gather_fusion
  57.3 2.1 %convolution_bitcast_fusion.7 = f32[16,16,64]{2,1,0:T(8,128)S(1)} fusion(f32[16,16,4,64]{3,0,2,1:T(8,128)} %bitcast.174, f32[16,4,64,64]{3,2,1,0:T(8,128)S(1)} %copy-done), kind=kOutput, calls=%fused_computation.68 | convolution fusion | flops 25165824 | bytes 1376256 | tf_op jit(solution)/shard_map/lsab,mlsb->mla/dot_general | solution.py:135
  59.4 1.8 %fusion.75 = f32[16,16,64]{2,0,1:T(8,128)S(1)} fusion(f32[16,16,64]{2,1,0:T(8,128)S(1)} %convolution_bitcast_fusion.7, f32[16,64,64]{2,1,0:T(8,128)} %param.16, f32[16,16,64]{2,1,0:T(8,128)} %convolution_bitcast_fusion.5), kind=kOutput, calls=%fused_computation.65 | convolution fusion | flops 6307840 | bytes 458752 | tf_op jit(solution)/shard_map/lab,mlb->mla/dot_general | solution.py:157
  61.2 3.4 %fusion.2 = f32[16,16,256]{2,1,0:T(8,128)S(1)} fusion(f32[18,256,256]{2,1,0:T(8,128)} %exponential_multiply_fusion, f32[16,6,320]{2,0,1:T(8,128)} %copy-done.5, f32[16,16,64]{2,0,1:T(8,128)S(1)} %convolution_bitcast_fusion.9, f32[16,16,256]{2,0,1:T(8,128)S(1)} %copy.105, f32[16]{0:T(128)S(1)} %copy-done.27), kind=kOutput, calls=%fused_computation.9 | convolution fusion | flops 100859904 | bytes 4931648 | tf_op jit(solution)/shard_map/iqp,miq->mip/dot_general | solution.py:132
  64.7 2.5 %fusion.6 = f32[16,16,256]{2,1,0:T(8,128)S(1)} fusion(f32[18,256,256]{2,1,0:T(8,128)S(1)} %bitcast.172, f32[16,6,320]{2,0,1:T(8,128)} %collective-permute-done, f32[16,16,64]{2,0,1:T(8,128)S(1)} %convolution_bitcast_fusion.9, f32[16,16,256]{2,0,1:T(8,128)S(1)} %copy.105, f32[16]{0:T(128)S(1)} %copy-done.26), kind=kOutput, calls=%fused_computation.13 | convolution fusion | flops 100859904 | bytes 4973056 | tf_op jit(solution)/shard_map/ipq,miq->mip/dot_general | solution.py:129
  67.3 1.4 fusion.10
  68.8 2.7 %fusion.71 = f32[16,16,256]{2,0,1:T(8,128)S(1)} fusion(f32[16,16,256]{2,1,0:T(8,128)S(1)} %fusion.2, f32[16,16,256]{2,1,0:T(8,128)S(1)} %fusion.6, f32[16,16,256]{2,1,0:T(8,128)S(1)} %fusion.10, f32[16,16,256]{2,1,0:T(8,128)S(1)} %copy-done.12, f32[17,256,256]{2,1,0:T(8,128)S(1)} %bitcast.168, f32[16,6,320]{2,0,1:T(8,128)} %collective-permute-done, ...), kind=kOutput, calls=%fused_computation.58 | convolution fusion | flops 101253120 | bytes 6234176 | tf_op jit(solution)/shard_map/ipq,miq->mip/dot_general | solution.py:129
  73.8 5.8 %fusion.16 = f32[16,16,256]{2,1,0:T(8,128)} fusion(f32[16,256]{1,0:T(8,128)S(1)} %copy-done.20, f32[16,256]{1,0:T(8,128)S(1)} %copy-done.22, f32[16,256]{1,0:T(8,128)S(1)} %copy-done.18, f32[16,16,256]{2,0,1:T(8,128)S(1)} %get-tuple-element.49, f32[16]{0:T(128)S(1)} %copy-done.32), kind=kOutput, calls=%fused_computation.23 | convolution fusion | flops 113311744 | bytes 573504 | tf_op jit(solution)/shard_map/ipq,miq->mip/dot_general | solution.py:122
  80.2 10.1 %all-to-all-start.1 = ((f32[32,2,16]{2,1,0:T(2,128)}), f32[32,2,16]{2,1,0:T(2,128)S(1)}, u32[]{:S(2)}, u32[]{:S(2)}) async-start(f32[32,2,16]{2,1,0:T(2,128)} %broadcast_in_dim.32), calls=%async_computation.1 | async-start | bytes 65536 | tf_op jit(solution)/shard_map/all_to_all | solution.py:36
  90.3 1.6 collective-permute-start.5
  92.2 10.2 %all-to-all-done.1 = f32[32,2,16]{2,1,0:T(2,128)S(1)} async-done(((f32[32,2,16]{2,1,0:T(2,128)}), f32[32,2,16]{2,1,0:T(2,128)S(1)}, u32[]{:S(2)}, u32[]{:S(2)}) %all-to-all-start.1) | async-done | bytes 4128 | tf_op jit(solution)/shard_map/all_to_all | solution.py:36
  103.2 7.0 %all-to-all-start.2 = ((f32[16,1,2080]{2,1,0:T(1,128)}), f32[16,1,2080]{2,1,0:T(1,128)}, u32[]{:S(2)}, u32[]{:S(2)}) async-start(f32[16,1,2080]{2,1,0:T(1,128)} %broadcast_in_dim.33), calls=%async_computation.2 | async-start | bytes 278528 | tf_op jit(solution)/shard_map/all_to_all | solution.py:36
  110.9 1.4 gather_fusion.2
  112.4 3.5 %fusion = f32[16,16,256]{2,1,0:T(8,128)S(1)} fusion(f32[18,256,256]{2,1,0:T(8,128)} %exponential_multiply_fusion, f32[16,6,320]{2,0,1:T(8,128)} %copy-done.7, f32[16,16,64]{2,0,1:T(8,128)S(1)} %convolution_bitcast_fusion.8, f32[16,16,256]{2,0,1:T(8,128)S(1)} %get-tuple-element.49, f32[16]{0:T(128)} %get-tuple-element.44), kind=kOutput, calls=%fused_computation.7 | convolution fusion | flops 100859904 | bytes 4932096 | tf_op jit(solution)/shard_map/iqp,miq->mip/dot_general | solution.py:132
  115.9 4.0 %fusion.4 = f32[16,16,256]{2,1,0:T(8,128)S(1)} fusion(f32[18,256,256]{2,1,0:T(8,128)} %exponential_multiply_fusion, f32[16,6,320]{2,0,1:T(8,128)S(1)} %collective-permute-done.4, f32[16,16,64]{2,0,1:T(8,128)S(1)} %convolution_bitcast_fusion.8, f32[16,16,256]{2,0,1:T(8,128)S(1)} %get-tuple-element.49, f32[16]{0:T(128)} %get-tuple-element.45), kind=kOutput, calls=%fused_computation.11 | convolution fusion | flops 100859904 | bytes 4907520 | tf_op jit(solution)/shard_map/ipq,miq->mip/dot_general | solution.py:129
  121.2 2.5 %fusion.62 = f32[16,16,256]{2,0,1:T(8,128)} fusion(f32[16,16,256]{2,1,0:T(8,128)S(1)} %fusion, f32[16,16,256]{2,1,0:T(8,128)S(1)} %fusion.4, f32[16,16,256]{2,1,0:T(8,128)S(1)} %fusion.8, f32[16,16,256]{2,1,0:T(8,128)S(1)} %copy-done.13, f32[17,256,256]{2,1,0:T(8,128)S(1)} %bitcast.170, f32[16,6,320]{2,0,1:T(8,128)S(1)} %collective-permute-done.4, ...), kind=kOutput, calls=%fused_computation.55 | convolution fusion | flops 101253120 | bytes 6234176 | tf_op jit(solution)/shard_map/ipq,miq->mip/dot_general | solution.py:129
  126.5 1.6 gather_fusion.3
  128.6 1.6 fusion.74
  130.2 1.8 %multiply_reduce_fusion.3 = (f32[16]{0:T(128)S(1)}, f32[16]{0:T(128)S(1)}, f32[16]{0:T(128)S(1)}, f32[16]{0:T(128)S(1)}, f32[16,16,256]{2,0,1:T(8,128)S(1)}) fusion(f32[16,16,256]{2,0,1:T(8,128)S(1)} %get-tuple-element.49, f32[16]{0:T(128)S(1)} %slice_divide_fusion, f32[16,16,256]{2,1,0:T(8,128)S(1)} %copy-done.2, f32[16,16,256]{2,0,1:T(8,128)S(1)} %copy-done.9, ...), kind=kOutput, calls=%fused_computation.117 | convolution fusion | flops 26017728 | bytes 2163008 | tf_op jit(solution)/shard_map/lpr,mlr->mlp/dot_general | solution.py:160
  132.0 12.9 %all_to_all.30 = f32[16,4,16]{2,1,0:T(4,128)S(1)} all-to-all(f32[16,4,16]{2,1,0:T(4,128)S(1)} %broadcast_in_dim.34), channel_id=1, replica_groups=mesh['band'=16,'lon'=32] {'band'}, dimensions={0} | all-to-all | bytes 8192 | tf_op jit(solution)/shard_map/all_to_all | solution.py:36
  145.0 18.9 %all_to_all.31 = f32[32,4,16]{2,1,0:T(4,128)S(1)} all-to-all(f32[32,4,16]{2,1,0:T(4,128)S(1)} %broadcast_in_dim.35), channel_id=1, replica_groups=mesh['band'=16,'lon'=32] {'lon'}, dimensions={0} | all-to-all | bytes 16384 | tf_op jit(solution)/shard_map/all_to_all | solution.py:36
  (157 shorter events, 25.5 us)
Async XLA Ops:
  0.6 56.6 %copy-start = (f32[16,4,64,64]{3,2,1,0:T(8,128)S(1)}, f32[16,4,64,64]{3,2,1,0:T(8,128)}, u32[]{:S(2)}) copy-start(f32[16,4,64,64]{3,2,1,0:T(8,128)} %param.15) | copy-start | bytes 3145732
  0.6 27.9 %copy-start.2 = (f32[16,16,256]{2,1,0:T(8,128)S(1)}, f32[16,16,256]{2,1,0:T(8,128)}, u32[]{:S(2)}) copy-start(f32[16,16,256]{2,1,0:T(8,128)} %param.11) | copy-start | bytes 786436
  0.7 28.7 %copy-start.16 = (s32[16,5]{0,1:T(8,128)S(1)}, s32[16,5]{0,1:T(8,128)}, u32[]{:S(2)}) copy-start(s32[16,5]{0,1:T(8,128)} %param.18) | copy-start | bytes 964
  0.7 29.3 %copy-start.29 = (s32[16,4]{0,1:T(4,128)S(1)}, s32[16,4]{0,1:T(4,128)}, u32[]{:S(2)}) copy-start(s32[16,4]{0,1:T(4,128)} %param.19) | copy-start | bytes 772
  0.7 30.1 %copy-start.30 = (s32[2,2]{1,0:T(2,128)S(1)}, s32[2,2]{1,0:T(2,128)}, u32[]{:S(2)}) copy-start(s32[2,2]{1,0:T(2,128)} %param.20) | copy-start | bytes 52
  1.6 35.6 %collective-permute-start.2 = (f32[3,2,256]{2,1,0:T(2,128)S(1)}, f32[3,2,256]{2,1,0:T(2,128)S(1)}, u32[]{:S(2)}, u32[]{:S(2)}) collective-permute-start(f32[3,2,256]{2,1,0:T(2,128)S(1)} %get-tuple-element.42), channel_id=1, source_target_pairs={{1,0},{2,1},{3,2},{4,3},{5,4},{6,5},{7,6},{8,7},{9,8},{10,9},{11,1... | collective-permute-start | bytes 18440 | tf_op jit(solution)/shard_map/ppermute | solution.py:26
  8.5 28.8 %collective-permute-start.1 = (f32[3,2,256]{2,1,0:T(2,128)S(1)}, f32[3,2,256]{2,1,0:T(2,128)S(1)}, u32[]{:S(2)}, u32[]{:S(2)}) collective-permute-start(f32[3,2,256]{2,1,0:T(2,128)S(1)} %get-tuple-element.41), channel_id=1, source_target_pairs={{0,1},{1,2},{2,3},{3,4},{4,5},{5,6},{6,7},{7,8},{8,9},{9,10},{10,1... | collective-permute-start | bytes 18440 | tf_op jit(solution)/shard_map/ppermute | solution.py:24
  12.3 41.9 %collective-permute-start.3 = (f32[16,6,320]{2,0,1:T(8,128)}, f32[16,6,320]{2,0,1:T(8,128)S(1)}, u32[]{:S(2)}, u32[]{:S(2)}) collective-permute-start(f32[16,6,320]{2,0,1:T(8,128)} %get-tuple-element.25), channel_id=1, source_target_pairs={{0,1},{1,2},{2,3},{3,4},{4,5},{5,6},{6,7},{7,8},{8,9},{9,10},{10,1... | collective-permute-start | bytes 368648 | tf_op jit(solution)/shard_map/ppermute | solution.py:24
  12.3 42.6 %collective-permute-start = (f32[16,6,320]{2,0,1:T(8,128)}, f32[16,6,320]{2,0,1:T(8,128)}, u32[]{:S(2)}, u32[]{:S(2)}) collective-permute-start(f32[16,6,320]{2,0,1:T(8,128)} %get-tuple-element.24), channel_id=1, source_target_pairs={{1,0},{2,1},{3,2},{4,3},{5,4},{6,5},{7,6},{8,7},{9,8},{10,9},{11,1... | collective-permute-start | bytes 368648 | tf_op jit(solution)/shard_map/ppermute | solution.py:26
  18.8 28.2 %all-to-all-start = ((f32[16,1,2048]{2,1,0:T(1,128)}), f32[16,1,2048]{2,1,0:T(1,128)S(1)}, u32[]{:S(2)}, u32[]{:S(2)}) async-start(f32[16,1,2048]{2,1,0:T(1,128)} %broadcast_in_dim.30), calls=%async_computation | async-start | bytes 262144 | tf_op jit(solution)/shard_map/all_to_all | solution.py:36
  28.6 8.0 %copy-start.17 = (f32[16,256]{1,0:T(8,128)}, f32[16,256]{1,0:T(8,128)S(1)}, u32[]{:S(2)}) copy-start(f32[16,256]{1,0:T(8,128)S(1)} %get-tuple-element.38) | copy-start | bytes 49156
  28.6 8.0 %copy-start.19 = (f32[16,256]{1,0:T(8,128)}, f32[16,256]{1,0:T(8,128)S(1)}, u32[]{:S(2)}) copy-start(f32[16,256]{1,0:T(8,128)S(1)} %get-tuple-element.39) | copy-start | bytes 49156
  28.6 8.0 %copy-start.21 = (f32[16,256]{1,0:T(8,128)}, f32[16,256]{1,0:T(8,128)S(1)}, u32[]{:S(2)}) copy-start(f32[16,256]{1,0:T(8,128)S(1)} %get-tuple-element.40) | copy-start | bytes 49156
  30.0 6.6 %copy-start.31 = (f32[16]{0:T(128)}, f32[16]{0:T(128)S(1)}, u32[]{:S(2)}) copy-start(f32[16]{0:T(128)S(1)} %get-tuple-element.47) | copy-start | bytes 196
  30.9 6.4 %copy-start.10 = (f32[3,16,256]{2,1,0:T(8,128)S(1)}, f32[3,16,256]{2,1,0:T(8,128)}, u32[]{:S(2)}) copy-start(f32[3,16,256]{2,1,0:T(8,128)} %param.13) | copy-start | bytes 147460
  47.4 17.3 %slice-start.4 = ((s8[4718592]{0:T(1024)(128)(4,1)}), s8[524288]{0:T(1024)(128)(4,1)S(1)}, s32[]{:S(2)}) async-start(s8[4718592]{0:T(1024)(128)(4,1)} %bitcast.171), calls=%async_computation.9 | async-start | bytes 1048576
  48.3 12.9 %copy-start.27 = (f32[16]{0:T(128)S(1)}, f32[16]{0:T(128)}, u32[]{:S(2)}) copy-start(f32[16]{0:T(128)} %get-tuple-element.44) | copy-start | bytes 196
  57.3 7.4 %slice-start.5 = ((s8[4718592]{0:T(1024)(128)(4,1)}), s8[4194304]{0:T(1024)(128)(4,1)S(1)}, s32[]{:S(2)}) async-start(s8[4718592]{0:T(1024)(128)(4,1)} %bitcast.171), calls=%async_computation.10 | async-start | bytes 8388608
  57.3 7.4 %copy-start.26 = (f32[16]{0:T(128)S(1)}, f32[16]{0:T(128)}, u32[]{:S(2)}) copy-start(f32[16]{0:T(128)} %get-tuple-element.45) | copy-start | bytes 196
  59.4 7.9 %slice-start = ((s8[4456448]{0:T(1024)(128)(4,1)}), s8[4194304]{0:T(1024)(128)(4,1)S(1)}, s32[]{:S(2)}) async-start(s8[4456448]{0:T(1024)(128)(4,1)} %bitcast.167), calls=%async_computation.5 | async-start | bytes 8388608
  61.2 6.1 %slice-start.1 = ((s8[4456448]{0:T(1024)(128)(4,1)}), s8[262144]{0:T(1024)(128)(4,1)S(1)}, s32[]{:S(2)}) async-start(s8[4456448]{0:T(1024)(128)(4,1)} %bitcast.167), calls=%async_computation.6 | async-start | bytes 524288
  61.2 6.1 %copy-start.6 = (f32[16,6,320]{2,0,1:T(8,128)S(1)}, f32[16,6,320]{2,0,1:T(8,128)}, u32[]{:S(2)}) copy-start(f32[16,6,320]{2,0,1:T(8,128)} %copy-done.5) | copy-start | bytes 368644
  73.7 18.2 %copy-start.23 = (s32[16]{0:T(128)S(1)}, s32[16]{0:T(128)}, u32[]{:S(2)}) copy-start(s32[16]{0:T(128)} %param.21) | copy-start | bytes 196
  73.7 37.2 %copy-start.14 = (s32[1024]{0:T(1024)S(1)}, s32[1024]{0:T(1024)}, u32[]{:S(2)}) copy-start(s32[1024]{0:T(1024)} %pad_clamp_fusion.1) | copy-start | bytes 12292
  80.2 22.2 %all-to-all-start.1 = ((f32[32,2,16]{2,1,0:T(2,128)}), f32[32,2,16]{2,1,0:T(2,128)S(1)}, u32[]{:S(2)}, u32[]{:S(2)}) async-start(f32[32,2,16]{2,1,0:T(2,128)} %broadcast_in_dim.32), calls=%async_computation.1 | async-start | bytes 65536 | tf_op jit(solution)/shard_map/all_to_all | solution.py:36
  90.3 20.0 %collective-permute-start.5 = (f32[16,6,320]{2,0,1:T(8,128)}, f32[16,6,320]{2,0,1:T(8,128)S(1)}, u32[]{:S(2)}, u32[]{:S(2)}) collective-permute-start(f32[16,6,320]{2,0,1:T(8,128)} %get-tuple-element.23), channel_id=1, source_target_pairs={{0,1},{1,2},{2,3},{3,4},{4,5},{5,6},{6,7},{7,8},{8,9},{9,10},{10,1... | collective-permute-start | bytes 368648 | tf_op jit(solution)/shard_map/ppermute | solution.py:24
  91.9 18.3 %collective-permute-start.4 = (f32[16,6,320]{2,0,1:T(8,128)S(1)}, f32[16,6,320]{2,0,1:T(8,128)S(1)}, u32[]{:S(2)}, u32[]{:S(2)}) collective-permute-start(f32[16,6,320]{2,0,1:T(8,128)S(1)} %get-tuple-element.22), channel_id=1, source_target_pairs={{1,0},{2,1},{3,2},{4,3},{5,4},{6,5},{7,6},{8,7},{9,8},{10,9},{11,1... | collective-permute-start | bytes 368648 | tf_op jit(solution)/shard_map/ppermute | solution.py:26
  103.2 21.3 %all-to-all-start.2 = ((f32[16,1,2080]{2,1,0:T(1,128)}), f32[16,1,2080]{2,1,0:T(1,128)}, u32[]{:S(2)}, u32[]{:S(2)}) async-start(f32[16,1,2080]{2,1,0:T(1,128)} %broadcast_in_dim.33), calls=%async_computation.2 | async-start | bytes 278528 | tf_op jit(solution)/shard_map/all_to_all | solution.py:36
  110.9 9.0 %slice-start.2 = ((s8[4456448]{0:T(1024)(128)(4,1)}), s8[262144]{0:T(1024)(128)(4,1)S(1)}, s32[]{:S(2)}) async-start(s8[4456448]{0:T(1024)(128)(4,1)} %bitcast.169), calls=%async_computation.7 | async-start | bytes 524288
  112.4 7.5 %slice-start.3 = ((s8[4456448]{0:T(1024)(128)(4,1)}), s8[4194304]{0:T(1024)(128)(4,1)S(1)}, s32[]{:S(2)}) async-start(s8[4456448]{0:T(1024)(128)(4,1)} %bitcast.169), calls=%async_computation.8 | async-start | bytes 8388608
  112.4 7.6 %copy-start.8 = (f32[16,6,320]{2,0,1:T(8,128)S(1)}, f32[16,6,320]{2,0,1:T(8,128)}, u32[]{:S(2)}) copy-start(f32[16,6,320]{2,0,1:T(8,128)} %copy-done.7) | copy-start | bytes 368644
  123.6 6.5 %copy-start.9 = (f32[16,16,256]{2,0,1:T(8,128)S(1)}, f32[16,16,256]{2,0,1:T(8,128)}, u32[]{:S(2)}) copy-start(f32[16,16,256]{2,0,1:T(8,128)} %fusion.62) | copy-start | bytes 786436
  (16 other events, 64.2 us)

commit v11 on v8

--- a/solution.py
+++ b/solution.py
@@ -177,14 +177,12 @@
     first_sums = jnp.stack(
         [jnp.sum(product, axis=(1, 2)) for product in (direction * direction, direction * applied)]
     )
-    first_sums = all_sum(first_sums, ("lon",))
     panel_coeffs = applied_local[3]
     payload = jnp.concatenate([panel_coeffs.reshape(-1), first_sums.reshape(-1)])
     band_payload = gathered(payload, "band")
     panel_size = panel_coeffs.size
-    norm_now, curvature_sum = jnp.sum(band_payload[:, panel_size:], axis=0).reshape(
-        first_sums.shape
-    )
+    first_sums = jnp.sum(band_payload[:, panel_size:], axis=0).reshape(first_sums.shape)
+    norm_now, curvature_sum = all_sum(first_sums, ("lon",))
     applied_twice = covariance_finish(
         applied_local, band_layout(band_payload[:, :panel_size], panel_coeffs)
     )

time: 166 us -> 166 us (level)
  waiting for transfers between devices: 10.2 us -> 7.65 us
    ppermute x3, starting transfers between devices: 10.4 us -> 13.7 us  [extended(): lax.ppermute(head, axis, [((i + 1) % count, i) for i in range(count)])]
    all_to_all x3, waiting for transfers between devices: 10.2 us -> 7.63 us  [gathered(): return lax.all_to_all(copies, axis, 0, 0, tiled=False)]
    unnamed x83 -> x85, local copies, waits for them, and re-layouts: 6.06 us -> 6.06 us
  transfers between devices with their start and end apart: 9 -> 9, of which waited for: 1 -> 1; matrix products, arithmetic and copies ran while one was open for 30% -> 33% of each run, Pallas kernels for 0% -> 0%
where the time goes in v11:
time: 166 us; the launch traced here: 165 us
  matrix products  49.8 us (30%)
  starting transfers between devices  37.5 us (23%)
  blocking collectives  30.6 us (18%)
  local copies, waits for them, and re-layouts  21.4 us (13%)
  other arithmetic  16.4 us (10%)
  waiting for transfers between devices  7.65 us (5%)
    all_to_all x2, blocking collectives, gathered(): return lax.all_to_all(copies, axis, 0, 0, tiled=False)  30.6 us
    all_to_all x3, starting transfers between devices, gathered(): return lax.all_to_all(copies, axis, 0, 0, tiled=False)  23.8 us
    ppermute x3, starting transfers between devices, extended(): lax.ppermute(head, axis, [((i + 1) % count, i) for i in range(count)])  13.7 us
    dot_general x4, matrix products, covariance_local(): jnp.einsum('ipq,miq->mip', ahead, offset_values(step), precision=MATMUL_P...  11.7 us
    dot_general x2, matrix products, covariance_local(): jnp.einsum('ipq,miq->mip', same_blocks, offset_values(0), precision=MATMU...  11.5 us
    mul x2, other arithmetic, matern_shape(): return (1.0 + scaled) * jnp.exp(-scaled)  9.82 us
    dot_general x4, matrix products, covariance_local(): jnp.einsum('iqp,miq->mip', behind, offset_values(-step), precision=MATMUL...  9.56 us
    all_to_all x3, waiting for transfers between devices, gathered(): return lax.all_to_all(copies, axis, 0, 0, tiled=False)  7.63 us
  transfers between devices with their start and end apart: 9, of which 1 were waited for; matrix products, arithmetic and copies ran while one was open for 33% of the time, Pallas kernels for 0%

profile of v11, /device:TPU:1, one launch (start us, length us, event | category | flops | bytes accessed | tf_op | source)
XLA Modules:
  0.0 164.7 jit_solution(13377171844005795085)
XLA Ops:
  1.6 6.9 %collective-permute-start.2 = (f32[3,2,256]{2,1,0:T(2,128)S(1)}, f32[3,2,256]{2,1,0:T(2,128)S(1)}, u32[]{:S(2)}, u32[]{:S(2)}) collective-permute-start(f32[3,2,256]{2,1,0:T(2,128)S(1)} %get-tuple-element.42), channel_id=1, source_target_pairs={{1,0},{2,1},{3,2},{4,3},{5,4},{6,5},{7,6},{8,7},{9,8},{10,9},{11,1... | collective-permute-start | bytes 18440 | tf_op jit(solution)/shard_map/ppermute | solution.py:26
  9.6 1.9 %convolution_bitcast_fusion.9 = f32[16,16,64]{2,0,1:T(8,128)S(1)} fusion(f32[16,256,64]{1,2,0:T(8,128)} %param.14, f32[16,16,256]{2,1,0:T(8,128)} %param.11), kind=kOutput, calls=%fused_computation.70 | convolution fusion | flops 25165824 | bytes 1376256 | tf_op jit(solution)/shard_map/lpr,mlp->mlr/dot_general | solution.py:109
  12.3 3.6 %collective-permute-start = (f32[16,6,320]{2,0,1:T(8,128)}, f32[16,6,320]{2,0,1:T(8,128)}, u32[]{:S(2)}, u32[]{:S(2)}) collective-permute-start(f32[16,6,320]{2,0,1:T(8,128)} %get-tuple-element.24), channel_id=1, source_target_pairs={{1,0},{2,1},{3,2},{4,3},{5,4},{6,5},{7,6},{8,7},{9,8},{10,9},{11,1... | collective-permute-start | bytes 368648 | tf_op jit(solution)/shard_map/ppermute | solution.py:26
  15.8 1.4 convolution_bitcast_fusion.6
  18.8 6.8 %all-to-all-start = ((f32[16,1,2048]{2,1,0:T(1,128)}), f32[16,1,2048]{2,1,0:T(1,128)S(1)}, u32[]{:S(2)}, u32[]{:S(2)}) async-start(f32[16,1,2048]{2,1,0:T(1,128)} %broadcast_in_dim.32), calls=%async_computation | async-start | bytes 262144 | tf_op jit(solution)/shard_map/all_to_all | solution.py:36
  30.9 5.7 %fusion.17 = f32[16,16,256]{2,1,0:T(8,128)} fusion(f32[16,256]{1,0:T(8,128)S(1)} %get-tuple-element.39, f32[16,256]{1,0:T(8,128)S(1)} %get-tuple-element.40, f32[16,256]{1,0:T(8,128)S(1)} %get-tuple-element.38, f32[16]{0:T(128)S(1)} %get-tuple-element.47, f32[16,16,256]{2,1,0:T(8,128)S(1)} %copy-done.2), kind=kOutput, calls=%fused_computation.24 | convolution fusion | flops 113311744 | bytes 573504 | tf_op jit(solution)/shard_map/ipq,miq->mip/dot_general | solution.py:122
  37.3 5.2 %exponential_multiply_fusion = f32[18,256,256]{2,1,0:T(8,128)} fusion(f32[18,256]{1,0:T(8,128)S(1)} %get-tuple-element.30, f32[18,256]{1,0:T(8,128)S(1)} %get-tuple-element.36, f32[18,256]{1,0:T(8,128)S(1)} %get-tuple-element.31, f32[18,256]{1,0:T(8,128)S(1)} %get-tuple-element.37, f32[18,256]{1,0:T(8,128)S(1)} %get-tuple-element.29, ...), kind=kLoop, calls=%fused_computation.4 | loop fusion | flops 14155776 | bytes 4829184 | tf_op jit(solution)/shard_map/mul | solution.py:51
  42.5 4.7 %exponential_multiply_fusion.1 = f32[17,256,256]{2,1,0:T(8,128)} fusion(f32[17,256]{1,0:T(8,128)S(1)} %get-tuple-element.27, f32[17,256]{1,0:T(8,128)S(1)} %get-tuple-element.34, f32[17,256]{1,0:T(8,128)S(1)} %get-tuple-element.28, f32[17,256]{1,0:T(8,128)S(1)} %get-tuple-element.33, f32[17,256]{1,0:T(8,128)S(1)} %get-tuple-element.26, ...), kind=kLoop, calls=%fused_computation.5 | loop fusion | flops 13369344 | bytes 4560896 | tf_op jit(solution)/shard_map/mul | solution.py:51
  48.4 1.7 %copy.111 = f32[16,16,2,64]{3,0,2,1:T(8,128)} copy(f32[16,16,2,64]{3,2,0,1:T(2,128)} %bitcast.184) | data formatting | bytes 262144 | tf_op jit(solution)/shard_map/transpose | solution.py:144
  50.1 1.6 gather_fusion.1
  52.7 1.5 convolution_bitcast_fusion.5
  55.8 1.5 gather_fusion
  57.4 2.1 %convolution_bitcast_fusion.7 = f32[16,16,64]{2,1,0:T(8,128)S(1)} fusion(f32[16,16,4,64]{3,0,2,1:T(8,128)} %bitcast.183, f32[16,4,64,64]{3,2,1,0:T(8,128)S(1)} %copy-done), kind=kOutput, calls=%fused_computation.68 | convolution fusion | flops 25165824 | bytes 1376256 | tf_op jit(solution)/shard_map/lsab,mlsb->mla/dot_general | solution.py:135
  59.5 1.8 %fusion.75 = f32[16,16,64]{2,0,1:T(8,128)S(1)} fusion(f32[16,16,64]{2,1,0:T(8,128)S(1)} %convolution_bitcast_fusion.7, f32[16,64,64]{2,1,0:T(8,128)} %param.16, f32[16,16,64]{2,1,0:T(8,128)} %convolution_bitcast_fusion.5), kind=kOutput, calls=%fused_computation.65 | convolution fusion | flops 6307840 | bytes 458752 | tf_op jit(solution)/shard_map/lab,mlb->mla/dot_general | solution.py:157
  61.3 3.4 %fusion.2 = f32[16,16,256]{2,1,0:T(8,128)S(1)} fusion(f32[18,256,256]{2,1,0:T(8,128)} %exponential_multiply_fusion, f32[16,6,320]{2,0,1:T(8,128)} %copy-done.5, f32[16,16,64]{2,0,1:T(8,128)S(1)} %convolution_bitcast_fusion.9, f32[16,16,256]{2,0,1:T(8,128)S(1)} %copy.105, f32[16]{0:T(128)S(1)} %copy-done.28), kind=kOutput, calls=%fused_computation.9 | convolution fusion | flops 100859904 | bytes 4931648 | tf_op jit(solution)/shard_map/iqp,miq->mip/dot_general | solution.py:132
  64.8 2.5 %fusion.6 = f32[16,16,256]{2,1,0:T(8,128)S(1)} fusion(f32[18,256,256]{2,1,0:T(8,128)S(1)} %bitcast.181, f32[16,6,320]{2,0,1:T(8,128)} %collective-permute-done, f32[16,16,64]{2,0,1:T(8,128)S(1)} %convolution_bitcast_fusion.9, f32[16,16,256]{2,0,1:T(8,128)S(1)} %copy.105, f32[16]{0:T(128)S(1)} %copy-done.26), kind=kOutput, calls=%fused_computation.13 | convolution fusion | flops 100859904 | bytes 4973056 | tf_op jit(solution)/shard_map/ipq,miq->mip/dot_general | solution.py:129
  67.4 1.4 fusion.10
  68.9 2.7 %fusion.71 = f32[16,16,256]{2,0,1:T(8,128)S(1)} fusion(f32[16,16,256]{2,1,0:T(8,128)S(1)} %fusion.2, f32[16,16,256]{2,1,0:T(8,128)S(1)} %fusion.6, f32[16,16,256]{2,1,0:T(8,128)S(1)} %fusion.10, f32[16,16,256]{2,1,0:T(8,128)S(1)} %copy-done.12, f32[17,256,256]{2,1,0:T(8,128)S(1)} %bitcast.177, f32[16,6,320]{2,0,1:T(8,128)} %collective-permute-done, ...), kind=kOutput, calls=%fused_computation.58 | convolution fusion | flops 101253120 | bytes 6234176 | tf_op jit(solution)/shard_map/ipq,miq->mip/dot_general | solution.py:129
  73.9 5.8 %fusion.16 = f32[16,16,256]{2,1,0:T(8,128)} fusion(f32[16,256]{1,0:T(8,128)S(1)} %copy-done.20, f32[16,256]{1,0:T(8,128)S(1)} %copy-done.22, f32[16,256]{1,0:T(8,128)S(1)} %copy-done.18, f32[16,16,256]{2,0,1:T(8,128)S(1)} %get-tuple-element.49, f32[16]{0:T(128)S(1)} %copy-done.33), kind=kOutput, calls=%fused_computation.23 | convolution fusion | flops 113311744 | bytes 573504 | tf_op jit(solution)/shard_map/ipq,miq->mip/dot_general | solution.py:122
  79.9 3.2 %collective-permute-start.4 = (f32[16,6,320]{2,0,1:T(8,128)S(1)}, f32[16,6,320]{2,0,1:T(8,128)S(1)}, u32[]{:S(2)}, u32[]{:S(2)}) collective-permute-start(f32[16,6,320]{2,0,1:T(8,128)S(1)} %get-tuple-element.22), channel_id=1, source_target_pairs={{1,0},{2,1},{3,2},{4,3},{5,4},{6,5},{7,6},{8,7},{9,8},{10,9},{11,1... | collective-permute-start | bytes 368648 | tf_op jit(solution)/shard_map/ppermute | solution.py:26
  84.1 7.0 %all-to-all-start.1 = ((f32[16,1,2080]{2,1,0:T(1,128)}), f32[16,1,2080]{2,1,0:T(1,128)}, u32[]{:S(2)}, u32[]{:S(2)}) async-start(f32[16,1,2080]{2,1,0:T(1,128)} %broadcast_in_dim.34), calls=%async_computation.1 | async-start | bytes 278528 | tf_op jit(solution)/shard_map/all_to_all | solution.py:36
  91.8 1.4 gather_fusion.2
  93.2 3.5 %fusion = f32[16,16,256]{2,1,0:T(8,128)S(1)} fusion(f32[18,256,256]{2,1,0:T(8,128)} %exponential_multiply_fusion, f32[16,6,320]{2,0,1:T(8,128)} %copy-done.7, f32[16,16,64]{2,0,1:T(8,128)S(1)} %convolution_bitcast_fusion.8, f32[16,16,256]{2,0,1:T(8,128)S(1)} %get-tuple-element.49, f32[16]{0:T(128)} %get-tuple-element.44), kind=kOutput, calls=%fused_computation.7 | convolution fusion | flops 100859904 | bytes 4932096 | tf_op jit(solution)/shard_map/iqp,miq->mip/dot_general | solution.py:132
  96.7 4.0 %fusion.4 = f32[16,16,256]{2,1,0:T(8,128)S(1)} fusion(f32[18,256,256]{2,1,0:T(8,128)} %exponential_multiply_fusion, f32[16,6,320]{2,0,1:T(8,128)S(1)} %collective-permute-done.4, f32[16,16,64]{2,0,1:T(8,128)S(1)} %convolution_bitcast_fusion.8, f32[16,16,256]{2,0,1:T(8,128)S(1)} %get-tuple-element.49, f32[16]{0:T(128)S(1)} %copy-done.27), kind=kOutput, calls=%fused_computation.11 | convolution fusion | flops 100859904 | bytes 4907072 | tf_op jit(solution)/shard_map/ipq,miq->mip/dot_general | solution.py:129
  102.0 2.5 %fusion.62 = f32[16,16,256]{2,0,1:T(8,128)} fusion(f32[16,16,256]{2,1,0:T(8,128)S(1)} %fusion, f32[16,16,256]{2,1,0:T(8,128)S(1)} %fusion.4, f32[16,16,256]{2,1,0:T(8,128)S(1)} %fusion.8, f32[16,16,256]{2,1,0:T(8,128)S(1)} %copy-done.13, f32[17,256,256]{2,1,0:T(8,128)S(1)} %bitcast.179, f32[16,6,320]{2,0,1:T(8,128)S(1)} %collective-permute-done.4, ...), kind=kOutput, calls=%fused_computation.55 | convolution fusion | flops 101253120 | bytes 6234176 | tf_op jit(solution)/shard_map/ipq,miq->mip/dot_general | solution.py:129
  107.1 10.1 %all-to-all-start.2 = ((f32[32,2,16]{2,1,0:T(2,128)}), f32[32,2,16]{2,1,0:T(2,128)}, u32[]{:S(2)}, u32[]{:S(2)}) async-start(f32[32,2,16]{2,1,0:T(2,128)} %broadcast_in_dim.36), calls=%async_computation.2 | async-start | bytes 65536 | tf_op jit(solution)/shard_map/all_to_all | solution.py:36
  118.1 1.6 gather_fusion.3
  120.1 1.6 fusion.74
  121.7 7.6 %all-to-all-done.2 = f32[32,2,16]{2,1,0:T(2,128)} async-done(((f32[32,2,16]{2,1,0:T(2,128)}), f32[32,2,16]{2,1,0:T(2,128)}, u32[]{:S(2)}, u32[]{:S(2)}) %all-to-all-start.2) | async-done | bytes 4128 | tf_op jit(solution)/shard_map/all_to_all | solution.py:36
  130.1 1.8 %multiply_reduce_fusion.3 = (f32[16]{0:T(128)S(1)}, f32[16]{0:T(128)S(1)}, f32[16]{0:T(128)S(1)}, f32[16]{0:T(128)S(1)}, f32[16,16,256]{2,0,1:T(8,128)S(1)}) fusion(f32[16,16,256]{2,0,1:T(8,128)S(1)} %get-tuple-element.49, f32[16]{0:T(128)S(1)} %bitcast_divide_fusion.1, f32[16,16,256]{2,1,0:T(8,128)S(1)} %copy-done.2, f32[16,16,256]{2,0,1:T(8,128)S(1)} %copy-done.9, ...), kind=kOutput, calls=%fused_computation.117 | convolution fusion | flops 26017728 | bytes 2163008 | tf_op jit(solution)/shard_map/lpr,mlr->mlp/dot_general | solution.py:160
  132.0 17.4 %all_to_all.30 = f32[32,4,16]{2,1,0:T(4,128)S(1)} all-to-all(f32[32,4,16]{2,1,0:T(4,128)S(1)} %broadcast_in_dim.37), channel_id=1, replica_groups=mesh['band'=16,'lon'=32] {'lon'}, dimensions={0} | all-to-all | bytes 16384 | tf_op jit(solution)/shard_map/all_to_all | solution.py:36
  149.5 13.2 %all_to_all.31 = f32[16,4,16]{2,1,0:T(4,128)S(1)} all-to-all(f32[16,4,16]{2,1,0:T(4,128)S(1)} %broadcast_in_dim.38), channel_id=1, replica_groups=mesh['band'=16,'lon'=32] {'band'}, dimensions={0} | all-to-all | bytes 8192 | tf_op jit(solution)/shard_map/all_to_all | solution.py:36
  (160 shorter events, 26.3 us)
Async XLA Ops:
  0.6 56.7 %copy-start = (f32[16,4,64,64]{3,2,1,0:T(8,128)S(1)}, f32[16,4,64,64]{3,2,1,0:T(8,128)}, u32[]{:S(2)}) copy-start(f32[16,4,64,64]{3,2,1,0:T(8,128)} %param.15) | copy-start | bytes 3145732
  0.6 27.9 %copy-start.2 = (f32[16,16,256]{2,1,0:T(8,128)S(1)}, f32[16,16,256]{2,1,0:T(8,128)}, u32[]{:S(2)}) copy-start(f32[16,16,256]{2,1,0:T(8,128)} %param.11) | copy-start | bytes 786436
  0.7 28.7 %copy-start.16 = (s32[16,5]{0,1:T(8,128)S(1)}, s32[16,5]{0,1:T(8,128)}, u32[]{:S(2)}) copy-start(s32[16,5]{0,1:T(8,128)} %param.18) | copy-start | bytes 964
  0.7 29.4 %copy-start.30 = (s32[16,4]{0,1:T(4,128)S(1)}, s32[16,4]{0,1:T(4,128)}, u32[]{:S(2)}) copy-start(s32[16,4]{0,1:T(4,128)} %param.19) | copy-start | bytes 772
  0.7 30.2 %copy-start.31 = (s32[2,2]{1,0:T(2,128)S(1)}, s32[2,2]{1,0:T(2,128)}, u32[]{:S(2)}) copy-start(s32[2,2]{1,0:T(2,128)} %param.20) | copy-start | bytes 52
  1.6 35.6 %collective-permute-start.2 = (f32[3,2,256]{2,1,0:T(2,128)S(1)}, f32[3,2,256]{2,1,0:T(2,128)S(1)}, u32[]{:S(2)}, u32[]{:S(2)}) collective-permute-start(f32[3,2,256]{2,1,0:T(2,128)S(1)} %get-tuple-element.42), channel_id=1, source_target_pairs={{1,0},{2,1},{3,2},{4,3},{5,4},{6,5},{7,6},{8,7},{9,8},{10,9},{11,1... | collective-permute-start | bytes 18440 | tf_op jit(solution)/shard_map/ppermute | solution.py:26
  8.5 28.8 %collective-permute-start.1 = (f32[3,2,256]{2,1,0:T(2,128)S(1)}, f32[3,2,256]{2,1,0:T(2,128)S(1)}, u32[]{:S(2)}, u32[]{:S(2)}) collective-permute-start(f32[3,2,256]{2,1,0:T(2,128)S(1)} %get-tuple-element.41), channel_id=1, source_target_pairs={{0,1},{1,2},{2,3},{3,4},{4,5},{5,6},{6,7},{7,8},{8,9},{9,10},{10,1... | collective-permute-start | bytes 18440 | tf_op jit(solution)/shard_map/ppermute | solution.py:24
  12.3 42.0 %collective-permute-start.3 = (f32[16,6,320]{2,0,1:T(8,128)}, f32[16,6,320]{2,0,1:T(8,128)S(1)}, u32[]{:S(2)}, u32[]{:S(2)}) collective-permute-start(f32[16,6,320]{2,0,1:T(8,128)} %get-tuple-element.25), channel_id=1, source_target_pairs={{0,1},{1,2},{2,3},{3,4},{4,5},{5,6},{6,7},{7,8},{8,9},{9,10},{10,1... | collective-permute-start | bytes 368648 | tf_op jit(solution)/shard_map/ppermute | solution.py:24
  12.3 42.7 %collective-permute-start = (f32[16,6,320]{2,0,1:T(8,128)}, f32[16,6,320]{2,0,1:T(8,128)}, u32[]{:S(2)}, u32[]{:S(2)}) collective-permute-start(f32[16,6,320]{2,0,1:T(8,128)} %get-tuple-element.24), channel_id=1, source_target_pairs={{1,0},{2,1},{3,2},{4,3},{5,4},{6,5},{7,6},{8,7},{9,8},{10,9},{11,1... | collective-permute-start | bytes 368648 | tf_op jit(solution)/shard_map/ppermute | solution.py:26
  18.8 28.3 %all-to-all-start = ((f32[16,1,2048]{2,1,0:T(1,128)}), f32[16,1,2048]{2,1,0:T(1,128)S(1)}, u32[]{:S(2)}, u32[]{:S(2)}) async-start(f32[16,1,2048]{2,1,0:T(1,128)} %broadcast_in_dim.32), calls=%async_computation | async-start | bytes 262144 | tf_op jit(solution)/shard_map/all_to_all | solution.py:36
  28.6 8.1 %copy-start.17 = (f32[16,256]{1,0:T(8,128)}, f32[16,256]{1,0:T(8,128)S(1)}, u32[]{:S(2)}) copy-start(f32[16,256]{1,0:T(8,128)S(1)} %get-tuple-element.38) | copy-start | bytes 49156
  28.6 8.1 %copy-start.19 = (f32[16,256]{1,0:T(8,128)}, f32[16,256]{1,0:T(8,128)S(1)}, u32[]{:S(2)}) copy-start(f32[16,256]{1,0:T(8,128)S(1)} %get-tuple-element.39) | copy-start | bytes 49156
  28.6 8.1 %copy-start.21 = (f32[16,256]{1,0:T(8,128)}, f32[16,256]{1,0:T(8,128)S(1)}, u32[]{:S(2)}) copy-start(f32[16,256]{1,0:T(8,128)S(1)} %get-tuple-element.40) | copy-start | bytes 49156
  30.0 6.6 %copy-start.32 = (f32[16]{0:T(128)}, f32[16]{0:T(128)S(1)}, u32[]{:S(2)}) copy-start(f32[16]{0:T(128)S(1)} %get-tuple-element.47) | copy-start | bytes 196
  30.9 6.4 %copy-start.10 = (f32[3,16,256]{2,1,0:T(8,128)S(1)}, f32[3,16,256]{2,1,0:T(8,128)}, u32[]{:S(2)}) copy-start(f32[3,16,256]{2,1,0:T(8,128)} %param.13) | copy-start | bytes 147460
  47.5 17.3 %slice-start.4 = ((s8[4718592]{0:T(1024)(128)(4,1)}), s8[524288]{0:T(1024)(128)(4,1)S(1)}, s32[]{:S(2)}) async-start(s8[4718592]{0:T(1024)(128)(4,1)} %bitcast.180), calls=%async_computation.9 | async-start | bytes 1048576
  48.4 12.9 %copy-start.28 = (f32[16]{0:T(128)S(1)}, f32[16]{0:T(128)}, u32[]{:S(2)}) copy-start(f32[16]{0:T(128)} %get-tuple-element.44) | copy-start | bytes 196
  57.4 7.4 %slice-start.5 = ((s8[4718592]{0:T(1024)(128)(4,1)}), s8[4194304]{0:T(1024)(128)(4,1)S(1)}, s32[]{:S(2)}) async-start(s8[4718592]{0:T(1024)(128)(4,1)} %bitcast.180), calls=%async_computation.10 | async-start | bytes 8388608
  57.4 7.4 %copy-start.26 = (f32[16]{0:T(128)S(1)}, f32[16]{0:T(128)}, u32[]{:S(2)}) copy-start(f32[16]{0:T(128)} %get-tuple-element.45) | copy-start | bytes 196
  59.5 7.9 %slice-start = ((s8[4456448]{0:T(1024)(128)(4,1)}), s8[4194304]{0:T(1024)(128)(4,1)S(1)}, s32[]{:S(2)}) async-start(s8[4456448]{0:T(1024)(128)(4,1)} %bitcast.176), calls=%async_computation.5 | async-start | bytes 8388608
  73.8 9.3 %copy-start.29 = (f32[16]{0:T(128)S(1)}, f32[16]{0:T(128)}, u32[]{:S(2)}) copy-start(f32[16]{0:T(128)} %multiply_reduce_fusion.5) | copy-start | bytes 196
  73.8 17.9 %copy-start.14 = (s32[1024]{0:T(1024)S(1)}, s32[1024]{0:T(1024)}, u32[]{:S(2)}) copy-start(s32[1024]{0:T(1024)} %pad_clamp_fusion.1) | copy-start | bytes 12292
  79.9 16.9 %copy-start.27 = (f32[16]{0:T(128)S(1)}, f32[16]{0:T(128)}, u32[]{:S(2)}) copy-start(f32[16]{0:T(128)} %get-tuple-element.45) | copy-start | bytes 196
  79.9 11.2 %collective-permute-start.5 = (f32[16,6,320]{2,0,1:T(8,128)}, f32[16,6,320]{2,0,1:T(8,128)S(1)}, u32[]{:S(2)}, u32[]{:S(2)}) collective-permute-start(f32[16,6,320]{2,0,1:T(8,128)} %get-tuple-element.23), channel_id=1, source_target_pairs={{0,1},{1,2},{2,3},{3,4},{4,5},{5,6},{6,7},{7,8},{8,9},{9,10},{10,1... | collective-permute-start | bytes 368648 | tf_op jit(solution)/shard_map/ppermute | solution.py:24
  79.9 11.2 %collective-permute-start.4 = (f32[16,6,320]{2,0,1:T(8,128)S(1)}, f32[16,6,320]{2,0,1:T(8,128)S(1)}, u32[]{:S(2)}, u32[]{:S(2)}) collective-permute-start(f32[16,6,320]{2,0,1:T(8,128)S(1)} %get-tuple-element.22), channel_id=1, source_target_pairs={{1,0},{2,1},{3,2},{4,3},{5,4},{6,5},{7,6},{8,7},{9,8},{10,9},{11,1... | collective-permute-start | bytes 368648 | tf_op jit(solution)/shard_map/ppermute | solution.py:26
  84.1 21.3 %all-to-all-start.1 = ((f32[16,1,2080]{2,1,0:T(1,128)}), f32[16,1,2080]{2,1,0:T(1,128)}, u32[]{:S(2)}, u32[]{:S(2)}) async-start(f32[16,1,2080]{2,1,0:T(1,128)} %broadcast_in_dim.34), calls=%async_computation.1 | async-start | bytes 278528 | tf_op jit(solution)/shard_map/all_to_all | solution.py:36
  91.7 9.0 %slice-start.2 = ((s8[4456448]{0:T(1024)(128)(4,1)}), s8[262144]{0:T(1024)(128)(4,1)S(1)}, s32[]{:S(2)}) async-start(s8[4456448]{0:T(1024)(128)(4,1)} %bitcast.178), calls=%async_computation.7 | async-start | bytes 524288
  93.2 7.5 %slice-start.3 = ((s8[4456448]{0:T(1024)(128)(4,1)}), s8[4194304]{0:T(1024)(128)(4,1)S(1)}, s32[]{:S(2)}) async-start(s8[4456448]{0:T(1024)(128)(4,1)} %bitcast.178), calls=%async_computation.8 | async-start | bytes 8388608
  93.2 7.6 %copy-start.8 = (f32[16,6,320]{2,0,1:T(8,128)S(1)}, f32[16,6,320]{2,0,1:T(8,128)}, u32[]{:S(2)}) copy-start(f32[16,6,320]{2,0,1:T(8,128)} %copy-done.7) | copy-start | bytes 368644
  104.5 15.3 %copy-start.11 = (f32[2,2,64,64]{3,2,1,0:T(8,128)S(1)}, f32[2,2,64,64]{3,2,1,0:T(8,128)}, u32[]{:S(2)}) copy-start(f32[2,2,64,64]{3,2,1,0:T(8,128)} %param.17) | copy-start | bytes 196612
  104.5 25.7 %copy-start.9 = (f32[16,16,256]{2,0,1:T(8,128)S(1)}, f32[16,16,256]{2,0,1:T(8,128)}, u32[]{:S(2)}) copy-start(f32[16,16,256]{2,0,1:T(8,128)} %fusion.62) | copy-start | bytes 786436
  107.1 22.3 %all-to-all-start.2 = ((f32[32,2,16]{2,1,0:T(2,128)}), f32[32,2,16]{2,1,0:T(2,128)}, u32[]{:S(2)}, u32[]{:S(2)}) async-start(f32[32,2,16]{2,1,0:T(2,128)} %broadcast_in_dim.36), calls=%async_computation.2 | async-start | bytes 65536 | tf_op jit(solution)/shard_map/all_to_all | solution.py:36
  (17 other events, 71.8 us)

commit v12 on v8

--- a/solution.py
+++ b/solution.py
@@ -136,7 +136,7 @@
             "lsab,mlsb->mla", leaf_couple, rim_coeffs[:, far_rows], precision=MATMUL_PRECISION
         )
         upward = jnp.einsum("lab,mla->mlb", transfer, coeffs, precision=MATMUL_PRECISION)
-        panel_coeffs = jnp.einsum("lk,mlb->mkb", membership, upward, precision=MATMUL_PRECISION)
+        panel_coeffs = jnp.sum(membership[None, :, :, None] * upward[:, :, None, :], axis=1)
         return direction, near_part, leaf_far, panel_coeffs
 
     def band_layout(band_panels, panel_coeffs):
@@ -153,7 +153,7 @@
             band_coeffs[:, gathered_rows],
             precision=MATMUL_PRECISION,
         )
-        downward = jnp.einsum("lk,mkb->mlb", membership, panel_far, precision=MATMUL_PRECISION)
+        downward = jnp.sum(membership[None, :, :, None] * panel_far[:, None, :, :], axis=2)
         leaf_far = leaf_far + jnp.einsum(
             "lab,mlb->mla", transfer, downward, precision=MATMUL_PRECISION
         )

time: 166 us -> 163 us (0.982)
  matrix products: 49.8 us -> 47 us
  local copies, waits for them, and re-layouts: 21.3 us -> 19.2 us
  other arithmetic: 15.7 us -> 17.5 us
    dot_general x4 -> x0, matrix products: 2.79 us -> none  [the longest x2 1.79 us: covariance_finish(): jnp.einsum('lk,mkb->mlb', membership, panel_far, precision=MATMUL_PRECISION)]
    reduce_sum x0 -> x4, other arithmetic: none -> 1.78 us  [the longest x2 1.52 us: covariance_finish(): jnp.sum(membership[None, :, :, None] * panel_far[:, None, :, :], axis=2)]
    unnamed x83 -> x85, local copies, waits for them, and re-layouts: 6.06 us -> 5.26 us
  transfers between devices with their start and end apart: 9 -> 9, of which waited for: 1 -> 1; matrix products, arithmetic and copies ran while one was open for 30% -> 29% of each run, Pallas kernels for 0% -> 0%
where the time goes in v12:
time: 163 us; the launch traced here: 161 us
  matrix products  47 us (29%)
  starting transfers between devices  35.9 us (22%)
  blocking collectives  30.3 us (19%)
  local copies, waits for them, and re-layouts  19.2 us (12%)
  other arithmetic  17.5 us (11%)
  waiting for transfers between devices  10.2 us (6%)
    all_to_all x2, blocking collectives, gathered(): return lax.all_to_all(copies, axis, 0, 0, tiled=False)  30.3 us
    all_to_all x3, starting transfers between devices, gathered(): return lax.all_to_all(copies, axis, 0, 0, tiled=False)  23.8 us
    dot_general x4, matrix products, covariance_local(): jnp.einsum('ipq,miq->mip', ahead, offset_values(step), precision=MATMUL_P...  11.7 us
    dot_general x2, matrix products, covariance_local(): jnp.einsum('ipq,miq->mip', same_blocks, offset_values(0), precision=MATMU...  11.5 us
    ppermute x3, starting transfers between devices, extended(): lax.ppermute(head, axis, [((i + 1) % count, i) for i in range(count)])  10.4 us
    all_to_all x3, waiting for transfers between devices, gathered(): return lax.all_to_all(copies, axis, 0, 0, tiled=False)  10.2 us
    mul x2, other arithmetic, matern_shape(): return (1.0 + scaled) * jnp.exp(-scaled)  9.83 us
    dot_general x4, matrix products, covariance_local(): jnp.einsum('iqp,miq->mip', behind, offset_values(-step), precision=MATMUL...  9.56 us
  transfers between devices with their start and end apart: 9, of which 1 were waited for; matrix products, arithmetic and copies ran while one was open for 29% of the time, Pallas kernels for 0%

profile of v12, /device:TPU:1, one launch (start us, length us, event | category | flops | bytes accessed | tf_op | source)
XLA Modules:
  0.0 161.5 jit_solution(2160063527869284389)
XLA Ops:
  1.6 6.9 %collective-permute-start.2 = (f32[3,2,256]{2,1,0:T(2,128)S(1)}, f32[3,2,256]{2,1,0:T(2,128)S(1)}, u32[]{:S(2)}, u32[]{:S(2)}) collective-permute-start(f32[3,2,256]{2,1,0:T(2,128)S(1)} %get-tuple-element.42), channel_id=1, source_target_pairs={{1,0},{2,1},{3,2},{4,3},{5,4},{6,5},{7,6},{8,7},{9,8},{10,9},{11,1... | collective-permute-start | bytes 18440 | tf_op jit(solution)/shard_map/ppermute | solution.py:26
  9.6 1.9 %convolution_bitcast_fusion.7 = f32[16,16,64]{2,0,1:T(8,128)S(1)} fusion(f32[16,256,64]{1,2,0:T(8,128)} %param.14, f32[16,16,256]{2,1,0:T(8,128)} %param.11), kind=kOutput, calls=%fused_computation.68 | convolution fusion | flops 25165824 | bytes 1376256 | tf_op jit(solution)/shard_map/lpr,mlp->mlr/dot_general | solution.py:109
  12.3 3.6 %collective-permute-start = (f32[16,6,320]{2,0,1:T(8,128)}, f32[16,6,320]{2,0,1:T(8,128)}, u32[]{:S(2)}, u32[]{:S(2)}) collective-permute-start(f32[16,6,320]{2,0,1:T(8,128)} %get-tuple-element.24), channel_id=1, source_target_pairs={{1,0},{2,1},{3,2},{4,3},{5,4},{6,5},{7,6},{8,7},{9,8},{10,9},{11,1... | collective-permute-start | bytes 368648 | tf_op jit(solution)/shard_map/ppermute | solution.py:26
  15.8 1.4 convolution_bitcast_fusion.4
  18.9 6.8 %all-to-all-start = ((f32[16,1,2048]{2,1,0:T(1,128)}), f32[16,1,2048]{2,1,0:T(1,128)S(1)}, u32[]{:S(2)}, u32[]{:S(2)}) async-start(f32[16,1,2048]{2,1,0:T(1,128)} %broadcast_in_dim.30), calls=%async_computation | async-start | bytes 262144 | tf_op jit(solution)/shard_map/all_to_all | solution.py:36
  28.0 5.7 %fusion.17 = f32[16,16,256]{2,1,0:T(8,128)} fusion(f32[16,256]{1,0:T(8,128)S(1)} %get-tuple-element.39, f32[16,256]{1,0:T(8,128)S(1)} %get-tuple-element.40, f32[16,256]{1,0:T(8,128)S(1)} %get-tuple-element.38, f32[16]{0:T(128)S(1)} %get-tuple-element.47, f32[16,16,256]{2,1,0:T(8,128)S(1)} %copy-done.2), kind=kOutput, calls=%fused_computation.24 | convolution fusion | flops 113311744 | bytes 573504 | tf_op jit(solution)/shard_map/ipq,miq->mip/dot_general | solution.py:122
  34.4 5.2 %exponential_multiply_fusion = f32[18,256,256]{2,1,0:T(8,128)} fusion(f32[18,256]{1,0:T(8,128)S(1)} %get-tuple-element.30, f32[18,256]{1,0:T(8,128)S(1)} %get-tuple-element.36, f32[18,256]{1,0:T(8,128)S(1)} %get-tuple-element.31, f32[18,256]{1,0:T(8,128)S(1)} %get-tuple-element.37, f32[18,256]{1,0:T(8,128)S(1)} %get-tuple-element.29, ...), kind=kLoop, calls=%fused_computation.4 | loop fusion | flops 14155776 | bytes 4829184 | tf_op jit(solution)/shard_map/mul | solution.py:51
  39.6 4.6 %exponential_multiply_fusion.1 = f32[17,256,256]{2,1,0:T(8,128)} fusion(f32[17,256]{1,0:T(8,128)S(1)} %get-tuple-element.27, f32[17,256]{1,0:T(8,128)S(1)} %get-tuple-element.34, f32[17,256]{1,0:T(8,128)S(1)} %get-tuple-element.28, f32[17,256]{1,0:T(8,128)S(1)} %get-tuple-element.33, f32[17,256]{1,0:T(8,128)S(1)} %get-tuple-element.26, ...), kind=kLoop, calls=%fused_computation.5 | loop fusion | flops 13369344 | bytes 4560896 | tf_op jit(solution)/shard_map/mul | solution.py:51
  45.5 1.7 %copy.111 = f32[16,16,2,64]{3,0,2,1:T(8,128)} copy(f32[16,16,2,64]{3,2,0,1:T(2,128)} %bitcast.158) | data formatting | bytes 262144 | tf_op jit(solution)/shard_map/transpose | solution.py:144
  47.1 1.6 %gather_fusion.1 = f32[4,16,64]{2,1,0:T(8,128)S(1)} fusion(f32[16,32,64]{2,0,1:T(8,128)} %bitcast.163, s32[1024]{0:T(1024)} %pad_clamp_fusion), kind=kCustom, calls=%fused_computation.1 | custom fusion | bytes 32784 | tf_op jit(solution)/shard_map/gather | solution.py:153
  49.9 1.4 multiply_reduce_fusion.8
  52.8 1.6 gather_fusion
  54.4 2.1 %convolution_bitcast_fusion.5 = f32[16,16,64]{2,1,0:T(8,128)S(1)} fusion(f32[16,16,4,64]{3,0,2,1:T(8,128)} %bitcast.157, f32[16,4,64,64]{3,2,1,0:T(8,128)S(1)} %copy-done), kind=kOutput, calls=%fused_computation.66 | convolution fusion | flops 25165824 | bytes 1376256 | tf_op jit(solution)/shard_map/lsab,mlsb->mla/dot_general | solution.py:135
  56.5 1.8 %fusion.75 = f32[16,16,64]{2,0,1:T(8,128)S(1)} fusion(f32[16,16,64]{2,1,0:T(8,128)S(1)} %convolution_bitcast_fusion.5, f32[16,64,64]{2,1,0:T(8,128)} %param.16, f32[16,16,64]{2,1,0:T(8,128)} %multiply_reduce_fusion.8), kind=kOutput, calls=%fused_computation.64 | convolution fusion | flops 6307840 | bytes 458752 | tf_op jit(solution)/shard_map/lab,mlb->mla/dot_general | solution.py:157
  58.3 3.4 %fusion.2 = f32[16,16,256]{2,1,0:T(8,128)S(1)} fusion(f32[18,256,256]{2,1,0:T(8,128)} %exponential_multiply_fusion, f32[16,6,320]{2,0,1:T(8,128)} %copy-done.5, f32[16,16,64]{2,0,1:T(8,128)S(1)} %convolution_bitcast_fusion.7, f32[16,16,256]{2,0,1:T(8,128)S(1)} %copy.105, f32[16]{0:T(128)S(1)} %copy-done.28), kind=kOutput, calls=%fused_computation.9 | convolution fusion | flops 100859904 | bytes 4931648 | tf_op jit(solution)/shard_map/iqp,miq->mip/dot_general | solution.py:132
  61.8 2.5 %fusion.6 = f32[16,16,256]{2,1,0:T(8,128)S(1)} fusion(f32[18,256,256]{2,1,0:T(8,128)S(1)} %bitcast.155, f32[16,6,320]{2,0,1:T(8,128)} %collective-permute-done, f32[16,16,64]{2,0,1:T(8,128)S(1)} %convolution_bitcast_fusion.7, f32[16,16,256]{2,0,1:T(8,128)S(1)} %copy.105, f32[16]{0:T(128)S(1)} %copy-done.27), kind=kOutput, calls=%fused_computation.13 | convolution fusion | flops 100859904 | bytes 4973056 | tf_op jit(solution)/shard_map/ipq,miq->mip/dot_general | solution.py:129
  64.4 1.4 fusion.10
  65.9 2.7 %fusion.71 = f32[16,16,256]{2,0,1:T(8,128)S(1)} fusion(f32[16,16,256]{2,1,0:T(8,128)S(1)} %fusion.2, f32[16,16,256]{2,1,0:T(8,128)S(1)} %fusion.6, f32[16,16,256]{2,1,0:T(8,128)S(1)} %fusion.10, f32[16,16,256]{2,1,0:T(8,128)S(1)} %copy-done.12, f32[17,256,256]{2,1,0:T(8,128)S(1)} %bitcast.151, f32[16,6,320]{2,0,1:T(8,128)} %collective-permute-done, ...), kind=kOutput, calls=%fused_computation.58 | convolution fusion | flops 101253120 | bytes 6234176 | tf_op jit(solution)/shard_map/ipq,miq->mip/dot_general | solution.py:129
  70.8 5.8 %fusion.16 = f32[16,16,256]{2,1,0:T(8,128)} fusion(f32[16,256]{1,0:T(8,128)S(1)} %copy-done.22, f32[16,256]{1,0:T(8,128)S(1)} %copy-done.24, f32[16,256]{1,0:T(8,128)S(1)} %copy-done.20, f32[16,16,256]{2,0,1:T(8,128)S(1)} %get-tuple-element.49, f32[16]{0:T(128)S(1)} %copy-done.33), kind=kOutput, calls=%fused_computation.23 | convolution fusion | flops 113311744 | bytes 573504 | tf_op jit(solution)/shard_map/ipq,miq->mip/dot_general | solution.py:122
  77.3 10.1 %all-to-all-start.1 = ((f32[32,2,16]{2,1,0:T(2,128)}), f32[32,2,16]{2,1,0:T(2,128)S(1)}, u32[]{:S(2)}, u32[]{:S(2)}) async-start(f32[32,2,16]{2,1,0:T(2,128)} %broadcast_in_dim.32), calls=%async_computation.1 | async-start | bytes 65536 | tf_op jit(solution)/shard_map/all_to_all | solution.py:36
  87.4 1.6 %collective-permute-start.5 = (f32[16,6,320]{2,0,1:T(8,128)}, f32[16,6,320]{2,0,1:T(8,128)S(1)}, u32[]{:S(2)}, u32[]{:S(2)}) collective-permute-start(f32[16,6,320]{2,0,1:T(8,128)} %get-tuple-element.23), channel_id=1, source_target_pairs={{0,1},{1,2},{2,3},{3,4},{4,5},{5,6},{6,7},{7,8},{8,9},{9,10},{10,1... | collective-permute-start | bytes 368648 | tf_op jit(solution)/shard_map/ppermute | solution.py:24
  89.3 10.2 %all-to-all-done.1 = f32[32,2,16]{2,1,0:T(2,128)S(1)} async-done(((f32[32,2,16]{2,1,0:T(2,128)}), f32[32,2,16]{2,1,0:T(2,128)S(1)}, u32[]{:S(2)}, u32[]{:S(2)}) %all-to-all-start.1) | async-done | bytes 4128 | tf_op jit(solution)/shard_map/all_to_all | solution.py:36
  100.4 7.0 %all-to-all-start.2 = ((f32[16,1,2080]{2,1,0:T(1,128)}), f32[16,1,2080]{2,1,0:T(1,128)}, u32[]{:S(2)}, u32[]{:S(2)}) async-start(f32[16,1,2080]{2,1,0:T(1,128)} %broadcast_in_dim.33), calls=%async_computation.2 | async-start | bytes 278528 | tf_op jit(solution)/shard_map/all_to_all | solution.py:36
  108.1 1.4 gather_fusion.2
  109.5 3.5 %fusion = f32[16,16,256]{2,1,0:T(8,128)S(1)} fusion(f32[18,256,256]{2,1,0:T(8,128)} %exponential_multiply_fusion, f32[16,6,320]{2,0,1:T(8,128)} %copy-done.7, f32[16,16,64]{2,0,1:T(8,128)S(1)} %convolution_bitcast_fusion.6, f32[16,16,256]{2,0,1:T(8,128)S(1)} %get-tuple-element.49, f32[16]{0:T(128)} %get-tuple-element.44), kind=kOutput, calls=%fused_computation.7 | convolution fusion | flops 100859904 | bytes 4932096 | tf_op jit(solution)/shard_map/iqp,miq->mip/dot_general | solution.py:132
  113.0 4.0 %fusion.4 = f32[16,16,256]{2,1,0:T(8,128)S(1)} fusion(f32[18,256,256]{2,1,0:T(8,128)} %exponential_multiply_fusion, f32[16,6,320]{2,0,1:T(8,128)S(1)} %collective-permute-done.4, f32[16,16,64]{2,0,1:T(8,128)S(1)} %convolution_bitcast_fusion.6, f32[16,16,256]{2,0,1:T(8,128)S(1)} %get-tuple-element.49, f32[16]{0:T(128)} %get-tuple-element.45), kind=kOutput, calls=%fused_computation.11 | convolution fusion | flops 100859904 | bytes 4907520 | tf_op jit(solution)/shard_map/ipq,miq->mip/dot_general | solution.py:129
  118.3 2.5 %fusion.62 = f32[16,16,256]{2,0,1:T(8,128)} fusion(f32[16,16,256]{2,1,0:T(8,128)S(1)} %fusion, f32[16,16,256]{2,1,0:T(8,128)S(1)} %fusion.4, f32[16,16,256]{2,1,0:T(8,128)S(1)} %fusion.8, f32[16,16,256]{2,1,0:T(8,128)S(1)} %copy-done.13, f32[17,256,256]{2,1,0:T(8,128)S(1)} %bitcast.153, f32[16,6,320]{2,0,1:T(8,128)S(1)} %collective-permute-done.4, ...), kind=kOutput, calls=%fused_computation.55 | convolution fusion | flops 101253120 | bytes 6234176 | tf_op jit(solution)/shard_map/ipq,miq->mip/dot_general | solution.py:129
  123.7 1.6 %gather_fusion.3 = f32[4,16,64]{2,1,0:T(8,128)S(1)} fusion(f32[16,32,64]{2,0,1:T(8,128)} %bitcast.162, s32[1024]{0:T(1024)} %pad_clamp_fusion), kind=kCustom, calls=%fused_computation.3 | custom fusion | bytes 32784 | tf_op jit(solution)/shard_map/gather | solution.py:153
  125.6 1.6 fusion.74
  127.1 1.8 %multiply_reduce_fusion.4 = (f32[16]{0:T(128)S(1)}, f32[16]{0:T(128)S(1)}, f32[16]{0:T(128)S(1)}, f32[16]{0:T(128)S(1)}, f32[16,16,256]{2,0,1:T(8,128)S(1)}) fusion(f32[16,16,256]{2,0,1:T(8,128)S(1)} %get-tuple-element.49, f32[16]{0:T(128)S(1)} %slice_divide_fusion, f32[16,16,256]{2,1,0:T(8,128)S(1)} %copy-done.2, f32[16,16,256]{2,0,1:T(8,128)S(1)} %copy-done.9, ...), kind=kOutput, calls=%fused_computation.114 | convolution fusion | flops 26017728 | bytes 2163008 | tf_op jit(solution)/shard_map/lpr,mlr->mlp/dot_general | solution.py:160
  129.0 17.2 %all_to_all.30 = f32[32,4,16]{2,1,0:T(4,128)S(1)} all-to-all(f32[32,4,16]{2,1,0:T(4,128)S(1)} %broadcast_in_dim.34), channel_id=1, replica_groups=mesh['band'=16,'lon'=32] {'lon'}, dimensions={0} | all-to-all | bytes 16384 | tf_op jit(solution)/shard_map/all_to_all | solution.py:36
  146.3 13.2 %all_to_all.31 = f32[16,4,16]{2,1,0:T(4,128)S(1)} all-to-all(f32[16,4,16]{2,1,0:T(4,128)S(1)} %broadcast_in_dim.35), channel_id=1, replica_groups=mesh['band'=16,'lon'=32] {'band'}, dimensions={0} | all-to-all | bytes 8192 | tf_op jit(solution)/shard_map/all_to_all | solution.py:36
  (164 shorter events, 22.5 us)
Async XLA Ops:
  0.6 53.7 %copy-start = (f32[16,4,64,64]{3,2,1,0:T(8,128)S(1)}, f32[16,4,64,64]{3,2,1,0:T(8,128)}, u32[]{:S(2)}) copy-start(f32[16,4,64,64]{3,2,1,0:T(8,128)} %param.15) | copy-start | bytes 3145732
  0.6 25.0 %copy-start.10 = (f32[3,16,256]{2,1,0:T(8,128)S(1)}, f32[3,16,256]{2,1,0:T(8,128)}, u32[]{:S(2)}) copy-start(f32[3,16,256]{2,1,0:T(8,128)} %param.13) | copy-start | bytes 147460
  0.7 25.1 %copy-start.2 = (f32[16,16,256]{2,1,0:T(8,128)S(1)}, f32[16,16,256]{2,1,0:T(8,128)}, u32[]{:S(2)}) copy-start(f32[16,16,256]{2,1,0:T(8,128)} %param.11) | copy-start | bytes 786436
  0.7 25.0 %copy-start.18 = (s32[16,5]{0,1:T(8,128)S(1)}, s32[16,5]{0,1:T(8,128)}, u32[]{:S(2)}) copy-start(s32[16,5]{0,1:T(8,128)} %param.18) | copy-start | bytes 964
  0.7 26.5 %copy-start.30 = (s32[16,4]{0,1:T(4,128)S(1)}, s32[16,4]{0,1:T(4,128)}, u32[]{:S(2)}) copy-start(s32[16,4]{0,1:T(4,128)} %param.19) | copy-start | bytes 772
  0.7 27.3 %copy-start.31 = (s32[2,2]{1,0:T(2,128)S(1)}, s32[2,2]{1,0:T(2,128)}, u32[]{:S(2)}) copy-start(s32[2,2]{1,0:T(2,128)} %param.20) | copy-start | bytes 52
  1.6 32.7 %collective-permute-start.2 = (f32[3,2,256]{2,1,0:T(2,128)S(1)}, f32[3,2,256]{2,1,0:T(2,128)S(1)}, u32[]{:S(2)}, u32[]{:S(2)}) collective-permute-start(f32[3,2,256]{2,1,0:T(2,128)S(1)} %get-tuple-element.42), channel_id=1, source_target_pairs={{1,0},{2,1},{3,2},{4,3},{5,4},{6,5},{7,6},{8,7},{9,8},{10,9},{11,1... | collective-permute-start | bytes 18440 | tf_op jit(solution)/shard_map/ppermute | solution.py:26
  8.5 25.9 %collective-permute-start.1 = (f32[3,2,256]{2,1,0:T(2,128)S(1)}, f32[3,2,256]{2,1,0:T(2,128)S(1)}, u32[]{:S(2)}, u32[]{:S(2)}) collective-permute-start(f32[3,2,256]{2,1,0:T(2,128)S(1)} %get-tuple-element.41), channel_id=1, source_target_pairs={{0,1},{1,2},{2,3},{3,4},{4,5},{5,6},{6,7},{7,8},{8,9},{9,10},{10,1... | collective-permute-start | bytes 18440 | tf_op jit(solution)/shard_map/ppermute | solution.py:24
  12.3 39.0 %collective-permute-start.3 = (f32[16,6,320]{2,0,1:T(8,128)}, f32[16,6,320]{2,0,1:T(8,128)S(1)}, u32[]{:S(2)}, u32[]{:S(2)}) collective-permute-start(f32[16,6,320]{2,0,1:T(8,128)} %get-tuple-element.25), channel_id=1, source_target_pairs={{0,1},{1,2},{2,3},{3,4},{4,5},{5,6},{6,7},{7,8},{8,9},{9,10},{10,1... | collective-permute-start | bytes 368648 | tf_op jit(solution)/shard_map/ppermute | solution.py:24
  12.3 39.7 %collective-permute-start = (f32[16,6,320]{2,0,1:T(8,128)}, f32[16,6,320]{2,0,1:T(8,128)}, u32[]{:S(2)}, u32[]{:S(2)}) collective-permute-start(f32[16,6,320]{2,0,1:T(8,128)} %get-tuple-element.24), channel_id=1, source_target_pairs={{1,0},{2,1},{3,2},{4,3},{5,4},{6,5},{7,6},{8,7},{9,8},{10,9},{11,1... | collective-permute-start | bytes 368648 | tf_op jit(solution)/shard_map/ppermute | solution.py:26
  17.9 15.8 %copy-start.16 = (f32[16,2]{0,1:T(2,128)}, f32[16,2]{0,1:T(2,128)S(1)}, u32[]{:S(2)}) copy-start(f32[16,2]{0,1:T(2,128)S(1)} %compare_convert_fusion) | copy-start | bytes 388
  18.9 25.4 %all-to-all-start = ((f32[16,1,2048]{2,1,0:T(1,128)}), f32[16,1,2048]{2,1,0:T(1,128)S(1)}, u32[]{:S(2)}, u32[]{:S(2)}) async-start(f32[16,1,2048]{2,1,0:T(1,128)} %broadcast_in_dim.30), calls=%async_computation | async-start | bytes 262144 | tf_op jit(solution)/shard_map/all_to_all | solution.py:36
  25.7 8.0 %copy-start.19 = (f32[16,256]{1,0:T(8,128)}, f32[16,256]{1,0:T(8,128)S(1)}, u32[]{:S(2)}) copy-start(f32[16,256]{1,0:T(8,128)S(1)} %get-tuple-element.38) | copy-start | bytes 49156
  25.7 8.0 %copy-start.21 = (f32[16,256]{1,0:T(8,128)}, f32[16,256]{1,0:T(8,128)S(1)}, u32[]{:S(2)}) copy-start(f32[16,256]{1,0:T(8,128)S(1)} %get-tuple-element.39) | copy-start | bytes 49156
  25.7 8.0 %copy-start.23 = (f32[16,256]{1,0:T(8,128)}, f32[16,256]{1,0:T(8,128)S(1)}, u32[]{:S(2)}) copy-start(f32[16,256]{1,0:T(8,128)S(1)} %get-tuple-element.40) | copy-start | bytes 49156
  27.1 6.6 %copy-start.32 = (f32[16]{0:T(128)}, f32[16]{0:T(128)S(1)}, u32[]{:S(2)}) copy-start(f32[16]{0:T(128)S(1)} %get-tuple-element.47) | copy-start | bytes 196
  44.6 17.2 %slice-start.4 = ((s8[4718592]{0:T(1024)(128)(4,1)}), s8[524288]{0:T(1024)(128)(4,1)S(1)}, s32[]{:S(2)}) async-start(s8[4718592]{0:T(1024)(128)(4,1)} %bitcast.154), calls=%async_computation.9 | async-start | bytes 1048576
  45.5 12.8 %copy-start.28 = (f32[16]{0:T(128)S(1)}, f32[16]{0:T(128)}, u32[]{:S(2)}) copy-start(f32[16]{0:T(128)} %get-tuple-element.44) | copy-start | bytes 196
  54.4 7.4 %slice-start.5 = ((s8[4718592]{0:T(1024)(128)(4,1)}), s8[4194304]{0:T(1024)(128)(4,1)S(1)}, s32[]{:S(2)}) async-start(s8[4718592]{0:T(1024)(128)(4,1)} %bitcast.154), calls=%async_computation.10 | async-start | bytes 8388608
  54.4 7.4 %copy-start.27 = (f32[16]{0:T(128)S(1)}, f32[16]{0:T(128)}, u32[]{:S(2)}) copy-start(f32[16]{0:T(128)} %get-tuple-element.45) | copy-start | bytes 196
  56.5 7.9 %slice-start = ((s8[4456448]{0:T(1024)(128)(4,1)}), s8[4194304]{0:T(1024)(128)(4,1)S(1)}, s32[]{:S(2)}) async-start(s8[4456448]{0:T(1024)(128)(4,1)} %bitcast.150), calls=%async_computation.5 | async-start | bytes 8388608
  58.3 6.1 %slice-start.1 = ((s8[4456448]{0:T(1024)(128)(4,1)}), s8[262144]{0:T(1024)(128)(4,1)S(1)}, s32[]{:S(2)}) async-start(s8[4456448]{0:T(1024)(128)(4,1)} %bitcast.150), calls=%async_computation.6 | async-start | bytes 524288
  70.8 18.2 %copy-start.17 = (f32[16,2]{0,1:T(2,128)S(1)}, f32[16,2]{0,1:T(2,128)}, u32[]{:S(2)}) copy-start(f32[16,2]{0,1:T(2,128)} %copy-done.16) | copy-start | bytes 388
  70.8 37.2 %copy-start.14 = (s32[1024]{0:T(1024)S(1)}, s32[1024]{0:T(1024)}, u32[]{:S(2)}) copy-start(s32[1024]{0:T(1024)} %pad_clamp_fusion.1) | copy-start | bytes 12292
  77.3 22.2 %all-to-all-start.1 = ((f32[32,2,16]{2,1,0:T(2,128)}), f32[32,2,16]{2,1,0:T(2,128)S(1)}, u32[]{:S(2)}, u32[]{:S(2)}) async-start(f32[32,2,16]{2,1,0:T(2,128)} %broadcast_in_dim.32), calls=%async_computation.1 | async-start | bytes 65536 | tf_op jit(solution)/shard_map/all_to_all | solution.py:36
  87.4 19.9 %collective-permute-start.5 = (f32[16,6,320]{2,0,1:T(8,128)}, f32[16,6,320]{2,0,1:T(8,128)S(1)}, u32[]{:S(2)}, u32[]{:S(2)}) collective-permute-start(f32[16,6,320]{2,0,1:T(8,128)} %get-tuple-element.23), channel_id=1, source_target_pairs={{0,1},{1,2},{2,3},{3,4},{4,5},{5,6},{6,7},{7,8},{8,9},{9,10},{10,1... | collective-permute-start | bytes 368648 | tf_op jit(solution)/shard_map/ppermute | solution.py:24
  89.0 18.3 %collective-permute-start.4 = (f32[16,6,320]{2,0,1:T(8,128)S(1)}, f32[16,6,320]{2,0,1:T(8,128)S(1)}, u32[]{:S(2)}, u32[]{:S(2)}) collective-permute-start(f32[16,6,320]{2,0,1:T(8,128)S(1)} %get-tuple-element.22), channel_id=1, source_target_pairs={{1,0},{2,1},{3,2},{4,3},{5,4},{6,5},{7,6},{8,7},{9,8},{10,9},{11,1... | collective-permute-start | bytes 368648 | tf_op jit(solution)/shard_map/ppermute | solution.py:26
  100.4 21.3 %all-to-all-start.2 = ((f32[16,1,2080]{2,1,0:T(1,128)}), f32[16,1,2080]{2,1,0:T(1,128)}, u32[]{:S(2)}, u32[]{:S(2)}) async-start(f32[16,1,2080]{2,1,0:T(1,128)} %broadcast_in_dim.33), calls=%async_computation.2 | async-start | bytes 278528 | tf_op jit(solution)/shard_map/all_to_all | solution.py:36
  108.0 9.0 %slice-start.2 = ((s8[4456448]{0:T(1024)(128)(4,1)}), s8[262144]{0:T(1024)(128)(4,1)S(1)}, s32[]{:S(2)}) async-start(s8[4456448]{0:T(1024)(128)(4,1)} %bitcast.152), calls=%async_computation.7 | async-start | bytes 524288
  109.5 7.5 %slice-start.3 = ((s8[4456448]{0:T(1024)(128)(4,1)}), s8[4194304]{0:T(1024)(128)(4,1)S(1)}, s32[]{:S(2)}) async-start(s8[4456448]{0:T(1024)(128)(4,1)} %bitcast.152), calls=%async_computation.8 | async-start | bytes 8388608
  109.5 7.6 %copy-start.8 = (f32[16,6,320]{2,0,1:T(8,128)S(1)}, f32[16,6,320]{2,0,1:T(8,128)}, u32[]{:S(2)}) copy-start(f32[16,6,320]{2,0,1:T(8,128)} %copy-done.7) | copy-start | bytes 368644
  120.7 6.4 %copy-start.9 = (f32[16,16,256]{2,0,1:T(8,128)S(1)}, f32[16,16,256]{2,0,1:T(8,128)}, u32[]{:S(2)}) copy-start(f32[16,16,256]{2,0,1:T(8,128)} %fusion.62) | copy-start | bytes 786436
  (17 other events, 70.3 us)

commit v13 on v12

--- a/solution.py
+++ b/solution.py
@@ -105,6 +105,22 @@
         jnp.float32
     )
 
+    far_steps = [step for step in range(-REACH, REACH + 1) if abs(step) >= 3]
+    far_pick = [
+        (far_rows == jnp.arange(local_leaves, dtype=jnp.int32)[:, None] + REACH + step).astype(
+            jnp.float32
+        )
+        for step in far_steps
+    ]
+
+    def far_coeffs(rim_coeffs):
+        picked = None
+        for step, pick in zip(far_steps, far_pick):
+            near_slice = rim_coeffs[:, REACH + step : REACH + step + local_leaves]
+            term = pick[None, :, :, None] * near_slice[:, :, None, :]
+            picked = term if picked is None else picked + term
+        return picked
+
     def covariance_local(direction):
         coeffs = jnp.einsum("lpr,mlp->mlr", leaf_basis, direction, precision=MATMUL_PRECISION)
         joined = jnp.concatenate([direction, coeffs], axis=2)
@@ -133,7 +149,7 @@
                 "iqp,miq->mip", behind, offset_values(-step), precision=MATMUL_PRECISION
             )
         leaf_far = jnp.einsum(
-            "lsab,mlsb->mla", leaf_couple, rim_coeffs[:, far_rows], precision=MATMUL_PRECISION
+            "lsab,mlsb->mla", leaf_couple, far_coeffs(rim_coeffs), precision=MATMUL_PRECISION
         )
         upward = jnp.einsum("lab,mla->mlb", transfer, coeffs, precision=MATMUL_PRECISION)
         panel_coeffs = jnp.sum(membership[None, :, :, None] * upward[:, :, None, :], axis=1)

time: 163 us -> 172 us (1.055)
  local copies, waits for them, and re-layouts: 19.2 us -> 24.7 us
  other arithmetic: 17.5 us -> 22.6 us
  waiting for transfers between devices: 10.2 us -> 6.67 us
    convert_element_type x0 -> x8, local copies, waits for them, and re-layouts: none -> 4.23 us  [on_device(): (far_rows == jnp.arange(local_leaves, dtype=jnp.int32)[:, None] + REACH +...]
    all_to_all x3, waiting for transfers between devices: 10.2 us -> 6.66 us  [gathered(): return lax.all_to_all(copies, axis, 0, 0, tiled=False)]
    all_to_all x3, starting transfers between devices: 23.8 us -> 20.3 us  [gathered(): return lax.all_to_all(copies, axis, 0, 0, tiled=False)]
    gather x2 -> x0, local copies, waits for them, and re-layouts: 2.98 us -> none  [covariance_local(): rim_coeffs[:, far_rows]]
    ppermute x3, starting transfers between devices: 1.65 us -> 4.47 us  [extended(): lax.ppermute(tail, axis, [(i, (i + 1) % count) for i in range(count)])]
    dot_general x4, matrix products: 9.56 us -> 11.8 us  [covariance_local(): jnp.einsum('iqp,miq->mip', behind, offset_values(-step), precision=MATMUL...]
    unnamed x85 -> x103, local copies, waits for them, and re-layouts: 5.26 us -> 4 us
  transfers between devices with their start and end apart: 9 -> 9, of which waited for: 1 -> 1; matrix products, arithmetic and copies ran while one was open for 29% -> 33% of each run, Pallas kernels for 0% -> 0%
where the time goes in v13:
time: 172 us; the launch traced here: 170 us
  matrix products  47.5 us (28%)
  starting transfers between devices  36 us (21%)
  blocking collectives  31 us (18%)
  local copies, waits for them, and re-layouts  24.7 us (14%)
  other arithmetic  22.6 us (13%)
  waiting for transfers between devices  6.67 us (4%)
    all_to_all x2, blocking collectives, gathered(): return lax.all_to_all(copies, axis, 0, 0, tiled=False)  31 us
    all_to_all x3, starting transfers between devices, gathered(): return lax.all_to_all(copies, axis, 0, 0, tiled=False)  20.3 us
    dot_general x4, matrix products, covariance_local(): jnp.einsum('iqp,miq->mip', behind, offset_values(-step), precision=MATMUL...  11.8 us
    dot_general x2, matrix products, covariance_local(): jnp.einsum('ipq,miq->mip', same_blocks, offset_values(0), precision=MATMU...  11.5 us
    ppermute x3, starting transfers between devices, extended(): lax.ppermute(head, axis, [((i + 1) % count, i) for i in range(count)])  11.3 us
    dot_general x4, matrix products, covariance_local(): jnp.einsum('ipq,miq->mip', ahead, offset_values(step), precision=MATMUL_P...  10.2 us
    mul x2, other arithmetic, matern_shape(): return (1.0 + scaled) * jnp.exp(-scaled)  9.76 us
    all_to_all x3, waiting for transfers between devices, gathered(): return lax.all_to_all(copies, axis, 0, 0, tiled=False)  6.66 us
  transfers between devices with their start and end apart: 9, of which 1 were waited for; matrix products, arithmetic and copies ran while one was open for 33% of the time, Pallas kernels for 0%

profile of v13, /device:TPU:1, one launch (start us, length us, event | category | flops | bytes accessed | tf_op | source)
XLA Modules:
  0.0 170.1 jit_solution(16425566807258052405)
XLA Ops:
  1.6 3.0 %collective-permute-start.1 = (f32[3,2,256]{2,1,0:T(2,128)S(1)}, f32[3,2,256]{2,1,0:T(2,128)S(1)}, u32[]{:S(2)}, u32[]{:S(2)}) collective-permute-start(f32[3,2,256]{2,1,0:T(2,128)S(1)} %get-tuple-element.63), channel_id=1, source_target_pairs={{0,1},{1,2},{2,3},{3,4},{4,5},{5,6},{6,7},{7,8},{8,9},{9,10},{10,1... | collective-permute-start | bytes 18440 | tf_op jit(solution)/shard_map/ppermute | solution.py:24
  4.6 3.9 %collective-permute-start.2 = (f32[3,2,256]{2,1,0:T(2,128)S(1)}, f32[3,2,256]{2,1,0:T(2,128)S(1)}, u32[]{:S(2)}, u32[]{:S(2)}) collective-permute-start(f32[3,2,256]{2,1,0:T(2,128)S(1)} %get-tuple-element.64), channel_id=1, source_target_pairs={{1,0},{2,1},{3,2},{4,3},{5,4},{6,5},{7,6},{8,7},{9,8},{10,9},{11,1... | collective-permute-start | bytes 18440 | tf_op jit(solution)/shard_map/ppermute | solution.py:26
  9.2 1.9 %convolution_bitcast_fusion.7 = f32[16,16,64]{2,0,1:T(8,128)S(1)} fusion(f32[16,256,64]{1,2,0:T(8,128)} %param.14, f32[16,16,256]{2,1,0:T(8,128)} %param.11), kind=kOutput, calls=%fused_computation.66 | convolution fusion | flops 25165824 | bytes 1376256 | tf_op jit(solution)/shard_map/lpr,mlp->mlr/dot_general | solution.py:125
  13.5 3.5 %all-to-all-start = ((f32[16,1,2048]{2,1,0:T(1,128)}), f32[16,1,2048]{2,1,0:T(1,128)S(1)}, u32[]{:S(2)}, u32[]{:S(2)}) async-start(f32[16,1,2048]{2,1,0:T(1,128)} %broadcast_in_dim.27), calls=%async_computation | async-start | bytes 262144 | tf_op jit(solution)/shard_map/all_to_all | solution.py:36
  18.8 7.1 %collective-permute-start = (f32[16,6,320]{2,0,1:T(8,128)}, f32[16,6,320]{2,0,1:T(8,128)}, u32[]{:S(2)}, u32[]{:S(2)}) collective-permute-start(f32[16,6,320]{2,0,1:T(8,128)} %get-tuple-element.46), channel_id=1, source_target_pairs={{1,0},{2,1},{3,2},{4,3},{5,4},{6,5},{7,6},{8,7},{9,8},{10,9},{11,1... | collective-permute-start | bytes 368648 | tf_op jit(solution)/shard_map/ppermute | solution.py:26
  27.6 5.7 %fusion.17 = f32[16,16,256]{2,1,0:T(8,128)} fusion(f32[16,256]{1,0:T(8,128)S(1)} %get-tuple-element.61, f32[16,256]{1,0:T(8,128)S(1)} %get-tuple-element.62, f32[16,256]{1,0:T(8,128)S(1)} %get-tuple-element.60, f32[16]{0:T(128)S(1)} %get-tuple-element.69, f32[16,16,256]{2,1,0:T(8,128)S(1)} %copy-done.2), kind=kOutput, calls=%fused_computation.22 | convolution fusion | flops 113311744 | bytes 573504 | tf_op jit(solution)/shard_map/ipq,miq->mip/dot_general | solution.py:138
  38.2 5.2 %exponential_multiply_fusion = f32[18,256,256]{2,1,0:T(8,128)} fusion(f32[18,256]{1,0:T(8,128)S(1)} %get-tuple-element.52, f32[18,256]{1,0:T(8,128)S(1)} %get-tuple-element.58, f32[18,256]{1,0:T(8,128)S(1)} %get-tuple-element.53, f32[18,256]{1,0:T(8,128)S(1)} %get-tuple-element.59, f32[18,256]{1,0:T(8,128)S(1)} %get-tuple-element.51, ...), kind=kLoop, calls=%fused_computation.2 | loop fusion | flops 14155776 | bytes 4829184 | tf_op jit(solution)/shard_map/mul | solution.py:51
  43.5 4.6 %exponential_multiply_fusion.1 = f32[17,256,256]{2,1,0:T(8,128)} fusion(f32[17,256]{1,0:T(8,128)S(1)} %get-tuple-element.49, f32[17,256]{1,0:T(8,128)S(1)} %get-tuple-element.56, f32[17,256]{1,0:T(8,128)S(1)} %get-tuple-element.50, f32[17,256]{1,0:T(8,128)S(1)} %get-tuple-element.55, f32[17,256]{1,0:T(8,128)S(1)} %get-tuple-element.48, ...), kind=kLoop, calls=%fused_computation.3 | loop fusion | flops 13369344 | bytes 4560896 | tf_op jit(solution)/shard_map/mul | solution.py:51
  49.3 1.6 gather_fusion
  53.3 3.5 %fusion.2 = f32[16,16,256]{2,1,0:T(8,128)S(1)} fusion(f32[18,256,256]{2,1,0:T(8,128)} %exponential_multiply_fusion, f32[16,22,320]{2,0,1:T(8,128)S(1)} %get-tuple-element.45, f32[16]{0:T(128)S(1)} %copy-done.37), kind=kOutput, calls=%fused_computation.7 | convolution fusion | flops 100728832 | bytes 4719104 | tf_op jit(solution)/shard_map/iqp,miq->mip/dot_general | solution.py:148
  56.8 1.7 %fusion.6 = f32[16,16,256]{2,1,0:T(8,128)S(1)} fusion(f32[18,256,256]{2,1,0:T(8,128)S(1)} %bitcast.147, f32[16,22,320]{2,0,1:T(8,128)S(1)} %get-tuple-element.44, f32[16]{0:T(128)S(1)} %copy-done.33), kind=kOutput, calls=%fused_computation.11 | convolution fusion | flops 100728832 | bytes 4719104 | tf_op jit(solution)/shard_map/ipq,miq->mip/dot_general | solution.py:145
  58.7 1.5 convolution_bitcast_fusion.5
  60.7 1.4 fusion.10
  62.2 1.9 %fusion.71 = f32[16,16,256]{2,0,1:T(8,128)S(1)} fusion(f32[16,16,256]{2,1,0:T(8,128)S(1)} %fusion.2, f32[16,16,256]{2,1,0:T(8,128)S(1)} %fusion.6, f32[16,16,256]{2,1,0:T(8,128)S(1)} %fusion.10, f32[16,16,256]{2,1,0:T(8,128)S(1)} %copy-done.7, f32[17,256,256]{2,1,0:T(8,128)S(1)} %bitcast.143, f32[16,22,320]{2,0,1:T(8,128)S(1)} %get-tuple-element.44, ...), kind=kOutput, calls=%fused_computation.56 | convolution fusion | flops 101122048 | bytes 6046208 | tf_op jit(solution)/shard_map/ipq,miq->mip/dot_general | solution.py:145
  65.2 5.8 %fusion.16 = f32[16,16,256]{2,1,0:T(8,128)} fusion(f32[16,256]{1,0:T(8,128)S(1)} %copy-done.28, f32[16,256]{1,0:T(8,128)S(1)} %copy-done.30, f32[16,256]{1,0:T(8,128)S(1)} %copy-done.26, f32[16,16,256]{2,0,1:T(8,128)S(1)} %get-tuple-element.78, f32[16]{0:T(128)S(1)} %copy-done.42), kind=kOutput, calls=%fused_computation.21 | convolution fusion | flops 113311744 | bytes 573504 | tf_op jit(solution)/shard_map/ipq,miq->mip/dot_general | solution.py:138
  73.4 9.8 %all-to-all-start.1 = ((f32[32,2,16]{2,1,0:T(2,128)}), f32[32,2,16]{2,1,0:T(2,128)}, u32[]{:S(2)}, u32[]{:S(2)}) async-start(f32[32,2,16]{2,1,0:T(2,128)} %broadcast_in_dim.29), calls=%async_computation.1 | async-start | bytes 65536 | tf_op jit(solution)/shard_map/all_to_all | solution.py:36
  84.5 1.4 collective-permute-start.5
  86.0 1.4 multiply_reduce_fusion.7
  88.7 6.7 %all-to-all-done.1 = f32[32,2,16]{2,1,0:T(2,128)} async-done(((f32[32,2,16]{2,1,0:T(2,128)}), f32[32,2,16]{2,1,0:T(2,128)}, u32[]{:S(2)}, u32[]{:S(2)}) %all-to-all-start.1) | async-done | bytes 4128 | tf_op jit(solution)/shard_map/all_to_all | solution.py:36
  99.4 7.0 %all-to-all-start.2 = ((f32[16,1,2080]{2,1,0:T(1,128)}), f32[16,1,2080]{2,1,0:T(1,128)}, u32[]{:S(2)}, u32[]{:S(2)}) async-start(f32[16,1,2080]{2,1,0:T(1,128)} %broadcast_in_dim.30), calls=%async_computation.2 | async-start | bytes 278528 | tf_op jit(solution)/shard_map/all_to_all | solution.py:36
  107.5 3.5 %fusion = f32[16,16,256]{2,1,0:T(8,128)S(1)} fusion(f32[18,256,256]{2,1,0:T(8,128)} %exponential_multiply_fusion, f32[16,22,320]{2,0,1:T(8,128)S(1)} %get-tuple-element.41, f32[16]{0:T(128)} %get-tuple-element.66), kind=kOutput, calls=%fused_computation.5 | convolution fusion | flops 100728832 | bytes 4719104 | tf_op jit(solution)/shard_map/iqp,miq->mip/dot_general | solution.py:148
  111.0 3.4 %fusion.8 = f32[16,16,256]{2,1,0:T(8,128)S(1)} fusion(f32[17,256,256]{2,1,0:T(8,128)} %exponential_multiply_fusion.1, f32[16,22,320]{2,0,1:T(8,128)S(1)} %get-tuple-element.41, f32[16]{0:T(128)S(1)} %copy-done.36), kind=kOutput, calls=%fused_computation.13 | convolution fusion | flops 100728832 | bytes 4719104 | tf_op jit(solution)/shard_map/iqp,miq->mip/dot_general | solution.py:148
  114.4 4.0 %fusion.4 = f32[16,16,256]{2,1,0:T(8,128)S(1)} fusion(f32[18,256,256]{2,1,0:T(8,128)} %exponential_multiply_fusion, f32[16,22,320]{2,0,1:T(8,128)S(1)} %get-tuple-element.40, f32[16]{0:T(128)S(1)} %copy-done.34), kind=kOutput, calls=%fused_computation.9 | convolution fusion | flops 100728832 | bytes 4719104 | tf_op jit(solution)/shard_map/ipq,miq->mip/dot_general | solution.py:145
  118.6 2.6 %fusion.62 = f32[16,16,256]{2,0,1:T(8,128)} fusion(f32[16,16,256]{2,1,0:T(8,128)S(1)} %fusion, f32[16,16,256]{2,1,0:T(8,128)S(1)} %fusion.4, f32[16,16,256]{2,1,0:T(8,128)S(1)} %fusion.8, f32[16,16,256]{2,1,0:T(8,128)S(1)} %copy-done.8, f32[17,256,256]{2,1,0:T(8,128)S(1)} %bitcast.145, f32[16,22,320]{2,0,1:T(8,128)S(1)} %get-tuple-element.40, ...), kind=kOutput, calls=%fused_computation.53 | convolution fusion | flops 101122048 | bytes 6046208 | tf_op jit(solution)/shard_map/ipq,miq->mip/dot_general | solution.py:145
  121.2 1.5 convolution_bitcast_fusion.2
  124.4 1.8 %reshape.195 = f32[16,16,2,64]{3,2,1,0:T(2,128)} reshape(f32[16,2048]{1,0:T(8,128)} %slice.365) | data formatting | bytes 262144 | tf_op jit(solution)/shard_map/reshape | solution.py:159
  126.2 1.7 copy.193
  127.9 2.2 %gather_fusion.1 = f32[4,16,64]{2,1,0:T(8,128)} fusion(f32[16,32,64]{2,0,1:T(8,128)} %bitcast.152, s32[1024]{0:T(1024)} %pad_clamp_fusion), kind=kCustom, calls=%fused_computation.1 | custom fusion | bytes 32784 | tf_op jit(solution)/shard_map/gather | solution.py:169
  132.0 1.6 fusion.74
  133.6 2.4 %multiply_reduce_fusion.4 = (f32[16]{0:T(128)S(1)}, f32[16]{0:T(128)S(1)}, f32[16]{0:T(128)S(1)}, f32[16]{0:T(128)S(1)}, f32[16,16,256]{2,0,1:T(8,128)}) fusion(f32[16,16,256]{2,0,1:T(8,128)S(1)} %get-tuple-element.78, f32[16]{0:T(128)S(1)} %slice_divide_fusion, f32[16,16,256]{2,1,0:T(8,128)} %param.11, f32[16,16,256]{2,0,1:T(8,128)} %fusion.62, ...), kind=kOutput, calls=%fused_computation.126 | convolution fusion | flops 26017728 | bytes 2163008 | tf_op jit(solution)/shard_map/lpr,mlr->mlp/dot_general | solution.py:176
  136.0 18.2 %all_to_all.30 = f32[32,4,16]{2,1,0:T(4,128)S(1)} all-to-all(f32[32,4,16]{2,1,0:T(4,128)S(1)} %broadcast_in_dim.31), channel_id=1, replica_groups=mesh['band'=16,'lon'=32] {'lon'}, dimensions={0} | all-to-all | bytes 16384 | tf_op jit(solution)/shard_map/all_to_all | solution.py:36
  154.2 12.9 %all_to_all.31 = f32[16,4,16]{2,1,0:T(4,128)S(1)} all-to-all(f32[16,4,16]{2,1,0:T(4,128)S(1)} %broadcast_in_dim.32), channel_id=1, replica_groups=mesh['band'=16,'lon'=32] {'band'}, dimensions={0} | all-to-all | bytes 8192 | tf_op jit(solution)/shard_map/all_to_all | solution.py:36
  (192 shorter events, 34.4 us)
Async XLA Ops:
  0.6 57.9 %copy-start = (f32[16,4,64,64]{3,2,1,0:T(8,128)S(1)}, f32[16,4,64,64]{3,2,1,0:T(8,128)}, u32[]{:S(2)}) copy-start(f32[16,4,64,64]{3,2,1,0:T(8,128)} %param.15) | copy-start | bytes 3145732
  0.6 26.1 %copy-start.5 = (f32[3,16,256]{2,1,0:T(8,128)S(1)}, f32[3,16,256]{2,1,0:T(8,128)}, u32[]{:S(2)}) copy-start(f32[3,16,256]{2,1,0:T(8,128)} %param.13) | copy-start | bytes 147460
  0.7 25.3 %copy-start.2 = (f32[16,16,256]{2,1,0:T(8,128)S(1)}, f32[16,16,256]{2,1,0:T(8,128)}, u32[]{:S(2)}) copy-start(f32[16,16,256]{2,1,0:T(8,128)} %param.11) | copy-start | bytes 786436
  0.7 26.0 %copy-start.24 = (s32[16,5]{0,1:T(8,128)S(1)}, s32[16,5]{0,1:T(8,128)}, u32[]{:S(2)}) copy-start(s32[16,5]{0,1:T(8,128)} %param.18) | copy-start | bytes 964
  0.7 26.1 %copy-start.40 = (s32[2,2]{1,0:T(2,128)S(1)}, s32[2,2]{1,0:T(2,128)}, u32[]{:S(2)}) copy-start(s32[2,2]{1,0:T(2,128)} %param.20) | copy-start | bytes 52
  0.7 26.2 %copy-start.39 = (s32[16,4]{0,1:T(4,128)S(1)}, s32[16,4]{0,1:T(4,128)}, u32[]{:S(2)}) copy-start(s32[16,4]{0,1:T(4,128)} %param.19) | copy-start | bytes 772
  1.6 36.6 %collective-permute-start.1 = (f32[3,2,256]{2,1,0:T(2,128)S(1)}, f32[3,2,256]{2,1,0:T(2,128)S(1)}, u32[]{:S(2)}, u32[]{:S(2)}) collective-permute-start(f32[3,2,256]{2,1,0:T(2,128)S(1)} %get-tuple-element.63), channel_id=1, source_target_pairs={{0,1},{1,2},{2,3},{3,4},{4,5},{5,6},{6,7},{7,8},{8,9},{9,10},{10,1... | collective-permute-start | bytes 18440 | tf_op jit(solution)/shard_map/ppermute | solution.py:24
  4.6 33.5 %collective-permute-start.2 = (f32[3,2,256]{2,1,0:T(2,128)S(1)}, f32[3,2,256]{2,1,0:T(2,128)S(1)}, u32[]{:S(2)}, u32[]{:S(2)}) collective-permute-start(f32[3,2,256]{2,1,0:T(2,128)S(1)} %get-tuple-element.64), channel_id=1, source_target_pairs={{1,0},{2,1},{3,2},{4,3},{5,4},{6,5},{7,6},{8,7},{9,8},{10,9},{11,1... | collective-permute-start | bytes 18440 | tf_op jit(solution)/shard_map/ppermute | solution.py:26
  13.5 34.6 %all-to-all-start = ((f32[16,1,2048]{2,1,0:T(1,128)}), f32[16,1,2048]{2,1,0:T(1,128)S(1)}, u32[]{:S(2)}, u32[]{:S(2)}) async-start(f32[16,1,2048]{2,1,0:T(1,128)} %broadcast_in_dim.27), calls=%async_computation | async-start | bytes 262144 | tf_op jit(solution)/shard_map/all_to_all | solution.py:36
  18.8 33.1 %collective-permute-start = (f32[16,6,320]{2,0,1:T(8,128)}, f32[16,6,320]{2,0,1:T(8,128)}, u32[]{:S(2)}, u32[]{:S(2)}) collective-permute-start(f32[16,6,320]{2,0,1:T(8,128)} %get-tuple-element.46), channel_id=1, source_target_pairs={{1,0},{2,1},{3,2},{4,3},{5,4},{6,5},{7,6},{8,7},{9,8},{10,9},{11,1... | collective-permute-start | bytes 368648 | tf_op jit(solution)/shard_map/ppermute | solution.py:26
  25.9 26.0 %collective-permute-start.3 = (f32[16,6,320]{2,0,1:T(8,128)}, f32[16,6,320]{2,0,1:T(8,128)}, u32[]{:S(2)}, u32[]{:S(2)}) collective-permute-start(f32[16,6,320]{2,0,1:T(8,128)} %get-tuple-element.47), channel_id=1, source_target_pairs={{0,1},{1,2},{2,3},{3,4},{4,5},{5,6},{6,7},{7,8},{8,9},{9,10},{10,1... | collective-permute-start | bytes 368648 | tf_op jit(solution)/shard_map/ppermute | solution.py:24
  26.8 6.6 %copy-start.25 = (f32[16,256]{1,0:T(8,128)}, f32[16,256]{1,0:T(8,128)S(1)}, u32[]{:S(2)}) copy-start(f32[16,256]{1,0:T(8,128)S(1)} %get-tuple-element.60) | copy-start | bytes 49156
  26.8 6.6 %copy-start.27 = (f32[16,256]{1,0:T(8,128)}, f32[16,256]{1,0:T(8,128)S(1)}, u32[]{:S(2)}) copy-start(f32[16,256]{1,0:T(8,128)S(1)} %get-tuple-element.61) | copy-start | bytes 49156
  26.8 6.5 %copy-start.29 = (f32[16,256]{1,0:T(8,128)}, f32[16,256]{1,0:T(8,128)S(1)}, u32[]{:S(2)}) copy-start(f32[16,256]{1,0:T(8,128)S(1)} %get-tuple-element.62) | copy-start | bytes 49156
  27.6 5.7 %copy-start.41 = (f32[16]{0:T(128)}, f32[16]{0:T(128)S(1)}, u32[]{:S(2)}) copy-start(f32[16]{0:T(128)S(1)} %get-tuple-element.69) | copy-start | bytes 196
  43.4 7.5 %copy-start.6 = (f32[2,2,64,64]{3,2,1,0:T(8,128)S(1)}, f32[2,2,64,64]{3,2,1,0:T(8,128)}, u32[]{:S(2)}) copy-start(f32[2,2,64,64]{3,2,1,0:T(8,128)} %param.17) | copy-start | bytes 196612
  43.4 13.3 %slice-start.4 = ((s8[4718592]{0:T(1024)(128)(4,1)}), s8[524288]{0:T(1024)(128)(4,1)S(1)}, s32[]{:S(2)}) async-start(s8[4718592]{0:T(1024)(128)(4,1)} %bitcast.146), calls=%async_computation.9 | async-start | bytes 1048576
  51.9 4.9 %slice-start.5 = ((s8[4718592]{0:T(1024)(128)(4,1)}), s8[4194304]{0:T(1024)(128)(4,1)S(1)}, s32[]{:S(2)}) async-start(s8[4718592]{0:T(1024)(128)(4,1)} %bitcast.146), calls=%async_computation.10 | async-start | bytes 8388608
  53.2 5.4 %copy-start.9 = (f32[16,4]{1,0:T(8,128)S(1)}, f32[16,4]{1,0:T(8,128)}, u32[]{:S(2)}) copy-start(f32[16,4]{1,0:T(8,128)} %copy.182) | copy-start | bytes 772
  53.2 5.4 %copy-start.11 = (f32[16,4]{1,0:T(8,128)S(1)}, f32[16,4]{1,0:T(8,128)}, u32[]{:S(2)}) copy-start(f32[16,4]{1,0:T(8,128)} %copy.181) | copy-start | bytes 772
  53.2 5.4 %copy-start.13 = (f32[16,4]{1,0:T(8,128)S(1)}, f32[16,4]{1,0:T(8,128)}, u32[]{:S(2)}) copy-start(f32[16,4]{1,0:T(8,128)} %copy.180) | copy-start | bytes 772
  53.2 5.4 %copy-start.15 = (f32[16,4]{1,0:T(8,128)S(1)}, f32[16,4]{1,0:T(8,128)}, u32[]{:S(2)}) copy-start(f32[16,4]{1,0:T(8,128)} %copy.179) | copy-start | bytes 772
  53.3 5.4 %copy-start.17 = (f32[16,4]{1,0:T(8,128)S(1)}, f32[16,4]{1,0:T(8,128)}, u32[]{:S(2)}) copy-start(f32[16,4]{1,0:T(8,128)} %copy.178) | copy-start | bytes 772
  53.3 5.4 %copy-start.19 = (f32[16,4]{1,0:T(8,128)S(1)}, f32[16,4]{1,0:T(8,128)}, u32[]{:S(2)}) copy-start(f32[16,4]{1,0:T(8,128)} %copy.183) | copy-start | bytes 772
  65.2 7.6 %copy-start.38 = (f32[16]{0:T(128)S(1)}, f32[16]{0:T(128)}, u32[]{:S(2)}) copy-start(f32[16]{0:T(128)} %multiply_reduce_fusion.6) | copy-start | bytes 196
  73.4 22.0 %all-to-all-start.1 = ((f32[32,2,16]{2,1,0:T(2,128)}), f32[32,2,16]{2,1,0:T(2,128)}, u32[]{:S(2)}, u32[]{:S(2)}) async-start(f32[32,2,16]{2,1,0:T(2,128)} %broadcast_in_dim.29), calls=%async_computation.1 | async-start | bytes 65536 | tf_op jit(solution)/shard_map/all_to_all | solution.py:36
  84.2 22.1 %collective-permute-start.4 = (f32[16,6,320]{2,0,1:T(8,128)}, f32[16,6,320]{2,0,1:T(8,128)}, u32[]{:S(2)}, u32[]{:S(2)}) collective-permute-start(f32[16,6,320]{2,0,1:T(8,128)} %get-tuple-element.42), channel_id=1, source_target_pairs={{1,0},{2,1},{3,2},{4,3},{5,4},{6,5},{7,6},{8,7},{9,8},{10,9},{11,1... | collective-permute-start | bytes 368648 | tf_op jit(solution)/shard_map/ppermute | solution.py:26
  84.5 21.8 %collective-permute-start.5 = (f32[16,6,320]{2,0,1:T(8,128)}, f32[16,6,320]{2,0,1:T(8,128)}, u32[]{:S(2)}, u32[]{:S(2)}) collective-permute-start(f32[16,6,320]{2,0,1:T(8,128)} %get-tuple-element.43), channel_id=1, source_target_pairs={{0,1},{1,2},{2,3},{3,4},{4,5},{5,6},{6,7},{7,8},{8,9},{9,10},{10,1... | collective-permute-start | bytes 368648 | tf_op jit(solution)/shard_map/ppermute | solution.py:24
  99.4 23.4 %all-to-all-start.2 = ((f32[16,1,2080]{2,1,0:T(1,128)}), f32[16,1,2080]{2,1,0:T(1,128)}, u32[]{:S(2)}, u32[]{:S(2)}) async-start(f32[16,1,2080]{2,1,0:T(1,128)} %broadcast_in_dim.30), calls=%async_computation.2 | async-start | bytes 278528 | tf_op jit(solution)/shard_map/all_to_all | solution.py:36
  107.4 7.0 %copy-start.34 = (f32[16]{0:T(128)S(1)}, f32[16]{0:T(128)}, u32[]{:S(2)}) copy-start(f32[16]{0:T(128)} %get-tuple-element.67) | copy-start | bytes 196
  107.4 11.1 %slice-start.2 = ((s8[4456448]{0:T(1024)(128)(4,1)}), s8[4194304]{0:T(1024)(128)(4,1)S(1)}, s32[]{:S(2)}) async-start(s8[4456448]{0:T(1024)(128)(4,1)} %bitcast.144), calls=%async_computation.7 | async-start | bytes 8388608
  111.0 7.6 %slice-start.3 = ((s8[4456448]{0:T(1024)(128)(4,1)}), s8[262144]{0:T(1024)(128)(4,1)S(1)}, s32[]{:S(2)}) async-start(s8[4456448]{0:T(1024)(128)(4,1)} %bitcast.144), calls=%async_computation.8 | async-start | bytes 524288
  (26 other events, 91.0 us)
